TPU v7x, 128 devices: a whole 4x4x4 slice. The times are simulated.
128 devices in a mesh: sens: 8 (over z, x_hi), loc: 16 (over y, x_lo, core).
Axes of the slice: x: 4 (x_hi: 2, x_lo: 2; x = x_hi * 2 + x_lo), y: 4, z: 4, core: 2. Of those that a mesh axis runs over, the one named last changes fastest.
Arguments:
- green: bfloat16 [16384, 48, 3, 256], P('loc', 'sens'), may hold values from -0.03125 to 0.03125
- records_buffer: bfloat16 [16, 2, 48, 3, 1024], P('loc', None, 'sens'), may hold values from -6 to 6
- owners: int32 [2], replicated, may hold values from 0 to 15
- onsets: int32 [2, 48], P(None, 'sens'), may hold values from 0 to 257
- codes: int32 [48, 3], P('sens'), may hold values from 0 to 3
Outputs:
- stack: float32 [16384, 2, 512], P(('loc', 'sens'))
Inputs may be any that keep to these rules, and one draw needn't show every extreme that they name: `onsets`: a window of 767 samples starting at the offset lies inside the record. `owners`: the block whose buffer holds the event's records. `codes`: a component with code q has weight 2 to the power -q.
All inputs are finite; a program needn't handle non-finite values.
Results may differ from a plain program's by a relative error of at most 0.0003.
Values may be sent and summed in bfloat16 or wider, within the bound.
No kernel may reach another device: no remote copies, remote signals or barrier semaphores. Data moves between devices by JAX's collectives and lax.ppermute only.
A program may use at most 128 MiB of HBM per device.

v0:
```python
import jax
import jax.numpy as jnp
from jax import lax
from jax.sharding import PartitionSpec as P

NT = 256
LAGS = 512
EV = 2


def from_root(x, axis, root):
    mine = lax.axis_index(axis) == root
    return lax.psum(jnp.where(mine, x, jnp.zeros_like(x)), axis)


def sensor_windows(traces, offsets, weight_codes, length, lag_count):

    def window_of(record_row, begin_at):
        return lax.dynamic_slice_in_dim(record_row, begin_at, length, 1)

    windows = jax.vmap(window_of)(traces, offsets)
    weighting = jnp.exp2(-weight_codes.astype(jnp.float32))
    weighted = (windows.astype(jnp.float32) * weighting[:, :, None]).astype(jnp.bfloat16)
    tap_count = length - lag_count + 1
    tiled = jnp.tile(weighted, (1, 1, tap_count))
    padded = jnp.concatenate(
        [tiled, jnp.zeros(weighted.shape[:2] + (tap_count,), jnp.bfloat16)], axis=2
    )
    shaped = padded.reshape(weighted.shape[0], 3, tap_count, length + 1)[..., :lag_count]
    return shaped.reshape(-1, lag_count)


def local(green, records_buffer, owners, onsets, codes):
    point_rows = green.shape[0]
    flat_green = green.reshape(point_rows, -1)
    length = NT + LAGS - 1
    blocks = []
    for event_idx in range(EV):
        root_dev = owners[event_idx]
        traces = from_root(records_buffer[0, event_idx], "loc", root_dev)
        operand = sensor_windows(traces, onsets[event_idx], codes, length, LAGS)
        blocks.append(operand)
    toeplitz = jnp.stack(blocks, axis=1).reshape(blocks[0].shape[0], -1)
    share = point_rows // lax.axis_size("sens")
    product = jnp.dot(flat_green, toeplitz, preferred_element_type=jnp.float32)
    totals = lax.psum(product.reshape(point_rows, EV, LAGS), "sens")
    return lax.dynamic_slice_in_dim(totals, lax.axis_index("sens") * share, share, 0)


def solution(mesh):
    return jax.shard_map(
        local,
        mesh=mesh,
        in_specs=(
            P("loc", "sens", None, None),
            P("loc", None, "sens", None, None),
            P(),
            P(None, "sens"),
            P("sens", None),
        ),
        out_specs=P(("loc", "sens"), None, None),
        check_vma=False,
    )
```

profile of v0, /device:TPU:0, one launch (start us, length us, event | category | flops | bytes accessed | tf_op | source)
XLA Modules:
  0.0 503.6 jit_solution(3373924187639122892)
XLA Ops:
  6.5 0.0 all-reduce.10.cloned.1.call-start
  6.5 1.3 fusion.9
  9.1 1.1 fusion.8
  10.2 1.5 copy.29
  11.7 2.3 copy.32
  14.0 0.0 copy-start
  14.0 0.0 copy-start.1
  14.0 2.3 select_bitcast_fusion
  16.3 0.0 all-reduce.10.cloned.1.call-update
  16.4 0.0 all-reduce.8.cloned.1.call-start
  16.4 0.0 copy-done
  16.4 0.0 copy-done.1
  16.5 12.7 %copy.36 = bf16[1024,6,3,256]{0,3,2,1:T(8,128)(2,1)} copy(bf16[1024,6,3,256]{3,0,2,1:T(8,128)(2,1)} %param.5) | data formatting | bytes 18874368 | tf_op args[0]
  29.2 126.7 %all-reduce.10.cloned.1.call-done = (bf16[6,3,1024]{1,0,2:T(8,128)(2,1)}, bf16[6,3,1024]{1,0,2:T(8,128)(2,1)}) async-done(((bf16[6,3,1024]{1,0,2:T(8,128)(2,1)}, bf16[6,3,1024]{1,0,2:T(8,128)(2,1)}), (bf16[6,3,1024]{1,0,2:T(8,128)(2,1)}, bf16[6,3,1024]{1,0,2:T(8,128)(2,1)})) %all-reduce.10.cloned.1.call-update) | async-done | bytes 73744 | tf_op jit(solution)/shard_map/psum | solution.py:13
  155.8 5.1 %gather_fusion.1 = bf16[6,3,767]{1,0,2:T(8,128)(2,1)S(1)} fusion(bf16[6,3,1024]{1,0,2:T(8,128)(2,1)} %get-tuple-element.5, s32[6]{0:T(128)S(1)} %get-tuple-element.12), kind=kCustom, calls=%fused_computation.1 | custom fusion | bytes 55296 | tf_op jit(solution)/shard_map/vmap()/gather | solution.py:19
  160.9 1.6 copy.33
  162.4 5.2 %gather_fusion = bf16[6,3,767]{1,0,2:T(8,128)(2,1)S(1)} fusion(bf16[6,3,1024]{1,0,2:T(8,128)(2,1)} %get-tuple-element.6, s32[6]{0:T(128)S(1)} %get-tuple-element.11), kind=kCustom, calls=%fused_computation | custom fusion | bytes 55296 | tf_op jit(solution)/shard_map/vmap()/gather | solution.py:19
  167.6 1.6 copy.30
  169.2 0.1 multiply_convert_fusion.1
  169.3 3.3 tile.8
  172.6 17.0 %tile.9 = bf16[6,3,196352]{2,0,1:T(8,128)(2,1)} reshape(bf16[6,3,256,767]{3,2,0,1:T(8,128)(2,1)} %tile.8) | data formatting | bytes 14137344 | tf_op jit(solution)/shard_map/tile | solution.py:25
  189.5 9.6 %concatenate.13 = bf16[6,3,196608]{2,0,1:T(8,128)(2,1)} pad(bf16[6,3,196352]{2,0,1:T(8,128)(2,1)} %tile.9, bf16[]{:T(256)} %constant.9.clone.1), padding=0_0x0_0x0_256 | pad | bytes 14146562 | tf_op jit(solution)/shard_map/concatenate | solution.py:26
  199.1 13.9 %reshape.94 = bf16[6,3,256,768]{3,2,0,1:T(8,128)(2,1)} reshape(bf16[6,3,196608]{2,0,1:T(8,128)(2,1)} %concatenate.13) | data formatting | bytes 14155776 | tf_op jit(solution)/shard_map/reshape | solution.py:29
  213.0 0.0 slice-start
  213.0 2.3 slice-done
  215.4 2.4 copy.31
  217.8 3.3 tile.20
  221.1 17.0 %tile.21 = bf16[6,3,196352]{2,0,1:T(8,128)(2,1)} reshape(bf16[6,3,256,767]{3,2,0,1:T(8,128)(2,1)} %tile.20) | data formatting | bytes 14137344 | tf_op jit(solution)/shard_map/tile | solution.py:25
  238.0 9.6 %concatenate.15 = bf16[6,3,196608]{2,0,1:T(8,128)(2,1)} pad(bf16[6,3,196352]{2,0,1:T(8,128)(2,1)} %tile.21, bf16[]{:T(256)} %constant.9.clone.1), padding=0_0x0_0x0_256 | pad | bytes 14146562 | tf_op jit(solution)/shard_map/concatenate | solution.py:26
  247.6 13.9 %reshape.95 = bf16[6,3,256,768]{3,2,0,1:T(8,128)(2,1)} reshape(bf16[6,3,196608]{2,0,1:T(8,128)(2,1)} %concatenate.15) | data formatting | bytes 14155776 | tf_op jit(solution)/shard_map/reshape | solution.py:29
  261.5 0.0 slice-start.1
  261.5 2.3 slice-done.1
  263.9 2.5 copy.34
  266.4 8.3 %pad_maximum_fusion = bf16[4608,2,512]{2,0,1:T(8,128)(2,1)} fusion(bf16[4608,1,512]{2,0,1:T(8,128)(2,1)} %bitcast.40, bf16[4608,1,512]{2,0,1:T(8,128)(2,1)} %bitcast.39), kind=kLoop, calls=%fused_computation.2 | loop fusion | flops 4718592 | bytes 18874368 | tf_op jit(solution)/shard_map/stack | solution.py:43
  274.7 12.2 %copy.35 = bf16[4608,2,512]{0,2,1:T(8,128)(2,1)} copy(bf16[4608,2,512]{2,0,1:T(8,128)(2,1)} %pad_maximum_fusion) | data formatting | bytes 18874368 | tf_op jit(solution)/shard_map/stack | solution.py:43
  286.8 16.0 %fusion.10 = f32[1024,1024]{1,0:T(8,128)} fusion(bf16[4608,1024]{0,1:T(8,128)(2,1)} %bitcast.42, bf16[1024,4608]{0,1:T(8,128)(2,1)} %bitcast.41), kind=kOutput, calls=%fused_computation.22 | convolution fusion | flops 9663676416 | bytes 23068672 | tf_op jit(solution)/shard_map/dot_general | solution.py:45
  302.8 7.2 %copy.37 = f32[1024,2,512]{2,1,0:T(2,128)} copy(f32[1024,2,512]{0,2,1:T(8,128)} %bitcast.43) | data formatting | bytes 8388608 | tf_op jit(solution)/shard_map/reshape | solution.py:46
  310.1 0.0 all-reduce.8.cloned.1.call-update
  310.1 184.8 %all-reduce.8.cloned.1.call-done = f32[1024,2,512]{2,1,0:T(2,128)} async-done(((f32[1024,2,512]{2,1,0:T(2,128)}), f32[1024,2,512]{2,1,0:T(2,128)}) %all-reduce.8.cloned.1.call-update) | async-done | bytes 4194320 | tf_op jit(solution)/shard_map/psum | solution.py:46
  494.9 1.9 constant_dynamic-slice_fusion
  (2 shorter events, 0.0 us)
Async XLA Ops:
  6.5 149.3 %all-reduce.10.cloned.1.call-start = ((), (), s32[]{:S(2)}) async-start(), calls=%async_computation.1 | async-start | bytes 8388608 | tf_op jit(solution)/shard_map/psum | solution.py:13
  14.0 2.4 copy-start
  14.0 2.4 copy-start.1
  16.4 478.6 %all-reduce.8.cloned.1.call-start = ((), (), s32[]{:S(2)}) async-start(), calls=%async_computation | async-start | bytes 8388608 | tf_op jit(solution)/shard_map/psum | solution.py:46
  213.0 2.3 slice-start
  261.5 2.3 slice-start.1
Sparse Core Ops, SparseCore 0:
  16.5 139.2 all-reduce.9
  310.2 184.6 all-reduce.7
where the time goes:
time: 505 us; the launch traced here: 504 us
  waiting for transfers between devices  312 us (62%)
  local copies, waits for them, and re-layouts  151 us (30%)
  matrix products  16 us (3%)
  between operations  14.7 us (3%)
  other arithmetic  10.7 us (2%)
    psum x1, waiting for transfers between devices, local(): totals = lax.psum(product.reshape(point_rows, EV, LAGS), 'sens')  185 us
    psum x1, waiting for transfers between devices, from_root(): return lax.psum(jnp.where(mine, x, jnp.zeros_like(x)), axis)  127 us
    another operation x4, local copies, waits for them, and re-layouts, sensor_windows(): tiled = jnp.tile(weighted, (1, 1, tap_count))  40.5 us
    reshape x2, local copies, waits for them, and re-layouts, sensor_windows(): padded.reshape(weighted.shape[0], 3, tap_count, length + 1)[..., :lag_count]  27.8 us
    concatenate x2, local copies, waits for them, and re-layouts, sensor_windows(): jnp.concatenate([tiled, jnp.zeros(weighted.shape[:2] + (tap_count,), jnp....  19.2 us
    dot_general x1, matrix products, local(): product = jnp.dot(flat_green, toeplitz, preferred_element_type=jnp.float32)  16 us
    gather x4, local copies, waits for them, and re-layouts, window_of(): return lax.dynamic_slice_in_dim(record_row, begin_at, length, 1)  13.4 us
    unnamed x5, local copies, waits for them, and re-layouts  12.7 us
  transfers between devices with their start and end apart: 2, of which 2 were waited for; matrix products, arithmetic and copies ran while one was open for 3% of the time, Pallas kernels for 0%

commit v1 on v0

--- a/solution.py
+++ b/solution.py
@@ -8,9 +8,16 @@
 EV = 2
 
 
-def from_root(x, axis, root):
-    mine = lax.axis_index(axis) == root
-    return lax.psum(jnp.where(mine, x, jnp.zeros_like(x)), axis)
+def from_owners(x, axis, roots):
+    size = lax.axis_size(axis)
+    me = lax.axis_index(axis)
+    bit = 1
+    while bit < size:
+        got = lax.ppermute(x, axis, [(i, i ^ bit) for i in range(size)])
+        keep = ((me // bit) % 2) == ((roots // bit) % 2)
+        x = jnp.where(keep.reshape((-1,) + (1,) * (x.ndim - 1)), x, got)
+        bit *= 2
+    return x
 
 
 def sensor_windows(traces, offsets, weight_codes, length, lag_count):
@@ -34,17 +41,16 @@
     point_rows = green.shape[0]
     flat_green = green.reshape(point_rows, -1)
     length = NT + LAGS - 1
+    traces_all = from_owners(records_buffer[0], "loc", owners)
     blocks = []
     for event_idx in range(EV):
-        root_dev = owners[event_idx]
-        traces = from_root(records_buffer[0, event_idx], "loc", root_dev)
-        operand = sensor_windows(traces, onsets[event_idx], codes, length, LAGS)
+        operand = sensor_windows(traces_all[event_idx], onsets[event_idx], codes, length, LAGS)
         blocks.append(operand)
     toeplitz = jnp.stack(blocks, axis=1).reshape(blocks[0].shape[0], -1)
-    share = point_rows // lax.axis_size("sens")
     product = jnp.dot(flat_green, toeplitz, preferred_element_type=jnp.float32)
-    totals = lax.psum(product.reshape(point_rows, EV, LAGS), "sens")
-    return lax.dynamic_slice_in_dim(totals, lax.axis_index("sens") * share, share, 0)
+    return lax.psum_scatter(
+        product.reshape(point_rows, EV, LAGS), "sens", scatter_dimension=0, tiled=True
+    )
 
 
 def solution(mesh):

time: 505 us -> 455 us (0.901); the launches traced: 504 us -> 447 us
  waiting for transfers between devices: 312 us -> 190 us
  local copies, waits for them, and re-layouts: 151 us -> 189 us
  other arithmetic: 10.7 us -> 30.5 us
  starting transfers between devices: 0.04 us -> 7.01 us
    psum x2 -> x0, waiting for transfers between devices: 312 us -> none  [the longest x1 185 us: local(): totals = lax.psum(product.reshape(point_rows, EV, LAGS), 'sens')]
    unnamed x2, waiting for transfers between devices: 0.03 us -> 184 us
    select_n x1 -> x4, other arithmetic: 2.34 us -> 22.1 us  [from_owners(): x = jnp.where(keep.reshape((-1,) + (1,) * (x.ndim - 1)), x, got)]
    ppermute x0 -> x4, local copies, waits for them, and re-layouts: none -> 14.9 us  [from_owners(): got = lax.ppermute(x, axis, [(i, i ^ bit) for i in range(size)])]
    select_n x0 -> x3, local copies, waits for them, and re-layouts: none -> 13.1 us  [from_owners(): x = jnp.where(keep.reshape((-1,) + (1,) * (x.ndim - 1)), x, got)]
    unnamed x5 -> x12, local copies, waits for them, and re-layouts: 12.7 us -> 20.3 us
    ppermute x0 -> x4, starting transfers between devices: none -> 7.01 us  [from_owners(): got = lax.ppermute(x, axis, [(i, i ^ bit) for i in range(size)])]
    ppermute x0 -> x4, waiting for transfers between devices: none -> 6.6 us  [from_owners(): got = lax.ppermute(x, axis, [(i, i ^ bit) for i in range(size)])]
  transfers between devices with their start and end apart: 2 -> 5, of which waited for: 2 -> 4; matrix products, arithmetic and copies ran while one was open for 3% -> 3% of each run, Pallas kernels for 0% -> 0%
where the time goes in v1:
time: 455 us; the launch traced here: 447 us
  waiting for transfers between devices  190 us (42%)
  local copies, waits for them, and re-layouts  189 us (42%)
  other arithmetic  30.5 us (7%)
  matrix products  16.3 us (4%)
  between operations  14.7 us (3%)
  starting transfers between devices  7.01 us (2%)
    unnamed x2, waiting for transfers between devices  184 us
    another operation x4, local copies, waits for them, and re-layouts, sensor_windows(): tiled = jnp.tile(weighted, (1, 1, tap_count))  40.9 us
    reshape x2, local copies, waits for them, and re-layouts, sensor_windows(): padded.reshape(weighted.shape[0], 3, tap_count, length + 1)[..., :lag_count]  27.8 us
    select_n x4, other arithmetic, from_owners(): x = jnp.where(keep.reshape((-1,) + (1,) * (x.ndim - 1)), x, got)  22.1 us
    unnamed x12, local copies, waits for them, and re-layouts  20.3 us
    concatenate x2, local copies, waits for them, and re-layouts, sensor_windows(): jnp.concatenate([tiled, jnp.zeros(weighted.shape[:2] + (tap_count,), jnp....  19.2 us
    gather x4, local copies, waits for them, and re-layouts, window_of(): return lax.dynamic_slice_in_dim(record_row, begin_at, length, 1)  17 us
    dot_general x1, matrix products, local(): product = jnp.dot(flat_green, toeplitz, preferred_element_type=jnp.float32)  16.3 us
  transfers between devices with their start and end apart: 5, of which 4 were waited for; matrix products, arithmetic and copies ran while one was open for 3% of the time, Pallas kernels for 0%

profile of v1, /device:TPU:0, one launch (start us, length us, event | category | flops | bytes accessed | tf_op | source)
XLA Modules:
  0.0 447.4 jit_solution(4277807318274782895)
XLA Ops:
  6.5 0.0 copy-start.2
  6.5 0.0 all-reduce.7.cloned.1.call-start
  6.5 4.5 %copy.43 = bf16[1,2,6,3,1024]{3,2,4,1,0:T(8,128)(2,1)} copy(bf16[1,2,6,3,1024]{4,1,3,2,0:T(2,128)(2,1)} %param.6) | data formatting | bytes 147456 | tf_op args[1]
  11.1 4.4 copy.44
  15.5 0.1 collective-permute-start
  15.6 0.0 copy-done.2
  15.7 1.1 collective-permute-done
  16.8 3.7 copy.45
  20.5 6.0 %broadcast_select_fusion = bf16[2,6,3,1024]{2,1,3,0:T(8,128)(2,1)} fusion(bf16[2,6,3,1024]{2,1,3,0:T(8,128)(2,1)} %copy.45, pred[2]{0:T(512)(128)(4,1)S(1)} %get-tuple-element.14, bf16[1,2,6,3,1024]{3,2,4,1,0:T(8,128)(2,1)} %copy.43), kind=kLoop, calls=%fused_computation.3 | loop fusion | flops 36864 | bytes 221186 | tf_op jit(solution)/shard_map/jit(_where)/select_n | solution.py:18
  26.5 4.4 copy.46
  30.9 1.7 collective-permute-start.1
  32.6 2.8 collective-permute-done.1
  35.4 3.7 copy.47
  39.1 6.0 %broadcast_select_fusion.1 = bf16[2,6,3,1024]{2,1,3,0:T(8,128)(2,1)} fusion(bf16[2,6,3,1024]{2,1,3,0:T(8,128)(2,1)} %broadcast_select_fusion, bf16[2,6,3,1024]{2,1,3,0:T(8,128)(2,1)} %copy.47, pred[2]{0:T(512)(128)(4,1)S(1)} %get-tuple-element.13), kind=kLoop, calls=%fused_computation.4 | loop fusion | flops 36864 | bytes 221186 | tf_op jit(solution)/shard_map/jit(_where)/select_n | solution.py:18
  45.1 0.0 copy-start
  45.1 4.4 copy.48
  49.5 1.7 collective-permute-start.2
  51.2 0.0 copy-done
  51.2 2.7 collective-permute-done.2
  53.9 3.7 copy.49
  57.6 6.0 %broadcast_select_fusion.2 = bf16[2,6,3,1024]{2,1,3,0:T(8,128)(2,1)} fusion(bf16[2,6,3,1024]{2,1,3,0:T(8,128)(2,1)} %broadcast_select_fusion.1, bf16[2,6,3,1024]{2,1,3,0:T(8,128)(2,1)} %copy.49, pred[2]{0:T(512)(128)(4,1)S(1)} %get-tuple-element.12), kind=kLoop, calls=%fused_computation.5 | loop fusion | flops 36864 | bytes 221186 | tf_op jit(solution)/shard_map/jit(_where)/select_n | solution.py:18
  63.7 0.0 copy-start.1
  63.7 4.4 copy.50
  68.1 3.5 collective-permute-start.3
  71.6 0.0 copy-done.1
  71.6 12.7 %copy.57 = bf16[1024,6,3,256]{0,3,2,1:T(8,128)(2,1)} copy(bf16[1024,6,3,256]{3,0,2,1:T(8,128)(2,1)} %param.5) | data formatting | bytes 18874368 | tf_op args[0]
  84.3 0.0 collective-permute-done.3
  84.3 3.7 copy.51
  88.1 4.1 broadcast_select_fusion.3
  92.1 1.6 slice_bitcast_fusion.1
  93.7 6.2 %gather_fusion = bf16[6,3,767]{1,0,2:T(8,128)(2,1)} fusion(bf16[6,3,1024]{1,0,2:T(8,128)(2,1)} %get-tuple-element.5, s32[6]{0:T(128)S(1)} %get-tuple-element.9), kind=kCustom, calls=%fused_computation | custom fusion | bytes 55296 | tf_op jit(solution)/shard_map/vmap()/gather | solution.py:26
  100.0 2.3 copy.52
  102.2 6.2 %gather_fusion.1 = bf16[6,3,767]{1,0,2:T(8,128)(2,1)} fusion(bf16[6,3,1024]{1,0,2:T(8,128)(2,1)S(1)} %get-tuple-element.6, s32[6]{0:T(128)S(1)} %get-tuple-element.10), kind=kCustom, calls=%fused_computation.1 | custom fusion | bytes 55296 | tf_op jit(solution)/shard_map/vmap()/gather | solution.py:26
  108.4 2.3 copy.54
  110.7 0.1 multiply_convert_fusion.1
  110.8 3.3 tile.8
  114.1 17.2 %tile.9 = bf16[6,3,196352]{2,0,1:T(8,128)(2,1)} reshape(bf16[6,3,256,767]{3,2,0,1:T(8,128)(2,1)} %tile.8) | data formatting | bytes 14137344 | tf_op jit(solution)/shard_map/tile | solution.py:32
  131.2 9.6 %concatenate.13 = bf16[6,3,196608]{2,0,1:T(8,128)(2,1)} pad(bf16[6,3,196352]{2,0,1:T(8,128)(2,1)} %tile.9, bf16[]{:T(256)} %constant.129.clone.1), padding=0_0x0_0x0_256 | pad | bytes 14146562 | tf_op jit(solution)/shard_map/concatenate | solution.py:33
  140.8 13.9 %reshape.96 = bf16[6,3,256,768]{3,2,0,1:T(8,128)(2,1)} reshape(bf16[6,3,196608]{2,0,1:T(8,128)(2,1)} %concatenate.13) | data formatting | bytes 14155776 | tf_op jit(solution)/shard_map/reshape | solution.py:36
  154.7 0.0 slice-start
  154.7 2.3 slice-done
  157.1 2.4 copy.53
  159.5 3.3 tile.20
  162.8 17.2 %tile.21 = bf16[6,3,196352]{2,0,1:T(8,128)(2,1)} reshape(bf16[6,3,256,767]{3,2,0,1:T(8,128)(2,1)} %tile.20) | data formatting | bytes 14137344 | tf_op jit(solution)/shard_map/tile | solution.py:32
  180.0 9.6 %concatenate.15 = bf16[6,3,196608]{2,0,1:T(8,128)(2,1)} pad(bf16[6,3,196352]{2,0,1:T(8,128)(2,1)} %tile.21, bf16[]{:T(256)} %constant.129.clone.1), padding=0_0x0_0x0_256 | pad | bytes 14146562 | tf_op jit(solution)/shard_map/concatenate | solution.py:33
  189.6 13.9 %reshape.97 = bf16[6,3,256,768]{3,2,0,1:T(8,128)(2,1)} reshape(bf16[6,3,196608]{2,0,1:T(8,128)(2,1)} %concatenate.15) | data formatting | bytes 14155776 | tf_op jit(solution)/shard_map/reshape | solution.py:36
  203.5 0.0 slice-start.1
  203.5 2.3 slice-done.1
  205.8 2.5 copy.55
  208.3 8.3 %pad_maximum_fusion = bf16[4608,2,512]{2,0,1:T(8,128)(2,1)} fusion(bf16[4608,1,512]{2,0,1:T(8,128)(2,1)} %bitcast.42, bf16[4608,1,512]{2,0,1:T(8,128)(2,1)} %bitcast.41), kind=kLoop, calls=%fused_computation.2 | loop fusion | flops 4718592 | bytes 18874368 | tf_op jit(solution)/shard_map/stack | solution.py:49
  216.6 12.7 %copy.56 = bf16[4608,2,512]{0,2,1:T(8,128)(2,1)} copy(bf16[4608,2,512]{2,0,1:T(8,128)(2,1)} %pad_maximum_fusion) | data formatting | bytes 18874368 | tf_op jit(solution)/shard_map/stack | solution.py:49
  229.3 16.3 %fusion.15 = f32[1024,1024]{1,0:T(8,128)} fusion(bf16[4608,1024]{0,1:T(8,128)(2,1)} %bitcast.44, bf16[1024,4608]{0,1:T(8,128)(2,1)} %bitcast.43), kind=kOutput, calls=%fused_computation.53 | convolution fusion | flops 9663676416 | bytes 23068672 | tf_op jit(solution)/shard_map/dot_general | solution.py:50
  245.6 7.3 %copy.58 = f32[1024,2,512]{2,1,0:T(2,128)} copy(f32[1024,2,512]{0,2,1:T(8,128)} %bitcast.45) | data formatting | bytes 8388608 | tf_op jit(solution)/shard_map/reshape | solution.py:52
  252.8 0.0 copy-start.3
  252.8 0.0 all-reduce.7.cloned.1.call-update
  252.8 0.6 copy-done.3
  253.5 0.6 dynamic-slice
  254.7 183.5 %all-reduce.7.cloned.1.call-done = f32[1024,2,512]{2,1,0:T(2,128)} async-done(((f32[1024,2,512]{2,1,0:T(2,128)}), f32[1024,2,512]{2,1,0:T(2,128)}) %all-reduce.7.cloned.1.call-update) | async-done | bytes 4194320
  438.2 1.9 constant_dynamic-slice_fusion
  (3 shorter events, 0.0 us)
Async XLA Ops:
  6.5 9.1 %copy-start.2 = (s32[2]{0:T(128)S(1)}, s32[2]{0:T(128)}, u32[]{:S(2)}) copy-start(s32[2]{0:T(128)} %param.7) | copy-start | bytes 28
  6.5 431.7 %all-reduce.7.cloned.1.call-start = ((), (), s32[]{:S(2)}) async-start(), calls=%async_computation | async-start | bytes 8388608
  15.5 1.3 collective-permute-start
  30.9 4.4 collective-permute-start.1
  45.1 6.1 %copy-start = (s32[6,3]{0,1:T(4,128)S(1)}, s32[6,3]{0,1:T(4,128)}, u32[]{:S(2)}) copy-start(s32[6,3]{0,1:T(4,128)} %param.9) | copy-start | bytes 220
  49.5 4.4 collective-permute-start.2
  63.7 7.9 %copy-start.1 = (s32[2,6]{1,0:T(2,128)S(1)}, s32[2,6]{1,0:T(2,128)}, u32[]{:S(2)}) copy-start(s32[2,6]{1,0:T(2,128)} %param.8) | copy-start | bytes 148
  68.1 16.3 %collective-permute-start.3 = (bf16[2,6,3,1024]{3,0,2,1:T(2,128)(2,1)S(1)}, bf16[2,6,3,1024]{3,0,2,1:T(2,128)(2,1)S(1)}, u32[]{:S(2)}, u32[]{:S(2)}) collective-permute-start(bf16[2,6,3,1024]{3,0,2,1:T(2,128)(2,1)S(1)} %copy.50), channel_id=1, source_target_pairs={{0,8},{1,9},{2,10},{3,11},{4,12},{5,13},{6,14},{7,15},{8,0},{9,1},... | collective-permute-start | bytes 221192 | tf_op jit(solution)/shard_map/ppermute | solution.py:16
  154.7 2.3 slice-start
  203.5 2.3 slice-start.1
  252.8 0.7 copy-start.3
Sparse Core Ops, SparseCore 0:
  253.0 185.2 all-reduce.6

commit v2 on v1

v2 whole, which is shorter than its diff:
```python
import jax
import jax.numpy as jnp
from jax import lax
from jax.experimental import pallas as pl
from jax.experimental.pallas import tpu as pltpu
from jax.sharding import Mesh
from jax.sharding import PartitionSpec as P

NT = 256
LAGS = 512
SAMPLES = 1024
EV = 2


def from_owners(x, axis, roots):
    size = lax.axis_size(axis)
    me = lax.axis_index(axis)
    bit = 1
    while bit < size:
        got = lax.ppermute(x, axis, [(i, i ^ bit) for i in range(size)])
        keep = ((me // bit) % 2) == ((roots // bit) % 2)
        x = jnp.where(keep.reshape((-1,) + (1,) * (x.ndim - 1)), x, got)
        bit *= 2
    return x


def _toeplitz_kernel(shift_ref, weight_ref, rev_ref, out_ref):
    sc = pl.program_id(0)
    rows = weight_ref.shape[0]
    w = weight_ref[sc]
    for e in range(rev_ref.shape[1]):
        row = rev_ref[0, e : e + 1, :]
        row = pltpu.roll(row, shift_ref[e * rows + sc], 1)
        row = (row * w).astype(jnp.bfloat16).astype(jnp.float32)
        wide = jnp.broadcast_to(row, (NT, SAMPLES))
        band = pltpu.roll(wide, 0, 1, stride=1, stride_axis=0)
        out_ref[:, e * LAGS : (e + 1) * LAGS] = band[:, :LAGS].astype(out_ref.dtype)


def toeplitz_reversed(traces, onsets, codes):
    ev, sens = traces.shape[0], traces.shape[1]
    rows = sens * 3
    rev = jnp.flip(traces.astype(jnp.float32), axis=-1).reshape(ev, rows, SAMPLES)
    rev = jnp.transpose(rev, (1, 0, 2))
    shifts = jnp.repeat(onsets.astype(jnp.int32), 3, axis=1)
    shifts = ((shifts - LAGS) % SAMPLES).reshape(-1)
    weights = jnp.exp2(-codes.astype(jnp.float32)).reshape(-1)
    return pl.pallas_call(
        _toeplitz_kernel,
        grid_spec=pltpu.PrefetchScalarGridSpec(
            num_scalar_prefetch=1,
            grid=(rows,),
            in_specs=[
                pl.BlockSpec(memory_space=pltpu.SMEM),
                pl.BlockSpec((1, ev, SAMPLES), lambda i, s: (i, 0, 0)),
            ],
            out_specs=pl.BlockSpec((NT, ev * LAGS), lambda i, s: (i, 0)),
        ),
        out_shape=jax.ShapeDtypeStruct((rows * NT, ev * LAGS), jnp.bfloat16),
        cost_estimate=pl.CostEstimate(
            flops=0, transcendentals=0, bytes_accessed=rows * NT * ev * LAGS * 2
        ),
    )(shifts, weights, rev)


def reduce_over_sens(product):
    return lax.psum_scatter(product, SENS_AXES, scatter_dimension=0, tiled=True)


def local(green, records_buffer, owners, onsets, codes):
    point_rows = green.shape[0]
    flat_green = green.reshape(point_rows, -1)
    traces = from_owners(records_buffer[0], "loc", owners)
    toeplitz = toeplitz_reversed(traces, onsets, codes)
    product = jnp.dot(flat_green, toeplitz, preferred_element_type=jnp.float32)
    totals = reduce_over_sens(product.reshape(point_rows, EV, LAGS))
    return jnp.flip(totals, axis=-1)


SENS_AXES = "sens"


def solution(mesh):
    return jax.shard_map(
        local,
        mesh=mesh,
        in_specs=(
            P("loc", "sens", None, None),
            P("loc", None, "sens", None, None),
            P(),
            P(None, "sens"),
            P("sens", None),
        ),
        out_specs=P(("loc", "sens"), None, None),
        check_vma=False,
    )
```

time: 455 us -> 272 us (0.60); the launches traced: 447 us -> 270 us
  local copies, waits for them, and re-layouts: 189 us -> 27.7 us
  other arithmetic: 30.5 us -> 3.98 us
  Pallas kernels: 0 us -> 12.4 us
    another operation x5 -> x0, local copies, waits for them, and re-layouts: 53.6 us -> none  [the longest x4 40.9 us: sensor_windows(): tiled = jnp.tile(weighted, (1, 1, tap_count))]
    reshape x3 -> x2, local copies, waits for them, and re-layouts: 35.1 us -> 7.89 us  [the longest x1 7.23 us: local(): totals = reduce_over_sens(product.reshape(point_rows, EV, LAGS))]
    select_n x4 -> x3, other arithmetic: 22.1 us -> 1.32 us  [from_owners(): x = jnp.where(keep.reshape((-1,) + (1,) * (x.ndim - 1)), x, got)]
    concatenate x2 -> x0, local copies, waits for them, and re-layouts: 19.2 us -> none  [sensor_windows(): jnp.concatenate([tiled, jnp.zeros(weighted.shape[:2] + (tap_count,), jnp....]
    gather x4 -> x0, local copies, waits for them, and re-layouts: 17 us -> none  [window_of(): return lax.dynamic_slice_in_dim(record_row, begin_at, length, 1)]
    ppermute x4 -> x0, local copies, waits for them, and re-layouts: 14.9 us -> none  [from_owners(): got = lax.ppermute(x, axis, [(i, i ^ bit) for i in range(size)])]
    select_n x3 -> x0, local copies, waits for them, and re-layouts: 13.1 us -> none  [from_owners(): x = jnp.where(keep.reshape((-1,) + (1,) * (x.ndim - 1)), x, got)]
    pallas_call x0 -> x1, Pallas kernels: none -> 12.4 us  [toeplitz_reversed(): pl.pallas_call(_toeplitz_kernel, grid_spec=pltpu.PrefetchScalarGridSpec(n...]
  transfers between devices with their start and end apart: 5 -> 5, of which waited for: 4 -> 4; matrix products, arithmetic and copies ran while one was open for 3% -> 6% of each run, Pallas kernels for 0% -> 0%
where the time goes in v2:
time: 272 us; the launch traced here: 270 us
  waiting for transfers between devices  189 us (69%)
  local copies, waits for them, and re-layouts  27.7 us (10%)
  matrix products  16 us (6%)
  between operations  14.1 us (5%)
  Pallas kernels  12.4 us (5%)
  starting transfers between devices  6.75 us (2%)
  other arithmetic  3.98 us (1%)
    unnamed x2, waiting for transfers between devices  184 us
    dot_general x1, matrix products, local(): product = jnp.dot(flat_green, toeplitz, preferred_element_type=jnp.float32)  16 us
    unnamed x5, local copies, waits for them, and re-layouts  14.3 us
    pallas_call x1, Pallas kernels, toeplitz_reversed(): pl.pallas_call(_toeplitz_kernel, grid_spec=pltpu.PrefetchScalarGridSpec(n...  12.4 us
    reshape x1, local copies, waits for them, and re-layouts, local(): totals = reduce_over_sens(product.reshape(point_rows, EV, LAGS))  7.23 us
    ppermute x4, starting transfers between devices, from_owners(): got = lax.ppermute(x, axis, [(i, i ^ bit) for i in range(size)])  6.75 us
  transfers between devices with their start and end apart: 5, of which 4 were waited for; matrix products, arithmetic and copies ran while one was open for 6% of the time, Pallas kernels for 0%

profile of v2, /device:TPU:0, one launch (start us, length us, event | category | flops | bytes accessed | tf_op | source)
XLA Modules:
  0.0 270.0 jit_solution(17619490353484998427)
XLA Ops:
  6.5 0.0 all-reduce.3.cloned.1.call-start
  6.5 0.0 collective-permute-start
  6.5 0.7 fusion.1
  7.2 0.8 collective-permute-done
  8.0 1.0 broadcast_select_fusion
  9.0 1.7 collective-permute-start.1
  10.7 0.7 multiply_exponential_fusion
  11.4 2.1 collective-permute-done.1
  13.5 0.1 broadcast_select_fusion.1
  13.6 1.7 collective-permute-start.2
  15.4 0.7 broadcast_add_fusion
  16.1 0.1 broadcast_in_dim.26
  16.1 0.1 sub.29
  16.2 1.9 collective-permute-done.2
  18.1 0.1 broadcast_select_fusion.2
  18.2 3.4 %collective-permute-start.3 = (bf16[2,6,3,1024]{3,0,2,1:T(2,128)(2,1)S(1)}, bf16[2,6,3,1024]{3,0,2,1:T(2,128)(2,1)S(1)}, u32[]{:S(2)}, u32[]{:S(2)}) collective-permute-start(bf16[2,6,3,1024]{3,0,2,1:T(2,128)(2,1)S(1)} %broadcast_select_fusion.2), channel_id=1, source_target_pairs={{0,8},{1,9},{2,10},{3,11},{4,12},{5,13},{6,14},{7,15},{8,0},{9,1},... | collective-permute-start | bytes 221192 | tf_op jit(solution)/shard_map/ppermute | solution.py:20
  21.6 0.5 and_select_fusion.7.shift_ref
  22.1 0.1 copy.11
  22.2 0.7 reshape.25.weight_ref
  22.8 12.6 %copy.12 = bf16[1024,6,3,256]{0,3,2,1:T(8,128)(2,1)} copy(bf16[1024,6,3,256]{3,0,2,1:T(8,128)(2,1)} %param.5) | data formatting | bytes 18874368 | tf_op args[0]
  35.4 0.0 collective-permute-done.3
  35.4 0.1 fusion
  35.6 3.0 %rev.8 = f32[2,6,3,1024]{3,0,2,1:T(2,128)} reverse(f32[2,6,3,1024]{3,0,2,1:T(2,128)S(1)} %fusion), dimensions={3} | reverse | bytes 294912 | tf_op jit(solution)/shard_map/jit(_flip)/rev | solution.py:43
  38.6 12.4 %shard_map.55 = bf16[4608,1024]{1,0:T(8,128)(2,1)} custom-call(s32[36]{0:T(128)} %and_select_fusion.7.shift_ref, f32[18]{0:T(128)} %reshape.25.weight_ref, f32[18,2,1024]{2,1,0:T(2,128)} %bitcast.14), custom_call_target="tpu_custom_call" | custom-call | bytes 9437184 | tf_op jit(solution)/shard_map/pallas_call | solution.py:48
  51.0 16.0 %fusion.9 = f32[1024,1024]{1,0:T(8,128)} fusion(bf16[4608,1024]{1,0:T(8,128)(2,1)} %shard_map.55, bf16[1024,4608]{0,1:T(8,128)(2,1)} %bitcast.12), kind=kOutput, calls=%fused_computation.41 | convolution fusion | flops 9663676416 | bytes 23068672 | tf_op jit(solution)/shard_map/dot_general | solution.py:75
  67.0 0.0 copy-start
  67.0 7.2 %copy.13 = f32[1024,2,512]{2,1,0:T(2,128)} copy(f32[1024,2,512]{0,2,1:T(8,128)} %bitcast.13) | data formatting | bytes 8388608 | tf_op jit(solution)/shard_map/reshape | solution.py:76
  74.2 0.0 all-reduce.3.cloned.1.call-update
  74.3 0.0 copy-done
  74.3 0.6 dynamic-slice
  75.5 184.3 %all-reduce.3.cloned.1.call-done = f32[1024,2,512]{2,1,0:T(2,128)} async-done(((f32[1024,2,512]{2,1,0:T(2,128)}), f32[1024,2,512]{2,1,0:T(2,128)}) %all-reduce.3.cloned.1.call-update) | async-done | bytes 4194320
  259.8 1.1 constant_dynamic-slice_fusion
  260.9 2.3 rev.9
Async XLA Ops:
  6.5 253.3 %all-reduce.3.cloned.1.call-start = ((), (), s32[]{:S(2)}) async-start(), calls=%async_computation | async-start | bytes 8388608
  6.5 1.5 collective-permute-start
  9.0 4.4 %collective-permute-start.1 = (bf16[2,6,3,1024]{3,0,2,1:T(2,128)(2,1)S(1)}, bf16[2,6,3,1024]{3,0,2,1:T(2,128)(2,1)S(1)}, u32[]{:S(2)}, u32[]{:S(2)}) collective-permute-start(bf16[2,6,3,1024]{3,0,2,1:T(2,128)(2,1)S(1)} %broadcast_select_fusion), channel_id=1, source_target_pairs={{0,2},{1,3},{2,0},{3,1},{4,6},{5,7},{6,4},{7,5},{8,10},{9,11},{10,... | collective-permute-start | bytes 221192 | tf_op jit(solution)/shard_map/ppermute | solution.py:20
  13.6 4.4 %collective-permute-start.2 = (bf16[2,6,3,1024]{3,0,2,1:T(2,128)(2,1)S(1)}, bf16[2,6,3,1024]{3,0,2,1:T(2,128)(2,1)S(1)}, u32[]{:S(2)}, u32[]{:S(2)}) collective-permute-start(bf16[2,6,3,1024]{3,0,2,1:T(2,128)(2,1)S(1)} %broadcast_select_fusion.1), channel_id=1, source_target_pairs={{0,4},{1,5},{2,6},{3,7},{4,0},{5,1},{6,2},{7,3},{8,12},{9,13},{10,... | collective-permute-start | bytes 221192 | tf_op jit(solution)/shard_map/ppermute | solution.py:20
  18.2 17.2 %collective-permute-start.3 = (bf16[2,6,3,1024]{3,0,2,1:T(2,128)(2,1)S(1)}, bf16[2,6,3,1024]{3,0,2,1:T(2,128)(2,1)S(1)}, u32[]{:S(2)}, u32[]{:S(2)}) collective-permute-start(bf16[2,6,3,1024]{3,0,2,1:T(2,128)(2,1)S(1)} %broadcast_select_fusion.2), channel_id=1, source_target_pairs={{0,8},{1,9},{2,10},{3,11},{4,12},{5,13},{6,14},{7,15},{8,0},{9,1},... | collective-permute-start | bytes 221192 | tf_op jit(solution)/shard_map/ppermute | solution.py:20
  67.0 7.3 %copy-start = (u32[128]{0:T(128)S(1)}, u32[128]{0:T(128)}, u32[]{:S(2)}) copy-start(u32[128]{0:T(128)} %constant.147) | copy-start | bytes 1540
Sparse Core Ops, SparseCore 0:
  74.4 185.3 all-reduce.2

commit v3 on v2

--- a/solution.py
+++ b/solution.py
@@ -63,8 +63,33 @@
     )(shifts, weights, rev)
 
 
-def reduce_over_sens(product):
-    return lax.psum_scatter(product, SENS_AXES, scatter_dimension=0, tiled=True)
+def reduce_over_sens(halves):
+    size = lax.axis_size("sens")
+    me = lax.axis_index("sens")
+    zs, xs = size // 2, 2
+    z, xh = me // xs, me % xs
+    quarter = halves[0].shape[0] // zs
+
+    def ring_perm(step):
+        return [(i, ((i // xs + step) % zs) * xs + i % xs) for i in range(size)]
+
+    def chunk(x, c):
+        return lax.dynamic_slice_in_dim(x, c * quarter, quarter, 0)
+
+    sums = []
+    for half, step in zip(halves, (1, zs - 1)):
+        acc = chunk(half, (z + zs - step) % zs)
+        for k in range(zs - 1):
+            got = lax.ppermute(acc, "sens", ring_perm(step))
+            c = (z + 4 * zs - step * (k + 2)) % zs
+            acc = got + chunk(half, c)
+        sums.append(acc)
+    mine = jnp.concatenate(sums, axis=1)
+    block = quarter // xs
+    theirs = lax.dynamic_slice_in_dim(mine, (1 - xh) * block, block, 0)
+    kept = lax.dynamic_slice_in_dim(mine, xh * block, block, 0)
+    got = lax.ppermute(theirs, "sens", [(i, i ^ 1) for i in range(size)])
+    return kept + got
 
 
 def local(green, records_buffer, owners, onsets, codes):
@@ -72,12 +97,12 @@
     flat_green = green.reshape(point_rows, -1)
     traces = from_owners(records_buffer[0], "loc", owners)
     toeplitz = toeplitz_reversed(traces, onsets, codes)
-    product = jnp.dot(flat_green, toeplitz, preferred_element_type=jnp.float32)
-    totals = reduce_over_sens(product.reshape(point_rows, EV, LAGS))
-    return jnp.flip(totals, axis=-1)
-
-
-SENS_AXES = "sens"
+    halves = [
+        jnp.dot(flat_green, toeplitz[:, e * LAGS : (e + 1) * LAGS], preferred_element_type=jnp.float32)
+        for e in range(EV)
+    ]
+    totals = reduce_over_sens(halves)
+    return jnp.flip(totals.reshape(-1, EV, LAGS), axis=-1)
 
 
 def solution(mesh):

time: 272 us -> 119 us (0.44)
  waiting for transfers between devices: 189 us -> 36.2 us
  starting transfers between devices: 6.75 us -> 21.5 us
  between operations: 14.1 us -> 0.11 us
  other arithmetic: 3.98 us -> 11.7 us
  local copies, waits for them, and re-layouts: 27.7 us -> 20.8 us
    unnamed x2 -> x0, waiting for transfers between devices: 184 us -> none
    ppermute x0 -> x7, waiting for transfers between devices: none -> 31.5 us  [the longest x6 23.8 us: reduce_over_sens(): got = lax.ppermute(acc, 'sens', ring_perm(step))]
    ppermute x0 -> x7, starting transfers between devices: none -> 14.8 us  [the longest x6 11.7 us: reduce_over_sens(): got = lax.ppermute(acc, 'sens', ring_perm(step))]
    add x0 -> x7, other arithmetic: none -> 7.65 us  [the longest x6 7.6 us: reduce_over_sens(): acc = got + chunk(half, c)]
    reshape x1, local copies, waits for them, and re-layouts: 7.23 us -> 0.23 us  [local(): return jnp.flip(totals.reshape(-1, EV, LAGS), axis=-1)]
    dot_general x1 -> x2, matrix products: 16 us -> 14.3 us  [local(): jnp.dot(flat_green, toeplitz[:, e * LAGS:(e + 1) * LAGS], preferred_eleme...]
    unnamed x5 -> x11, local copies, waits for them, and re-layouts: 14.3 us -> 12.7 us
  transfers between devices with their start and end apart: 5 -> 11, of which waited for: 4 -> 10; matrix products, arithmetic and copies ran while one was open for 6% -> 24% of each run, Pallas kernels for 0% -> 0%
where the time goes in v3:
time: 119 us; the launch traced here: 117 us
  waiting for transfers between devices  36.2 us (30%)
  starting transfers between devices  21.5 us (18%)
  local copies, waits for them, and re-layouts  20.8 us (17%)
  matrix products  14.3 us (12%)
  Pallas kernels  12.5 us (11%)
  other arithmetic  11.7 us (10%)
    ppermute x6, waiting for transfers between devices, reduce_over_sens(): got = lax.ppermute(acc, 'sens', ring_perm(step))  23.8 us
    dot_general x2, matrix products, local(): jnp.dot(flat_green, toeplitz[:, e * LAGS:(e + 1) * LAGS], preferred_eleme...  14.3 us
    unnamed x11, local copies, waits for them, and re-layouts  12.7 us
    pallas_call x1, Pallas kernels, toeplitz_reversed(): pl.pallas_call(_toeplitz_kernel, grid_spec=pltpu.PrefetchScalarGridSpec(n...  12.5 us
    ppermute x6, starting transfers between devices, reduce_over_sens(): got = lax.ppermute(acc, 'sens', ring_perm(step))  11.7 us
    ppermute x1, waiting for transfers between devices, reduce_over_sens(): got = lax.ppermute(theirs, 'sens', [(i, i ^ 1) for i in range(size)])  7.66 us
    add x6, other arithmetic, reduce_over_sens(): acc = got + chunk(half, c)  7.6 us
    ppermute x4, starting transfers between devices, from_owners(): got = lax.ppermute(x, axis, [(i, i ^ bit) for i in range(size)])  6.75 us
  transfers between devices with their start and end apart: 11, of which 10 were waited for; matrix products, arithmetic and copies ran while one was open for 24% of the time, Pallas kernels for 0%

profile of v3, /device:TPU:0, one launch (start us, length us, event | category | flops | bytes accessed | tf_op | source)
XLA Modules:
  0.0 117.2 jit_solution(8453126250279677091)
XLA Ops:
  0.0 0.0 collective-permute-start
  0.0 0.7 fusion.8
  0.7 0.8 collective-permute-done
  1.5 1.0 broadcast_select_fusion
  2.5 1.7 %collective-permute-start.1 = (bf16[2,6,3,1024]{3,0,2,1:T(2,128)(2,1)S(1)}, bf16[2,6,3,1024]{3,0,2,1:T(2,128)(2,1)S(1)}, u32[]{:S(2)}, u32[]{:S(2)}) collective-permute-start(bf16[2,6,3,1024]{3,0,2,1:T(2,128)(2,1)S(1)} %broadcast_select_fusion), channel_id=1, source_target_pairs={{0,2},{1,3},{2,0},{3,1},{4,6},{5,7},{6,4},{7,5},{8,10},{9,11},{10,... | collective-permute-start | bytes 221192 | tf_op jit(solution)/shard_map/ppermute | solution.py:20
  4.2 0.7 multiply_exponential_fusion
  4.9 2.1 %collective-permute-done.1 = bf16[2,6,3,1024]{3,0,2,1:T(2,128)(2,1)S(1)} collective-permute-done((bf16[2,6,3,1024]{3,0,2,1:T(2,128)(2,1)S(1)}, bf16[2,6,3,1024]{3,0,2,1:T(2,128)(2,1)S(1)}, u32[]{:S(2)}, u32[]{:S(2)}) %collective-permute-start.1) | collective-permute-done | bytes 73760 | tf_op jit(solution)/shard_map/ppermute | solution.py:20
  6.9 0.1 broadcast_select_fusion.1
  7.1 1.7 %collective-permute-start.2 = (bf16[2,6,3,1024]{3,0,2,1:T(2,128)(2,1)S(1)}, bf16[2,6,3,1024]{3,0,2,1:T(2,128)(2,1)S(1)}, u32[]{:S(2)}, u32[]{:S(2)}) collective-permute-start(bf16[2,6,3,1024]{3,0,2,1:T(2,128)(2,1)S(1)} %broadcast_select_fusion.1), channel_id=1, source_target_pairs={{0,4},{1,5},{2,6},{3,7},{4,0},{5,1},{6,2},{7,3},{8,12},{9,13},{10,... | collective-permute-start | bytes 221192 | tf_op jit(solution)/shard_map/ppermute | solution.py:20
  8.8 0.7 broadcast_add_fusion
  9.5 0.1 broadcast_in_dim.26
  9.6 0.1 sub.59
  9.7 1.9 %collective-permute-done.2 = bf16[2,6,3,1024]{3,0,2,1:T(2,128)(2,1)S(1)} collective-permute-done((bf16[2,6,3,1024]{3,0,2,1:T(2,128)(2,1)S(1)}, bf16[2,6,3,1024]{3,0,2,1:T(2,128)(2,1)S(1)}, u32[]{:S(2)}, u32[]{:S(2)}) %collective-permute-start.2) | collective-permute-done | bytes 73760 | tf_op jit(solution)/shard_map/ppermute | solution.py:20
  11.5 0.1 broadcast_select_fusion.2
  11.7 3.4 %collective-permute-start.3 = (bf16[2,6,3,1024]{3,0,2,1:T(2,128)(2,1)S(1)}, bf16[2,6,3,1024]{3,0,2,1:T(2,128)(2,1)S(1)}, u32[]{:S(2)}, u32[]{:S(2)}) collective-permute-start(bf16[2,6,3,1024]{3,0,2,1:T(2,128)(2,1)S(1)} %broadcast_select_fusion.2), channel_id=1, source_target_pairs={{0,8},{1,9},{2,10},{3,11},{4,12},{5,13},{6,14},{7,15},{8,0},{9,1},... | collective-permute-start | bytes 221192 | tf_op jit(solution)/shard_map/ppermute | solution.py:20
  15.0 0.5 and_select_fusion.7.shift_ref
  15.5 0.1 copy.8
  15.6 0.7 reshape.25.weight_ref
  16.3 12.7 %copy.9 = bf16[1024,6,3,256]{0,3,2,1:T(8,128)(2,1)} copy(bf16[1024,6,3,256]{3,0,2,1:T(8,128)(2,1)} %param.5) | data formatting | bytes 18874368 | tf_op args[0]
  29.0 0.0 collective-permute-done.3
  29.0 0.1 fusion.7
  29.2 3.0 %rev.8 = f32[2,6,3,1024]{3,0,2,1:T(2,128)} reverse(f32[2,6,3,1024]{3,0,2,1:T(2,128)S(1)} %fusion.7), dimensions={3} | reverse | bytes 294912 | tf_op jit(solution)/shard_map/jit(_flip)/rev | solution.py:43
  32.2 0.0 slice-start
  32.2 12.5 %shard_map.55 = bf16[4608,1024]{1,0:T(8,128)(2,1)} custom-call(s32[36]{0:T(128)} %and_select_fusion.7.shift_ref, f32[18]{0:T(128)} %reshape.25.weight_ref, f32[18,2,1024]{2,1,0:T(2,128)} %bitcast.30), custom_call_target="tpu_custom_call" | custom-call | bytes 9437184 | tf_op jit(solution)/shard_map/pallas_call | solution.py:48
  44.7 0.0 slice-start.1
  44.7 0.0 slice-start.2
  44.7 0.0 copy-start
  44.7 9.2 %fusion = f32[512,1024]{1,0:T(8,128)S(1)} fusion(bf16[1024,4608]{0,1:T(8,128)(2,1)} %bitcast.25, bf16[4608,1024]{1,0:T(8,128)(2,1)} %shard_map.55), kind=kOutput, calls=%fused_computation | convolution fusion | flops 4831838208 | bytes 16252928 | tf_op jit(solution)/shard_map/dot_general | solution.py:101
  53.9 0.0 copy-start.1
  53.9 0.8 dynamic-slice_bitcast_fusion
  54.8 4.0 %collective-permute-start.7 = (f32[256,512]{0,1:T(8,128)}, f32[256,512]{0,1:T(8,128)}, u32[]{:S(2)}, u32[]{:S(2)}) collective-permute-start(f32[256,512]{0,1:T(8,128)} %dynamic-slice_bitcast_fusion), channel_id=1, source_target_pairs={{0,96},{16,112},{32,0},{48,16},{64,32},{80,48},{96,64},{112,80},{1... | collective-permute-start | bytes 1572872 | tf_op jit(solution)/shard_map/ppermute | solution.py:83
  58.8 0.0 slice-done
  58.8 0.0 slice-done.1
  58.8 0.0 slice-done.2
  58.8 0.0 copy-done
  58.8 5.1 %fusion.2 = f32[512,1024]{1,0:T(8,128)S(1)} fusion(bf16[1024,4608]{0,1:T(8,128)(2,1)S(1)} %bitcast.28, bf16[4608,1024]{1,0:T(8,128)(2,1)S(1)} %copy-done), kind=kOutput, calls=%fused_computation.2 | convolution fusion | flops 4831838208 | bytes 16252928 | tf_op jit(solution)/shard_map/dot_general | solution.py:101
  63.9 0.0 copy-done.1
  63.9 0.8 dynamic-slice_bitcast_fusion.1
  64.8 0.0 collective-permute-start.4
  64.8 3.3 %collective-permute-done.7 = f32[256,512]{0,1:T(8,128)} collective-permute-done((f32[256,512]{0,1:T(8,128)}, f32[256,512]{0,1:T(8,128)}, u32[]{:S(2)}, u32[]{:S(2)}) %collective-permute-start.7) | collective-permute-done | bytes 524320 | tf_op jit(solution)/shard_map/ppermute | solution.py:83
  68.1 1.3 %bitcast_add_fusion.2 = f32[256,512]{0,1:T(8,128)S(1)} fusion(f32[256,512]{0,1:T(8,128)} %collective-permute-done.7, f32[512,1024]{1,0:T(8,128)} %copy-done.1, s32[]{:T(128)S(6)} %select_n.180), kind=kLoop, calls=%fused_computation.13 | loop fusion | flops 131072 | bytes 1572868 | tf_op jit(solution)/shard_map/add | solution.py:85
  69.3 3.8 %collective-permute-start.8 = (f32[256,512]{0,1:T(8,128)S(1)}, f32[256,512]{0,1:T(8,128)}, u32[]{:S(2)}, u32[]{:S(2)}) collective-permute-start(f32[256,512]{0,1:T(8,128)S(1)} %bitcast_add_fusion.2), channel_id=1, source_target_pairs={{0,96},{16,112},{32,0},{48,16},{64,32},{80,48},{96,64},{112,80},{1... | collective-permute-start | bytes 1572872 | tf_op jit(solution)/shard_map/ppermute | solution.py:83
  73.1 4.2 %collective-permute-done.4 = f32[256,512]{0,1:T(8,128)S(1)} collective-permute-done((f32[256,512]{0,1:T(8,128)}, f32[256,512]{0,1:T(8,128)S(1)}, u32[]{:S(2)}, u32[]{:S(2)}) %collective-permute-start.4) | collective-permute-done | bytes 524320 | tf_op jit(solution)/shard_map/ppermute | solution.py:83
  77.3 0.9 bitcast_add_fusion.5
  78.2 0.0 collective-permute-start.5
  78.2 2.9 %collective-permute-done.8 = f32[256,512]{0,1:T(8,128)} collective-permute-done((f32[256,512]{0,1:T(8,128)S(1)}, f32[256,512]{0,1:T(8,128)}, u32[]{:S(2)}, u32[]{:S(2)}) %collective-permute-start.8) | collective-permute-done | bytes 524320 | tf_op jit(solution)/shard_map/ppermute | solution.py:83
  81.1 1.3 %bitcast_add_fusion.1 = f32[256,512]{0,1:T(8,128)S(1)} fusion(f32[256,512]{0,1:T(8,128)} %collective-permute-done.8, f32[512,1024]{1,0:T(8,128)} %copy-done.1, s32[]{:T(128)S(6)} %select_n.182), kind=kLoop, calls=%fused_computation.12 | loop fusion | flops 131072 | bytes 1572868 | tf_op jit(solution)/shard_map/add | solution.py:85
  82.4 3.9 %collective-permute-start.9 = (f32[256,512]{0,1:T(8,128)S(1)}, f32[256,512]{0,1:T(8,128)S(1)}, u32[]{:S(2)}, u32[]{:S(2)}) collective-permute-start(f32[256,512]{0,1:T(8,128)S(1)} %bitcast_add_fusion.1), channel_id=1, source_target_pairs={{0,96},{16,112},{32,0},{48,16},{64,32},{80,48},{96,64},{112,80},{1... | collective-permute-start | bytes 1572872 | tf_op jit(solution)/shard_map/ppermute | solution.py:83
  86.2 3.7 %collective-permute-done.5 = f32[256,512]{0,1:T(8,128)} collective-permute-done((f32[256,512]{0,1:T(8,128)}, f32[256,512]{0,1:T(8,128)}, u32[]{:S(2)}, u32[]{:S(2)}) %collective-permute-start.5) | collective-permute-done | bytes 524320 | tf_op jit(solution)/shard_map/ppermute | solution.py:83
  89.9 1.9 %bitcast_add_fusion.4 = f32[256,512]{0,1:T(8,128)} fusion(f32[256,512]{0,1:T(8,128)} %collective-permute-done.5, f32[512,1024]{1,0:T(8,128)S(1)} %fusion.2, s32[]{:T(128)S(6)} %select_n.174), kind=kLoop, calls=%fused_computation.15 | loop fusion | flops 131072 | bytes 1572868 | tf_op jit(solution)/shard_map/add | solution.py:85
  91.9 0.0 collective-permute-start.6
  91.9 1.4 %collective-permute-done.9 = f32[256,512]{0,1:T(8,128)S(1)} collective-permute-done((f32[256,512]{0,1:T(8,128)S(1)}, f32[256,512]{0,1:T(8,128)S(1)}, u32[]{:S(2)}, u32[]{:S(2)}) %collective-permute-start.9) | collective-permute-done | bytes 524320 | tf_op jit(solution)/shard_map/ppermute | solution.py:83
  93.3 1.1 bitcast_add_fusion
  94.4 8.3 %collective-permute-done.6 = f32[256,512]{0,1:T(8,128)} collective-permute-done((f32[256,512]{0,1:T(8,128)}, f32[256,512]{0,1:T(8,128)}, u32[]{:S(2)}, u32[]{:S(2)}) %collective-permute-start.6) | collective-permute-done | bytes 524320 | tf_op jit(solution)/shard_map/ppermute | solution.py:83
  102.7 1.1 bitcast_add_fusion.3
  103.9 3.1 %collective-permute-start.10 = (f32[128,1024]{0,1:T(8,128)S(1)}, f32[128,1024]{0,1:T(8,128)S(1)}, u32[]{:S(2)}, u32[]{:S(2)}) collective-permute-start(f32[128,1024]{0,1:T(8,128)S(1)} %fusion.4), channel_id=1, source_target_pairs={{0,16},{16,0},{32,48},{48,32},{64,80},{80,64},{96,112},{112,96},{1... | collective-permute-start | bytes 1572872 | tf_op jit(solution)/shard_map/ppermute | solution.py:91
  107.0 7.7 %collective-permute-done.10 = f32[128,1024]{0,1:T(8,128)S(1)} collective-permute-done((f32[128,1024]{0,1:T(8,128)S(1)}, f32[128,1024]{0,1:T(8,128)S(1)}, u32[]{:S(2)}, u32[]{:S(2)}) %collective-permute-start.10) | collective-permute-done | bytes 524320 | tf_op jit(solution)/shard_map/ppermute | solution.py:91
  114.6 0.1 fusion.6
  114.7 0.2 copy.10
  114.9 2.3 %rev.9 = f32[128,2,512]{2,1,0:T(2,128)} reverse(f32[128,2,512]{2,1,0:T(2,128)S(1)} %copy.10), dimensions={2} | reverse | bytes 1048576 | tf_op jit(solution)/shard_map/jit(_flip)/rev | solution.py:105
  (2 shorter events, 0.0 us)
Async XLA Ops:
  0.0 1.5 %collective-permute-start = (bf16[2,6,3,1024]{3,0,2,1:T(2,128)(2,1)}, bf16[2,6,3,1024]{3,0,2,1:T(2,128)(2,1)S(1)}, u32[]{:S(2)}, u32[]{:S(2)}) collective-permute-start(bf16[2,6,3,1024]{3,0,2,1:T(2,128)(2,1)} %bitcast.31), channel_id=1, source_target_pairs={{0,1},{1,0},{2,3},{3,2},{4,5},{5,4},{6,7},{7,6},{8,9},{9,8},{10,11... | collective-permute-start | bytes 221192 | tf_op jit(solution)/shard_map/ppermute | solution.py:20
  2.5 4.4 %collective-permute-start.1 = (bf16[2,6,3,1024]{3,0,2,1:T(2,128)(2,1)S(1)}, bf16[2,6,3,1024]{3,0,2,1:T(2,128)(2,1)S(1)}, u32[]{:S(2)}, u32[]{:S(2)}) collective-permute-start(bf16[2,6,3,1024]{3,0,2,1:T(2,128)(2,1)S(1)} %broadcast_select_fusion), channel_id=1, source_target_pairs={{0,2},{1,3},{2,0},{3,1},{4,6},{5,7},{6,4},{7,5},{8,10},{9,11},{10,... | collective-permute-start | bytes 221192 | tf_op jit(solution)/shard_map/ppermute | solution.py:20
  7.1 4.4 %collective-permute-start.2 = (bf16[2,6,3,1024]{3,0,2,1:T(2,128)(2,1)S(1)}, bf16[2,6,3,1024]{3,0,2,1:T(2,128)(2,1)S(1)}, u32[]{:S(2)}, u32[]{:S(2)}) collective-permute-start(bf16[2,6,3,1024]{3,0,2,1:T(2,128)(2,1)S(1)} %broadcast_select_fusion.1), channel_id=1, source_target_pairs={{0,4},{1,5},{2,6},{3,7},{4,0},{5,1},{6,2},{7,3},{8,12},{9,13},{10,... | collective-permute-start | bytes 221192 | tf_op jit(solution)/shard_map/ppermute | solution.py:20
  11.7 17.3 %collective-permute-start.3 = (bf16[2,6,3,1024]{3,0,2,1:T(2,128)(2,1)S(1)}, bf16[2,6,3,1024]{3,0,2,1:T(2,128)(2,1)S(1)}, u32[]{:S(2)}, u32[]{:S(2)}) collective-permute-start(bf16[2,6,3,1024]{3,0,2,1:T(2,128)(2,1)S(1)} %broadcast_select_fusion.2), channel_id=1, source_target_pairs={{0,8},{1,9},{2,10},{3,11},{4,12},{5,13},{6,14},{7,15},{8,0},{9,1},... | collective-permute-start | bytes 221192 | tf_op jit(solution)/shard_map/ppermute | solution.py:20
  32.2 26.6 %slice-start = ((s8[9437184]{0:T(1024)(128)(4,1)}), s8[1048576]{0:T(1024)(128)(4,1)S(1)}, s32[]{:S(2)}) async-start(s8[9437184]{0:T(1024)(128)(4,1)} %bitcast.26), calls=%async_computation | async-start | bytes 2097152
  44.7 14.1 %slice-start.1 = ((s8[9437184]{0:T(1024)(128)(4,1)}), s8[4194304]{0:T(1024)(128)(4,1)S(1)}, s32[]{:S(2)}) async-start(s8[9437184]{0:T(1024)(128)(4,1)} %bitcast.26), calls=%async_computation.1 | async-start | bytes 8388608
  44.7 14.1 %slice-start.2 = ((s8[9437184]{0:T(1024)(128)(4,1)}), s8[4194304]{0:T(1024)(128)(4,1)S(1)}, s32[]{:S(2)}) async-start(s8[9437184]{0:T(1024)(128)(4,1)} %bitcast.26), calls=%async_computation.2 | async-start | bytes 8388608
  44.7 14.1 %copy-start = (bf16[4608,1024]{1,0:T(8,128)(2,1)S(1)}, bf16[4608,1024]{1,0:T(8,128)(2,1)}, u32[]{:S(2)}) copy-start(bf16[4608,1024]{1,0:T(8,128)(2,1)} %shard_map.55) | copy-start | bytes 28311556
  53.9 10.0 %copy-start.1 = (f32[512,1024]{1,0:T(8,128)}, f32[512,1024]{1,0:T(8,128)S(1)}, u32[]{:S(2)}) copy-start(f32[512,1024]{1,0:T(8,128)S(1)} %fusion) | copy-start | bytes 6291460
  54.8 13.3 %collective-permute-start.7 = (f32[256,512]{0,1:T(8,128)}, f32[256,512]{0,1:T(8,128)}, u32[]{:S(2)}, u32[]{:S(2)}) collective-permute-start(f32[256,512]{0,1:T(8,128)} %dynamic-slice_bitcast_fusion), channel_id=1, source_target_pairs={{0,96},{16,112},{32,0},{48,16},{64,32},{80,48},{96,64},{112,80},{1... | collective-permute-start | bytes 1572872 | tf_op jit(solution)/shard_map/ppermute | solution.py:83
  64.8 12.5 %collective-permute-start.4 = (f32[256,512]{0,1:T(8,128)}, f32[256,512]{0,1:T(8,128)S(1)}, u32[]{:S(2)}, u32[]{:S(2)}) collective-permute-start(f32[256,512]{0,1:T(8,128)} %dynamic-slice_bitcast_fusion.1), channel_id=1, source_target_pairs={{0,32},{16,48},{32,64},{48,80},{64,96},{80,112},{96,0},{112,16},{1... | collective-permute-start | bytes 1572872 | tf_op jit(solution)/shard_map/ppermute | solution.py:83
  69.3 11.8 %collective-permute-start.8 = (f32[256,512]{0,1:T(8,128)S(1)}, f32[256,512]{0,1:T(8,128)}, u32[]{:S(2)}, u32[]{:S(2)}) collective-permute-start(f32[256,512]{0,1:T(8,128)S(1)} %bitcast_add_fusion.2), channel_id=1, source_target_pairs={{0,96},{16,112},{32,0},{48,16},{64,32},{80,48},{96,64},{112,80},{1... | collective-permute-start | bytes 1572872 | tf_op jit(solution)/shard_map/ppermute | solution.py:83
  78.2 11.7 %collective-permute-start.5 = (f32[256,512]{0,1:T(8,128)}, f32[256,512]{0,1:T(8,128)}, u32[]{:S(2)}, u32[]{:S(2)}) collective-permute-start(f32[256,512]{0,1:T(8,128)} %bitcast_add_fusion.5), channel_id=1, source_target_pairs={{0,32},{16,48},{32,64},{48,80},{64,96},{80,112},{96,0},{112,16},{1... | collective-permute-start | bytes 1572872 | tf_op jit(solution)/shard_map/ppermute | solution.py:83
  82.4 10.9 %collective-permute-start.9 = (f32[256,512]{0,1:T(8,128)S(1)}, f32[256,512]{0,1:T(8,128)S(1)}, u32[]{:S(2)}, u32[]{:S(2)}) collective-permute-start(f32[256,512]{0,1:T(8,128)S(1)} %bitcast_add_fusion.1), channel_id=1, source_target_pairs={{0,96},{16,112},{32,0},{48,16},{64,32},{80,48},{96,64},{112,80},{1... | collective-permute-start | bytes 1572872 | tf_op jit(solution)/shard_map/ppermute | solution.py:83
  91.9 10.8 %collective-permute-start.6 = (f32[256,512]{0,1:T(8,128)}, f32[256,512]{0,1:T(8,128)}, u32[]{:S(2)}, u32[]{:S(2)}) collective-permute-start(f32[256,512]{0,1:T(8,128)} %bitcast_add_fusion.4), channel_id=1, source_target_pairs={{0,32},{16,48},{32,64},{48,80},{64,96},{80,112},{96,0},{112,16},{1... | collective-permute-start | bytes 1572872 | tf_op jit(solution)/shard_map/ppermute | solution.py:83
  103.9 10.8 %collective-permute-start.10 = (f32[128,1024]{0,1:T(8,128)S(1)}, f32[128,1024]{0,1:T(8,128)S(1)}, u32[]{:S(2)}, u32[]{:S(2)}) collective-permute-start(f32[128,1024]{0,1:T(8,128)S(1)} %fusion.4), channel_id=1, source_target_pairs={{0,16},{16,0},{32,48},{48,32},{64,80},{80,64},{96,112},{112,96},{1... | collective-permute-start | bytes 1572872 | tf_op jit(solution)/shard_map/ppermute | solution.py:91

commit v4 on v3

--- a/solution.py
+++ b/solution.py
@@ -97,8 +97,16 @@
     flat_green = green.reshape(point_rows, -1)
     traces = from_owners(records_buffer[0], "loc", owners)
     toeplitz = toeplitz_reversed(traces, onsets, codes)
+    rows = green.shape[1] * green.shape[2]
+    green_t = jnp.transpose(green, (1, 2, 0, 3)).reshape(rows, point_rows, NT)
+    toeplitz = toeplitz.reshape(rows, NT, EV * LAGS)
     halves = [
-        jnp.dot(flat_green, toeplitz[:, e * LAGS : (e + 1) * LAGS], preferred_element_type=jnp.float32)
+        jnp.einsum(
+            "rpt,rtn->pn",
+            green_t,
+            toeplitz[:, :, e * LAGS : (e + 1) * LAGS],
+            preferred_element_type=jnp.float32,
+        )
         for e in range(EV)
     ]
     totals = reduce_over_sens(halves)

time: 119 us -> 107 us (0.90)
  local copies, waits for them, and re-layouts: 20.8 us -> 7.28 us
  matrix products: 14.3 us -> 16.9 us
    unnamed x11 -> x4, local copies, waits for them, and re-layouts: 12.7 us -> 0.01 us
    dot_general x2, matrix products: 14.3 us -> 16.9 us  [local(): jnp.einsum('rpt,rtn->pn', green_t, toeplitz[:, :, e * LAGS:(e + 1) * LAGS...]
    ppermute x4, waiting for transfers between devices: 4.74 us -> 6.04 us  [from_owners(): got = lax.ppermute(x, axis, [(i, i ^ bit) for i in range(size)])]
  transfers between devices with their start and end apart: 11 -> 11, of which waited for: 10 -> 8; matrix products, arithmetic and copies ran while one was open for 24% -> 17% of each run, Pallas kernels for 0% -> 0%
where the time goes in v4:
time: 107 us; the launch traced here: 106 us
  waiting for transfers between devices  36.8 us (34%)
  starting transfers between devices  21.1 us (20%)
  matrix products  16.9 us (16%)
  Pallas kernels  12.4 us (12%)
  other arithmetic  11.8 us (11%)
  local copies, waits for them, and re-layouts  7.28 us (7%)
    ppermute x6, waiting for transfers between devices, reduce_over_sens(): got = lax.ppermute(acc, 'sens', ring_perm(step))  23.1 us
    dot_general x2, matrix products, local(): jnp.einsum('rpt,rtn->pn', green_t, toeplitz[:, :, e * LAGS:(e + 1) * LAGS...  16.9 us
    pallas_call x1, Pallas kernels, toeplitz_reversed(): pl.pallas_call(_toeplitz_kernel, grid_spec=pltpu.PrefetchScalarGridSpec(n...  12.4 us
    ppermute x6, starting transfers between devices, reduce_over_sens(): got = lax.ppermute(acc, 'sens', ring_perm(step))  11.2 us
    ppermute x1, waiting for transfers between devices, reduce_over_sens(): got = lax.ppermute(theirs, 'sens', [(i, i ^ 1) for i in range(size)])  7.67 us
    add x6, other arithmetic, reduce_over_sens(): acc = got + chunk(half, c)  7.6 us
    ppermute x4, starting transfers between devices, from_owners(): got = lax.ppermute(x, axis, [(i, i ^ bit) for i in range(size)])  6.75 us
    ppermute x4, waiting for transfers between devices, from_owners(): got = lax.ppermute(x, axis, [(i, i ^ bit) for i in range(size)])  6.04 us
  transfers between devices with their start and end apart: 11, of which 8 were waited for; matrix products, arithmetic and copies ran while one was open for 17% of the time, Pallas kernels for 0%

profile of v4, /device:TPU:0, one launch (start us, length us, event | category | flops | bytes accessed | tf_op | source)
XLA Modules:
  0.0 106.3 jit_solution(4223192201165322125)
XLA Ops:
  0.0 0.0 collective-permute-start
  0.0 0.7 fusion.14
  0.7 0.8 collective-permute-done
  1.5 1.0 broadcast_select_fusion
  2.5 1.7 %collective-permute-start.1 = (bf16[2,6,3,1024]{3,0,2,1:T(2,128)(2,1)S(1)}, bf16[2,6,3,1024]{3,0,2,1:T(2,128)(2,1)S(1)}, u32[]{:S(2)}, u32[]{:S(2)}) collective-permute-start(bf16[2,6,3,1024]{3,0,2,1:T(2,128)(2,1)S(1)} %broadcast_select_fusion), channel_id=1, source_target_pairs={{0,2},{1,3},{2,0},{3,1},{4,6},{5,7},{6,4},{7,5},{8,10},{9,11},{10,... | collective-permute-start | bytes 221192 | tf_op jit(solution)/shard_map/ppermute | solution.py:20
  4.2 0.7 multiply_exponential_fusion
  4.9 2.1 %collective-permute-done.1 = bf16[2,6,3,1024]{3,0,2,1:T(2,128)(2,1)S(1)} collective-permute-done((bf16[2,6,3,1024]{3,0,2,1:T(2,128)(2,1)S(1)}, bf16[2,6,3,1024]{3,0,2,1:T(2,128)(2,1)S(1)}, u32[]{:S(2)}, u32[]{:S(2)}) %collective-permute-start.1) | collective-permute-done | bytes 73760 | tf_op jit(solution)/shard_map/ppermute | solution.py:20
  6.9 0.1 broadcast_select_fusion.1
  7.1 1.7 %collective-permute-start.2 = (bf16[2,6,3,1024]{3,0,2,1:T(2,128)(2,1)S(1)}, bf16[2,6,3,1024]{3,0,2,1:T(2,128)(2,1)S(1)}, u32[]{:S(2)}, u32[]{:S(2)}) collective-permute-start(bf16[2,6,3,1024]{3,0,2,1:T(2,128)(2,1)S(1)} %broadcast_select_fusion.1), channel_id=1, source_target_pairs={{0,4},{1,5},{2,6},{3,7},{4,0},{5,1},{6,2},{7,3},{8,12},{9,13},{10,... | collective-permute-start | bytes 221192 | tf_op jit(solution)/shard_map/ppermute | solution.py:20
  8.8 0.7 broadcast_add_fusion
  9.5 0.1 broadcast_in_dim.26
  9.6 0.1 sub.59
  9.7 1.9 %collective-permute-done.2 = bf16[2,6,3,1024]{3,0,2,1:T(2,128)(2,1)S(1)} collective-permute-done((bf16[2,6,3,1024]{3,0,2,1:T(2,128)(2,1)S(1)}, bf16[2,6,3,1024]{3,0,2,1:T(2,128)(2,1)S(1)}, u32[]{:S(2)}, u32[]{:S(2)}) %collective-permute-start.2) | collective-permute-done | bytes 73760 | tf_op jit(solution)/shard_map/ppermute | solution.py:20
  11.5 0.1 broadcast_select_fusion.2
  11.7 3.4 %collective-permute-start.3 = (bf16[2,6,3,1024]{3,0,2,1:T(2,128)(2,1)S(1)}, bf16[2,6,3,1024]{3,0,2,1:T(2,128)(2,1)S(1)}, u32[]{:S(2)}, u32[]{:S(2)}) collective-permute-start(bf16[2,6,3,1024]{3,0,2,1:T(2,128)(2,1)S(1)} %broadcast_select_fusion.2), channel_id=1, source_target_pairs={{0,8},{1,9},{2,10},{3,11},{4,12},{5,13},{6,14},{7,15},{8,0},{9,1},... | collective-permute-start | bytes 221192 | tf_op jit(solution)/shard_map/ppermute | solution.py:20
  15.0 0.6 and_select_fusion.7.shift_ref
  15.6 0.1 copy.10
  15.7 0.6 reshape.28.weight_ref
  16.3 1.3 %collective-permute-done.3 = bf16[2,6,3,1024]{3,0,2,1:T(2,128)(2,1)S(1)} collective-permute-done((bf16[2,6,3,1024]{3,0,2,1:T(2,128)(2,1)S(1)}, bf16[2,6,3,1024]{3,0,2,1:T(2,128)(2,1)S(1)}, u32[]{:S(2)}, u32[]{:S(2)}) %collective-permute-start.3) | collective-permute-done | bytes 73760 | tf_op jit(solution)/shard_map/ppermute | solution.py:20
  17.6 0.1 fusion.13
  17.8 3.0 %rev.8 = f32[2,6,3,1024]{3,0,2,1:T(2,128)} reverse(f32[2,6,3,1024]{3,0,2,1:T(2,128)S(1)} %fusion.13), dimensions={3} | reverse | bytes 294912 | tf_op jit(solution)/shard_map/jit(_flip)/rev | solution.py:43
  20.8 12.4 %shard_map.55 = bf16[4608,1024]{1,0:T(8,128)(2,1)} custom-call(s32[36]{0:T(128)} %and_select_fusion.7.shift_ref, f32[18]{0:T(128)} %reshape.28.weight_ref, f32[18,2,1024]{2,1,0:T(2,128)} %bitcast.35), custom_call_target="tpu_custom_call" | custom-call | bytes 9437184 | tf_op jit(solution)/shard_map/pallas_call | solution.py:48
  33.1 0.0 copy-start
  33.1 9.2 %fusion.7 = f32[512,1024]{1,0:T(8,128)S(1)} fusion(bf16[18,1024,256]{2,1,0:T(8,128)(2,1)} %bitcast.37, bf16[18,256,1024]{2,1,0:T(8,128)(2,1)} %bitcast.32), kind=kOutput, calls=%fused_computation.5 | convolution fusion | flops 4831838208 | bytes 16252928 | tf_op jit(solution)/shard_map/rpt,rtn->pn/dot_general | solution.py:104
  42.4 0.0 copy-start.1
  42.4 4.2 %collective-permute-start.7 = (f32[256,512]{0,1:T(8,128)S(1)}, f32[256,512]{0,1:T(8,128)}, u32[]{:S(2)}, u32[]{:S(2)}) collective-permute-start(f32[256,512]{0,1:T(8,128)S(1)} %dynamic-slice_bitcast_fusion), channel_id=1, source_target_pairs={{0,96},{16,112},{32,0},{48,16},{64,32},{80,48},{96,64},{112,80},{1... | collective-permute-start | bytes 1572872 | tf_op jit(solution)/shard_map/ppermute | solution.py:83
  46.6 0.0 copy-done
  46.6 7.7 %fusion.4 = f32[512,1024]{1,0:T(8,128)S(1)} fusion(bf16[18,1024,256]{2,1,0:T(8,128)(2,1)} %bitcast.38, bf16[18,256,1024]{2,1,0:T(8,128)(2,1)S(1)} %bitcast.33), kind=kOutput, calls=%fused_computation.4 | convolution fusion | flops 4831838208 | bytes 16252928 | tf_op jit(solution)/shard_map/rpt,rtn->pn/dot_general | solution.py:104
  54.3 0.0 copy-done.1
  54.3 0.8 dynamic-slice_bitcast_fusion.1
  55.2 0.0 collective-permute-start.4
  55.2 0.0 collective-permute-done.7
  55.2 1.3 %bitcast_add_fusion.2 = f32[256,512]{0,1:T(8,128)S(1)} fusion(f32[256,512]{0,1:T(8,128)} %collective-permute-done.7, f32[512,1024]{1,0:T(8,128)} %copy-done.1, s32[]{:T(128)S(6)} %select_n.180), kind=kLoop, calls=%fused_computation.15 | loop fusion | flops 131072 | bytes 1572868 | tf_op jit(solution)/shard_map/add | solution.py:85
  56.4 3.6 %collective-permute-start.8 = (f32[256,512]{0,1:T(8,128)S(1)}, f32[256,512]{0,1:T(8,128)}, u32[]{:S(2)}, u32[]{:S(2)}) collective-permute-start(f32[256,512]{0,1:T(8,128)S(1)} %bitcast_add_fusion.2), channel_id=1, source_target_pairs={{0,96},{16,112},{32,0},{48,16},{64,32},{80,48},{96,64},{112,80},{1... | collective-permute-start | bytes 1572872 | tf_op jit(solution)/shard_map/ppermute | solution.py:83
  60.1 7.0 %collective-permute-done.4 = f32[256,512]{0,1:T(8,128)S(1)} collective-permute-done((f32[256,512]{0,1:T(8,128)}, f32[256,512]{0,1:T(8,128)S(1)}, u32[]{:S(2)}, u32[]{:S(2)}) %collective-permute-start.4) | collective-permute-done | bytes 524320 | tf_op jit(solution)/shard_map/ppermute | solution.py:83
  67.1 0.9 bitcast_add_fusion.5
  68.0 0.0 collective-permute-start.5
  68.0 0.0 collective-permute-done.8
  68.0 1.3 %bitcast_add_fusion.1 = f32[256,512]{0,1:T(8,128)S(1)} fusion(f32[256,512]{0,1:T(8,128)} %collective-permute-done.8, f32[512,1024]{1,0:T(8,128)} %copy-done.1, s32[]{:T(128)S(6)} %select_n.182), kind=kLoop, calls=%fused_computation.14 | loop fusion | flops 131072 | bytes 1572868 | tf_op jit(solution)/shard_map/add | solution.py:85
  69.3 3.4 %collective-permute-start.9 = (f32[256,512]{0,1:T(8,128)S(1)}, f32[256,512]{0,1:T(8,128)S(1)}, u32[]{:S(2)}, u32[]{:S(2)}) collective-permute-start(f32[256,512]{0,1:T(8,128)S(1)} %bitcast_add_fusion.1), channel_id=1, source_target_pairs={{0,96},{16,112},{32,0},{48,16},{64,32},{80,48},{96,64},{112,80},{1... | collective-permute-start | bytes 1572872 | tf_op jit(solution)/shard_map/ppermute | solution.py:83
  72.6 6.5 %collective-permute-done.5 = f32[256,512]{0,1:T(8,128)} collective-permute-done((f32[256,512]{0,1:T(8,128)}, f32[256,512]{0,1:T(8,128)}, u32[]{:S(2)}, u32[]{:S(2)}) %collective-permute-start.5) | collective-permute-done | bytes 524320 | tf_op jit(solution)/shard_map/ppermute | solution.py:83
  79.1 1.9 %bitcast_add_fusion.4 = f32[256,512]{0,1:T(8,128)} fusion(f32[256,512]{0,1:T(8,128)} %collective-permute-done.5, f32[512,1024]{1,0:T(8,128)S(1)} %fusion.4, s32[]{:T(128)S(6)} %select_n.174), kind=kLoop, calls=%fused_computation.17 | loop fusion | flops 131072 | bytes 1572868 | tf_op jit(solution)/shard_map/add | solution.py:85
  81.1 0.0 collective-permute-start.6
  81.1 0.0 collective-permute-done.9
  81.1 1.1 %bitcast_add_fusion = f32[256,512]{0,1:T(8,128)S(1)} fusion(f32[256,512]{0,1:T(8,128)S(1)} %collective-permute-done.9, f32[512,1024]{1,0:T(8,128)} %copy-done.1, s32[]{:T(128)S(6)} %select_n.184), kind=kLoop, calls=%fused_computation.13 | loop fusion | flops 131072 | bytes 1572868 | tf_op jit(solution)/shard_map/add | solution.py:85
  82.2 9.6 %collective-permute-done.6 = f32[256,512]{0,1:T(8,128)} collective-permute-done((f32[256,512]{0,1:T(8,128)}, f32[256,512]{0,1:T(8,128)}, u32[]{:S(2)}, u32[]{:S(2)}) %collective-permute-start.6) | collective-permute-done | bytes 524320 | tf_op jit(solution)/shard_map/ppermute | solution.py:83
  91.8 1.1 %bitcast_add_fusion.3 = f32[256,512]{0,1:T(8,128)S(1)} fusion(f32[256,512]{0,1:T(8,128)} %collective-permute-done.6, f32[512,1024]{1,0:T(8,128)S(1)} %fusion.4, s32[]{:T(128)S(6)} %select_n.176), kind=kLoop, calls=%fused_computation.16 | loop fusion | flops 131072 | bytes 1572868 | tf_op jit(solution)/shard_map/add | solution.py:85
  92.9 3.1 %collective-permute-start.10 = (f32[128,1024]{0,1:T(8,128)S(1)}, f32[128,1024]{0,1:T(8,128)S(1)}, u32[]{:S(2)}, u32[]{:S(2)}) collective-permute-start(f32[128,1024]{0,1:T(8,128)S(1)} %fusion.10), channel_id=1, source_target_pairs={{0,16},{16,0},{32,48},{48,32},{64,80},{80,64},{96,112},{112,96},{1... | collective-permute-start | bytes 1572872 | tf_op jit(solution)/shard_map/ppermute | solution.py:91
  96.0 7.7 %collective-permute-done.10 = f32[128,1024]{0,1:T(8,128)S(1)} collective-permute-done((f32[128,1024]{0,1:T(8,128)S(1)}, f32[128,1024]{0,1:T(8,128)S(1)}, u32[]{:S(2)}, u32[]{:S(2)}) %collective-permute-start.10) | collective-permute-done | bytes 524320 | tf_op jit(solution)/shard_map/ppermute | solution.py:91
  103.7 0.1 fusion.12
  103.8 0.2 copy.13
  104.0 2.3 %rev.9 = f32[128,2,512]{2,1,0:T(2,128)} reverse(f32[128,2,512]{2,1,0:T(2,128)S(1)} %copy.13), dimensions={2} | reverse | bytes 1048576 | tf_op jit(solution)/shard_map/jit(_flip)/rev | solution.py:113
  (2 shorter events, 0.1 us)
Async XLA Ops:
  0.0 1.5 %collective-permute-start = (bf16[2,6,3,1024]{3,0,2,1:T(2,128)(2,1)}, bf16[2,6,3,1024]{3,0,2,1:T(2,128)(2,1)S(1)}, u32[]{:S(2)}, u32[]{:S(2)}) collective-permute-start(bf16[2,6,3,1024]{3,0,2,1:T(2,128)(2,1)} %bitcast.36), channel_id=1, source_target_pairs={{0,1},{1,0},{2,3},{3,2},{4,5},{5,4},{6,7},{7,6},{8,9},{9,8},{10,11... | collective-permute-start | bytes 221192 | tf_op jit(solution)/shard_map/ppermute | solution.py:20
  2.5 4.4 %collective-permute-start.1 = (bf16[2,6,3,1024]{3,0,2,1:T(2,128)(2,1)S(1)}, bf16[2,6,3,1024]{3,0,2,1:T(2,128)(2,1)S(1)}, u32[]{:S(2)}, u32[]{:S(2)}) collective-permute-start(bf16[2,6,3,1024]{3,0,2,1:T(2,128)(2,1)S(1)} %broadcast_select_fusion), channel_id=1, source_target_pairs={{0,2},{1,3},{2,0},{3,1},{4,6},{5,7},{6,4},{7,5},{8,10},{9,11},{10,... | collective-permute-start | bytes 221192 | tf_op jit(solution)/shard_map/ppermute | solution.py:20
  7.1 4.4 %collective-permute-start.2 = (bf16[2,6,3,1024]{3,0,2,1:T(2,128)(2,1)S(1)}, bf16[2,6,3,1024]{3,0,2,1:T(2,128)(2,1)S(1)}, u32[]{:S(2)}, u32[]{:S(2)}) collective-permute-start(bf16[2,6,3,1024]{3,0,2,1:T(2,128)(2,1)S(1)} %broadcast_select_fusion.1), channel_id=1, source_target_pairs={{0,4},{1,5},{2,6},{3,7},{4,0},{5,1},{6,2},{7,3},{8,12},{9,13},{10,... | collective-permute-start | bytes 221192 | tf_op jit(solution)/shard_map/ppermute | solution.py:20
  11.7 5.9 %collective-permute-start.3 = (bf16[2,6,3,1024]{3,0,2,1:T(2,128)(2,1)S(1)}, bf16[2,6,3,1024]{3,0,2,1:T(2,128)(2,1)S(1)}, u32[]{:S(2)}, u32[]{:S(2)}) collective-permute-start(bf16[2,6,3,1024]{3,0,2,1:T(2,128)(2,1)S(1)} %broadcast_select_fusion.2), channel_id=1, source_target_pairs={{0,8},{1,9},{2,10},{3,11},{4,12},{5,13},{6,14},{7,15},{8,0},{9,1},... | collective-permute-start | bytes 221192 | tf_op jit(solution)/shard_map/ppermute | solution.py:20
  33.1 13.5 %copy-start = (bf16[4608,1024]{1,0:T(8,128)(2,1)S(1)}, bf16[4608,1024]{1,0:T(8,128)(2,1)}, u32[]{:S(2)}) copy-start(bf16[4608,1024]{1,0:T(8,128)(2,1)} %shard_map.55) | copy-start | bytes 28311556
  42.4 11.9 %copy-start.1 = (f32[512,1024]{1,0:T(8,128)}, f32[512,1024]{1,0:T(8,128)S(1)}, u32[]{:S(2)}) copy-start(f32[512,1024]{1,0:T(8,128)S(1)} %fusion.7) | copy-start | bytes 6291460
  42.4 12.7 %collective-permute-start.7 = (f32[256,512]{0,1:T(8,128)S(1)}, f32[256,512]{0,1:T(8,128)}, u32[]{:S(2)}, u32[]{:S(2)}) collective-permute-start(f32[256,512]{0,1:T(8,128)S(1)} %dynamic-slice_bitcast_fusion), channel_id=1, source_target_pairs={{0,96},{16,112},{32,0},{48,16},{64,32},{80,48},{96,64},{112,80},{1... | collective-permute-start | bytes 1572872 | tf_op jit(solution)/shard_map/ppermute | solution.py:83
  55.2 11.9 %collective-permute-start.4 = (f32[256,512]{0,1:T(8,128)}, f32[256,512]{0,1:T(8,128)S(1)}, u32[]{:S(2)}, u32[]{:S(2)}) collective-permute-start(f32[256,512]{0,1:T(8,128)} %dynamic-slice_bitcast_fusion.1), channel_id=1, source_target_pairs={{0,32},{16,48},{32,64},{48,80},{64,96},{80,112},{96,0},{112,16},{1... | collective-permute-start | bytes 1572872 | tf_op jit(solution)/shard_map/ppermute | solution.py:83
  56.4 11.6 %collective-permute-start.8 = (f32[256,512]{0,1:T(8,128)S(1)}, f32[256,512]{0,1:T(8,128)}, u32[]{:S(2)}, u32[]{:S(2)}) collective-permute-start(f32[256,512]{0,1:T(8,128)S(1)} %bitcast_add_fusion.2), channel_id=1, source_target_pairs={{0,96},{16,112},{32,0},{48,16},{64,32},{80,48},{96,64},{112,80},{1... | collective-permute-start | bytes 1572872 | tf_op jit(solution)/shard_map/ppermute | solution.py:83
  68.0 11.1 %collective-permute-start.5 = (f32[256,512]{0,1:T(8,128)}, f32[256,512]{0,1:T(8,128)}, u32[]{:S(2)}, u32[]{:S(2)}) collective-permute-start(f32[256,512]{0,1:T(8,128)} %bitcast_add_fusion.5), channel_id=1, source_target_pairs={{0,32},{16,48},{32,64},{48,80},{64,96},{80,112},{96,0},{112,16},{1... | collective-permute-start | bytes 1572872 | tf_op jit(solution)/shard_map/ppermute | solution.py:83
  69.3 11.8 %collective-permute-start.9 = (f32[256,512]{0,1:T(8,128)S(1)}, f32[256,512]{0,1:T(8,128)S(1)}, u32[]{:S(2)}, u32[]{:S(2)}) collective-permute-start(f32[256,512]{0,1:T(8,128)S(1)} %bitcast_add_fusion.1), channel_id=1, source_target_pairs={{0,96},{16,112},{32,0},{48,16},{64,32},{80,48},{96,64},{112,80},{1... | collective-permute-start | bytes 1572872 | tf_op jit(solution)/shard_map/ppermute | solution.py:83
  81.1 10.7 %collective-permute-start.6 = (f32[256,512]{0,1:T(8,128)}, f32[256,512]{0,1:T(8,128)}, u32[]{:S(2)}, u32[]{:S(2)}) collective-permute-start(f32[256,512]{0,1:T(8,128)} %bitcast_add_fusion.4), channel_id=1, source_target_pairs={{0,32},{16,48},{32,64},{48,80},{64,96},{80,112},{96,0},{112,16},{1... | collective-permute-start | bytes 1572872 | tf_op jit(solution)/shard_map/ppermute | solution.py:83
  92.9 10.8 %collective-permute-start.10 = (f32[128,1024]{0,1:T(8,128)S(1)}, f32[128,1024]{0,1:T(8,128)S(1)}, u32[]{:S(2)}, u32[]{:S(2)}) collective-permute-start(f32[128,1024]{0,1:T(8,128)S(1)} %fusion.10), channel_id=1, source_target_pairs={{0,16},{16,0},{32,48},{48,32},{64,80},{80,64},{96,112},{112,96},{1... | collective-permute-start | bytes 1572872 | tf_op jit(solution)/shard_map/ppermute | solution.py:91

commit v5 on v2

v5 whole, which is shorter than its diff:
```python
import jax
import jax.numpy as jnp
from jax import lax
from jax.experimental import pallas as pl
from jax.experimental.pallas import tpu as pltpu
from jax.sharding import PartitionSpec as P

NT = 256
LAGS = 512
SAMPLES = 1024
EV = 2
WIDE = LAGS + NT


def from_owners(x, axis, roots, radix=4):
    size = lax.axis_size(axis)
    me = lax.axis_index(axis)
    span = 1
    while span < size:
        radix = min(radix, size // span)
        digit = (roots // span) % radix
        mine = (me // span) % radix
        out = x
        for d in range(1, radix):
            perm = [(i, i - ((i // span) % radix) * span + (((i // span) % radix + d) % radix) * span) for i in range(size)]
            got = lax.ppermute(x, axis, perm)
            src = (mine + radix - d) % radix
            out = jnp.where((src == digit).reshape((-1,) + (1,) * (x.ndim - 1)), got, out)
        x = out
        span *= radix
    return x


def _toeplitz_kernel(shift_ref, weight_ref, rev_ref, out_ref):
    sc = pl.program_id(0)
    row = rev_ref[0]
    row = pltpu.roll(row, shift_ref[sc], 1)
    row = (row * weight_ref[sc]).astype(jnp.bfloat16).astype(jnp.float32)
    row = jnp.concatenate([row[:, :LAGS], row[:, SAMPLES - NT :]], axis=1)
    wide = jnp.broadcast_to(row, (NT, WIDE))
    band = pltpu.roll(wide, 0, 1, stride=1, stride_axis=0)
    out_ref[...] = band[:, :LAGS].astype(out_ref.dtype)


def toeplitz_reversed(rev, shifts, weights):
    rows = rev.shape[0]
    return pl.pallas_call(
        _toeplitz_kernel,
        grid_spec=pltpu.PrefetchScalarGridSpec(
            num_scalar_prefetch=1,
            grid=(rows,),
            in_specs=[
                pl.BlockSpec(memory_space=pltpu.SMEM),
                pl.BlockSpec((1, 1, SAMPLES), lambda i, s: (i, 0, 0)),
            ],
            out_specs=pl.BlockSpec((NT, LAGS), lambda i, s: (i, 0)),
        ),
        out_shape=jax.ShapeDtypeStruct((rows * NT, LAGS), jnp.bfloat16),
        cost_estimate=pl.CostEstimate(flops=0, transcendentals=0, bytes_accessed=rows * NT * LAGS * 2),
    )(shifts, weights, rev)


def local(green, records_buffer, owners, onsets, codes):
    point_rows = green.shape[0]
    rows = green.shape[1] * green.shape[2]
    green_t = jnp.transpose(green, (1, 2, 0, 3)).reshape(rows, point_rows, NT)
    flipped = jnp.flip(records_buffer[0], axis=-1)
    traces = from_owners(flipped, "loc", owners)
    rev = traces.astype(jnp.float32).reshape(EV, rows, 1, SAMPLES)
    shifts = (jnp.repeat(onsets.astype(jnp.int32), 3, axis=1) - LAGS) % SAMPLES
    weights = jnp.exp2(-codes.astype(jnp.float32)).reshape(-1)

    size = lax.axis_size("sens")
    me = lax.axis_index("sens")
    xs = 2
    zs = size // xs
    z, xh = me // xs, me % xs
    quarter = point_rows // zs
    block = quarter // xs

    def piece(band, c):
        g = lax.dynamic_slice_in_dim(green_t, c * quarter, quarter, 1)
        return jnp.einsum("rpt,rtn->pn", g, band.reshape(rows, NT, LAGS), preferred_element_type=jnp.float32)

    def ring_perm(step):
        return [(i, ((i // xs + step) % zs) * xs + i % xs) for i in range(size)]

    outs = []
    for e, step in zip(range(EV), (1, zs - 1)):
        band = toeplitz_reversed(rev[e], shifts[e], weights)
        acc = piece(band, (z + zs - step) % zs)
        for k in range(zs - 1):
            got = lax.ppermute(acc, "sens", ring_perm(step))
            acc = got + piece(band, (z + 4 * zs - step * (k + 2)) % zs)
        theirs = lax.dynamic_slice_in_dim(acc, (1 - xh) * block, block, 0)
        kept = lax.dynamic_slice_in_dim(acc, xh * block, block, 0)
        got = lax.ppermute(theirs, "sens", [(i, i ^ 1) for i in range(size)])
        outs.append(jnp.flip(kept, axis=-1) + jnp.flip(got, axis=-1))
    return jnp.stack(outs, axis=1)


def solution(mesh):
    return jax.shard_map(
        local,
        mesh=mesh,
        in_specs=(
            P("loc", "sens", None, None),
            P("loc", None, "sens", None, None),
            P(),
            P(None, "sens"),
            P("sens", None),
        ),
        out_specs=P(("loc", "sens"), None, None),
        check_vma=False,
    )
```

time: 272 us -> 106 us (0.39)
  waiting for transfers between devices: 189 us -> 26.8 us
  local copies, waits for them, and re-layouts: 27.7 us -> 8.4 us
  starting transfers between devices: 6.75 us -> 21.7 us
  between operations: 14.1 us -> 0.3 us
  Pallas kernels: 12.4 us -> 22.7 us
  matrix products: 16 us -> 21.4 us
    unnamed x2 -> x0, waiting for transfers between devices: 184 us -> none
    ppermute x4 -> x14, waiting for transfers between devices: 4.74 us -> 26.8 us  [the longest x6 16.6 us: local(): got = lax.ppermute(acc, 'sens', ring_perm(step))]
    ppermute x4 -> x14, starting transfers between devices: 6.75 us -> 21.7 us  [the longest x6 10.1 us: local(): got = lax.ppermute(acc, 'sens', ring_perm(step))]
    unnamed x5 -> x14, local copies, waits for them, and re-layouts: 14.3 us -> 0.03 us
    pallas_call x1 -> x2, Pallas kernels: 12.4 us -> 22.7 us  [toeplitz_reversed(): pl.pallas_call(_toeplitz_kernel, grid_spec=pltpu.PrefetchScalarGridSpec(n...]
    reshape x2 -> x1, local copies, waits for them, and re-layouts: 7.89 us -> 0.65 us  [local(): weights = jnp.exp2(-codes.astype(jnp.float32)).reshape(-1)]
    dot_general x1 -> x8, matrix products: 16 us -> 21.4 us  [piece(): jnp.einsum('rpt,rtn->pn', g, band.reshape(rows, NT, LAGS), preferred_elem...]
  transfers between devices with their start and end apart: 5 -> 14, of which waited for: 4 -> 9; matrix products, arithmetic and copies ran while one was open for 6% -> 21% of each run, Pallas kernels for 0% -> 11%
where the time goes in v5:
time: 106 us; the launch traced here: 104 us
  waiting for transfers between devices  26.8 us (25%)
  Pallas kernels  22.7 us (21%)
  starting transfers between devices  21.7 us (20%)
  matrix products  21.4 us (20%)
  local copies, waits for them, and re-layouts  8.4 us (8%)
  other arithmetic  2.98 us (3%)
    pallas_call x2, Pallas kernels, toeplitz_reversed(): pl.pallas_call(_toeplitz_kernel, grid_spec=pltpu.PrefetchScalarGridSpec(n...  22.7 us
    dot_general x8, matrix products, piece(): jnp.einsum('rpt,rtn->pn', g, band.reshape(rows, NT, LAGS), preferred_elem...  21.4 us
    ppermute x6, waiting for transfers between devices, local(): got = lax.ppermute(acc, 'sens', ring_perm(step))  16.6 us
    ppermute x6, starting transfers between devices, local(): got = lax.ppermute(acc, 'sens', ring_perm(step))  10.1 us
    ppermute x6, starting transfers between devices, from_owners(): got = lax.ppermute(x, axis, perm)  6.58 us
    ppermute x6, waiting for transfers between devices, from_owners(): got = lax.ppermute(x, axis, perm)  5.97 us
    ppermute x2, starting transfers between devices, local(): got = lax.ppermute(theirs, 'sens', [(i, i ^ 1) for i in range(size)])  5.08 us
    ppermute x2, waiting for transfers between devices, local(): got = lax.ppermute(theirs, 'sens', [(i, i ^ 1) for i in range(size)])  4.25 us
  transfers between devices with their start and end apart: 14, of which 9 were waited for; matrix products, arithmetic and copies ran while one was open for 21% of the time, Pallas kernels for 11%

profile of v5, /device:TPU:0, one launch (start us, length us, event | category | flops | bytes accessed | tf_op | source)
XLA Modules:
  0.0 104.3 jit_solution(7684675803026975934)
XLA Ops:
  0.0 3.4 %rev.17 = bf16[2,6,3,1024]{3,0,2,1:T(2,128)(2,1)S(1)} reverse(bf16[2,6,3,1024]{3,0,2,1:T(2,128)(2,1)} %bitcast.58), dimensions={3} | reverse | bytes 147456 | tf_op jit(solution)/shard_map/jit(_flip)/rev | solution.py:67
  3.4 1.1 %collective-permute-start = (bf16[2,6,3,1024]{3,0,2,1:T(2,128)(2,1)S(1)}, bf16[2,6,3,1024]{3,0,2,1:T(2,128)(2,1)S(1)}, u32[]{:S(2)}, u32[]{:S(2)}) collective-permute-start(bf16[2,6,3,1024]{3,0,2,1:T(2,128)(2,1)S(1)} %rev.17), channel_id=1, source_target_pairs={{0,3},{1,0},{2,1},{3,2},{4,7},{5,4},{6,5},{7,6},{8,11},{9,8},{10,9... | collective-permute-start | bytes 221192 | tf_op jit(solution)/shard_map/ppermute | solution.py:26
  4.5 0.7 collective-permute-start.1
  5.1 0.2 collective-permute-start.2
  5.3 0.7 broadcast_add_fusion
  6.0 0.1 broadcast_in_dim.36
  6.0 0.1 sub.68
  6.1 0.5 slice_bitcast_fusion.1
  6.7 0.7 multiply_exponential_fusion
  7.3 0.7 broadcast_compare_fusion
  8.1 0.0 collective-permute-done
  8.1 1.6 %collective-permute-done.1 = bf16[2,6,3,1024]{3,0,2,1:T(2,128)(2,1)S(1)} collective-permute-done((bf16[2,6,3,1024]{3,0,2,1:T(2,128)(2,1)S(1)}, bf16[2,6,3,1024]{3,0,2,1:T(2,128)(2,1)S(1)}, u32[]{:S(2)}, u32[]{:S(2)}) %collective-permute-start.1) | collective-permute-done | bytes 73760 | tf_op jit(solution)/shard_map/ppermute | solution.py:26
  9.7 0.0 collective-permute-done.2
  9.7 0.2 broadcast_select_fusion.4
  10.0 3.1 %collective-permute-start.3 = (bf16[2,6,3,1024]{3,0,2,1:T(2,128)(2,1)S(1)}, bf16[2,6,3,1024]{3,0,2,1:T(2,128)(2,1)S(1)}, u32[]{:S(2)}, u32[]{:S(2)}) collective-permute-start(bf16[2,6,3,1024]{3,0,2,1:T(2,128)(2,1)S(1)} %broadcast_select_fusion.4), channel_id=1, source_target_pairs={{0,12},{1,13},{2,14},{3,15},{4,0},{5,1},{6,2},{7,3},{8,4},{9,5},{1... | collective-permute-start | bytes 221192 | tf_op jit(solution)/shard_map/ppermute | solution.py:26
  13.1 0.6 collective-permute-start.4
  13.7 1.0 collective-permute-start.5
  14.7 0.1 copy.8
  14.8 0.7 reshape.39.weight_ref
  15.4 0.0 collective-permute-done.3
  15.4 3.6 %collective-permute-done.4 = bf16[2,6,3,1024]{3,0,2,1:T(2,128)(2,1)S(1)} collective-permute-done((bf16[2,6,3,1024]{3,0,2,1:T(2,128)(2,1)S(1)}, bf16[2,6,3,1024]{3,0,2,1:T(2,128)(2,1)S(1)}, u32[]{:S(2)}, u32[]{:S(2)}) %collective-permute-start.4) | collective-permute-done | bytes 73760 | tf_op jit(solution)/shard_map/ppermute | solution.py:26
  19.0 0.7 collective-permute-done.5
  19.7 0.2 fusion.46
  20.0 0.8 fusion.57
  20.7 11.2 %shard_map.56 = bf16[4608,512]{1,0:T(8,128)(2,1)} custom-call(s32[18]{0:T(128)} %get-tuple-element.16.shift_ref, f32[18]{0:T(128)} %reshape.39.weight_ref, f32[18,1,1024]{2,1,0:T(1,128)} %bitcast.57), custom_call_target="tpu_custom_call" | custom-call | bytes 4718592 | tf_op jit(solution)/shard_map/pallas_call | solution.py:47
  32.0 4.4 %fusion.28 = f32[256,512]{1,0:T(8,128)S(1)} fusion(bf16[18,256,512]{2,1,0:T(8,128)(2,1)} %bitcast.44, bf16[18,1024,256]{2,1,0:T(8,128)(2,1)} %bitcast.59, s32[]{:T(128)S(6)} %select_n.184), kind=kOutput, calls=%fused_computation.20 | convolution fusion | flops 1207959552 | bytes 7602180 | tf_op jit(solution)/shard_map/rpt,rtn->pn/dot_general | solution.py:83
  36.4 4.1 %collective-permute-start.10 = (f32[256,512]{1,0:T(8,128)S(1)}, f32[256,512]{1,0:T(8,128)S(1)}, u32[]{:S(2)}, u32[]{:S(2)}) collective-permute-start(f32[256,512]{1,0:T(8,128)S(1)} %fusion.28), channel_id=1, source_target_pairs={{0,96},{16,112},{32,0},{48,16},{64,32},{80,48},{96,64},{112,80},{1... | collective-permute-start | bytes 1572872 | tf_op jit(solution)/shard_map/ppermute | solution.py:93
  40.5 11.5 %shard_map.55 = bf16[4608,512]{1,0:T(8,128)(2,1)} custom-call(s32[18]{0:T(128)} %get-tuple-element.15.shift_ref, f32[18]{0:T(128)} %reshape.39.weight_ref, f32[18,1,1024]{2,1,0:T(1,128)} %bitcast.56), custom_call_target="tpu_custom_call" | custom-call | bytes 4718592 | tf_op jit(solution)/shard_map/pallas_call | solution.py:47
  52.0 0.0 slice-start.2
  52.0 4.6 %fusion.16 = f32[256,512]{1,0:T(8,128)S(1)} fusion(bf16[18,256,512]{2,1,0:T(8,128)(2,1)} %bitcast.50, bf16[18,1024,256]{2,1,0:T(8,128)(2,1)} %bitcast.60, s32[]{:T(128)S(6)} %select_n.154), kind=kOutput, calls=%fused_computation.16 | convolution fusion | flops 1207959552 | bytes 7602180 | tf_op jit(solution)/shard_map/rpt,rtn->pn/dot_general | solution.py:83
  56.6 0.0 slice-start.6
  56.6 0.0 slice-start.3
  56.6 0.1 collective-permute-start.6
  56.7 0.0 collective-permute-done.10
  56.7 0.0 slice-done
  56.7 0.0 slice-done.1
  56.7 3.9 %fusion.40 = f32[256,512]{1,0:T(8,128)S(1)} fusion(f32[256,512]{1,0:T(8,128)S(1)} %collective-permute-done.10, bf16[18,256,512]{2,1,0:T(8,128)(2,1)S(1)} %bitcast.47, bf16[18,1024,256]{2,1,0:T(8,128)(2,1)} %bitcast.61, s32[]{:T(128)S(6)} %select_n.186), kind=kOutput, calls=%fused_computation.24 | convolution fusion | flops 1208090624 | bytes 8126468 | tf_op jit(solution)/shard_map/rpt,rtn->pn/dot_general | solution.py:83
  60.6 2.5 %collective-permute-start.11 = (f32[256,512]{1,0:T(8,128)S(1)}, f32[256,512]{1,0:T(8,128)S(1)}, u32[]{:S(2)}, u32[]{:S(2)}) collective-permute-start(f32[256,512]{1,0:T(8,128)S(1)} %fusion.40), channel_id=1, source_target_pairs={{0,96},{16,112},{32,0},{48,16},{64,32},{80,48},{96,64},{112,80},{1... | collective-permute-start | bytes 1572872 | tf_op jit(solution)/shard_map/ppermute | solution.py:93
  63.1 1.4 %fusion.34 = f32[256,512]{1,0:T(8,128)S(1)} fusion(bf16[18,256,512]{2,1,0:T(8,128)(2,1)S(1)} %bitcast.48, bf16[18,1024,256]{2,1,0:T(8,128)(2,1)S(1)} %bitcast.65, s32[]{:T(128)S(6)} %select_n.188), kind=kOutput, calls=%fused_computation.22 | convolution fusion | flops 1207959552 | bytes 7602180 | tf_op jit(solution)/shard_map/rpt,rtn->pn/dot_general | solution.py:83
  64.5 5.2 %collective-permute-done.6 = f32[256,512]{1,0:T(8,128)S(1)} collective-permute-done((f32[256,512]{1,0:T(8,128)S(1)}, f32[256,512]{1,0:T(8,128)S(1)}, u32[]{:S(2)}, u32[]{:S(2)}) %collective-permute-start.6) | collective-permute-done | bytes 524320 | tf_op jit(solution)/shard_map/ppermute | solution.py:93
  69.7 1.4 %fusion.43 = f32[256,512]{1,0:T(8,128)S(1)} fusion(f32[256,512]{1,0:T(8,128)S(1)} %collective-permute-done.6, bf16[18,256,512]{2,1,0:T(8,128)(2,1)S(1)} %bitcast.53, bf16[18,1024,256]{2,1,0:T(8,128)(2,1)S(1)} %bitcast.66, s32[]{:T(128)S(6)} %select_n.175), kind=kOutput, calls=%fused_computation.25 | convolution fusion | flops 1208090624 | bytes 8126468 | tf_op jit(solution)/shard_map/rpt,rtn->pn/dot_general | solution.py:83
  71.1 0.1 collective-permute-start.7
  71.2 1.4 %collective-permute-done.11 = f32[256,512]{1,0:T(8,128)S(1)} collective-permute-done((f32[256,512]{1,0:T(8,128)S(1)}, f32[256,512]{1,0:T(8,128)S(1)}, u32[]{:S(2)}, u32[]{:S(2)}) %collective-permute-start.11) | collective-permute-done | bytes 524320 | tf_op jit(solution)/shard_map/ppermute | solution.py:93
  72.6 0.1 add.221
  72.7 3.3 %collective-permute-start.12 = (f32[256,512]{1,0:T(8,128)S(1)}, f32[256,512]{1,0:T(8,128)S(1)}, u32[]{:S(2)}, u32[]{:S(2)}) collective-permute-start(f32[256,512]{1,0:T(8,128)S(1)} %add.221), channel_id=1, source_target_pairs={{0,96},{16,112},{32,0},{48,16},{64,32},{80,48},{96,64},{112,80},{1... | collective-permute-start | bytes 1572872 | tf_op jit(solution)/shard_map/ppermute | solution.py:93
  75.9 1.4 %fusion.37 = f32[256,512]{1,0:T(8,128)S(1)} fusion(bf16[18,256,512]{2,1,0:T(8,128)(2,1)S(1)} %bitcast.49, bf16[18,1024,256]{2,1,0:T(8,128)(2,1)S(1)} %bitcast.67, s32[]{:T(128)S(6)} %select_n.190), kind=kOutput, calls=%fused_computation.23 | convolution fusion | flops 1207959552 | bytes 7602180 | tf_op jit(solution)/shard_map/rpt,rtn->pn/dot_general | solution.py:83
  77.3 1.4 %fusion.22 = f32[256,512]{1,0:T(8,128)S(1)} fusion(bf16[18,256,512]{2,1,0:T(8,128)(2,1)S(1)} %bitcast.54, bf16[18,1024,256]{2,1,0:T(8,128)(2,1)S(1)} %bitcast.68, s32[]{:T(128)S(6)} %select_n.177), kind=kOutput, calls=%fused_computation.18 | convolution fusion | flops 1207959552 | bytes 7602180 | tf_op jit(solution)/shard_map/rpt,rtn->pn/dot_general | solution.py:83
  78.7 4.5 %collective-permute-done.7 = f32[256,512]{1,0:T(8,128)S(1)} collective-permute-done((f32[256,512]{1,0:T(8,128)S(1)}, f32[256,512]{1,0:T(8,128)S(1)}, u32[]{:S(2)}, u32[]{:S(2)}) %collective-permute-start.7) | collective-permute-done | bytes 524320 | tf_op jit(solution)/shard_map/ppermute | solution.py:93
  83.2 0.1 add.206
  83.3 0.1 collective-permute-start.8
  83.4 0.7 collective-permute-done.12
  84.0 0.1 add.224
  84.2 2.6 %collective-permute-start.13 = (f32[128,512]{1,0:T(8,128)S(1)}, f32[128,512]{1,0:T(8,128)S(1)}, u32[]{:S(2)}, u32[]{:S(2)}) collective-permute-start(f32[128,512]{1,0:T(8,128)S(1)} %get-tuple-element.11), channel_id=1, source_target_pairs={{0,16},{16,0},{32,48},{48,32},{64,80},{80,64},{96,112},{112,96},{1... | collective-permute-start | bytes 786440 | tf_op jit(solution)/shard_map/ppermute | solution.py:97
  86.8 3.0 %fusion.25 = f32[256,512]{1,0:T(8,128)S(1)} fusion(bf16[18,256,512]{2,1,0:T(8,128)(2,1)S(1)} %bitcast.55, bf16[18,1024,256]{2,1,0:T(8,128)(2,1)} %bitcast.62, s32[]{:T(128)S(6)} %select_n.179), kind=kOutput, calls=%fused_computation.19 | convolution fusion | flops 1207959552 | bytes 7602180 | tf_op jit(solution)/shard_map/rpt,rtn->pn/dot_general | solution.py:83
  89.8 4.7 %collective-permute-done.8 = f32[256,512]{1,0:T(8,128)S(1)} collective-permute-done((f32[256,512]{1,0:T(8,128)S(1)}, f32[256,512]{1,0:T(8,128)S(1)}, u32[]{:S(2)}, u32[]{:S(2)}) %collective-permute-start.8) | collective-permute-done | bytes 524320 | tf_op jit(solution)/shard_map/ppermute | solution.py:93
  94.5 0.1 add.209
  94.7 2.5 %collective-permute-start.9 = (f32[128,512]{1,0:T(8,128)S(1)}, f32[128,512]{1,0:T(8,128)S(1)}, u32[]{:S(2)}, u32[]{:S(2)}) collective-permute-start(f32[128,512]{1,0:T(8,128)S(1)} %get-tuple-element.9), channel_id=1, source_target_pairs={{0,16},{16,0},{32,48},{48,32},{64,80},{80,64},{96,112},{112,96},{1... | collective-permute-start | bytes 786440 | tf_op jit(solution)/shard_map/ppermute | solution.py:97
  97.2 0.4 rev.20
  97.5 0.4 rev.18
  97.9 0.0 collective-permute-done.13
  97.9 0.4 rev.21
  98.4 4.2 %collective-permute-done.9 = f32[128,512]{1,0:T(8,128)S(1)} collective-permute-done((f32[128,512]{1,0:T(8,128)S(1)}, f32[128,512]{1,0:T(8,128)S(1)}, u32[]{:S(2)}, u32[]{:S(2)}) %collective-permute-start.9) | collective-permute-done | bytes 262176 | tf_op jit(solution)/shard_map/ppermute | solution.py:97
  102.6 0.4 rev.19
  103.1 1.2 %copy.9 = f32[128,2,512]{2,1,0:T(2,128)} copy(f32[128,2,512]{2,0,1:T(8,128)S(1)} %pad_maximum_fusion) | data formatting | bytes 1048576 | tf_op jit(solution)/shard_map/stack | solution.py:99
  (20 shorter events, 0.3 us)
Async XLA Ops:
  3.4 4.7 %collective-permute-start = (bf16[2,6,3,1024]{3,0,2,1:T(2,128)(2,1)S(1)}, bf16[2,6,3,1024]{3,0,2,1:T(2,128)(2,1)S(1)}, u32[]{:S(2)}, u32[]{:S(2)}) collective-permute-start(bf16[2,6,3,1024]{3,0,2,1:T(2,128)(2,1)S(1)} %rev.17), channel_id=1, source_target_pairs={{0,3},{1,0},{2,1},{3,2},{4,7},{5,4},{6,5},{7,6},{8,11},{9,8},{10,9... | collective-permute-start | bytes 221192 | tf_op jit(solution)/shard_map/ppermute | solution.py:26
  4.5 5.2 %collective-permute-start.1 = (bf16[2,6,3,1024]{3,0,2,1:T(2,128)(2,1)S(1)}, bf16[2,6,3,1024]{3,0,2,1:T(2,128)(2,1)S(1)}, u32[]{:S(2)}, u32[]{:S(2)}) collective-permute-start(bf16[2,6,3,1024]{3,0,2,1:T(2,128)(2,1)S(1)} %rev.17), channel_id=1, source_target_pairs={{0,2},{1,3},{2,0},{3,1},{4,6},{5,7},{6,4},{7,5},{8,10},{9,11},{10,... | collective-permute-start | bytes 221192 | tf_op jit(solution)/shard_map/ppermute | solution.py:26
  5.1 4.6 %collective-permute-start.2 = (bf16[2,6,3,1024]{3,0,2,1:T(2,128)(2,1)S(1)}, bf16[2,6,3,1024]{3,0,2,1:T(2,128)(2,1)S(1)}, u32[]{:S(2)}, u32[]{:S(2)}) collective-permute-start(bf16[2,6,3,1024]{3,0,2,1:T(2,128)(2,1)S(1)} %rev.17), channel_id=1, source_target_pairs={{0,1},{1,2},{2,3},{3,0},{4,5},{5,6},{6,7},{7,4},{8,9},{9,10},{10,1... | collective-permute-start | bytes 221192 | tf_op jit(solution)/shard_map/ppermute | solution.py:26
  10.0 5.5 %collective-permute-start.3 = (bf16[2,6,3,1024]{3,0,2,1:T(2,128)(2,1)S(1)}, bf16[2,6,3,1024]{3,0,2,1:T(2,128)(2,1)S(1)}, u32[]{:S(2)}, u32[]{:S(2)}) collective-permute-start(bf16[2,6,3,1024]{3,0,2,1:T(2,128)(2,1)S(1)} %broadcast_select_fusion.4), channel_id=1, source_target_pairs={{0,12},{1,13},{2,14},{3,15},{4,0},{5,1},{6,2},{7,3},{8,4},{9,5},{1... | collective-permute-start | bytes 221192 | tf_op jit(solution)/shard_map/ppermute | solution.py:26
  13.1 5.9 %collective-permute-start.4 = (bf16[2,6,3,1024]{3,0,2,1:T(2,128)(2,1)S(1)}, bf16[2,6,3,1024]{3,0,2,1:T(2,128)(2,1)S(1)}, u32[]{:S(2)}, u32[]{:S(2)}) collective-permute-start(bf16[2,6,3,1024]{3,0,2,1:T(2,128)(2,1)S(1)} %broadcast_select_fusion.4), channel_id=1, source_target_pairs={{0,8},{1,9},{2,10},{3,11},{4,12},{5,13},{6,14},{7,15},{8,0},{9,1},... | collective-permute-start | bytes 221192 | tf_op jit(solution)/shard_map/ppermute | solution.py:26
  13.7 6.1 %collective-permute-start.5 = (bf16[2,6,3,1024]{3,0,2,1:T(2,128)(2,1)S(1)}, bf16[2,6,3,1024]{3,0,2,1:T(2,128)(2,1)S(1)}, u32[]{:S(2)}, u32[]{:S(2)}) collective-permute-start(bf16[2,6,3,1024]{3,0,2,1:T(2,128)(2,1)S(1)} %broadcast_select_fusion.4), channel_id=1, source_target_pairs={{0,4},{1,5},{2,6},{3,7},{4,8},{5,9},{6,10},{7,11},{8,12},{9,13},{1... | collective-permute-start | bytes 221192 | tf_op jit(solution)/shard_map/ppermute | solution.py:26
  36.4 20.3 %collective-permute-start.10 = (f32[256,512]{1,0:T(8,128)S(1)}, f32[256,512]{1,0:T(8,128)S(1)}, u32[]{:S(2)}, u32[]{:S(2)}) collective-permute-start(f32[256,512]{1,0:T(8,128)S(1)} %fusion.28), channel_id=1, source_target_pairs={{0,96},{16,112},{32,0},{48,16},{64,32},{80,48},{96,64},{112,80},{1... | collective-permute-start | bytes 1572872 | tf_op jit(solution)/shard_map/ppermute | solution.py:93
  40.5 22.6 %slice-start.4 = ((s8[9437184]{0:T(1024)(128)(4,1)}), s8[1048576]{0:T(1024)(128)(4,1)S(1)}, s32[]{:S(2)}) async-start(s8[9437184]{0:T(1024)(128)(4,1)} %bitcast.63), calls=%async_computation.4 | async-start | bytes 2097152
  52.0 4.7 %slice-start = ((s8[4718592]{0:T(1024)(128)(4,1)}), s8[4194304]{0:T(1024)(128)(4,1)S(1)}, s32[]{:S(2)}) async-start(s8[4718592]{0:T(1024)(128)(4,1)} %bitcast.45), calls=%async_computation | async-start | bytes 8388608
  52.0 4.7 %slice-start.1 = ((s8[4718592]{0:T(1024)(128)(4,1)}), s8[524288]{0:T(1024)(128)(4,1)S(1)}, s32[]{:S(2)}) async-start(s8[4718592]{0:T(1024)(128)(4,1)} %bitcast.45), calls=%async_computation.1 | async-start | bytes 1048576
  52.0 11.1 %slice-start.5 = ((s8[9437184]{0:T(1024)(128)(4,1)}), s8[4194304]{0:T(1024)(128)(4,1)S(1)}, s32[]{:S(2)}) async-start(s8[9437184]{0:T(1024)(128)(4,1)} %bitcast.63), calls=%async_computation.5 | async-start | bytes 8388608
  52.0 17.7 %slice-start.2 = ((s8[4718592]{0:T(1024)(128)(4,1)}), s8[4194304]{0:T(1024)(128)(4,1)S(1)}, s32[]{:S(2)}) async-start(s8[4718592]{0:T(1024)(128)(4,1)} %bitcast.51), calls=%async_computation.2 | async-start | bytes 8388608
  56.6 6.5 %slice-start.6 = ((s8[9437184]{0:T(1024)(128)(4,1)}), s8[4194304]{0:T(1024)(128)(4,1)S(1)}, s32[]{:S(2)}) async-start(s8[9437184]{0:T(1024)(128)(4,1)} %bitcast.63), calls=%async_computation.6 | async-start | bytes 8388608
  56.6 13.1 %slice-start.3 = ((s8[4718592]{0:T(1024)(128)(4,1)}), s8[524288]{0:T(1024)(128)(4,1)S(1)}, s32[]{:S(2)}) async-start(s8[4718592]{0:T(1024)(128)(4,1)} %bitcast.51), calls=%async_computation.3 | async-start | bytes 1048576
  56.6 13.1 %collective-permute-start.6 = (f32[256,512]{1,0:T(8,128)S(1)}, f32[256,512]{1,0:T(8,128)S(1)}, u32[]{:S(2)}, u32[]{:S(2)}) collective-permute-start(f32[256,512]{1,0:T(8,128)S(1)} %fusion.16), channel_id=1, source_target_pairs={{0,32},{16,48},{32,64},{48,80},{64,96},{80,112},{96,0},{112,16},{1... | collective-permute-start | bytes 1572872 | tf_op jit(solution)/shard_map/ppermute | solution.py:93
  60.6 12.0 %collective-permute-start.11 = (f32[256,512]{1,0:T(8,128)S(1)}, f32[256,512]{1,0:T(8,128)S(1)}, u32[]{:S(2)}, u32[]{:S(2)}) collective-permute-start(f32[256,512]{1,0:T(8,128)S(1)} %fusion.40), channel_id=1, source_target_pairs={{0,96},{16,112},{32,0},{48,16},{64,32},{80,48},{96,64},{112,80},{1... | collective-permute-start | bytes 1572872 | tf_op jit(solution)/shard_map/ppermute | solution.py:93
  71.1 12.1 %collective-permute-start.7 = (f32[256,512]{1,0:T(8,128)S(1)}, f32[256,512]{1,0:T(8,128)S(1)}, u32[]{:S(2)}, u32[]{:S(2)}) collective-permute-start(f32[256,512]{1,0:T(8,128)S(1)} %fusion.43), channel_id=1, source_target_pairs={{0,32},{16,48},{32,64},{48,80},{64,96},{80,112},{96,0},{112,16},{1... | collective-permute-start | bytes 1572872 | tf_op jit(solution)/shard_map/ppermute | solution.py:93
  72.7 11.4 %collective-permute-start.12 = (f32[256,512]{1,0:T(8,128)S(1)}, f32[256,512]{1,0:T(8,128)S(1)}, u32[]{:S(2)}, u32[]{:S(2)}) collective-permute-start(f32[256,512]{1,0:T(8,128)S(1)} %add.221), channel_id=1, source_target_pairs={{0,96},{16,112},{32,0},{48,16},{64,32},{80,48},{96,64},{112,80},{1... | collective-permute-start | bytes 1572872 | tf_op jit(solution)/shard_map/ppermute | solution.py:93
  83.3 11.2 %collective-permute-start.8 = (f32[256,512]{1,0:T(8,128)S(1)}, f32[256,512]{1,0:T(8,128)S(1)}, u32[]{:S(2)}, u32[]{:S(2)}) collective-permute-start(f32[256,512]{1,0:T(8,128)S(1)} %add.206), channel_id=1, source_target_pairs={{0,32},{16,48},{32,64},{48,80},{64,96},{80,112},{96,0},{112,16},{1... | collective-permute-start | bytes 1572872 | tf_op jit(solution)/shard_map/ppermute | solution.py:93
  84.2 13.8 %collective-permute-start.13 = (f32[128,512]{1,0:T(8,128)S(1)}, f32[128,512]{1,0:T(8,128)S(1)}, u32[]{:S(2)}, u32[]{:S(2)}) collective-permute-start(f32[128,512]{1,0:T(8,128)S(1)} %get-tuple-element.11), channel_id=1, source_target_pairs={{0,16},{16,0},{32,48},{48,32},{64,80},{80,64},{96,112},{112,96},{1... | collective-permute-start | bytes 786440 | tf_op jit(solution)/shard_map/ppermute | solution.py:97
  94.7 8.0 %collective-permute-start.9 = (f32[128,512]{1,0:T(8,128)S(1)}, f32[128,512]{1,0:T(8,128)S(1)}, u32[]{:S(2)}, u32[]{:S(2)}) collective-permute-start(f32[128,512]{1,0:T(8,128)S(1)} %get-tuple-element.9), channel_id=1, source_target_pairs={{0,16},{16,0},{32,48},{48,32},{64,80},{80,64},{96,112},{112,96},{1... | collective-permute-start | bytes 786440 | tf_op jit(solution)/shard_map/ppermute | solution.py:97

commit v6 on v5

--- a/solution.py
+++ b/solution.py
@@ -32,29 +32,29 @@
 
 
 def _toeplitz_kernel(shift_ref, weight_ref, rev_ref, out_ref):
-    sc = pl.program_id(0)
-    row = rev_ref[0]
-    row = pltpu.roll(row, shift_ref[sc], 1)
-    row = (row * weight_ref[sc]).astype(jnp.bfloat16).astype(jnp.float32)
-    row = jnp.concatenate([row[:, :LAGS], row[:, SAMPLES - NT :]], axis=1)
-    wide = jnp.broadcast_to(row, (NT, WIDE))
-    band = pltpu.roll(wide, 0, 1, stride=1, stride_axis=0)
-    out_ref[...] = band[:, :LAGS].astype(out_ref.dtype)
+    def body(r, carry):
+        row = rev_ref[r]
+        row = pltpu.roll(row, shift_ref[r], 1)
+        row = (row * weight_ref[r]).astype(jnp.bfloat16).astype(jnp.float32)
+        row = jnp.concatenate([row[:, :LAGS], row[:, SAMPLES - NT :]], axis=1)
+        wide = jnp.broadcast_to(row, (NT, WIDE))
+        band = pltpu.roll(wide, 0, 1, stride=1, stride_axis=0)
+        out_ref[pl.ds(pl.multiple_of(r * NT, NT), NT), :] = band[:, :LAGS].astype(out_ref.dtype)
+        return carry
+
+    lax.fori_loop(0, rev_ref.shape[0], body, 0)
 
 
 def toeplitz_reversed(rev, shifts, weights):
     rows = rev.shape[0]
     return pl.pallas_call(
         _toeplitz_kernel,
-        grid_spec=pltpu.PrefetchScalarGridSpec(
-            num_scalar_prefetch=1,
-            grid=(rows,),
-            in_specs=[
-                pl.BlockSpec(memory_space=pltpu.SMEM),
-                pl.BlockSpec((1, 1, SAMPLES), lambda i, s: (i, 0, 0)),
-            ],
-            out_specs=pl.BlockSpec((NT, LAGS), lambda i, s: (i, 0)),
-        ),
+        in_specs=[
+            pl.BlockSpec(memory_space=pltpu.SMEM),
+            pl.BlockSpec(memory_space=pltpu.SMEM),
+            pl.BlockSpec(memory_space=pltpu.VMEM),
+        ],
+        out_specs=pl.BlockSpec(memory_space=pltpu.VMEM),
         out_shape=jax.ShapeDtypeStruct((rows * NT, LAGS), jnp.bfloat16),
         cost_estimate=pl.CostEstimate(flops=0, transcendentals=0, bytes_accessed=rows * NT * LAGS * 2),
     )(shifts, weights, rev)

time: 106 us -> 95.6 us (0.902); the launches traced: 104 us -> 95.1 us
  Pallas kernels: 22.7 us -> 13.6 us
    pallas_call x2, Pallas kernels: 22.7 us -> 13.6 us  [toeplitz_reversed(): pl.pallas_call(_toeplitz_kernel, in_specs=[pl.BlockSpec(memory_space=pltp...]
  transfers between devices with their start and end apart: 14 -> 14, of which waited for: 9 -> 9; matrix products, arithmetic and copies ran while one was open for 21% -> 23% of each run, Pallas kernels for 11% -> 7%
where the time goes in v6:
time: 95.6 us; the launch traced here: 95.1 us
  waiting for transfers between devices  26.8 us (28%)
  starting transfers between devices  21.7 us (23%)
  matrix products  21.4 us (22%)
  Pallas kernels  13.6 us (14%)
  local copies, waits for them, and re-layouts  8.4 us (9%)
  other arithmetic  2.98 us (3%)
    dot_general x8, matrix products, piece(): jnp.einsum('rpt,rtn->pn', g, band.reshape(rows, NT, LAGS), preferred_elem...  21.4 us
    ppermute x6, waiting for transfers between devices, local(): got = lax.ppermute(acc, 'sens', ring_perm(step))  16.6 us
    pallas_call x2, Pallas kernels, toeplitz_reversed(): pl.pallas_call(_toeplitz_kernel, in_specs=[pl.BlockSpec(memory_space=pltp...  13.6 us
    ppermute x6, starting transfers between devices, local(): got = lax.ppermute(acc, 'sens', ring_perm(step))  10.1 us
    ppermute x6, starting transfers between devices, from_owners(): got = lax.ppermute(x, axis, perm)  6.58 us
    ppermute x6, waiting for transfers between devices, from_owners(): got = lax.ppermute(x, axis, perm)  5.97 us
    ppermute x2, starting transfers between devices, local(): got = lax.ppermute(theirs, 'sens', [(i, i ^ 1) for i in range(size)])  5.08 us
    ppermute x2, waiting for transfers between devices, local(): got = lax.ppermute(theirs, 'sens', [(i, i ^ 1) for i in range(size)])  4.25 us
  transfers between devices with their start and end apart: 14, of which 9 were waited for; matrix products, arithmetic and copies ran while one was open for 23% of the time, Pallas kernels for 7%

profile of v6, /device:TPU:0, one launch (start us, length us, event | category | flops | bytes accessed | tf_op | source)
XLA Modules:
  0.0 95.1 jit_solution(9699160395696235093)
XLA Ops:
  0.0 3.4 %rev.17 = bf16[2,6,3,1024]{3,0,2,1:T(2,128)(2,1)S(1)} reverse(bf16[2,6,3,1024]{3,0,2,1:T(2,128)(2,1)} %bitcast.58), dimensions={3} | reverse | bytes 147456 | tf_op jit(solution)/shard_map/jit(_flip)/rev | solution.py:67
  3.4 1.1 %collective-permute-start = (bf16[2,6,3,1024]{3,0,2,1:T(2,128)(2,1)S(1)}, bf16[2,6,3,1024]{3,0,2,1:T(2,128)(2,1)S(1)}, u32[]{:S(2)}, u32[]{:S(2)}) collective-permute-start(bf16[2,6,3,1024]{3,0,2,1:T(2,128)(2,1)S(1)} %rev.17), channel_id=1, source_target_pairs={{0,3},{1,0},{2,1},{3,2},{4,7},{5,4},{6,5},{7,6},{8,11},{9,8},{10,9... | collective-permute-start | bytes 221192 | tf_op jit(solution)/shard_map/ppermute | solution.py:26
  4.5 0.7 collective-permute-start.1
  5.1 0.2 collective-permute-start.2
  5.3 0.7 broadcast_add_fusion
  6.0 0.1 broadcast_in_dim.36
  6.0 0.1 sub.68
  6.1 0.5 slice_bitcast_fusion.1
  6.7 0.7 multiply_exponential_fusion
  7.3 0.7 broadcast_compare_fusion
  8.1 0.0 collective-permute-done
  8.1 1.6 %collective-permute-done.1 = bf16[2,6,3,1024]{3,0,2,1:T(2,128)(2,1)S(1)} collective-permute-done((bf16[2,6,3,1024]{3,0,2,1:T(2,128)(2,1)S(1)}, bf16[2,6,3,1024]{3,0,2,1:T(2,128)(2,1)S(1)}, u32[]{:S(2)}, u32[]{:S(2)}) %collective-permute-start.1) | collective-permute-done | bytes 73760 | tf_op jit(solution)/shard_map/ppermute | solution.py:26
  9.7 0.0 collective-permute-done.2
  9.7 0.2 broadcast_select_fusion.4
  10.0 3.1 %collective-permute-start.3 = (bf16[2,6,3,1024]{3,0,2,1:T(2,128)(2,1)S(1)}, bf16[2,6,3,1024]{3,0,2,1:T(2,128)(2,1)S(1)}, u32[]{:S(2)}, u32[]{:S(2)}) collective-permute-start(bf16[2,6,3,1024]{3,0,2,1:T(2,128)(2,1)S(1)} %broadcast_select_fusion.4), channel_id=1, source_target_pairs={{0,12},{1,13},{2,14},{3,15},{4,0},{5,1},{6,2},{7,3},{8,4},{9,5},{1... | collective-permute-start | bytes 221192 | tf_op jit(solution)/shard_map/ppermute | solution.py:26
  13.1 0.6 collective-permute-start.4
  13.7 1.0 %collective-permute-start.5 = (bf16[2,6,3,1024]{3,0,2,1:T(2,128)(2,1)S(1)}, bf16[2,6,3,1024]{3,0,2,1:T(2,128)(2,1)S(1)}, u32[]{:S(2)}, u32[]{:S(2)}) collective-permute-start(bf16[2,6,3,1024]{3,0,2,1:T(2,128)(2,1)S(1)} %broadcast_select_fusion.4), channel_id=1, source_target_pairs={{0,4},{1,5},{2,6},{3,7},{4,8},{5,9},{6,10},{7,11},{8,12},{9,13},{1... | collective-permute-start | bytes 221192 | tf_op jit(solution)/shard_map/ppermute | solution.py:26
  14.7 0.1 copy.8
  14.8 0.7 reshape.39.weight_ref
  15.4 0.0 collective-permute-done.3
  15.4 3.6 %collective-permute-done.4 = bf16[2,6,3,1024]{3,0,2,1:T(2,128)(2,1)S(1)} collective-permute-done((bf16[2,6,3,1024]{3,0,2,1:T(2,128)(2,1)S(1)}, bf16[2,6,3,1024]{3,0,2,1:T(2,128)(2,1)S(1)}, u32[]{:S(2)}, u32[]{:S(2)}) %collective-permute-start.4) | collective-permute-done | bytes 73760 | tf_op jit(solution)/shard_map/ppermute | solution.py:26
  19.0 0.7 collective-permute-done.5
  19.7 0.2 fusion.46
  20.0 0.8 fusion.57
  20.7 6.7 %shard_map.56 = bf16[4608,512]{1,0:T(8,128)(2,1)} custom-call(s32[18]{0:T(128)} %get-tuple-element.16.shift_ref, f32[18]{0:T(128)} %reshape.39.weight_ref, f32[18,1,1024]{2,1,0:T(1,128)} %bitcast.57), custom_call_target="tpu_custom_call" | custom-call | bytes 4718592 | tf_op jit(solution)/shard_map/pallas_call | solution.py:50
  27.4 4.4 %fusion.28 = f32[256,512]{1,0:T(8,128)S(1)} fusion(bf16[18,256,512]{2,1,0:T(8,128)(2,1)} %bitcast.44, bf16[18,1024,256]{2,1,0:T(8,128)(2,1)} %bitcast.59, s32[]{:T(128)S(6)} %select_n.184), kind=kOutput, calls=%fused_computation.20 | convolution fusion | flops 1207959552 | bytes 7602180 | tf_op jit(solution)/shard_map/rpt,rtn->pn/dot_general | solution.py:83
  31.9 4.1 %collective-permute-start.10 = (f32[256,512]{1,0:T(8,128)S(1)}, f32[256,512]{1,0:T(8,128)S(1)}, u32[]{:S(2)}, u32[]{:S(2)}) collective-permute-start(f32[256,512]{1,0:T(8,128)S(1)} %fusion.28), channel_id=1, source_target_pairs={{0,96},{16,112},{32,0},{48,16},{64,32},{80,48},{96,64},{112,80},{1... | collective-permute-start | bytes 1572872 | tf_op jit(solution)/shard_map/ppermute | solution.py:93
  36.0 6.8 %shard_map.55 = bf16[4608,512]{1,0:T(8,128)(2,1)} custom-call(s32[18]{0:T(128)} %get-tuple-element.15.shift_ref, f32[18]{0:T(128)} %reshape.39.weight_ref, f32[18,1,1024]{2,1,0:T(1,128)} %bitcast.56), custom_call_target="tpu_custom_call" | custom-call | bytes 4718592 | tf_op jit(solution)/shard_map/pallas_call | solution.py:50
  42.8 4.6 %fusion.16 = f32[256,512]{1,0:T(8,128)S(1)} fusion(bf16[18,256,512]{2,1,0:T(8,128)(2,1)} %bitcast.50, bf16[18,1024,256]{2,1,0:T(8,128)(2,1)} %bitcast.60, s32[]{:T(128)S(6)} %select_n.154), kind=kOutput, calls=%fused_computation.16 | convolution fusion | flops 1207959552 | bytes 7602180 | tf_op jit(solution)/shard_map/rpt,rtn->pn/dot_general | solution.py:83
  47.4 0.0 slice-start.6
  47.4 0.0 slice-start.3
  47.5 0.1 collective-permute-start.6
  47.5 0.0 collective-permute-done.10
  47.6 0.0 slice-done
  47.6 0.0 slice-done.1
  47.6 3.9 %fusion.40 = f32[256,512]{1,0:T(8,128)S(1)} fusion(f32[256,512]{1,0:T(8,128)S(1)} %collective-permute-done.10, bf16[18,256,512]{2,1,0:T(8,128)(2,1)S(1)} %bitcast.47, bf16[18,1024,256]{2,1,0:T(8,128)(2,1)} %bitcast.61, s32[]{:T(128)S(6)} %select_n.186), kind=kOutput, calls=%fused_computation.24 | convolution fusion | flops 1208090624 | bytes 8126468 | tf_op jit(solution)/shard_map/rpt,rtn->pn/dot_general | solution.py:83
  51.4 2.5 %collective-permute-start.11 = (f32[256,512]{1,0:T(8,128)S(1)}, f32[256,512]{1,0:T(8,128)S(1)}, u32[]{:S(2)}, u32[]{:S(2)}) collective-permute-start(f32[256,512]{1,0:T(8,128)S(1)} %fusion.40), channel_id=1, source_target_pairs={{0,96},{16,112},{32,0},{48,16},{64,32},{80,48},{96,64},{112,80},{1... | collective-permute-start | bytes 1572872 | tf_op jit(solution)/shard_map/ppermute | solution.py:93
  53.9 0.0 slice-done.4
  53.9 1.4 %fusion.34 = f32[256,512]{1,0:T(8,128)S(1)} fusion(bf16[18,256,512]{2,1,0:T(8,128)(2,1)S(1)} %bitcast.48, bf16[18,1024,256]{2,1,0:T(8,128)(2,1)S(1)} %bitcast.65, s32[]{:T(128)S(6)} %select_n.188), kind=kOutput, calls=%fused_computation.22 | convolution fusion | flops 1207959552 | bytes 7602180 | tf_op jit(solution)/shard_map/rpt,rtn->pn/dot_general | solution.py:83
  55.3 5.2 %collective-permute-done.6 = f32[256,512]{1,0:T(8,128)S(1)} collective-permute-done((f32[256,512]{1,0:T(8,128)S(1)}, f32[256,512]{1,0:T(8,128)S(1)}, u32[]{:S(2)}, u32[]{:S(2)}) %collective-permute-start.6) | collective-permute-done | bytes 524320 | tf_op jit(solution)/shard_map/ppermute | solution.py:93
  60.5 1.4 %fusion.43 = f32[256,512]{1,0:T(8,128)S(1)} fusion(f32[256,512]{1,0:T(8,128)S(1)} %collective-permute-done.6, bf16[18,256,512]{2,1,0:T(8,128)(2,1)S(1)} %bitcast.53, bf16[18,1024,256]{2,1,0:T(8,128)(2,1)S(1)} %bitcast.66, s32[]{:T(128)S(6)} %select_n.175), kind=kOutput, calls=%fused_computation.25 | convolution fusion | flops 1208090624 | bytes 8126468 | tf_op jit(solution)/shard_map/rpt,rtn->pn/dot_general | solution.py:83
  61.9 0.1 collective-permute-start.7
  62.0 1.4 %collective-permute-done.11 = f32[256,512]{1,0:T(8,128)S(1)} collective-permute-done((f32[256,512]{1,0:T(8,128)S(1)}, f32[256,512]{1,0:T(8,128)S(1)}, u32[]{:S(2)}, u32[]{:S(2)}) %collective-permute-start.11) | collective-permute-done | bytes 524320 | tf_op jit(solution)/shard_map/ppermute | solution.py:93
  63.5 0.1 add.221
  63.5 3.3 %collective-permute-start.12 = (f32[256,512]{1,0:T(8,128)S(1)}, f32[256,512]{1,0:T(8,128)S(1)}, u32[]{:S(2)}, u32[]{:S(2)}) collective-permute-start(f32[256,512]{1,0:T(8,128)S(1)} %add.221), channel_id=1, source_target_pairs={{0,96},{16,112},{32,0},{48,16},{64,32},{80,48},{96,64},{112,80},{1... | collective-permute-start | bytes 1572872 | tf_op jit(solution)/shard_map/ppermute | solution.py:93
  66.8 1.4 %fusion.37 = f32[256,512]{1,0:T(8,128)S(1)} fusion(bf16[18,256,512]{2,1,0:T(8,128)(2,1)S(1)} %bitcast.49, bf16[18,1024,256]{2,1,0:T(8,128)(2,1)S(1)} %bitcast.67, s32[]{:T(128)S(6)} %select_n.190), kind=kOutput, calls=%fused_computation.23 | convolution fusion | flops 1207959552 | bytes 7602180 | tf_op jit(solution)/shard_map/rpt,rtn->pn/dot_general | solution.py:83
  68.2 1.4 %fusion.22 = f32[256,512]{1,0:T(8,128)S(1)} fusion(bf16[18,256,512]{2,1,0:T(8,128)(2,1)S(1)} %bitcast.54, bf16[18,1024,256]{2,1,0:T(8,128)(2,1)S(1)} %bitcast.68, s32[]{:T(128)S(6)} %select_n.177), kind=kOutput, calls=%fused_computation.18 | convolution fusion | flops 1207959552 | bytes 7602180 | tf_op jit(solution)/shard_map/rpt,rtn->pn/dot_general | solution.py:83
  69.5 4.5 %collective-permute-done.7 = f32[256,512]{1,0:T(8,128)S(1)} collective-permute-done((f32[256,512]{1,0:T(8,128)S(1)}, f32[256,512]{1,0:T(8,128)S(1)}, u32[]{:S(2)}, u32[]{:S(2)}) %collective-permute-start.7) | collective-permute-done | bytes 524320 | tf_op jit(solution)/shard_map/ppermute | solution.py:93
  74.1 0.1 add.206
  74.1 0.1 collective-permute-start.8
  74.2 0.7 collective-permute-done.12
  74.9 0.1 add.224
  75.0 2.6 %collective-permute-start.13 = (f32[128,512]{1,0:T(8,128)S(1)}, f32[128,512]{1,0:T(8,128)S(1)}, u32[]{:S(2)}, u32[]{:S(2)}) collective-permute-start(f32[128,512]{1,0:T(8,128)S(1)} %get-tuple-element.11), channel_id=1, source_target_pairs={{0,16},{16,0},{32,48},{48,32},{64,80},{80,64},{96,112},{112,96},{1... | collective-permute-start | bytes 786440 | tf_op jit(solution)/shard_map/ppermute | solution.py:97
  77.6 3.0 %fusion.25 = f32[256,512]{1,0:T(8,128)S(1)} fusion(bf16[18,256,512]{2,1,0:T(8,128)(2,1)S(1)} %bitcast.55, bf16[18,1024,256]{2,1,0:T(8,128)(2,1)} %bitcast.62, s32[]{:T(128)S(6)} %select_n.179), kind=kOutput, calls=%fused_computation.19 | convolution fusion | flops 1207959552 | bytes 7602180 | tf_op jit(solution)/shard_map/rpt,rtn->pn/dot_general | solution.py:83
  80.7 4.7 %collective-permute-done.8 = f32[256,512]{1,0:T(8,128)S(1)} collective-permute-done((f32[256,512]{1,0:T(8,128)S(1)}, f32[256,512]{1,0:T(8,128)S(1)}, u32[]{:S(2)}, u32[]{:S(2)}) %collective-permute-start.8) | collective-permute-done | bytes 524320 | tf_op jit(solution)/shard_map/ppermute | solution.py:93
  85.4 0.1 add.209
  85.5 2.5 %collective-permute-start.9 = (f32[128,512]{1,0:T(8,128)S(1)}, f32[128,512]{1,0:T(8,128)S(1)}, u32[]{:S(2)}, u32[]{:S(2)}) collective-permute-start(f32[128,512]{1,0:T(8,128)S(1)} %get-tuple-element.9), channel_id=1, source_target_pairs={{0,16},{16,0},{32,48},{48,32},{64,80},{80,64},{96,112},{112,96},{1... | collective-permute-start | bytes 786440 | tf_op jit(solution)/shard_map/ppermute | solution.py:97
  88.0 0.4 rev.20
  88.4 0.4 rev.18
  88.8 0.0 collective-permute-done.13
  88.8 0.4 rev.21
  89.2 4.2 %collective-permute-done.9 = f32[128,512]{1,0:T(8,128)S(1)} collective-permute-done((f32[128,512]{1,0:T(8,128)S(1)}, f32[128,512]{1,0:T(8,128)S(1)}, u32[]{:S(2)}, u32[]{:S(2)}) %collective-permute-start.9) | collective-permute-done | bytes 262176 | tf_op jit(solution)/shard_map/ppermute | solution.py:97
  93.5 0.4 rev.19
  93.9 1.2 %copy.9 = f32[128,2,512]{2,1,0:T(2,128)} copy(f32[128,2,512]{2,0,1:T(8,128)S(1)} %pad_maximum_fusion) | data formatting | bytes 1048576 | tf_op jit(solution)/shard_map/stack | solution.py:99
  (20 shorter events, 0.3 us)
Async XLA Ops:
  3.4 4.7 %collective-permute-start = (bf16[2,6,3,1024]{3,0,2,1:T(2,128)(2,1)S(1)}, bf16[2,6,3,1024]{3,0,2,1:T(2,128)(2,1)S(1)}, u32[]{:S(2)}, u32[]{:S(2)}) collective-permute-start(bf16[2,6,3,1024]{3,0,2,1:T(2,128)(2,1)S(1)} %rev.17), channel_id=1, source_target_pairs={{0,3},{1,0},{2,1},{3,2},{4,7},{5,4},{6,5},{7,6},{8,11},{9,8},{10,9... | collective-permute-start | bytes 221192 | tf_op jit(solution)/shard_map/ppermute | solution.py:26
  4.5 5.2 %collective-permute-start.1 = (bf16[2,6,3,1024]{3,0,2,1:T(2,128)(2,1)S(1)}, bf16[2,6,3,1024]{3,0,2,1:T(2,128)(2,1)S(1)}, u32[]{:S(2)}, u32[]{:S(2)}) collective-permute-start(bf16[2,6,3,1024]{3,0,2,1:T(2,128)(2,1)S(1)} %rev.17), channel_id=1, source_target_pairs={{0,2},{1,3},{2,0},{3,1},{4,6},{5,7},{6,4},{7,5},{8,10},{9,11},{10,... | collective-permute-start | bytes 221192 | tf_op jit(solution)/shard_map/ppermute | solution.py:26
  5.1 4.6 %collective-permute-start.2 = (bf16[2,6,3,1024]{3,0,2,1:T(2,128)(2,1)S(1)}, bf16[2,6,3,1024]{3,0,2,1:T(2,128)(2,1)S(1)}, u32[]{:S(2)}, u32[]{:S(2)}) collective-permute-start(bf16[2,6,3,1024]{3,0,2,1:T(2,128)(2,1)S(1)} %rev.17), channel_id=1, source_target_pairs={{0,1},{1,2},{2,3},{3,0},{4,5},{5,6},{6,7},{7,4},{8,9},{9,10},{10,1... | collective-permute-start | bytes 221192 | tf_op jit(solution)/shard_map/ppermute | solution.py:26
  10.0 5.5 %collective-permute-start.3 = (bf16[2,6,3,1024]{3,0,2,1:T(2,128)(2,1)S(1)}, bf16[2,6,3,1024]{3,0,2,1:T(2,128)(2,1)S(1)}, u32[]{:S(2)}, u32[]{:S(2)}) collective-permute-start(bf16[2,6,3,1024]{3,0,2,1:T(2,128)(2,1)S(1)} %broadcast_select_fusion.4), channel_id=1, source_target_pairs={{0,12},{1,13},{2,14},{3,15},{4,0},{5,1},{6,2},{7,3},{8,4},{9,5},{1... | collective-permute-start | bytes 221192 | tf_op jit(solution)/shard_map/ppermute | solution.py:26
  13.1 5.9 %collective-permute-start.4 = (bf16[2,6,3,1024]{3,0,2,1:T(2,128)(2,1)S(1)}, bf16[2,6,3,1024]{3,0,2,1:T(2,128)(2,1)S(1)}, u32[]{:S(2)}, u32[]{:S(2)}) collective-permute-start(bf16[2,6,3,1024]{3,0,2,1:T(2,128)(2,1)S(1)} %broadcast_select_fusion.4), channel_id=1, source_target_pairs={{0,8},{1,9},{2,10},{3,11},{4,12},{5,13},{6,14},{7,15},{8,0},{9,1},... | collective-permute-start | bytes 221192 | tf_op jit(solution)/shard_map/ppermute | solution.py:26
  13.7 6.1 %collective-permute-start.5 = (bf16[2,6,3,1024]{3,0,2,1:T(2,128)(2,1)S(1)}, bf16[2,6,3,1024]{3,0,2,1:T(2,128)(2,1)S(1)}, u32[]{:S(2)}, u32[]{:S(2)}) collective-permute-start(bf16[2,6,3,1024]{3,0,2,1:T(2,128)(2,1)S(1)} %broadcast_select_fusion.4), channel_id=1, source_target_pairs={{0,4},{1,5},{2,6},{3,7},{4,8},{5,9},{6,10},{7,11},{8,12},{9,13},{1... | collective-permute-start | bytes 221192 | tf_op jit(solution)/shard_map/ppermute | solution.py:26
  31.9 15.7 %collective-permute-start.10 = (f32[256,512]{1,0:T(8,128)S(1)}, f32[256,512]{1,0:T(8,128)S(1)}, u32[]{:S(2)}, u32[]{:S(2)}) collective-permute-start(f32[256,512]{1,0:T(8,128)S(1)} %fusion.28), channel_id=1, source_target_pairs={{0,96},{16,112},{32,0},{48,16},{64,32},{80,48},{96,64},{112,80},{1... | collective-permute-start | bytes 1572872 | tf_op jit(solution)/shard_map/ppermute | solution.py:93
  36.0 17.9 %slice-start.4 = ((s8[9437184]{0:T(1024)(128)(4,1)}), s8[1048576]{0:T(1024)(128)(4,1)S(1)}, s32[]{:S(2)}) async-start(s8[9437184]{0:T(1024)(128)(4,1)} %bitcast.63), calls=%async_computation.4 | async-start | bytes 2097152
  42.8 4.7 %slice-start = ((s8[4718592]{0:T(1024)(128)(4,1)}), s8[4194304]{0:T(1024)(128)(4,1)S(1)}, s32[]{:S(2)}) async-start(s8[4718592]{0:T(1024)(128)(4,1)} %bitcast.45), calls=%async_computation | async-start | bytes 8388608
  42.8 4.7 %slice-start.1 = ((s8[4718592]{0:T(1024)(128)(4,1)}), s8[524288]{0:T(1024)(128)(4,1)S(1)}, s32[]{:S(2)}) async-start(s8[4718592]{0:T(1024)(128)(4,1)} %bitcast.45), calls=%async_computation.1 | async-start | bytes 1048576
  42.8 11.1 %slice-start.5 = ((s8[9437184]{0:T(1024)(128)(4,1)}), s8[4194304]{0:T(1024)(128)(4,1)S(1)}, s32[]{:S(2)}) async-start(s8[9437184]{0:T(1024)(128)(4,1)} %bitcast.63), calls=%async_computation.5 | async-start | bytes 8388608
  42.8 17.7 %slice-start.2 = ((s8[4718592]{0:T(1024)(128)(4,1)}), s8[4194304]{0:T(1024)(128)(4,1)S(1)}, s32[]{:S(2)}) async-start(s8[4718592]{0:T(1024)(128)(4,1)} %bitcast.51), calls=%async_computation.2 | async-start | bytes 8388608
  47.4 6.5 %slice-start.6 = ((s8[9437184]{0:T(1024)(128)(4,1)}), s8[4194304]{0:T(1024)(128)(4,1)S(1)}, s32[]{:S(2)}) async-start(s8[9437184]{0:T(1024)(128)(4,1)} %bitcast.63), calls=%async_computation.6 | async-start | bytes 8388608
  47.4 13.1 %slice-start.3 = ((s8[4718592]{0:T(1024)(128)(4,1)}), s8[524288]{0:T(1024)(128)(4,1)S(1)}, s32[]{:S(2)}) async-start(s8[4718592]{0:T(1024)(128)(4,1)} %bitcast.51), calls=%async_computation.3 | async-start | bytes 1048576
  47.5 13.1 %collective-permute-start.6 = (f32[256,512]{1,0:T(8,128)S(1)}, f32[256,512]{1,0:T(8,128)S(1)}, u32[]{:S(2)}, u32[]{:S(2)}) collective-permute-start(f32[256,512]{1,0:T(8,128)S(1)} %fusion.16), channel_id=1, source_target_pairs={{0,32},{16,48},{32,64},{48,80},{64,96},{80,112},{96,0},{112,16},{1... | collective-permute-start | bytes 1572872 | tf_op jit(solution)/shard_map/ppermute | solution.py:93
  51.4 12.0 %collective-permute-start.11 = (f32[256,512]{1,0:T(8,128)S(1)}, f32[256,512]{1,0:T(8,128)S(1)}, u32[]{:S(2)}, u32[]{:S(2)}) collective-permute-start(f32[256,512]{1,0:T(8,128)S(1)} %fusion.40), channel_id=1, source_target_pairs={{0,96},{16,112},{32,0},{48,16},{64,32},{80,48},{96,64},{112,80},{1... | collective-permute-start | bytes 1572872 | tf_op jit(solution)/shard_map/ppermute | solution.py:93
  61.9 12.1 %collective-permute-start.7 = (f32[256,512]{1,0:T(8,128)S(1)}, f32[256,512]{1,0:T(8,128)S(1)}, u32[]{:S(2)}, u32[]{:S(2)}) collective-permute-start(f32[256,512]{1,0:T(8,128)S(1)} %fusion.43), channel_id=1, source_target_pairs={{0,32},{16,48},{32,64},{48,80},{64,96},{80,112},{96,0},{112,16},{1... | collective-permute-start | bytes 1572872 | tf_op jit(solution)/shard_map/ppermute | solution.py:93
  63.5 11.4 %collective-permute-start.12 = (f32[256,512]{1,0:T(8,128)S(1)}, f32[256,512]{1,0:T(8,128)S(1)}, u32[]{:S(2)}, u32[]{:S(2)}) collective-permute-start(f32[256,512]{1,0:T(8,128)S(1)} %add.221), channel_id=1, source_target_pairs={{0,96},{16,112},{32,0},{48,16},{64,32},{80,48},{96,64},{112,80},{1... | collective-permute-start | bytes 1572872 | tf_op jit(solution)/shard_map/ppermute | solution.py:93
  74.1 11.2 %collective-permute-start.8 = (f32[256,512]{1,0:T(8,128)S(1)}, f32[256,512]{1,0:T(8,128)S(1)}, u32[]{:S(2)}, u32[]{:S(2)}) collective-permute-start(f32[256,512]{1,0:T(8,128)S(1)} %add.206), channel_id=1, source_target_pairs={{0,32},{16,48},{32,64},{48,80},{64,96},{80,112},{96,0},{112,16},{1... | collective-permute-start | bytes 1572872 | tf_op jit(solution)/shard_map/ppermute | solution.py:93
  75.0 13.8 %collective-permute-start.13 = (f32[128,512]{1,0:T(8,128)S(1)}, f32[128,512]{1,0:T(8,128)S(1)}, u32[]{:S(2)}, u32[]{:S(2)}) collective-permute-start(f32[128,512]{1,0:T(8,128)S(1)} %get-tuple-element.11), channel_id=1, source_target_pairs={{0,16},{16,0},{32,48},{48,32},{64,80},{80,64},{96,112},{112,96},{1... | collective-permute-start | bytes 786440 | tf_op jit(solution)/shard_map/ppermute | solution.py:97
  85.5 8.0 %collective-permute-start.9 = (f32[128,512]{1,0:T(8,128)S(1)}, f32[128,512]{1,0:T(8,128)S(1)}, u32[]{:S(2)}, u32[]{:S(2)}) collective-permute-start(f32[128,512]{1,0:T(8,128)S(1)} %get-tuple-element.9), channel_id=1, source_target_pairs={{0,16},{16,0},{32,48},{48,32},{64,80},{80,64},{96,112},{112,96},{1... | collective-permute-start | bytes 786440 | tf_op jit(solution)/shard_map/ppermute | solution.py:97

commit v7 on v6

--- a/solution.py
+++ b/solution.py
@@ -12,7 +12,7 @@
 WIDE = LAGS + NT
 
 
-def from_owners(x, axis, roots, radix=4):
+def from_owners(x, axis, roots, radix=16):
     size = lax.axis_size(axis)
     me = lax.axis_index(axis)
     span = 1
@@ -66,9 +66,10 @@
     green_t = jnp.transpose(green, (1, 2, 0, 3)).reshape(rows, point_rows, NT)
     flipped = jnp.flip(records_buffer[0], axis=-1)
     traces = from_owners(flipped, "loc", owners)
-    rev = traces.astype(jnp.float32).reshape(EV, rows, 1, SAMPLES)
-    shifts = (jnp.repeat(onsets.astype(jnp.int32), 3, axis=1) - LAGS) % SAMPLES
-    weights = jnp.exp2(-codes.astype(jnp.float32)).reshape(-1)
+    rev = traces.astype(jnp.float32).reshape(EV * rows, 1, SAMPLES)
+    shifts = ((jnp.repeat(onsets.astype(jnp.int32), 3, axis=1) - LAGS) % SAMPLES).reshape(-1)
+    weights = jnp.tile(jnp.exp2(-codes.astype(jnp.float32)).reshape(-1), EV)
+    bands = toeplitz_reversed(rev, shifts, weights).reshape(EV, rows * NT, LAGS)
 
     size = lax.axis_size("sens")
     me = lax.axis_index("sens")
@@ -87,7 +88,7 @@
 
     outs = []
     for e, step in zip(range(EV), (1, zs - 1)):
-        band = toeplitz_reversed(rev[e], shifts[e], weights)
+        band = bands[e]
         acc = piece(band, (z + zs - step) % zs)
         for k in range(zs - 1):
             got = lax.ppermute(acc, "sens", ring_perm(step))

time: 95.6 us -> 123 us (1.29)
  waiting for transfers between devices: 26.8 us -> 38 us
  starting transfers between devices: 21.7 us -> 32.3 us
  local copies, waits for them, and re-layouts: 8.4 us -> 16.8 us
  matrix products: 21.4 us -> 19.3 us
  Pallas kernels: 13.6 us -> 11.9 us
    ppermute x6 -> x15, starting transfers between devices: 6.58 us -> 17.4 us  [from_owners(): got = lax.ppermute(x, axis, perm)]
    ppermute x6, waiting for transfers between devices: 16.6 us -> 23.4 us  [local(): got = lax.ppermute(acc, 'sens', ring_perm(step))]
    slice x1, local copies, waits for them, and re-layouts: 0.76 us -> 6.6 us  [local(): band = bands[e]]
    ppermute x6 -> x15, waiting for transfers between devices: 5.97 us -> 9.05 us  [from_owners(): got = lax.ppermute(x, axis, perm)]
    unnamed x14, local copies, waits for them, and re-layouts: 0.03 us -> 2.17 us
    dot_general x8, matrix products: 21.4 us -> 19.3 us  [piece(): jnp.einsum('rpt,rtn->pn', g, band.reshape(rows, NT, LAGS), preferred_elem...]
    pallas_call x2 -> x1, Pallas kernels: 13.6 us -> 11.9 us  [toeplitz_reversed(): pl.pallas_call(_toeplitz_kernel, in_specs=[pl.BlockSpec(memory_space=pltp...]
    ppermute x2, starting transfers between devices: 5.08 us -> 3.69 us  [local(): got = lax.ppermute(theirs, 'sens', [(i, i ^ 1) for i in range(size)])]
  transfers between devices with their start and end apart: 14 -> 23, of which waited for: 9 -> 11; matrix products, arithmetic and copies ran while one was open for 23% -> 17% of each run, Pallas kernels for 7% -> 0%
where the time goes in v7:
time: 123 us; the launch traced here: 122 us
  waiting for transfers between devices  38 us (31%)
  starting transfers between devices  32.3 us (26%)
  matrix products  19.3 us (16%)
  local copies, waits for them, and re-layouts  16.8 us (14%)
  Pallas kernels  11.9 us (10%)
  other arithmetic  3.56 us (3%)
    ppermute x6, waiting for transfers between devices, local(): got = lax.ppermute(acc, 'sens', ring_perm(step))  23.4 us
    dot_general x8, matrix products, piece(): jnp.einsum('rpt,rtn->pn', g, band.reshape(rows, NT, LAGS), preferred_elem...  19.3 us
    ppermute x15, starting transfers between devices, from_owners(): got = lax.ppermute(x, axis, perm)  17.4 us
    pallas_call x1, Pallas kernels, toeplitz_reversed(): pl.pallas_call(_toeplitz_kernel, in_specs=[pl.BlockSpec(memory_space=pltp...  11.9 us
    ppermute x6, starting transfers between devices, local(): got = lax.ppermute(acc, 'sens', ring_perm(step))  11.3 us
    ppermute x15, waiting for transfers between devices, from_owners(): got = lax.ppermute(x, axis, perm)  9.05 us
    slice x1, local copies, waits for them, and re-layouts, local(): band = bands[e]  6.6 us
    ppermute x2, waiting for transfers between devices, local(): got = lax.ppermute(theirs, 'sens', [(i, i ^ 1) for i in range(size)])  5.5 us
  transfers between devices with their start and end apart: 23, of which 11 were waited for; matrix products, arithmetic and copies ran while one was open for 17% of the time, Pallas kernels for 0%

profile of v7, /device:TPU:0, one launch (start us, length us, event | category | flops | bytes accessed | tf_op | source)
XLA Modules:
  0.0 122.1 jit_solution(15555169184179436374)
XLA Ops:
  0.0 3.4 %rev.17 = bf16[2,6,3,1024]{3,0,2,1:T(2,128)(2,1)S(1)} reverse(bf16[2,6,3,1024]{3,0,2,1:T(2,128)(2,1)} %bitcast.48), dimensions={3} | reverse | bytes 147456 | tf_op jit(solution)/shard_map/jit(_flip)/rev | solution.py:67
  3.4 3.5 %collective-permute-start = (bf16[2,6,3,1024]{3,0,2,1:T(2,128)(2,1)S(1)}, bf16[2,6,3,1024]{3,0,2,1:T(2,128)(2,1)S(1)}, u32[]{:S(2)}, u32[]{:S(2)}) collective-permute-start(bf16[2,6,3,1024]{3,0,2,1:T(2,128)(2,1)S(1)} %rev.17), channel_id=1, source_target_pairs={{0,15},{1,0},{2,1},{3,2},{4,3},{5,4},{6,5},{7,6},{8,7},{9,8},{10,9... | collective-permute-start | bytes 221192 | tf_op jit(solution)/shard_map/ppermute | solution.py:26
  6.9 0.6 collective-permute-start.1
  7.6 0.4 collective-permute-start.11
  7.9 2.1 %collective-permute-start.12 = (bf16[2,6,3,1024]{3,0,2,1:T(2,128)(2,1)S(1)}, bf16[2,6,3,1024]{3,0,2,1:T(2,128)(2,1)S(1)}, u32[]{:S(2)}, u32[]{:S(2)}) collective-permute-start(bf16[2,6,3,1024]{3,0,2,1:T(2,128)(2,1)S(1)} %rev.17), channel_id=1, source_target_pairs={{0,3},{1,4},{2,5},{3,6},{4,7},{5,8},{6,9},{7,10},{8,11},{9,12},{10... | collective-permute-start | bytes 221192 | tf_op jit(solution)/shard_map/ppermute | solution.py:26
  10.1 0.7 broadcast_compare_fusion
  10.8 0.7 multiply_exponential_fusion
  11.5 1.4 %collective-permute-start.13 = (bf16[2,6,3,1024]{3,0,2,1:T(2,128)(2,1)S(1)}, bf16[2,6,3,1024]{3,0,2,1:T(2,128)(2,1)S(1)}, u32[]{:S(2)}, u32[]{:S(2)}) collective-permute-start(bf16[2,6,3,1024]{3,0,2,1:T(2,128)(2,1)S(1)} %rev.17), channel_id=1, source_target_pairs={{0,2},{1,3},{2,4},{3,5},{4,6},{5,7},{6,8},{7,9},{8,10},{9,11},{10,... | collective-permute-start | bytes 221192 | tf_op jit(solution)/shard_map/ppermute | solution.py:26
  12.9 1.0 collective-permute-done.10
  13.9 2.1 %collective-permute-start.2 = (bf16[2,6,3,1024]{3,0,2,1:T(2,128)(2,1)S(1)}, bf16[2,6,3,1024]{3,0,2,1:T(2,128)(2,1)S(1)}, u32[]{:S(2)}, u32[]{:S(2)}) collective-permute-start(bf16[2,6,3,1024]{3,0,2,1:T(2,128)(2,1)S(1)} %rev.17), channel_id=1, source_target_pairs={{0,13},{1,14},{2,15},{3,0},{4,1},{5,2},{6,3},{7,4},{8,5},{9,6},{10... | collective-permute-start | bytes 221192 | tf_op jit(solution)/shard_map/ppermute | solution.py:26
  15.9 2.9 %collective-permute-done.11 = bf16[2,6,3,1024]{3,0,2,1:T(2,128)(2,1)S(1)} collective-permute-done((bf16[2,6,3,1024]{3,0,2,1:T(2,128)(2,1)S(1)}, bf16[2,6,3,1024]{3,0,2,1:T(2,128)(2,1)S(1)}, u32[]{:S(2)}, u32[]{:S(2)}) %collective-permute-start.11) | collective-permute-done | bytes 73760 | tf_op jit(solution)/shard_map/ppermute | solution.py:26
  18.8 0.4 collective-permute-done.12
  19.2 0.7 broadcast_add_fusion
  19.9 0.1 broadcast_in_dim.81
  20.0 0.1 sub.89
  20.1 1.0 collective-permute-start.5
  21.1 2.6 %collective-permute-start.6 = (bf16[2,6,3,1024]{3,0,2,1:T(2,128)(2,1)S(1)}, bf16[2,6,3,1024]{3,0,2,1:T(2,128)(2,1)S(1)}, u32[]{:S(2)}, u32[]{:S(2)}) collective-permute-start(bf16[2,6,3,1024]{3,0,2,1:T(2,128)(2,1)S(1)} %rev.17), channel_id=1, source_target_pairs={{0,9},{1,10},{2,11},{3,12},{4,13},{5,14},{6,15},{7,0},{8,1},{9,2},... | collective-permute-start | bytes 221192 | tf_op jit(solution)/shard_map/ppermute | solution.py:26
  23.7 1.1 collective-permute-start.7
  24.7 0.9 collective-permute-start.8
  25.6 1.7 %collective-permute-start.9 = (bf16[2,6,3,1024]{3,0,2,1:T(2,128)(2,1)S(1)}, bf16[2,6,3,1024]{3,0,2,1:T(2,128)(2,1)S(1)}, u32[]{:S(2)}, u32[]{:S(2)}) collective-permute-start(bf16[2,6,3,1024]{3,0,2,1:T(2,128)(2,1)S(1)} %rev.17), channel_id=1, source_target_pairs={{0,6},{1,7},{2,8},{3,9},{4,10},{5,11},{6,12},{7,13},{8,14},{9,15},... | collective-permute-start | bytes 221192 | tf_op jit(solution)/shard_map/ppermute | solution.py:26
  27.3 0.5 and_select_fusion.1.shift_ref
  27.8 0.1 copy.9
  27.9 0.1 tile.10
  28.0 0.6 tile.12.weight_ref
  28.6 1.5 %collective-permute-done.7 = bf16[2,6,3,1024]{3,0,2,1:T(2,128)(2,1)S(1)} collective-permute-done((bf16[2,6,3,1024]{3,0,2,1:T(2,128)(2,1)S(1)}, bf16[2,6,3,1024]{3,0,2,1:T(2,128)(2,1)S(1)}, u32[]{:S(2)}, u32[]{:S(2)}) %collective-permute-start.7) | collective-permute-done | bytes 73760 | tf_op jit(solution)/shard_map/ppermute | solution.py:26
  30.1 1.0 collective-permute-done.8
  31.1 2.2 %collective-permute-done.9 = bf16[2,6,3,1024]{3,0,2,1:T(2,128)(2,1)S(1)} collective-permute-done((bf16[2,6,3,1024]{3,0,2,1:T(2,128)(2,1)S(1)}, bf16[2,6,3,1024]{3,0,2,1:T(2,128)(2,1)S(1)}, u32[]{:S(2)}, u32[]{:S(2)}) %collective-permute-start.9) | collective-permute-done | bytes 73760 | tf_op jit(solution)/shard_map/ppermute | solution.py:26
  33.3 0.6 fusion.46
  33.9 0.1 copy.10
  34.0 0.9 reshape.62.rev_ref
  34.8 11.9 %shard_map.55 = bf16[9216,512]{1,0:T(8,128)(2,1)} custom-call(s32[36]{0:T(128)} %and_select_fusion.1.shift_ref, f32[36]{0:T(128)} %tile.12.weight_ref, f32[36,1,1024]{2,1,0:T(1,128)} %reshape.62.rev_ref), custom_call_target="tpu_custom_call" | custom-call | bytes 9437184 | tf_op jit(solution)/shard_map/pallas_call | solution.py:50
  46.7 6.6 %fusion.57 = (bf16[4608,512]{1,0:T(8,128)(2,1)S(1)}, bf16[4608,512]{1,0:T(8,128)(2,1)}) fusion(bf16[9216,512]{1,0:T(8,128)(2,1)} %shard_map.55), kind=kLoop, calls=%fused_computation.82 | loop fusion | bytes 18874368 | tf_op jit(solution)/shard_map/slice | solution.py:91
  53.3 2.1 %copy-done = bf16[4608,512]{1,0:T(8,128)(2,1)} copy-done((bf16[4608,512]{1,0:T(8,128)(2,1)}, bf16[4608,512]{1,0:T(8,128)(2,1)S(1)}, u32[]{:S(2)}) %copy-start) | copy-done | bytes 4718616
  55.5 3.1 %fusion.16 = f32[256,512]{1,0:T(8,128)S(1)} fusion(bf16[18,256,512]{2,1,0:T(8,128)(2,1)S(1)} %bitcast.44, bf16[18,1024,256]{2,1,0:T(8,128)(2,1)} %bitcast.49, s32[]{:T(128)S(6)} %select_n.204), kind=kOutput, calls=%fused_computation.16 | convolution fusion | flops 1207959552 | bytes 7602180 | tf_op jit(solution)/shard_map/rpt,rtn->pn/dot_general | solution.py:84
  58.6 2.0 %collective-permute-start.15 = (f32[256,512]{1,0:T(8,128)S(1)}, f32[256,512]{1,0:T(8,128)S(1)}, u32[]{:S(2)}, u32[]{:S(2)}) collective-permute-start(f32[256,512]{1,0:T(8,128)S(1)} %fusion.16), channel_id=1, source_target_pairs={{0,32},{16,48},{32,64},{48,80},{64,96},{80,112},{96,0},{112,16},{1... | collective-permute-start | bytes 1572872 | tf_op jit(solution)/shard_map/ppermute | solution.py:94
  60.6 4.6 %fusion.28 = f32[256,512]{1,0:T(8,128)S(1)} fusion(bf16[18,256,512]{2,1,0:T(8,128)(2,1)} %bitcast.38, bf16[18,1024,256]{2,1,0:T(8,128)(2,1)} %bitcast.50, s32[]{:T(128)S(6)} %select_n.248), kind=kOutput, calls=%fused_computation.20 | convolution fusion | flops 1207959552 | bytes 7602180 | tf_op jit(solution)/shard_map/rpt,rtn->pn/dot_general | solution.py:84
  65.2 0.0 slice-start.4
  65.2 2.4 %collective-permute-start.19 = (f32[256,512]{1,0:T(8,128)S(1)}, f32[256,512]{1,0:T(8,128)S(1)}, u32[]{:S(2)}, u32[]{:S(2)}) collective-permute-start(f32[256,512]{1,0:T(8,128)S(1)} %fusion.28), channel_id=1, source_target_pairs={{0,96},{16,112},{32,0},{48,16},{64,32},{80,48},{96,64},{112,80},{1... | collective-permute-start | bytes 1572872 | tf_op jit(solution)/shard_map/ppermute | solution.py:94
  67.6 7.3 %collective-permute-done.15 = f32[256,512]{1,0:T(8,128)S(1)} collective-permute-done((f32[256,512]{1,0:T(8,128)S(1)}, f32[256,512]{1,0:T(8,128)S(1)}, u32[]{:S(2)}, u32[]{:S(2)}) %collective-permute-start.15) | collective-permute-done | bytes 524320 | tf_op jit(solution)/shard_map/ppermute | solution.py:94
  74.9 3.0 %fusion.43 = f32[256,512]{1,0:T(8,128)S(1)} fusion(f32[256,512]{1,0:T(8,128)S(1)} %collective-permute-done.15, bf16[18,256,512]{2,1,0:T(8,128)(2,1)S(1)} %bitcast.45, bf16[18,1024,256]{2,1,0:T(8,128)(2,1)} %bitcast.51, s32[]{:T(128)S(6)} %select_n.239), kind=kOutput, calls=%fused_computation.25 | convolution fusion | flops 1208090624 | bytes 8126468 | tf_op jit(solution)/shard_map/rpt,rtn->pn/dot_general | solution.py:84
  78.0 0.3 collective-permute-start.16
  78.3 1.4 %fusion.22 = f32[256,512]{1,0:T(8,128)S(1)} fusion(bf16[18,256,512]{2,1,0:T(8,128)(2,1)S(1)} %bitcast.46, bf16[18,1024,256]{2,1,0:T(8,128)(2,1)S(1)} %bitcast.55, s32[]{:T(128)S(6)} %select_n.241), kind=kOutput, calls=%fused_computation.18 | convolution fusion | flops 1207959552 | bytes 7602180 | tf_op jit(solution)/shard_map/rpt,rtn->pn/dot_general | solution.py:84
  79.7 1.4 %fusion.40 = f32[256,512]{1,0:T(8,128)S(1)} fusion(f32[256,512]{1,0:T(8,128)S(1)} %collective-permute-done.19, bf16[18,256,512]{2,1,0:T(8,128)(2,1)S(1)} %bitcast.41, bf16[18,1024,256]{2,1,0:T(8,128)(2,1)S(1)} %bitcast.56, s32[]{:T(128)S(6)} %select_n.250), kind=kOutput, calls=%fused_computation.24 | convolution fusion | flops 1208090624 | bytes 8126468 | tf_op jit(solution)/shard_map/rpt,rtn->pn/dot_general | solution.py:84
  81.1 3.3 %collective-permute-start.20 = (f32[256,512]{1,0:T(8,128)S(1)}, f32[256,512]{1,0:T(8,128)S(1)}, u32[]{:S(2)}, u32[]{:S(2)}) collective-permute-start(f32[256,512]{1,0:T(8,128)S(1)} %fusion.40), channel_id=1, source_target_pairs={{0,96},{16,112},{32,0},{48,16},{64,32},{80,48},{96,64},{112,80},{1... | collective-permute-start | bytes 1572872 | tf_op jit(solution)/shard_map/ppermute | solution.py:94
  84.4 8.5 %collective-permute-done.16 = f32[256,512]{1,0:T(8,128)S(1)} collective-permute-done((f32[256,512]{1,0:T(8,128)S(1)}, f32[256,512]{1,0:T(8,128)S(1)}, u32[]{:S(2)}, u32[]{:S(2)}) %collective-permute-start.16) | collective-permute-done | bytes 524320 | tf_op jit(solution)/shard_map/ppermute | solution.py:94
  92.9 0.1 add.269
  93.0 0.1 collective-permute-start.17
  93.0 1.4 %fusion.25 = f32[256,512]{1,0:T(8,128)S(1)} fusion(bf16[18,256,512]{2,1,0:T(8,128)(2,1)S(1)} %bitcast.47, bf16[18,1024,256]{2,1,0:T(8,128)(2,1)S(1)} %bitcast.57, s32[]{:T(128)S(6)} %select_n.243), kind=kOutput, calls=%fused_computation.19 | convolution fusion | flops 1207959552 | bytes 7602180 | tf_op jit(solution)/shard_map/rpt,rtn->pn/dot_general | solution.py:84
  94.4 1.4 %fusion.34 = f32[256,512]{1,0:T(8,128)S(1)} fusion(bf16[18,256,512]{2,1,0:T(8,128)(2,1)S(1)} %bitcast.42, bf16[18,1024,256]{2,1,0:T(8,128)(2,1)S(1)} %bitcast.58, s32[]{:T(128)S(6)} %select_n.252), kind=kOutput, calls=%fused_computation.22 | convolution fusion | flops 1207959552 | bytes 7602180 | tf_op jit(solution)/shard_map/rpt,rtn->pn/dot_general | solution.py:84
  95.8 0.1 add.284
  95.9 3.3 %collective-permute-start.21 = (f32[256,512]{1,0:T(8,128)S(1)}, f32[256,512]{1,0:T(8,128)S(1)}, u32[]{:S(2)}, u32[]{:S(2)}) collective-permute-start(f32[256,512]{1,0:T(8,128)S(1)} %add.284), channel_id=1, source_target_pairs={{0,96},{16,112},{32,0},{48,16},{64,32},{80,48},{96,64},{112,80},{1... | collective-permute-start | bytes 1572872 | tf_op jit(solution)/shard_map/ppermute | solution.py:94
  99.2 7.6 %collective-permute-done.17 = f32[256,512]{1,0:T(8,128)S(1)} collective-permute-done((f32[256,512]{1,0:T(8,128)S(1)}, f32[256,512]{1,0:T(8,128)S(1)}, u32[]{:S(2)}, u32[]{:S(2)}) %collective-permute-start.17) | collective-permute-done | bytes 524320 | tf_op jit(solution)/shard_map/ppermute | solution.py:94
  106.8 0.1 add.272
  106.9 1.1 collective-permute-start.18
  108.0 3.0 %fusion.37 = f32[256,512]{1,0:T(8,128)S(1)} fusion(bf16[18,256,512]{2,1,0:T(8,128)(2,1)S(1)} %bitcast.43, bf16[18,1024,256]{2,1,0:T(8,128)(2,1)} %bitcast.52, s32[]{:T(128)S(6)} %select_n.254), kind=kOutput, calls=%fused_computation.23 | convolution fusion | flops 1207959552 | bytes 7602180 | tf_op jit(solution)/shard_map/rpt,rtn->pn/dot_general | solution.py:84
  111.1 0.1 add.287
  111.2 2.5 %collective-permute-start.22 = (f32[128,512]{1,0:T(8,128)S(1)}, f32[128,512]{1,0:T(8,128)S(1)}, u32[]{:S(2)}, u32[]{:S(2)}) collective-permute-start(f32[128,512]{1,0:T(8,128)S(1)} %get-tuple-element.11), channel_id=1, source_target_pairs={{0,16},{16,0},{32,48},{48,32},{64,80},{80,64},{96,112},{112,96},{1... | collective-permute-start | bytes 786440 | tf_op jit(solution)/shard_map/ppermute | solution.py:98
  113.8 0.4 rev.18
  114.1 0.4 rev.20
  114.5 3.0 %collective-permute-done.18 = f32[128,512]{1,0:T(8,128)S(1)} collective-permute-done((f32[128,512]{1,0:T(8,128)S(1)}, f32[128,512]{1,0:T(8,128)S(1)}, u32[]{:S(2)}, u32[]{:S(2)}) %collective-permute-start.18) | collective-permute-done | bytes 262176 | tf_op jit(solution)/shard_map/ppermute | solution.py:98
  117.5 0.4 rev.19
  117.9 2.6 %collective-permute-done.22 = f32[128,512]{1,0:T(8,128)S(1)} collective-permute-done((f32[128,512]{1,0:T(8,128)S(1)}, f32[128,512]{1,0:T(8,128)S(1)}, u32[]{:S(2)}, u32[]{:S(2)}) %collective-permute-start.22) | collective-permute-done | bytes 262176 | tf_op jit(solution)/shard_map/ppermute | solution.py:98
  120.5 0.4 rev.21
  120.9 1.2 copy.12
  (37 shorter events, 0.3 us)
Async XLA Ops:
  3.4 8.1 %collective-permute-start = (bf16[2,6,3,1024]{3,0,2,1:T(2,128)(2,1)S(1)}, bf16[2,6,3,1024]{3,0,2,1:T(2,128)(2,1)S(1)}, u32[]{:S(2)}, u32[]{:S(2)}) collective-permute-start(bf16[2,6,3,1024]{3,0,2,1:T(2,128)(2,1)S(1)} %rev.17), channel_id=1, source_target_pairs={{0,15},{1,0},{2,1},{3,2},{4,3},{5,4},{6,5},{7,6},{8,7},{9,8},{10,9... | collective-permute-start | bytes 221192 | tf_op jit(solution)/shard_map/ppermute | solution.py:26
  6.9 5.9 %collective-permute-start.1 = (bf16[2,6,3,1024]{3,0,2,1:T(2,128)(2,1)S(1)}, bf16[2,6,3,1024]{3,0,2,1:T(2,128)(2,1)S(1)}, u32[]{:S(2)}, u32[]{:S(2)}) collective-permute-start(bf16[2,6,3,1024]{3,0,2,1:T(2,128)(2,1)S(1)} %rev.17), channel_id=1, source_target_pairs={{0,14},{1,15},{2,0},{3,1},{4,2},{5,3},{6,4},{7,5},{8,6},{9,7},{10,... | collective-permute-start | bytes 221192 | tf_op jit(solution)/shard_map/ppermute | solution.py:26
  7.6 6.3 %collective-permute-start.10 = (bf16[2,6,3,1024]{3,0,2,1:T(2,128)(2,1)S(1)}, bf16[2,6,3,1024]{3,0,2,1:T(2,128)(2,1)S(1)}, u32[]{:S(2)}, u32[]{:S(2)}) collective-permute-start(bf16[2,6,3,1024]{3,0,2,1:T(2,128)(2,1)S(1)} %rev.17), channel_id=1, source_target_pairs={{0,5},{1,6},{2,7},{3,8},{4,9},{5,10},{6,11},{7,12},{8,13},{9,14},{... | collective-permute-start | bytes 221192 | tf_op jit(solution)/shard_map/ppermute | solution.py:26
  7.6 11.2 %collective-permute-start.11 = (bf16[2,6,3,1024]{3,0,2,1:T(2,128)(2,1)S(1)}, bf16[2,6,3,1024]{3,0,2,1:T(2,128)(2,1)S(1)}, u32[]{:S(2)}, u32[]{:S(2)}) collective-permute-start(bf16[2,6,3,1024]{3,0,2,1:T(2,128)(2,1)S(1)} %rev.17), channel_id=1, source_target_pairs={{0,4},{1,5},{2,6},{3,7},{4,8},{5,9},{6,10},{7,11},{8,12},{9,13},{1... | collective-permute-start | bytes 221192 | tf_op jit(solution)/shard_map/ppermute | solution.py:26
  7.9 11.3 %collective-permute-start.12 = (bf16[2,6,3,1024]{3,0,2,1:T(2,128)(2,1)S(1)}, bf16[2,6,3,1024]{3,0,2,1:T(2,128)(2,1)S(1)}, u32[]{:S(2)}, u32[]{:S(2)}) collective-permute-start(bf16[2,6,3,1024]{3,0,2,1:T(2,128)(2,1)S(1)} %rev.17), channel_id=1, source_target_pairs={{0,3},{1,4},{2,5},{3,6},{4,7},{5,8},{6,9},{7,10},{8,11},{9,12},{10... | collective-permute-start | bytes 221192 | tf_op jit(solution)/shard_map/ppermute | solution.py:26
  11.5 8.6 %collective-permute-start.13 = (bf16[2,6,3,1024]{3,0,2,1:T(2,128)(2,1)S(1)}, bf16[2,6,3,1024]{3,0,2,1:T(2,128)(2,1)S(1)}, u32[]{:S(2)}, u32[]{:S(2)}) collective-permute-start(bf16[2,6,3,1024]{3,0,2,1:T(2,128)(2,1)S(1)} %rev.17), channel_id=1, source_target_pairs={{0,2},{1,3},{2,4},{3,5},{4,6},{5,7},{6,8},{7,9},{8,10},{9,11},{10,... | collective-permute-start | bytes 221192 | tf_op jit(solution)/shard_map/ppermute | solution.py:26
  12.8 8.2 %collective-permute-start.14 = (bf16[2,6,3,1024]{3,0,2,1:T(2,128)(2,1)S(1)}, bf16[2,6,3,1024]{3,0,2,1:T(2,128)(2,1)S(1)}, u32[]{:S(2)}, u32[]{:S(2)}) collective-permute-start(bf16[2,6,3,1024]{3,0,2,1:T(2,128)(2,1)S(1)} %rev.17), channel_id=1, source_target_pairs={{0,1},{1,2},{2,3},{3,4},{4,5},{5,6},{6,7},{7,8},{8,9},{9,10},{10,1... | collective-permute-start | bytes 221192 | tf_op jit(solution)/shard_map/ppermute | solution.py:26
  13.9 9.8 %collective-permute-start.2 = (bf16[2,6,3,1024]{3,0,2,1:T(2,128)(2,1)S(1)}, bf16[2,6,3,1024]{3,0,2,1:T(2,128)(2,1)S(1)}, u32[]{:S(2)}, u32[]{:S(2)}) collective-permute-start(bf16[2,6,3,1024]{3,0,2,1:T(2,128)(2,1)S(1)} %rev.17), channel_id=1, source_target_pairs={{0,13},{1,14},{2,15},{3,0},{4,1},{5,2},{6,3},{7,4},{8,5},{9,6},{10... | collective-permute-start | bytes 221192 | tf_op jit(solution)/shard_map/ppermute | solution.py:26
  18.8 5.9 %collective-permute-start.3 = (bf16[2,6,3,1024]{3,0,2,1:T(2,128)(2,1)S(1)}, bf16[2,6,3,1024]{3,0,2,1:T(2,128)(2,1)S(1)}, u32[]{:S(2)}, u32[]{:S(2)}) collective-permute-start(bf16[2,6,3,1024]{3,0,2,1:T(2,128)(2,1)S(1)} %rev.17), channel_id=1, source_target_pairs={{0,12},{1,13},{2,14},{3,15},{4,0},{5,1},{6,2},{7,3},{8,4},{9,5},{1... | collective-permute-start | bytes 221192 | tf_op jit(solution)/shard_map/ppermute | solution.py:26
  19.2 6.4 %collective-permute-start.4 = (bf16[2,6,3,1024]{3,0,2,1:T(2,128)(2,1)S(1)}, bf16[2,6,3,1024]{3,0,2,1:T(2,128)(2,1)S(1)}, u32[]{:S(2)}, u32[]{:S(2)}) collective-permute-start(bf16[2,6,3,1024]{3,0,2,1:T(2,128)(2,1)S(1)} %rev.17), channel_id=1, source_target_pairs={{0,11},{1,12},{2,13},{3,14},{4,15},{5,0},{6,1},{7,2},{8,3},{9,4},{... | collective-permute-start | bytes 221192 | tf_op jit(solution)/shard_map/ppermute | solution.py:26
  20.1 8.5 %collective-permute-start.5 = (bf16[2,6,3,1024]{3,0,2,1:T(2,128)(2,1)S(1)}, bf16[2,6,3,1024]{3,0,2,1:T(2,128)(2,1)S(1)}, u32[]{:S(2)}, u32[]{:S(2)}) collective-permute-start(bf16[2,6,3,1024]{3,0,2,1:T(2,128)(2,1)S(1)} %rev.17), channel_id=1, source_target_pairs={{0,10},{1,11},{2,12},{3,13},{4,14},{5,15},{6,0},{7,1},{8,2},{9,3},... | collective-permute-start | bytes 221192 | tf_op jit(solution)/shard_map/ppermute | solution.py:26
  21.1 7.5 %collective-permute-start.6 = (bf16[2,6,3,1024]{3,0,2,1:T(2,128)(2,1)S(1)}, bf16[2,6,3,1024]{3,0,2,1:T(2,128)(2,1)S(1)}, u32[]{:S(2)}, u32[]{:S(2)}) collective-permute-start(bf16[2,6,3,1024]{3,0,2,1:T(2,128)(2,1)S(1)} %rev.17), channel_id=1, source_target_pairs={{0,9},{1,10},{2,11},{3,12},{4,13},{5,14},{6,15},{7,0},{8,1},{9,2},... | collective-permute-start | bytes 221192 | tf_op jit(solution)/shard_map/ppermute | solution.py:26
  23.7 6.4 %collective-permute-start.7 = (bf16[2,6,3,1024]{3,0,2,1:T(2,128)(2,1)S(1)}, bf16[2,6,3,1024]{3,0,2,1:T(2,128)(2,1)S(1)}, u32[]{:S(2)}, u32[]{:S(2)}) collective-permute-start(bf16[2,6,3,1024]{3,0,2,1:T(2,128)(2,1)S(1)} %rev.17), channel_id=1, source_target_pairs={{0,8},{1,9},{2,10},{3,11},{4,12},{5,13},{6,14},{7,15},{8,0},{9,1},... | collective-permute-start | bytes 221192 | tf_op jit(solution)/shard_map/ppermute | solution.py:26
  24.7 6.4 %collective-permute-start.8 = (bf16[2,6,3,1024]{3,0,2,1:T(2,128)(2,1)S(1)}, bf16[2,6,3,1024]{3,0,2,1:T(2,128)(2,1)S(1)}, u32[]{:S(2)}, u32[]{:S(2)}) collective-permute-start(bf16[2,6,3,1024]{3,0,2,1:T(2,128)(2,1)S(1)} %rev.17), channel_id=1, source_target_pairs={{0,7},{1,8},{2,9},{3,10},{4,11},{5,12},{6,13},{7,14},{8,15},{9,0},... | collective-permute-start | bytes 221192 | tf_op jit(solution)/shard_map/ppermute | solution.py:26
  25.6 7.7 %collective-permute-start.9 = (bf16[2,6,3,1024]{3,0,2,1:T(2,128)(2,1)S(1)}, bf16[2,6,3,1024]{3,0,2,1:T(2,128)(2,1)S(1)}, u32[]{:S(2)}, u32[]{:S(2)}) collective-permute-start(bf16[2,6,3,1024]{3,0,2,1:T(2,128)(2,1)S(1)} %rev.17), channel_id=1, source_target_pairs={{0,6},{1,7},{2,8},{3,9},{4,10},{5,11},{6,12},{7,13},{8,14},{9,15},... | collective-permute-start | bytes 221192 | tf_op jit(solution)/shard_map/ppermute | solution.py:26
  53.3 2.1 %copy-start = (bf16[4608,512]{1,0:T(8,128)(2,1)}, bf16[4608,512]{1,0:T(8,128)(2,1)S(1)}, u32[]{:S(2)}) copy-start(bf16[4608,512]{1,0:T(8,128)(2,1)S(1)} %get-tuple-element.7) | copy-start | bytes 14155780
  55.5 22.8 %slice-start.2 = ((s8[9437184]{0:T(1024)(128)(4,1)}), s8[1048576]{0:T(1024)(128)(4,1)S(1)}, s32[]{:S(2)}) async-start(s8[9437184]{0:T(1024)(128)(4,1)} %bitcast.53), calls=%async_computation.2 | async-start | bytes 2097152
  58.6 16.3 %collective-permute-start.15 = (f32[256,512]{1,0:T(8,128)S(1)}, f32[256,512]{1,0:T(8,128)S(1)}, u32[]{:S(2)}, u32[]{:S(2)}) collective-permute-start(f32[256,512]{1,0:T(8,128)S(1)} %fusion.16), channel_id=1, source_target_pairs={{0,32},{16,48},{32,64},{48,80},{64,96},{80,112},{96,0},{112,16},{1... | collective-permute-start | bytes 1572872 | tf_op jit(solution)/shard_map/ppermute | solution.py:94
  60.6 14.3 %copy-start.1 = (bf16[4608,512]{1,0:T(8,128)(2,1)S(1)}, bf16[4608,512]{1,0:T(8,128)(2,1)}, u32[]{:S(2)}) copy-start(bf16[4608,512]{1,0:T(8,128)(2,1)} %copy-done) | copy-start | bytes 14155780
  60.6 17.7 %slice-start.3 = ((s8[9437184]{0:T(1024)(128)(4,1)}), s8[4194304]{0:T(1024)(128)(4,1)S(1)}, s32[]{:S(2)}) async-start(s8[9437184]{0:T(1024)(128)(4,1)} %bitcast.53), calls=%async_computation.3 | async-start | bytes 8388608
  60.6 19.1 %slice-start = ((s8[4718592]{0:T(1024)(128)(4,1)}), s8[4194304]{0:T(1024)(128)(4,1)S(1)}, s32[]{:S(2)}) async-start(s8[4718592]{0:T(1024)(128)(4,1)} %bitcast.39), calls=%async_computation | async-start | bytes 8388608
  65.2 13.1 %slice-start.4 = ((s8[9437184]{0:T(1024)(128)(4,1)}), s8[4194304]{0:T(1024)(128)(4,1)S(1)}, s32[]{:S(2)}) async-start(s8[9437184]{0:T(1024)(128)(4,1)} %bitcast.53), calls=%async_computation.4 | async-start | bytes 8388608
  65.2 14.5 %slice-start.1 = ((s8[4718592]{0:T(1024)(128)(4,1)}), s8[524288]{0:T(1024)(128)(4,1)S(1)}, s32[]{:S(2)}) async-start(s8[4718592]{0:T(1024)(128)(4,1)} %bitcast.39), calls=%async_computation.1 | async-start | bytes 1048576
  65.2 14.5 %collective-permute-start.19 = (f32[256,512]{1,0:T(8,128)S(1)}, f32[256,512]{1,0:T(8,128)S(1)}, u32[]{:S(2)}, u32[]{:S(2)}) collective-permute-start(f32[256,512]{1,0:T(8,128)S(1)} %fusion.28), channel_id=1, source_target_pairs={{0,96},{16,112},{32,0},{48,16},{64,32},{80,48},{96,64},{112,80},{1... | collective-permute-start | bytes 1572872 | tf_op jit(solution)/shard_map/ppermute | solution.py:94
  78.0 14.9 %collective-permute-start.16 = (f32[256,512]{1,0:T(8,128)S(1)}, f32[256,512]{1,0:T(8,128)S(1)}, u32[]{:S(2)}, u32[]{:S(2)}) collective-permute-start(f32[256,512]{1,0:T(8,128)S(1)} %fusion.43), channel_id=1, source_target_pairs={{0,32},{16,48},{32,64},{48,80},{64,96},{80,112},{96,0},{112,16},{1... | collective-permute-start | bytes 1572872 | tf_op jit(solution)/shard_map/ppermute | solution.py:94
  81.1 14.7 %collective-permute-start.20 = (f32[256,512]{1,0:T(8,128)S(1)}, f32[256,512]{1,0:T(8,128)S(1)}, u32[]{:S(2)}, u32[]{:S(2)}) collective-permute-start(f32[256,512]{1,0:T(8,128)S(1)} %fusion.40), channel_id=1, source_target_pairs={{0,96},{16,112},{32,0},{48,16},{64,32},{80,48},{96,64},{112,80},{1... | collective-permute-start | bytes 1572872 | tf_op jit(solution)/shard_map/ppermute | solution.py:94
  93.0 13.8 %collective-permute-start.17 = (f32[256,512]{1,0:T(8,128)S(1)}, f32[256,512]{1,0:T(8,128)S(1)}, u32[]{:S(2)}, u32[]{:S(2)}) collective-permute-start(f32[256,512]{1,0:T(8,128)S(1)} %add.269), channel_id=1, source_target_pairs={{0,32},{16,48},{32,64},{48,80},{64,96},{80,112},{96,0},{112,16},{1... | collective-permute-start | bytes 1572872 | tf_op jit(solution)/shard_map/ppermute | solution.py:94
  95.9 15.2 %collective-permute-start.21 = (f32[256,512]{1,0:T(8,128)S(1)}, f32[256,512]{1,0:T(8,128)S(1)}, u32[]{:S(2)}, u32[]{:S(2)}) collective-permute-start(f32[256,512]{1,0:T(8,128)S(1)} %add.284), channel_id=1, source_target_pairs={{0,96},{16,112},{32,0},{48,16},{64,32},{80,48},{96,64},{112,80},{1... | collective-permute-start | bytes 1572872 | tf_op jit(solution)/shard_map/ppermute | solution.py:94
  106.9 10.6 %collective-permute-start.18 = (f32[128,512]{1,0:T(8,128)S(1)}, f32[128,512]{1,0:T(8,128)S(1)}, u32[]{:S(2)}, u32[]{:S(2)}) collective-permute-start(f32[128,512]{1,0:T(8,128)S(1)} %get-tuple-element.9), channel_id=1, source_target_pairs={{0,16},{16,0},{32,48},{48,32},{64,80},{80,64},{96,112},{112,96},{1... | collective-permute-start | bytes 786440 | tf_op jit(solution)/shard_map/ppermute | solution.py:98
  111.2 9.2 %collective-permute-start.22 = (f32[128,512]{1,0:T(8,128)S(1)}, f32[128,512]{1,0:T(8,128)S(1)}, u32[]{:S(2)}, u32[]{:S(2)}) collective-permute-start(f32[128,512]{1,0:T(8,128)S(1)} %get-tuple-element.11), channel_id=1, source_target_pairs={{0,16},{16,0},{32,48},{48,32},{64,80},{80,64},{96,112},{112,96},{1... | collective-permute-start | bytes 786440 | tf_op jit(solution)/shard_map/ppermute | solution.py:98

commit v8 on v7

--- a/solution.py
+++ b/solution.py
@@ -12,7 +12,7 @@
 WIDE = LAGS + NT
 
 
-def from_owners(x, axis, roots, radix=16):
+def from_owners(x, axis, roots, radix=4):
     size = lax.axis_size(axis)
     me = lax.axis_index(axis)
     span = 1
@@ -31,22 +31,27 @@
     return x
 
 
-def _toeplitz_kernel(shift_ref, weight_ref, rev_ref, out_ref):
+def _toeplitz_kernel(shift_ref, weight_ref, rev_ref, *out_refs):
+    rows = weight_ref.shape[0]
+
     def body(r, carry):
-        row = rev_ref[r]
-        row = pltpu.roll(row, shift_ref[r], 1)
-        row = (row * weight_ref[r]).astype(jnp.bfloat16).astype(jnp.float32)
-        row = jnp.concatenate([row[:, :LAGS], row[:, SAMPLES - NT :]], axis=1)
-        wide = jnp.broadcast_to(row, (NT, WIDE))
-        band = pltpu.roll(wide, 0, 1, stride=1, stride_axis=0)
-        out_ref[pl.ds(pl.multiple_of(r * NT, NT), NT), :] = band[:, :LAGS].astype(out_ref.dtype)
+        for e, out_ref in enumerate(out_refs):
+            row = rev_ref[e * rows + r]
+            row = pltpu.roll(row, shift_ref[e * rows + r], 1)
+            row = (row * weight_ref[r]).astype(jnp.bfloat16).astype(jnp.float32)
+            row = jnp.concatenate([row[:, :LAGS], row[:, SAMPLES - NT :]], axis=1)
+            wide = jnp.broadcast_to(row, (NT, WIDE))
+            band = pltpu.roll(wide, 0, 1, stride=1, stride_axis=0)
+            out_ref[pl.ds(pl.multiple_of(r * NT, NT), NT), :] = band[:, :LAGS].astype(out_ref.dtype)
         return carry
 
-    lax.fori_loop(0, rev_ref.shape[0], body, 0)
+    lax.fori_loop(0, rows, body, 0)
 
 
 def toeplitz_reversed(rev, shifts, weights):
-    rows = rev.shape[0]
+    rows = weights.shape[0]
+    ev = rev.shape[0] // rows
+    band = jax.ShapeDtypeStruct((rows * NT, LAGS), jnp.bfloat16)
     return pl.pallas_call(
         _toeplitz_kernel,
         in_specs=[
@@ -54,9 +59,9 @@
             pl.BlockSpec(memory_space=pltpu.SMEM),
             pl.BlockSpec(memory_space=pltpu.VMEM),
         ],
-        out_specs=pl.BlockSpec(memory_space=pltpu.VMEM),
-        out_shape=jax.ShapeDtypeStruct((rows * NT, LAGS), jnp.bfloat16),
-        cost_estimate=pl.CostEstimate(flops=0, transcendentals=0, bytes_accessed=rows * NT * LAGS * 2),
+        out_specs=[pl.BlockSpec(memory_space=pltpu.VMEM)] * ev,
+        out_shape=[band] * ev,
+        cost_estimate=pl.CostEstimate(flops=0, transcendentals=0, bytes_accessed=ev * rows * NT * LAGS * 2),
     )(shifts, weights, rev)
 
 
@@ -68,8 +73,8 @@
     traces = from_owners(flipped, "loc", owners)
     rev = traces.astype(jnp.float32).reshape(EV * rows, 1, SAMPLES)
     shifts = ((jnp.repeat(onsets.astype(jnp.int32), 3, axis=1) - LAGS) % SAMPLES).reshape(-1)
-    weights = jnp.tile(jnp.exp2(-codes.astype(jnp.float32)).reshape(-1), EV)
-    bands = toeplitz_reversed(rev, shifts, weights).reshape(EV, rows * NT, LAGS)
+    weights = jnp.exp2(-codes.astype(jnp.float32)).reshape(-1)
+    bands = toeplitz_reversed(rev, shifts, weights)
 
     size = lax.axis_size("sens")
     me = lax.axis_index("sens")

time: 123 us -> 90.5 us (0.74)
  starting transfers between devices: 32.3 us -> 21.4 us
  waiting for transfers between devices: 38 us -> 27.5 us
  local copies, waits for them, and re-layouts: 16.8 us -> 7.99 us
  Pallas kernels: 11.9 us -> 9.12 us
    ppermute x15 -> x6, starting transfers between devices: 17.4 us -> 6.58 us  [from_owners(): got = lax.ppermute(x, axis, perm)]
    ppermute x6, waiting for transfers between devices: 23.4 us -> 16 us  [local(): got = lax.ppermute(acc, 'sens', ring_perm(step))]
    slice x1 -> x0, local copies, waits for them, and re-layouts: 6.6 us -> none  [local(): band = bands[e]]
    ppermute x15 -> x6, waiting for transfers between devices: 9.05 us -> 5.97 us  [from_owners(): got = lax.ppermute(x, axis, perm)]
    pallas_call x1, Pallas kernels: 11.9 us -> 9.12 us  [toeplitz_reversed(): pl.pallas_call(_toeplitz_kernel, in_specs=[pl.BlockSpec(memory_space=pltp...]
    unnamed x14, local copies, waits for them, and re-layouts: 2.17 us -> 0.03 us
  transfers between devices with their start and end apart: 23 -> 14, of which waited for: 11 -> 8; matrix products, arithmetic and copies ran while one was open for 17% -> 23% of each run, Pallas kernels for 0% -> 0%
where the time goes in v8:
time: 90.5 us; the launch traced here: 90.2 us
  waiting for transfers between devices  27.5 us (30%)
  starting transfers between devices  21.4 us (24%)
  matrix products  20.3 us (22%)
  Pallas kernels  9.12 us (10%)
  local copies, waits for them, and re-layouts  7.99 us (9%)
  other arithmetic  3.57 us (4%)
    dot_general x8, matrix products, piece(): jnp.einsum('rpt,rtn->pn', g, band.reshape(rows, NT, LAGS), preferred_elem...  20.3 us
    ppermute x6, waiting for transfers between devices, local(): got = lax.ppermute(acc, 'sens', ring_perm(step))  16 us
    ppermute x6, starting transfers between devices, local(): got = lax.ppermute(acc, 'sens', ring_perm(step))  11.1 us
    pallas_call x1, Pallas kernels, toeplitz_reversed(): pl.pallas_call(_toeplitz_kernel, in_specs=[pl.BlockSpec(memory_space=pltp...  9.12 us
    ppermute x6, starting transfers between devices, from_owners(): got = lax.ppermute(x, axis, perm)  6.58 us
    ppermute x6, waiting for transfers between devices, from_owners(): got = lax.ppermute(x, axis, perm)  5.97 us
    ppermute x2, waiting for transfers between devices, local(): got = lax.ppermute(theirs, 'sens', [(i, i ^ 1) for i in range(size)])  5.52 us
    ppermute x2, starting transfers between devices, local(): got = lax.ppermute(theirs, 'sens', [(i, i ^ 1) for i in range(size)])  3.69 us
  transfers between devices with their start and end apart: 14, of which 8 were waited for; matrix products, arithmetic and copies ran while one was open for 23% of the time, Pallas kernels for 0%

profile of v8, /device:TPU:0, one launch (start us, length us, event | category | flops | bytes accessed | tf_op | source)
XLA Modules:
  0.0 90.2 jit_solution(1314107593701435409)
XLA Ops:
  0.0 3.4 %rev.17 = bf16[2,6,3,1024]{3,0,2,1:T(2,128)(2,1)S(1)} reverse(bf16[2,6,3,1024]{3,0,2,1:T(2,128)(2,1)} %bitcast.38), dimensions={3} | reverse | bytes 147456 | tf_op jit(solution)/shard_map/jit(_flip)/rev | solution.py:72
  3.4 1.1 %collective-permute-start = (bf16[2,6,3,1024]{3,0,2,1:T(2,128)(2,1)S(1)}, bf16[2,6,3,1024]{3,0,2,1:T(2,128)(2,1)S(1)}, u32[]{:S(2)}, u32[]{:S(2)}) collective-permute-start(bf16[2,6,3,1024]{3,0,2,1:T(2,128)(2,1)S(1)} %rev.17), channel_id=1, source_target_pairs={{0,3},{1,0},{2,1},{3,2},{4,7},{5,4},{6,5},{7,6},{8,11},{9,8},{10,9... | collective-permute-start | bytes 221192 | tf_op jit(solution)/shard_map/ppermute | solution.py:26
  4.5 0.7 collective-permute-start.1
  5.1 0.2 collective-permute-start.2
  5.3 0.7 broadcast_add_fusion
  6.0 0.7 multiply_exponential_fusion
  6.7 0.7 broadcast_compare_fusion
  7.4 0.1 broadcast_in_dim.36
  7.4 0.1 sub.68
  7.5 0.0 collective-permute-done
  7.5 2.2 %collective-permute-done.1 = bf16[2,6,3,1024]{3,0,2,1:T(2,128)(2,1)S(1)} collective-permute-done((bf16[2,6,3,1024]{3,0,2,1:T(2,128)(2,1)S(1)}, bf16[2,6,3,1024]{3,0,2,1:T(2,128)(2,1)S(1)}, u32[]{:S(2)}, u32[]{:S(2)}) %collective-permute-start.1) | collective-permute-done | bytes 73760 | tf_op jit(solution)/shard_map/ppermute | solution.py:26
  9.7 0.0 collective-permute-done.2
  9.7 0.2 broadcast_select_fusion.4
  10.0 3.1 %collective-permute-start.3 = (bf16[2,6,3,1024]{3,0,2,1:T(2,128)(2,1)S(1)}, bf16[2,6,3,1024]{3,0,2,1:T(2,128)(2,1)S(1)}, u32[]{:S(2)}, u32[]{:S(2)}) collective-permute-start(bf16[2,6,3,1024]{3,0,2,1:T(2,128)(2,1)S(1)} %broadcast_select_fusion.4), channel_id=1, source_target_pairs={{0,12},{1,13},{2,14},{3,15},{4,0},{5,1},{6,2},{7,3},{8,4},{9,5},{1... | collective-permute-start | bytes 221192 | tf_op jit(solution)/shard_map/ppermute | solution.py:26
  13.1 0.6 collective-permute-start.4
  13.7 1.0 %collective-permute-start.5 = (bf16[2,6,3,1024]{3,0,2,1:T(2,128)(2,1)S(1)}, bf16[2,6,3,1024]{3,0,2,1:T(2,128)(2,1)S(1)}, u32[]{:S(2)}, u32[]{:S(2)}) collective-permute-start(bf16[2,6,3,1024]{3,0,2,1:T(2,128)(2,1)S(1)} %broadcast_select_fusion.4), channel_id=1, source_target_pairs={{0,4},{1,5},{2,6},{3,7},{4,8},{5,9},{6,10},{7,11},{8,12},{9,13},{1... | collective-permute-start | bytes 221192 | tf_op jit(solution)/shard_map/ppermute | solution.py:26
  14.7 0.6 and_select_fusion.3.shift_ref
  15.3 0.1 copy.9
  15.4 0.6 reshape.41.weight_ref
  15.9 0.0 collective-permute-done.3
  15.9 3.0 %collective-permute-done.4 = bf16[2,6,3,1024]{3,0,2,1:T(2,128)(2,1)S(1)} collective-permute-done((bf16[2,6,3,1024]{3,0,2,1:T(2,128)(2,1)S(1)}, bf16[2,6,3,1024]{3,0,2,1:T(2,128)(2,1)S(1)}, u32[]{:S(2)}, u32[]{:S(2)}) %collective-permute-start.4) | collective-permute-done | bytes 73760 | tf_op jit(solution)/shard_map/ppermute | solution.py:26
  19.0 0.7 collective-permute-done.5
  19.7 0.2 fusion.46
  19.9 0.1 copy.10
  20.0 0.9 reshape.56.rev_ref
  20.9 9.1 %shard_map.55 = (bf16[4608,512]{1,0:T(8,128)(2,1)}, bf16[4608,512]{1,0:T(8,128)(2,1)}) custom-call(s32[36]{0:T(128)} %and_select_fusion.3.shift_ref, f32[18]{0:T(128)} %reshape.41.weight_ref, f32[36,1,1024]{2,1,0:T(1,128)} %reshape.56.rev_ref), custom_call_target="tpu_custom_call" | custom-call | bytes 9437184 | tf_op jit(solution)/shard_map/pallas_call | solution.py:55
  30.0 4.4 %fusion.16 = f32[256,512]{1,0:T(8,128)S(1)} fusion(bf16[18,256,512]{2,1,0:T(8,128)(2,1)} %bitcast.55, bf16[18,1024,256]{2,1,0:T(8,128)(2,1)} %bitcast.39, s32[]{:T(128)S(6)} %select_n.155), kind=kOutput, calls=%fused_computation.16 | convolution fusion | flops 1207959552 | bytes 7602180 | tf_op jit(solution)/shard_map/rpt,rtn->pn/dot_general | solution.py:89
  34.5 2.0 %collective-permute-start.6 = (f32[256,512]{1,0:T(8,128)S(1)}, f32[256,512]{1,0:T(8,128)S(1)}, u32[]{:S(2)}, u32[]{:S(2)}) collective-permute-start(f32[256,512]{1,0:T(8,128)S(1)} %fusion.16), channel_id=1, source_target_pairs={{0,32},{16,48},{32,64},{48,80},{64,96},{80,112},{96,0},{112,16},{1... | collective-permute-start | bytes 1572872 | tf_op jit(solution)/shard_map/ppermute | solution.py:99
  36.5 4.6 %fusion.28 = f32[256,512]{1,0:T(8,128)S(1)} fusion(bf16[18,256,512]{2,1,0:T(8,128)(2,1)} %bitcast.49, bf16[18,1024,256]{2,1,0:T(8,128)(2,1)} %bitcast.40, s32[]{:T(128)S(6)} %select_n.185), kind=kOutput, calls=%fused_computation.20 | convolution fusion | flops 1207959552 | bytes 7602180 | tf_op jit(solution)/shard_map/rpt,rtn->pn/dot_general | solution.py:89
  41.0 0.0 slice-start.2
  41.1 0.0 slice-start.6
  41.1 0.0 slice-start.4
  41.1 2.4 %collective-permute-start.10 = (f32[256,512]{1,0:T(8,128)S(1)}, f32[256,512]{1,0:T(8,128)S(1)}, u32[]{:S(2)}, u32[]{:S(2)}) collective-permute-start(f32[256,512]{1,0:T(8,128)S(1)} %fusion.28), channel_id=1, source_target_pairs={{0,96},{16,112},{32,0},{48,16},{64,32},{80,48},{96,64},{112,80},{1... | collective-permute-start | bytes 1572872 | tf_op jit(solution)/shard_map/ppermute | solution.py:99
  43.5 4.9 %collective-permute-done.6 = f32[256,512]{1,0:T(8,128)S(1)} collective-permute-done((f32[256,512]{1,0:T(8,128)S(1)}, f32[256,512]{1,0:T(8,128)S(1)}, u32[]{:S(2)}, u32[]{:S(2)}) %collective-permute-start.6) | collective-permute-done | bytes 524320 | tf_op jit(solution)/shard_map/ppermute | solution.py:99
  48.4 4.4 %fusion.43 = f32[256,512]{1,0:T(8,128)S(1)} fusion(f32[256,512]{1,0:T(8,128)S(1)} %collective-permute-done.6, bf16[18,256,512]{2,1,0:T(8,128)(2,1)} %bitcast.56, bf16[18,1024,256]{2,1,0:T(8,128)(2,1)} %bitcast.41, s32[]{:T(128)S(6)} %select_n.176), kind=kOutput, calls=%fused_computation.25 | convolution fusion | flops 1208090624 | bytes 8126468 | tf_op jit(solution)/shard_map/rpt,rtn->pn/dot_general | solution.py:89
  52.8 0.1 collective-permute-start.7
  52.9 0.0 slice-done
  52.9 0.0 slice-done.1
  53.0 1.4 %fusion.22 = f32[256,512]{1,0:T(8,128)S(1)} fusion(bf16[18,256,512]{2,1,0:T(8,128)(2,1)S(1)} %bitcast.59, bf16[18,1024,256]{2,1,0:T(8,128)(2,1)S(1)} %bitcast.44, s32[]{:T(128)S(6)} %select_n.178), kind=kOutput, calls=%fused_computation.18 | convolution fusion | flops 1207959552 | bytes 7602180 | tf_op jit(solution)/shard_map/rpt,rtn->pn/dot_general | solution.py:89
  54.4 0.0 collective-permute-done.10
  54.4 1.4 %fusion.40 = f32[256,512]{1,0:T(8,128)S(1)} fusion(f32[256,512]{1,0:T(8,128)S(1)} %collective-permute-done.10, bf16[18,256,512]{2,1,0:T(8,128)(2,1)S(1)} %bitcast.52, bf16[18,1024,256]{2,1,0:T(8,128)(2,1)S(1)} %bitcast.45, s32[]{:T(128)S(6)} %select_n.187), kind=kOutput, calls=%fused_computation.24 | convolution fusion | flops 1208090624 | bytes 8126468 | tf_op jit(solution)/shard_map/rpt,rtn->pn/dot_general | solution.py:89
  55.8 3.3 %collective-permute-start.11 = (f32[256,512]{1,0:T(8,128)S(1)}, f32[256,512]{1,0:T(8,128)S(1)}, u32[]{:S(2)}, u32[]{:S(2)}) collective-permute-start(f32[256,512]{1,0:T(8,128)S(1)} %fusion.40), channel_id=1, source_target_pairs={{0,96},{16,112},{32,0},{48,16},{64,32},{80,48},{96,64},{112,80},{1... | collective-permute-start | bytes 1572872 | tf_op jit(solution)/shard_map/ppermute | solution.py:99
  59.1 6.0 %collective-permute-done.7 = f32[256,512]{1,0:T(8,128)S(1)} collective-permute-done((f32[256,512]{1,0:T(8,128)S(1)}, f32[256,512]{1,0:T(8,128)S(1)}, u32[]{:S(2)}, u32[]{:S(2)}) %collective-permute-start.7) | collective-permute-done | bytes 524320 | tf_op jit(solution)/shard_map/ppermute | solution.py:99
  65.0 0.1 add.208
  65.1 0.1 collective-permute-start.8
  65.2 1.4 %fusion.25 = f32[256,512]{1,0:T(8,128)S(1)} fusion(bf16[18,256,512]{2,1,0:T(8,128)(2,1)S(1)} %bitcast.60, bf16[18,1024,256]{2,1,0:T(8,128)(2,1)S(1)} %bitcast.46, s32[]{:T(128)S(6)} %select_n.180), kind=kOutput, calls=%fused_computation.19 | convolution fusion | flops 1207959552 | bytes 7602180 | tf_op jit(solution)/shard_map/rpt,rtn->pn/dot_general | solution.py:89
  66.6 1.4 %fusion.34 = f32[256,512]{1,0:T(8,128)S(1)} fusion(bf16[18,256,512]{2,1,0:T(8,128)(2,1)S(1)} %bitcast.53, bf16[18,1024,256]{2,1,0:T(8,128)(2,1)S(1)} %bitcast.47, s32[]{:T(128)S(6)} %select_n.189), kind=kOutput, calls=%fused_computation.22 | convolution fusion | flops 1207959552 | bytes 7602180 | tf_op jit(solution)/shard_map/rpt,rtn->pn/dot_general | solution.py:89
  68.0 0.0 collective-permute-done.11
  68.0 0.1 add.223
  68.1 3.3 %collective-permute-start.12 = (f32[256,512]{1,0:T(8,128)S(1)}, f32[256,512]{1,0:T(8,128)S(1)}, u32[]{:S(2)}, u32[]{:S(2)}) collective-permute-start(f32[256,512]{1,0:T(8,128)S(1)} %add.223), channel_id=1, source_target_pairs={{0,96},{16,112},{32,0},{48,16},{64,32},{80,48},{96,64},{112,80},{1... | collective-permute-start | bytes 1572872 | tf_op jit(solution)/shard_map/ppermute | solution.py:99
  71.4 5.1 %collective-permute-done.8 = f32[256,512]{1,0:T(8,128)S(1)} collective-permute-done((f32[256,512]{1,0:T(8,128)S(1)}, f32[256,512]{1,0:T(8,128)S(1)}, u32[]{:S(2)}, u32[]{:S(2)}) %collective-permute-start.8) | collective-permute-done | bytes 524320 | tf_op jit(solution)/shard_map/ppermute | solution.py:99
  76.4 0.1 add.211
  76.6 2.4 %collective-permute-start.9 = (f32[128,512]{1,0:T(8,128)S(1)}, f32[128,512]{1,0:T(8,128)S(1)}, u32[]{:S(2)}, u32[]{:S(2)}) collective-permute-start(f32[128,512]{1,0:T(8,128)S(1)} %get-tuple-element.13), channel_id=1, source_target_pairs={{0,16},{16,0},{32,48},{48,32},{64,80},{80,64},{96,112},{112,96},{1... | collective-permute-start | bytes 786440 | tf_op jit(solution)/shard_map/ppermute | solution.py:103
  79.0 1.4 %fusion.37 = f32[256,512]{1,0:T(8,128)S(1)} fusion(bf16[18,256,512]{2,1,0:T(8,128)(2,1)S(1)} %bitcast.54, bf16[18,1024,256]{2,1,0:T(8,128)(2,1)S(1)} %bitcast.48, s32[]{:T(128)S(6)} %select_n.191), kind=kOutput, calls=%fused_computation.23 | convolution fusion | flops 1207959552 | bytes 7602180 | tf_op jit(solution)/shard_map/rpt,rtn->pn/dot_general | solution.py:89
  80.4 0.0 collective-permute-done.12
  80.4 0.1 add.226
  80.5 1.2 %collective-permute-start.13 = (f32[128,512]{1,0:T(8,128)S(1)}, f32[128,512]{1,0:T(8,128)S(1)}, u32[]{:S(2)}, u32[]{:S(2)}) collective-permute-start(f32[128,512]{1,0:T(8,128)S(1)} %get-tuple-element.15), channel_id=1, source_target_pairs={{0,16},{16,0},{32,48},{48,32},{64,80},{80,64},{96,112},{112,96},{1... | collective-permute-start | bytes 786440 | tf_op jit(solution)/shard_map/ppermute | solution.py:103
  81.8 0.4 rev.18
  82.1 0.4 rev.20
  82.5 2.6 %collective-permute-done.9 = f32[128,512]{1,0:T(8,128)S(1)} collective-permute-done((f32[128,512]{1,0:T(8,128)S(1)}, f32[128,512]{1,0:T(8,128)S(1)}, u32[]{:S(2)}, u32[]{:S(2)}) %collective-permute-start.9) | collective-permute-done | bytes 262176 | tf_op jit(solution)/shard_map/ppermute | solution.py:103
  85.1 0.4 rev.19
  85.5 2.9 %collective-permute-done.13 = f32[128,512]{1,0:T(8,128)S(1)} collective-permute-done((f32[128,512]{1,0:T(8,128)S(1)}, f32[128,512]{1,0:T(8,128)S(1)}, u32[]{:S(2)}, u32[]{:S(2)}) %collective-permute-start.13) | collective-permute-done | bytes 262176 | tf_op jit(solution)/shard_map/ppermute | solution.py:103
  88.5 0.4 rev.21
  89.0 1.2 %copy.12 = f32[128,2,512]{2,1,0:T(2,128)} copy(f32[128,2,512]{2,0,1:T(8,128)S(1)} %pad_maximum_fusion) | data formatting | bytes 1048576 | tf_op jit(solution)/shard_map/stack | solution.py:105
  (19 shorter events, 0.3 us)
Async XLA Ops:
  3.4 4.1 %collective-permute-start = (bf16[2,6,3,1024]{3,0,2,1:T(2,128)(2,1)S(1)}, bf16[2,6,3,1024]{3,0,2,1:T(2,128)(2,1)S(1)}, u32[]{:S(2)}, u32[]{:S(2)}) collective-permute-start(bf16[2,6,3,1024]{3,0,2,1:T(2,128)(2,1)S(1)} %rev.17), channel_id=1, source_target_pairs={{0,3},{1,0},{2,1},{3,2},{4,7},{5,4},{6,5},{7,6},{8,11},{9,8},{10,9... | collective-permute-start | bytes 221192 | tf_op jit(solution)/shard_map/ppermute | solution.py:26
  4.5 5.2 %collective-permute-start.1 = (bf16[2,6,3,1024]{3,0,2,1:T(2,128)(2,1)S(1)}, bf16[2,6,3,1024]{3,0,2,1:T(2,128)(2,1)S(1)}, u32[]{:S(2)}, u32[]{:S(2)}) collective-permute-start(bf16[2,6,3,1024]{3,0,2,1:T(2,128)(2,1)S(1)} %rev.17), channel_id=1, source_target_pairs={{0,2},{1,3},{2,0},{3,1},{4,6},{5,7},{6,4},{7,5},{8,10},{9,11},{10,... | collective-permute-start | bytes 221192 | tf_op jit(solution)/shard_map/ppermute | solution.py:26
  5.1 4.6 %collective-permute-start.2 = (bf16[2,6,3,1024]{3,0,2,1:T(2,128)(2,1)S(1)}, bf16[2,6,3,1024]{3,0,2,1:T(2,128)(2,1)S(1)}, u32[]{:S(2)}, u32[]{:S(2)}) collective-permute-start(bf16[2,6,3,1024]{3,0,2,1:T(2,128)(2,1)S(1)} %rev.17), channel_id=1, source_target_pairs={{0,1},{1,2},{2,3},{3,0},{4,5},{5,6},{6,7},{7,4},{8,9},{9,10},{10,1... | collective-permute-start | bytes 221192 | tf_op jit(solution)/shard_map/ppermute | solution.py:26
  10.0 6.0 %collective-permute-start.3 = (bf16[2,6,3,1024]{3,0,2,1:T(2,128)(2,1)S(1)}, bf16[2,6,3,1024]{3,0,2,1:T(2,128)(2,1)S(1)}, u32[]{:S(2)}, u32[]{:S(2)}) collective-permute-start(bf16[2,6,3,1024]{3,0,2,1:T(2,128)(2,1)S(1)} %broadcast_select_fusion.4), channel_id=1, source_target_pairs={{0,12},{1,13},{2,14},{3,15},{4,0},{5,1},{6,2},{7,3},{8,4},{9,5},{1... | collective-permute-start | bytes 221192 | tf_op jit(solution)/shard_map/ppermute | solution.py:26
  13.1 5.9 %collective-permute-start.4 = (bf16[2,6,3,1024]{3,0,2,1:T(2,128)(2,1)S(1)}, bf16[2,6,3,1024]{3,0,2,1:T(2,128)(2,1)S(1)}, u32[]{:S(2)}, u32[]{:S(2)}) collective-permute-start(bf16[2,6,3,1024]{3,0,2,1:T(2,128)(2,1)S(1)} %broadcast_select_fusion.4), channel_id=1, source_target_pairs={{0,8},{1,9},{2,10},{3,11},{4,12},{5,13},{6,14},{7,15},{8,0},{9,1},... | collective-permute-start | bytes 221192 | tf_op jit(solution)/shard_map/ppermute | solution.py:26
  13.7 6.0 %collective-permute-start.5 = (bf16[2,6,3,1024]{3,0,2,1:T(2,128)(2,1)S(1)}, bf16[2,6,3,1024]{3,0,2,1:T(2,128)(2,1)S(1)}, u32[]{:S(2)}, u32[]{:S(2)}) collective-permute-start(bf16[2,6,3,1024]{3,0,2,1:T(2,128)(2,1)S(1)} %broadcast_select_fusion.4), channel_id=1, source_target_pairs={{0,4},{1,5},{2,6},{3,7},{4,8},{5,9},{6,10},{7,11},{8,12},{9,13},{1... | collective-permute-start | bytes 221192 | tf_op jit(solution)/shard_map/ppermute | solution.py:26
  34.5 13.9 %collective-permute-start.6 = (f32[256,512]{1,0:T(8,128)S(1)}, f32[256,512]{1,0:T(8,128)S(1)}, u32[]{:S(2)}, u32[]{:S(2)}) collective-permute-start(f32[256,512]{1,0:T(8,128)S(1)} %fusion.16), channel_id=1, source_target_pairs={{0,32},{16,48},{32,64},{48,80},{64,96},{80,112},{96,0},{112,16},{1... | collective-permute-start | bytes 1572872 | tf_op jit(solution)/shard_map/ppermute | solution.py:99
  36.4 16.5 %slice-start = ((s8[9437184]{0:T(1024)(128)(4,1)}), s8[4194304]{0:T(1024)(128)(4,1)S(1)}, s32[]{:S(2)}) async-start(s8[9437184]{0:T(1024)(128)(4,1)} %bitcast.42), calls=%async_computation | async-start | bytes 8388608
  36.4 16.5 %slice-start.1 = ((s8[9437184]{0:T(1024)(128)(4,1)}), s8[4194304]{0:T(1024)(128)(4,1)S(1)}, s32[]{:S(2)}) async-start(s8[9437184]{0:T(1024)(128)(4,1)} %bitcast.42), calls=%async_computation.1 | async-start | bytes 8388608
  36.4 16.5 %slice-start.5 = ((s8[4718592]{0:T(1024)(128)(4,1)}), s8[4194304]{0:T(1024)(128)(4,1)S(1)}, s32[]{:S(2)}) async-start(s8[4718592]{0:T(1024)(128)(4,1)} %bitcast.57), calls=%async_computation.5 | async-start | bytes 8388608
  36.4 17.9 %slice-start.3 = ((s8[4718592]{0:T(1024)(128)(4,1)}), s8[4194304]{0:T(1024)(128)(4,1)S(1)}, s32[]{:S(2)}) async-start(s8[4718592]{0:T(1024)(128)(4,1)} %bitcast.50), calls=%async_computation.3 | async-start | bytes 8388608
  41.0 11.9 %slice-start.2 = ((s8[9437184]{0:T(1024)(128)(4,1)}), s8[1048576]{0:T(1024)(128)(4,1)S(1)}, s32[]{:S(2)}) async-start(s8[9437184]{0:T(1024)(128)(4,1)} %bitcast.42), calls=%async_computation.2 | async-start | bytes 2097152
  41.1 11.9 %slice-start.6 = ((s8[4718592]{0:T(1024)(128)(4,1)}), s8[524288]{0:T(1024)(128)(4,1)S(1)}, s32[]{:S(2)}) async-start(s8[4718592]{0:T(1024)(128)(4,1)} %bitcast.57), calls=%async_computation.6 | async-start | bytes 1048576
  41.1 13.3 %slice-start.4 = ((s8[4718592]{0:T(1024)(128)(4,1)}), s8[524288]{0:T(1024)(128)(4,1)S(1)}, s32[]{:S(2)}) async-start(s8[4718592]{0:T(1024)(128)(4,1)} %bitcast.50), calls=%async_computation.4 | async-start | bytes 1048576
  41.1 13.3 %collective-permute-start.10 = (f32[256,512]{1,0:T(8,128)S(1)}, f32[256,512]{1,0:T(8,128)S(1)}, u32[]{:S(2)}, u32[]{:S(2)}) collective-permute-start(f32[256,512]{1,0:T(8,128)S(1)} %fusion.28), channel_id=1, source_target_pairs={{0,96},{16,112},{32,0},{48,16},{64,32},{80,48},{96,64},{112,80},{1... | collective-permute-start | bytes 1572872 | tf_op jit(solution)/shard_map/ppermute | solution.py:99
  52.8 12.2 %collective-permute-start.7 = (f32[256,512]{1,0:T(8,128)S(1)}, f32[256,512]{1,0:T(8,128)S(1)}, u32[]{:S(2)}, u32[]{:S(2)}) collective-permute-start(f32[256,512]{1,0:T(8,128)S(1)} %fusion.43), channel_id=1, source_target_pairs={{0,32},{16,48},{32,64},{48,80},{64,96},{80,112},{96,0},{112,16},{1... | collective-permute-start | bytes 1572872 | tf_op jit(solution)/shard_map/ppermute | solution.py:99
  55.8 12.2 %collective-permute-start.11 = (f32[256,512]{1,0:T(8,128)S(1)}, f32[256,512]{1,0:T(8,128)S(1)}, u32[]{:S(2)}, u32[]{:S(2)}) collective-permute-start(f32[256,512]{1,0:T(8,128)S(1)} %fusion.40), channel_id=1, source_target_pairs={{0,96},{16,112},{32,0},{48,16},{64,32},{80,48},{96,64},{112,80},{1... | collective-permute-start | bytes 1572872 | tf_op jit(solution)/shard_map/ppermute | solution.py:99
  65.1 11.3 %collective-permute-start.8 = (f32[256,512]{1,0:T(8,128)S(1)}, f32[256,512]{1,0:T(8,128)S(1)}, u32[]{:S(2)}, u32[]{:S(2)}) collective-permute-start(f32[256,512]{1,0:T(8,128)S(1)} %add.208), channel_id=1, source_target_pairs={{0,32},{16,48},{32,64},{48,80},{64,96},{80,112},{96,0},{112,16},{1... | collective-permute-start | bytes 1572872 | tf_op jit(solution)/shard_map/ppermute | solution.py:99
  68.1 12.3 %collective-permute-start.12 = (f32[256,512]{1,0:T(8,128)S(1)}, f32[256,512]{1,0:T(8,128)S(1)}, u32[]{:S(2)}, u32[]{:S(2)}) collective-permute-start(f32[256,512]{1,0:T(8,128)S(1)} %add.223), channel_id=1, source_target_pairs={{0,96},{16,112},{32,0},{48,16},{64,32},{80,48},{96,64},{112,80},{1... | collective-permute-start | bytes 1572872 | tf_op jit(solution)/shard_map/ppermute | solution.py:99
  76.6 8.6 %collective-permute-start.9 = (f32[128,512]{1,0:T(8,128)S(1)}, f32[128,512]{1,0:T(8,128)S(1)}, u32[]{:S(2)}, u32[]{:S(2)}) collective-permute-start(f32[128,512]{1,0:T(8,128)S(1)} %get-tuple-element.13), channel_id=1, source_target_pairs={{0,16},{16,0},{32,48},{48,32},{64,80},{80,64},{96,112},{112,96},{1... | collective-permute-start | bytes 786440 | tf_op jit(solution)/shard_map/ppermute | solution.py:103
  80.5 8.0 %collective-permute-start.13 = (f32[128,512]{1,0:T(8,128)S(1)}, f32[128,512]{1,0:T(8,128)S(1)}, u32[]{:S(2)}, u32[]{:S(2)}) collective-permute-start(f32[128,512]{1,0:T(8,128)S(1)} %get-tuple-element.15), channel_id=1, source_target_pairs={{0,16},{16,0},{32,48},{48,32},{64,80},{80,64},{96,112},{112,96},{1... | collective-permute-start | bytes 786440 | tf_op jit(solution)/shard_map/ppermute | solution.py:103

commit v9 on v8

--- a/solution.py
+++ b/solution.py
@@ -97,7 +97,8 @@
         acc = piece(band, (z + zs - step) % zs)
         for k in range(zs - 1):
             got = lax.ppermute(acc, "sens", ring_perm(step))
-            acc = got + piece(band, (z + 4 * zs - step * (k + 2)) % zs)
+            part = lax.optimization_barrier(piece(band, (z + 4 * zs - step * (k + 2)) % zs))
+            acc = got + part
         theirs = lax.dynamic_slice_in_dim(acc, (1 - xh) * block, block, 0)
         kept = lax.dynamic_slice_in_dim(acc, xh * block, block, 0)
         got = lax.ppermute(theirs, "sens", [(i, i ^ 1) for i in range(size)])

time: 90.5 us -> 87.5 us (0.967)
  matrix products: 20.3 us -> 17.4 us
  waiting for transfers between devices: 27.5 us -> 25.5 us
  starting transfers between devices: 21.4 us -> 23.3 us
    dot_general x8, matrix products: 20.3 us -> 17.4 us  [piece(): jnp.einsum('rpt,rtn->pn', g, band.reshape(rows, NT, LAGS), preferred_elem...]
    ppermute x2, starting transfers between devices: 3.69 us -> 5.02 us  [local(): got = lax.ppermute(theirs, 'sens', [(i, i ^ 1) for i in range(size)])]
    ppermute x2, waiting for transfers between devices: 5.52 us -> 4.19 us  [local(): got = lax.ppermute(theirs, 'sens', [(i, i ^ 1) for i in range(size)])]
  transfers between devices with their start and end apart: 14 -> 14, of which waited for: 8 -> 11; matrix products, arithmetic and copies ran while one was open for 23% -> 21% of each run, Pallas kernels for 0% -> 0%
where the time goes in v9:
time: 87.5 us; the launch traced here: 87.1 us
  waiting for transfers between devices  25.5 us (29%)
  starting transfers between devices  23.3 us (27%)
  matrix products  17.4 us (20%)
  Pallas kernels  9.12 us (10%)
  local copies, waits for them, and re-layouts  7.95 us (9%)
  other arithmetic  3.68 us (4%)
    dot_general x8, matrix products, piece(): jnp.einsum('rpt,rtn->pn', g, band.reshape(rows, NT, LAGS), preferred_elem...  17.4 us
    ppermute x6, waiting for transfers between devices, local(): got = lax.ppermute(acc, 'sens', ring_perm(step))  15.2 us
    ppermute x6, starting transfers between devices, local(): got = lax.ppermute(acc, 'sens', ring_perm(step))  11.7 us
    pallas_call x1, Pallas kernels, toeplitz_reversed(): pl.pallas_call(_toeplitz_kernel, in_specs=[pl.BlockSpec(memory_space=pltp...  9.12 us
    ppermute x6, starting transfers between devices, from_owners(): got = lax.ppermute(x, axis, perm)  6.58 us
    ppermute x6, waiting for transfers between devices, from_owners(): got = lax.ppermute(x, axis, perm)  6.05 us
    ppermute x2, starting transfers between devices, local(): got = lax.ppermute(theirs, 'sens', [(i, i ^ 1) for i in range(size)])  5.02 us
    ppermute x2, waiting for transfers between devices, local(): got = lax.ppermute(theirs, 'sens', [(i, i ^ 1) for i in range(size)])  4.19 us
  transfers between devices with their start and end apart: 14, of which 11 were waited for; matrix products, arithmetic and copies ran while one was open for 21% of the time, Pallas kernels for 0%

profile of v9, /device:TPU:0, one launch (start us, length us, event | category | flops | bytes accessed | tf_op | source)
XLA Modules:
  0.0 87.1 jit_solution(12577770867656844859)
XLA Ops:
  0.0 3.4 %rev.17 = bf16[2,6,3,1024]{3,0,2,1:T(2,128)(2,1)S(1)} reverse(bf16[2,6,3,1024]{3,0,2,1:T(2,128)(2,1)} %bitcast.34), dimensions={3} | reverse | bytes 147456 | tf_op jit(solution)/shard_map/jit(_flip)/rev | solution.py:72
  3.4 1.1 %collective-permute-start = (bf16[2,6,3,1024]{3,0,2,1:T(2,128)(2,1)S(1)}, bf16[2,6,3,1024]{3,0,2,1:T(2,128)(2,1)S(1)}, u32[]{:S(2)}, u32[]{:S(2)}) collective-permute-start(bf16[2,6,3,1024]{3,0,2,1:T(2,128)(2,1)S(1)} %rev.17), channel_id=1, source_target_pairs={{0,3},{1,0},{2,1},{3,2},{4,7},{5,4},{6,5},{7,6},{8,11},{9,8},{10,9... | collective-permute-start | bytes 221192 | tf_op jit(solution)/shard_map/ppermute | solution.py:26
  4.5 0.7 collective-permute-start.1
  5.1 0.2 collective-permute-start.2
  5.3 0.7 broadcast_add_fusion
  6.0 0.7 multiply_exponential_fusion
  6.7 0.7 broadcast_compare_fusion
  7.4 0.1 broadcast_in_dim.36
  7.4 0.1 sub.68
  7.5 0.0 collective-permute-done
  7.5 2.2 %collective-permute-done.1 = bf16[2,6,3,1024]{3,0,2,1:T(2,128)(2,1)S(1)} collective-permute-done((bf16[2,6,3,1024]{3,0,2,1:T(2,128)(2,1)S(1)}, bf16[2,6,3,1024]{3,0,2,1:T(2,128)(2,1)S(1)}, u32[]{:S(2)}, u32[]{:S(2)}) %collective-permute-start.1) | collective-permute-done | bytes 73760 | tf_op jit(solution)/shard_map/ppermute | solution.py:26
  9.7 0.0 collective-permute-done.2
  9.7 0.2 broadcast_select_fusion.4
  10.0 3.1 %collective-permute-start.3 = (bf16[2,6,3,1024]{3,0,2,1:T(2,128)(2,1)S(1)}, bf16[2,6,3,1024]{3,0,2,1:T(2,128)(2,1)S(1)}, u32[]{:S(2)}, u32[]{:S(2)}) collective-permute-start(bf16[2,6,3,1024]{3,0,2,1:T(2,128)(2,1)S(1)} %broadcast_select_fusion.4), channel_id=1, source_target_pairs={{0,12},{1,13},{2,14},{3,15},{4,0},{5,1},{6,2},{7,3},{8,4},{9,5},{1... | collective-permute-start | bytes 221192 | tf_op jit(solution)/shard_map/ppermute | solution.py:26
  13.1 0.6 collective-permute-start.4
  13.7 1.0 %collective-permute-start.5 = (bf16[2,6,3,1024]{3,0,2,1:T(2,128)(2,1)S(1)}, bf16[2,6,3,1024]{3,0,2,1:T(2,128)(2,1)S(1)}, u32[]{:S(2)}, u32[]{:S(2)}) collective-permute-start(bf16[2,6,3,1024]{3,0,2,1:T(2,128)(2,1)S(1)} %broadcast_select_fusion.4), channel_id=1, source_target_pairs={{0,4},{1,5},{2,6},{3,7},{4,8},{5,9},{6,10},{7,11},{8,12},{9,13},{1... | collective-permute-start | bytes 221192 | tf_op jit(solution)/shard_map/ppermute | solution.py:26
  14.7 0.6 and_select_fusion.3.shift_ref
  15.2 0.1 copy.9
  15.3 0.6 reshape.41.weight_ref
  15.9 0.0 collective-permute-done.3
  15.9 3.1 %collective-permute-done.4 = bf16[2,6,3,1024]{3,0,2,1:T(2,128)(2,1)S(1)} collective-permute-done((bf16[2,6,3,1024]{3,0,2,1:T(2,128)(2,1)S(1)}, bf16[2,6,3,1024]{3,0,2,1:T(2,128)(2,1)S(1)}, u32[]{:S(2)}, u32[]{:S(2)}) %collective-permute-start.4) | collective-permute-done | bytes 73760 | tf_op jit(solution)/shard_map/ppermute | solution.py:26
  19.0 0.7 collective-permute-done.5
  19.7 0.2 fusion.40
  19.9 0.1 copy.10
  20.0 0.9 reshape.56.rev_ref
  20.9 9.1 %shard_map.55 = (bf16[4608,512]{1,0:T(8,128)(2,1)}, bf16[4608,512]{1,0:T(8,128)(2,1)}) custom-call(s32[36]{0:T(128)} %and_select_fusion.3.shift_ref, f32[18]{0:T(128)} %reshape.41.weight_ref, f32[36,1,1024]{2,1,0:T(1,128)} %reshape.56.rev_ref), custom_call_target="tpu_custom_call" | custom-call | bytes 9437184 | tf_op jit(solution)/shard_map/pallas_call | solution.py:55
  30.0 4.6 %fusion.16 = f32[256,512]{1,0:T(8,128)S(1)} fusion(bf16[18,256,512]{2,1,0:T(8,128)(2,1)} %bitcast.49, bf16[18,1024,256]{2,1,0:T(8,128)(2,1)} %bitcast.35, s32[]{:T(128)S(6)} %select_n.155), kind=kOutput, calls=%fused_computation.16 | convolution fusion | flops 1207959552 | bytes 7602180 | tf_op jit(solution)/shard_map/rpt,rtn->pn/dot_general | solution.py:89
  34.6 0.0 slice-start.2
  34.6 0.0 copy-start
  34.6 2.0 %collective-permute-start.6 = (f32[256,512]{1,0:T(8,128)S(1)}, f32[256,512]{1,0:T(8,128)S(1)}, u32[]{:S(2)}, u32[]{:S(2)}) collective-permute-start(f32[256,512]{1,0:T(8,128)S(1)} %fusion.16), channel_id=1, source_target_pairs={{0,32},{16,48},{32,64},{48,80},{64,96},{80,112},{96,0},{112,16},{1... | collective-permute-start | bytes 1572872 | tf_op jit(solution)/shard_map/ppermute | solution.py:99
  36.6 4.6 %fusion.19 = f32[256,512]{1,0:T(8,128)S(1)} fusion(bf16[18,256,512]{2,1,0:T(8,128)(2,1)} %bitcast.50, bf16[18,1024,256]{2,1,0:T(8,128)(2,1)} %bitcast.36, s32[]{:T(128)S(6)} %select_n.176), kind=kOutput, calls=%fused_computation.17 | convolution fusion | flops 1207959552 | bytes 7602180 | tf_op jit(solution)/shard_map/rpt,rtn->pn/dot_general | solution.py:89
  41.2 0.0 slice-start.4
  41.2 1.4 %fusion.28 = f32[256,512]{1,0:T(8,128)S(1)} fusion(bf16[18,256,512]{2,1,0:T(8,128)(2,1)S(1)} %bitcast.45, bf16[18,1024,256]{2,1,0:T(8,128)(2,1)S(1)} %bitcast.39, s32[]{:T(128)S(6)} %select_n.185), kind=kOutput, calls=%fused_computation.20 | convolution fusion | flops 1207959552 | bytes 7602180 | tf_op jit(solution)/shard_map/rpt,rtn->pn/dot_general | solution.py:89
  42.6 2.4 %collective-permute-start.10 = (f32[256,512]{1,0:T(8,128)S(1)}, f32[256,512]{1,0:T(8,128)S(1)}, u32[]{:S(2)}, u32[]{:S(2)}) collective-permute-start(f32[256,512]{1,0:T(8,128)S(1)} %fusion.28), channel_id=1, source_target_pairs={{0,96},{16,112},{32,0},{48,16},{64,32},{80,48},{96,64},{112,80},{1... | collective-permute-start | bytes 1572872 | tf_op jit(solution)/shard_map/ppermute | solution.py:99
  45.0 3.5 %collective-permute-done.6 = f32[256,512]{1,0:T(8,128)S(1)} collective-permute-done((f32[256,512]{1,0:T(8,128)S(1)}, f32[256,512]{1,0:T(8,128)S(1)}, u32[]{:S(2)}, u32[]{:S(2)}) %collective-permute-start.6) | collective-permute-done | bytes 524320 | tf_op jit(solution)/shard_map/ppermute | solution.py:99
  48.6 0.1 add.205
  48.6 0.1 collective-permute-start.7
  48.8 1.4 %fusion.22 = f32[256,512]{1,0:T(8,128)S(1)} fusion(bf16[18,256,512]{2,1,0:T(8,128)(2,1)S(1)} %bitcast.53, bf16[18,1024,256]{2,1,0:T(8,128)(2,1)S(1)} %bitcast.40, s32[]{:T(128)S(6)} %select_n.178), kind=kOutput, calls=%fused_computation.18 | convolution fusion | flops 1207959552 | bytes 7602180 | tf_op jit(solution)/shard_map/rpt,rtn->pn/dot_general | solution.py:89
  50.1 1.4 %fusion.31 = f32[256,512]{1,0:T(8,128)S(1)} fusion(bf16[18,256,512]{2,1,0:T(8,128)(2,1)S(1)} %bitcast.46, bf16[18,1024,256]{2,1,0:T(8,128)(2,1)S(1)} %bitcast.41, s32[]{:T(128)S(6)} %select_n.187), kind=kOutput, calls=%fused_computation.21 | convolution fusion | flops 1207959552 | bytes 7602180 | tf_op jit(solution)/shard_map/rpt,rtn->pn/dot_general | solution.py:89
  51.5 3.1 %collective-permute-done.10 = f32[256,512]{1,0:T(8,128)S(1)} collective-permute-done((f32[256,512]{1,0:T(8,128)S(1)}, f32[256,512]{1,0:T(8,128)S(1)}, u32[]{:S(2)}, u32[]{:S(2)}) %collective-permute-start.10) | collective-permute-done | bytes 524320 | tf_op jit(solution)/shard_map/ppermute | solution.py:99
  54.6 0.1 add.220
  54.7 3.3 %collective-permute-start.11 = (f32[256,512]{1,0:T(8,128)S(1)}, f32[256,512]{1,0:T(8,128)S(1)}, u32[]{:S(2)}, u32[]{:S(2)}) collective-permute-start(f32[256,512]{1,0:T(8,128)S(1)} %add.220), channel_id=1, source_target_pairs={{0,96},{16,112},{32,0},{48,16},{64,32},{80,48},{96,64},{112,80},{1... | collective-permute-start | bytes 1572872 | tf_op jit(solution)/shard_map/ppermute | solution.py:99
  58.0 2.9 %collective-permute-done.7 = f32[256,512]{1,0:T(8,128)S(1)} collective-permute-done((f32[256,512]{1,0:T(8,128)S(1)}, f32[256,512]{1,0:T(8,128)S(1)}, u32[]{:S(2)}, u32[]{:S(2)}) %collective-permute-start.7) | collective-permute-done | bytes 524320 | tf_op jit(solution)/shard_map/ppermute | solution.py:99
  60.9 0.1 add.208
  60.9 0.1 collective-permute-start.8
  61.0 1.4 %fusion.25 = f32[256,512]{1,0:T(8,128)S(1)} fusion(bf16[18,256,512]{2,1,0:T(8,128)(2,1)S(1)} %bitcast.54, bf16[18,1024,256]{2,1,0:T(8,128)(2,1)S(1)} %bitcast.42, s32[]{:T(128)S(6)} %select_n.180), kind=kOutput, calls=%fused_computation.19 | convolution fusion | flops 1207959552 | bytes 7602180 | tf_op jit(solution)/shard_map/rpt,rtn->pn/dot_general | solution.py:89
  62.4 1.4 %fusion.34 = f32[256,512]{1,0:T(8,128)S(1)} fusion(bf16[18,256,512]{2,1,0:T(8,128)(2,1)S(1)} %bitcast.47, bf16[18,1024,256]{2,1,0:T(8,128)(2,1)S(1)} %bitcast.43, s32[]{:T(128)S(6)} %select_n.189), kind=kOutput, calls=%fused_computation.22 | convolution fusion | flops 1207959552 | bytes 7602180 | tf_op jit(solution)/shard_map/rpt,rtn->pn/dot_general | solution.py:89
  63.8 2.3 %collective-permute-done.11 = f32[256,512]{1,0:T(8,128)S(1)} collective-permute-done((f32[256,512]{1,0:T(8,128)S(1)}, f32[256,512]{1,0:T(8,128)S(1)}, u32[]{:S(2)}, u32[]{:S(2)}) %collective-permute-start.11) | collective-permute-done | bytes 524320 | tf_op jit(solution)/shard_map/ppermute | solution.py:99
  66.1 0.1 add.223
  66.2 3.8 %collective-permute-start.12 = (f32[256,512]{1,0:T(8,128)S(1)}, f32[256,512]{1,0:T(8,128)S(1)}, u32[]{:S(2)}, u32[]{:S(2)}) collective-permute-start(f32[256,512]{1,0:T(8,128)S(1)} %add.223), channel_id=1, source_target_pairs={{0,96},{16,112},{32,0},{48,16},{64,32},{80,48},{96,64},{112,80},{1... | collective-permute-start | bytes 1572872 | tf_op jit(solution)/shard_map/ppermute | solution.py:99
  70.0 2.2 %collective-permute-done.8 = f32[256,512]{1,0:T(8,128)S(1)} collective-permute-done((f32[256,512]{1,0:T(8,128)S(1)}, f32[256,512]{1,0:T(8,128)S(1)}, u32[]{:S(2)}, u32[]{:S(2)}) %collective-permute-start.8) | collective-permute-done | bytes 524320 | tf_op jit(solution)/shard_map/ppermute | solution.py:99
  72.2 0.1 add.211
  72.4 2.4 %collective-permute-start.9 = (f32[128,512]{1,0:T(8,128)S(1)}, f32[128,512]{1,0:T(8,128)S(1)}, u32[]{:S(2)}, u32[]{:S(2)}) collective-permute-start(f32[128,512]{1,0:T(8,128)S(1)} %get-tuple-element.13), channel_id=1, source_target_pairs={{0,16},{16,0},{32,48},{48,32},{64,80},{80,64},{96,112},{112,96},{1... | collective-permute-start | bytes 786440 | tf_op jit(solution)/shard_map/ppermute | solution.py:104
  74.8 1.4 %fusion.37 = f32[256,512]{1,0:T(8,128)S(1)} fusion(bf16[18,256,512]{2,1,0:T(8,128)(2,1)S(1)} %bitcast.48, bf16[18,1024,256]{2,1,0:T(8,128)(2,1)S(1)} %bitcast.44, s32[]{:T(128)S(6)} %select_n.191), kind=kOutput, calls=%fused_computation.23 | convolution fusion | flops 1207959552 | bytes 7602180 | tf_op jit(solution)/shard_map/rpt,rtn->pn/dot_general | solution.py:89
  76.2 1.2 %collective-permute-done.12 = f32[256,512]{1,0:T(8,128)S(1)} collective-permute-done((f32[256,512]{1,0:T(8,128)S(1)}, f32[256,512]{1,0:T(8,128)S(1)}, u32[]{:S(2)}, u32[]{:S(2)}) %collective-permute-start.12) | collective-permute-done | bytes 524320 | tf_op jit(solution)/shard_map/ppermute | solution.py:99
  77.4 0.1 add.226
  77.5 2.6 %collective-permute-start.13 = (f32[128,512]{1,0:T(8,128)S(1)}, f32[128,512]{1,0:T(8,128)S(1)}, u32[]{:S(2)}, u32[]{:S(2)}) collective-permute-start(f32[128,512]{1,0:T(8,128)S(1)} %get-tuple-element.15), channel_id=1, source_target_pairs={{0,16},{16,0},{32,48},{48,32},{64,80},{80,64},{96,112},{112,96},{1... | collective-permute-start | bytes 786440 | tf_op jit(solution)/shard_map/ppermute | solution.py:104
  80.1 0.4 rev.18
  80.4 0.4 rev.20
  80.8 1.5 %collective-permute-done.9 = f32[128,512]{1,0:T(8,128)S(1)} collective-permute-done((f32[128,512]{1,0:T(8,128)S(1)}, f32[128,512]{1,0:T(8,128)S(1)}, u32[]{:S(2)}, u32[]{:S(2)}) %collective-permute-start.9) | collective-permute-done | bytes 262176 | tf_op jit(solution)/shard_map/ppermute | solution.py:104
  82.3 0.4 rev.19
  82.8 2.7 %collective-permute-done.13 = f32[128,512]{1,0:T(8,128)S(1)} collective-permute-done((f32[128,512]{1,0:T(8,128)S(1)}, f32[128,512]{1,0:T(8,128)S(1)}, u32[]{:S(2)}, u32[]{:S(2)}) %collective-permute-start.13) | collective-permute-done | bytes 262176 | tf_op jit(solution)/shard_map/ppermute | solution.py:104
  85.5 0.4 rev.21
  85.9 1.2 %copy.12 = f32[128,2,512]{2,1,0:T(2,128)} copy(f32[128,2,512]{2,0,1:T(8,128)S(1)} %pad_maximum_fusion) | data formatting | bytes 1048576 | tf_op jit(solution)/shard_map/stack | solution.py:106
  (18 shorter events, 0.3 us)
Async XLA Ops:
  3.4 4.1 %collective-permute-start = (bf16[2,6,3,1024]{3,0,2,1:T(2,128)(2,1)S(1)}, bf16[2,6,3,1024]{3,0,2,1:T(2,128)(2,1)S(1)}, u32[]{:S(2)}, u32[]{:S(2)}) collective-permute-start(bf16[2,6,3,1024]{3,0,2,1:T(2,128)(2,1)S(1)} %rev.17), channel_id=1, source_target_pairs={{0,3},{1,0},{2,1},{3,2},{4,7},{5,4},{6,5},{7,6},{8,11},{9,8},{10,9... | collective-permute-start | bytes 221192 | tf_op jit(solution)/shard_map/ppermute | solution.py:26
  4.5 5.2 %collective-permute-start.1 = (bf16[2,6,3,1024]{3,0,2,1:T(2,128)(2,1)S(1)}, bf16[2,6,3,1024]{3,0,2,1:T(2,128)(2,1)S(1)}, u32[]{:S(2)}, u32[]{:S(2)}) collective-permute-start(bf16[2,6,3,1024]{3,0,2,1:T(2,128)(2,1)S(1)} %rev.17), channel_id=1, source_target_pairs={{0,2},{1,3},{2,0},{3,1},{4,6},{5,7},{6,4},{7,5},{8,10},{9,11},{10,... | collective-permute-start | bytes 221192 | tf_op jit(solution)/shard_map/ppermute | solution.py:26
  5.1 4.6 %collective-permute-start.2 = (bf16[2,6,3,1024]{3,0,2,1:T(2,128)(2,1)S(1)}, bf16[2,6,3,1024]{3,0,2,1:T(2,128)(2,1)S(1)}, u32[]{:S(2)}, u32[]{:S(2)}) collective-permute-start(bf16[2,6,3,1024]{3,0,2,1:T(2,128)(2,1)S(1)} %rev.17), channel_id=1, source_target_pairs={{0,1},{1,2},{2,3},{3,0},{4,5},{5,6},{6,7},{7,4},{8,9},{9,10},{10,1... | collective-permute-start | bytes 221192 | tf_op jit(solution)/shard_map/ppermute | solution.py:26
  10.0 5.9 %collective-permute-start.3 = (bf16[2,6,3,1024]{3,0,2,1:T(2,128)(2,1)S(1)}, bf16[2,6,3,1024]{3,0,2,1:T(2,128)(2,1)S(1)}, u32[]{:S(2)}, u32[]{:S(2)}) collective-permute-start(bf16[2,6,3,1024]{3,0,2,1:T(2,128)(2,1)S(1)} %broadcast_select_fusion.4), channel_id=1, source_target_pairs={{0,12},{1,13},{2,14},{3,15},{4,0},{5,1},{6,2},{7,3},{8,4},{9,5},{1... | collective-permute-start | bytes 221192 | tf_op jit(solution)/shard_map/ppermute | solution.py:26
  13.1 5.9 %collective-permute-start.4 = (bf16[2,6,3,1024]{3,0,2,1:T(2,128)(2,1)S(1)}, bf16[2,6,3,1024]{3,0,2,1:T(2,128)(2,1)S(1)}, u32[]{:S(2)}, u32[]{:S(2)}) collective-permute-start(bf16[2,6,3,1024]{3,0,2,1:T(2,128)(2,1)S(1)} %broadcast_select_fusion.4), channel_id=1, source_target_pairs={{0,8},{1,9},{2,10},{3,11},{4,12},{5,13},{6,14},{7,15},{8,0},{9,1},... | collective-permute-start | bytes 221192 | tf_op jit(solution)/shard_map/ppermute | solution.py:26
  13.7 6.0 %collective-permute-start.5 = (bf16[2,6,3,1024]{3,0,2,1:T(2,128)(2,1)S(1)}, bf16[2,6,3,1024]{3,0,2,1:T(2,128)(2,1)S(1)}, u32[]{:S(2)}, u32[]{:S(2)}) collective-permute-start(bf16[2,6,3,1024]{3,0,2,1:T(2,128)(2,1)S(1)} %broadcast_select_fusion.4), channel_id=1, source_target_pairs={{0,4},{1,5},{2,6},{3,7},{4,8},{5,9},{6,10},{7,11},{8,12},{9,13},{1... | collective-permute-start | bytes 221192 | tf_op jit(solution)/shard_map/ppermute | solution.py:26
  30.0 11.2 %slice-start = ((s8[9437184]{0:T(1024)(128)(4,1)}), s8[4194304]{0:T(1024)(128)(4,1)S(1)}, s32[]{:S(2)}) async-start(s8[9437184]{0:T(1024)(128)(4,1)} %bitcast.37), calls=%async_computation | async-start | bytes 8388608
  30.0 11.2 %slice-start.1 = ((s8[9437184]{0:T(1024)(128)(4,1)}), s8[4194304]{0:T(1024)(128)(4,1)S(1)}, s32[]{:S(2)}) async-start(s8[9437184]{0:T(1024)(128)(4,1)} %bitcast.37), calls=%async_computation.1 | async-start | bytes 8388608
  34.6 6.6 %slice-start.2 = ((s8[9437184]{0:T(1024)(128)(4,1)}), s8[1048576]{0:T(1024)(128)(4,1)S(1)}, s32[]{:S(2)}) async-start(s8[9437184]{0:T(1024)(128)(4,1)} %bitcast.37), calls=%async_computation.2 | async-start | bytes 2097152
  34.6 6.6 %copy-start = (bf16[4608,512]{1,0:T(8,128)(2,1)S(1)}, bf16[4608,512]{1,0:T(8,128)(2,1)}, u32[]{:S(2)}) copy-start(bf16[4608,512]{1,0:T(8,128)(2,1)} %get-tuple-element.8) | copy-start | bytes 14155780
  34.6 13.9 %collective-permute-start.6 = (f32[256,512]{1,0:T(8,128)S(1)}, f32[256,512]{1,0:T(8,128)S(1)}, u32[]{:S(2)}, u32[]{:S(2)}) collective-permute-start(f32[256,512]{1,0:T(8,128)S(1)} %fusion.16), channel_id=1, source_target_pairs={{0,32},{16,48},{32,64},{48,80},{64,96},{80,112},{96,0},{112,16},{1... | collective-permute-start | bytes 1572872 | tf_op jit(solution)/shard_map/ppermute | solution.py:99
  36.6 12.1 %slice-start.3 = ((s8[4718592]{0:T(1024)(128)(4,1)}), s8[4194304]{0:T(1024)(128)(4,1)S(1)}, s32[]{:S(2)}) async-start(s8[4718592]{0:T(1024)(128)(4,1)} %bitcast.51), calls=%async_computation.3 | async-start | bytes 8388608
  41.2 7.5 %slice-start.4 = ((s8[4718592]{0:T(1024)(128)(4,1)}), s8[524288]{0:T(1024)(128)(4,1)S(1)}, s32[]{:S(2)}) async-start(s8[4718592]{0:T(1024)(128)(4,1)} %bitcast.51), calls=%async_computation.4 | async-start | bytes 1048576
  42.6 12.0 %collective-permute-start.10 = (f32[256,512]{1,0:T(8,128)S(1)}, f32[256,512]{1,0:T(8,128)S(1)}, u32[]{:S(2)}, u32[]{:S(2)}) collective-permute-start(f32[256,512]{1,0:T(8,128)S(1)} %fusion.28), channel_id=1, source_target_pairs={{0,96},{16,112},{32,0},{48,16},{64,32},{80,48},{96,64},{112,80},{1... | collective-permute-start | bytes 1572872 | tf_op jit(solution)/shard_map/ppermute | solution.py:99
  48.6 12.2 %collective-permute-start.7 = (f32[256,512]{1,0:T(8,128)S(1)}, f32[256,512]{1,0:T(8,128)S(1)}, u32[]{:S(2)}, u32[]{:S(2)}) collective-permute-start(f32[256,512]{1,0:T(8,128)S(1)} %add.205), channel_id=1, source_target_pairs={{0,32},{16,48},{32,64},{48,80},{64,96},{80,112},{96,0},{112,16},{1... | collective-permute-start | bytes 1572872 | tf_op jit(solution)/shard_map/ppermute | solution.py:99
  54.7 11.5 %collective-permute-start.11 = (f32[256,512]{1,0:T(8,128)S(1)}, f32[256,512]{1,0:T(8,128)S(1)}, u32[]{:S(2)}, u32[]{:S(2)}) collective-permute-start(f32[256,512]{1,0:T(8,128)S(1)} %add.220), channel_id=1, source_target_pairs={{0,96},{16,112},{32,0},{48,16},{64,32},{80,48},{96,64},{112,80},{1... | collective-permute-start | bytes 1572872 | tf_op jit(solution)/shard_map/ppermute | solution.py:99
  60.9 11.3 %collective-permute-start.8 = (f32[256,512]{1,0:T(8,128)S(1)}, f32[256,512]{1,0:T(8,128)S(1)}, u32[]{:S(2)}, u32[]{:S(2)}) collective-permute-start(f32[256,512]{1,0:T(8,128)S(1)} %add.208), channel_id=1, source_target_pairs={{0,32},{16,48},{32,64},{48,80},{64,96},{80,112},{96,0},{112,16},{1... | collective-permute-start | bytes 1572872 | tf_op jit(solution)/shard_map/ppermute | solution.py:99
  66.2 11.2 %collective-permute-start.12 = (f32[256,512]{1,0:T(8,128)S(1)}, f32[256,512]{1,0:T(8,128)S(1)}, u32[]{:S(2)}, u32[]{:S(2)}) collective-permute-start(f32[256,512]{1,0:T(8,128)S(1)} %add.223), channel_id=1, source_target_pairs={{0,96},{16,112},{32,0},{48,16},{64,32},{80,48},{96,64},{112,80},{1... | collective-permute-start | bytes 1572872 | tf_op jit(solution)/shard_map/ppermute | solution.py:99
  72.4 10.0 %collective-permute-start.9 = (f32[128,512]{1,0:T(8,128)S(1)}, f32[128,512]{1,0:T(8,128)S(1)}, u32[]{:S(2)}, u32[]{:S(2)}) collective-permute-start(f32[128,512]{1,0:T(8,128)S(1)} %get-tuple-element.13), channel_id=1, source_target_pairs={{0,16},{16,0},{32,48},{48,32},{64,80},{80,64},{96,112},{112,96},{1... | collective-permute-start | bytes 786440 | tf_op jit(solution)/shard_map/ppermute | solution.py:104
  77.5 8.0 %collective-permute-start.13 = (f32[128,512]{1,0:T(8,128)S(1)}, f32[128,512]{1,0:T(8,128)S(1)}, u32[]{:S(2)}, u32[]{:S(2)}) collective-permute-start(f32[128,512]{1,0:T(8,128)S(1)} %get-tuple-element.15), channel_id=1, source_target_pairs={{0,16},{16,0},{32,48},{48,32},{64,80},{80,64},{96,112},{112,96},{1... | collective-permute-start | bytes 786440 | tf_op jit(solution)/shard_map/ppermute | solution.py:104

commit v10 on v8

--- a/solution.py
+++ b/solution.py
@@ -10,6 +10,7 @@
 SAMPLES = 1024
 EV = 2
 WIDE = LAGS + NT
+HALF = LAGS // 2
 
 
 def from_owners(x, axis, roots, radix=4):
@@ -35,14 +36,17 @@
     rows = weight_ref.shape[0]
 
     def body(r, carry):
-        for e, out_ref in enumerate(out_refs):
+        for e in range(len(out_refs) // 2):
+            out_ref = out_refs[2 * e : 2 * e + 2]
             row = rev_ref[e * rows + r]
             row = pltpu.roll(row, shift_ref[e * rows + r], 1)
             row = (row * weight_ref[r]).astype(jnp.bfloat16).astype(jnp.float32)
             row = jnp.concatenate([row[:, :LAGS], row[:, SAMPLES - NT :]], axis=1)
             wide = jnp.broadcast_to(row, (NT, WIDE))
             band = pltpu.roll(wide, 0, 1, stride=1, stride_axis=0)
-            out_ref[pl.ds(pl.multiple_of(r * NT, NT), NT), :] = band[:, :LAGS].astype(out_ref.dtype)
+            at = pl.ds(pl.multiple_of(r * NT, NT), NT)
+            for h, ref in enumerate(out_ref):
+                ref[at, :] = band[:, h * HALF : (h + 1) * HALF].astype(ref.dtype)
         return carry
 
     lax.fori_loop(0, rows, body, 0)
@@ -51,7 +55,7 @@
 def toeplitz_reversed(rev, shifts, weights):
     rows = weights.shape[0]
     ev = rev.shape[0] // rows
-    band = jax.ShapeDtypeStruct((rows * NT, LAGS), jnp.bfloat16)
+    band = jax.ShapeDtypeStruct((rows * NT, HALF), jnp.bfloat16)
     return pl.pallas_call(
         _toeplitz_kernel,
         in_specs=[
@@ -59,8 +63,8 @@
             pl.BlockSpec(memory_space=pltpu.SMEM),
             pl.BlockSpec(memory_space=pltpu.VMEM),
         ],
-        out_specs=[pl.BlockSpec(memory_space=pltpu.VMEM)] * ev,
-        out_shape=[band] * ev,
+        out_specs=[pl.BlockSpec(memory_space=pltpu.VMEM)] * (2 * ev),
+        out_shape=[band] * (2 * ev),
         cost_estimate=pl.CostEstimate(flops=0, transcendentals=0, bytes_accessed=ev * rows * NT * LAGS * 2),
     )(shifts, weights, rev)
 
@@ -84,24 +88,37 @@
     quarter = point_rows // zs
     block = quarter // xs
 
-    def piece(band, c):
-        g = lax.dynamic_slice_in_dim(green_t, c * quarter, quarter, 1)
-        return jnp.einsum("rpt,rtn->pn", g, band.reshape(rows, NT, LAGS), preferred_element_type=jnp.float32)
+    def piece(band, start, count):
+        g = lax.dynamic_slice_in_dim(green_t, start, count, 1)
+        return jnp.einsum("rpt,rtn->pn", g, band.reshape(rows, NT, -1), preferred_element_type=jnp.float32)
 
     def ring_perm(step):
         return [(i, ((i // xs + step) % zs) * xs + i % xs) for i in range(size)]
 
+    swap = [(i, i ^ 1) for i in range(size)]
+
     outs = []
     for e, step in zip(range(EV), (1, zs - 1)):
-        band = bands[e]
-        acc = piece(band, (z + zs - step) % zs)
+        first, second = bands[2 * e], bands[2 * e + 1]
+
+        whole = piece(second, 0, point_rows).reshape(zs, xs, block, HALF)
+        theirs = lax.dynamic_index_in_dim(whole, 1 - xh, 1, keepdims=False)
+        mine = lax.dynamic_index_in_dim(whole, xh, 1, keepdims=False)
+        paired = mine + lax.ppermute(theirs, "sens", swap)
+        acc_x = lax.dynamic_index_in_dim(paired, (z + zs - step) % zs, 0, keepdims=False)
+
+        acc_z = piece(first, ((z + zs - step) % zs) * quarter, quarter)
         for k in range(zs - 1):
-            got = lax.ppermute(acc, "sens", ring_perm(step))
-            acc = got + piece(band, (z + 4 * zs - step * (k + 2)) % zs)
-        theirs = lax.dynamic_slice_in_dim(acc, (1 - xh) * block, block, 0)
-        kept = lax.dynamic_slice_in_dim(acc, xh * block, block, 0)
-        got = lax.ppermute(theirs, "sens", [(i, i ^ 1) for i in range(size)])
-        outs.append(jnp.flip(kept, axis=-1) + jnp.flip(got, axis=-1))
+            c = (z + 4 * zs - step * (k + 2)) % zs
+            got_z = lax.ppermute(acc_z, "sens", ring_perm(step))
+            part = lax.optimization_barrier(piece(first, c * quarter, quarter))
+            acc_z = got_z + part
+            got_x = lax.ppermute(acc_x, "sens", ring_perm(step))
+            acc_x = got_x + lax.dynamic_index_in_dim(paired, c, 0, keepdims=False)
+        theirs = lax.dynamic_slice_in_dim(acc_z, (1 - xh) * block, block, 0)
+        kept = lax.dynamic_slice_in_dim(acc_z, xh * block, block, 0)
+        acc_z = kept + lax.ppermute(theirs, "sens", swap)
+        outs.append(jnp.flip(jnp.concatenate([acc_z, acc_x], axis=1), axis=-1))
     return jnp.stack(outs, axis=1)
 
 

time: 90.5 us -> 121 us (1.34)
  matrix products: 20.3 us -> 34 us
  waiting for transfers between devices: 27.5 us -> 15 us
  starting transfers between devices: 21.4 us -> 33.4 us
  local copies, waits for them, and re-layouts: 7.99 us -> 18.9 us
  other arithmetic: 3.57 us -> 9.34 us
    dot_general x8 -> x10, matrix products: 20.3 us -> 34 us  [piece(): jnp.einsum('rpt,rtn->pn', g, band.reshape(rows, NT, -1), preferred_elemen...]
    ppermute x8 -> x16, waiting for transfers between devices: 21.5 us -> 8.98 us  [the longest x6 7.19 us: local(): got_x = lax.ppermute(acc_x, 'sens', ring_perm(step))]
    ppermute x8 -> x16, starting transfers between devices: 14.8 us -> 26.8 us  [the longest x6 11.3 us: local(): got_z = lax.ppermute(acc_z, 'sens', ring_perm(step))]
    dynamic_slice x2 -> x7, local copies, waits for them, and re-layouts: 0.09 us -> 8.75 us  [the longest x3 5.61 us: local(): mine = lax.dynamic_index_in_dim(whole, xh, 1, keepdims=False)]
    add x4 -> x16, other arithmetic: 0.32 us -> 6.2 us  [the longest x6 3.84 us: local(): acc_z = got_z + part]
    reshape x0 -> x2, local copies, waits for them, and re-layouts: none -> 2.74 us  [local(): whole = piece(second, 0, point_rows).reshape(zs, xs, block, HALF)]
  transfers between devices with their start and end apart: 14 -> 22, of which waited for: 8 -> 7; matrix products, arithmetic and copies ran while one was open for 23% -> 43% of each run, Pallas kernels for 0% -> 0%
where the time goes in v10:
time: 121 us; the launch traced here: 120 us
  matrix products  34 us (28%)
  starting transfers between devices  33.4 us (28%)
  local copies, waits for them, and re-layouts  18.9 us (16%)
  waiting for transfers between devices  15 us (12%)
  other arithmetic  9.34 us (8%)
  Pallas kernels  9.03 us (7%)
    dot_general x10, matrix products, piece(): jnp.einsum('rpt,rtn->pn', g, band.reshape(rows, NT, -1), preferred_elemen...  34 us
    ppermute x6, starting transfers between devices, local(): got_z = lax.ppermute(acc_z, 'sens', ring_perm(step))  11.3 us
    pallas_call x1, Pallas kernels, toeplitz_reversed(): pl.pallas_call(_toeplitz_kernel, in_specs=[pl.BlockSpec(memory_space=pltp...  9.03 us
    ppermute x6, starting transfers between devices, local(): got_x = lax.ppermute(acc_x, 'sens', ring_perm(step))  8.31 us
    ppermute x6, waiting for transfers between devices, local(): got_x = lax.ppermute(acc_x, 'sens', ring_perm(step))  7.19 us
    ppermute x6, starting transfers between devices, from_owners(): got = lax.ppermute(x, axis, perm)  6.58 us
    ppermute x6, waiting for transfers between devices, from_owners(): got = lax.ppermute(x, axis, perm)  6.05 us
    dynamic_slice x3, local copies, waits for them, and re-layouts, local(): mine = lax.dynamic_index_in_dim(whole, xh, 1, keepdims=False)  5.61 us
  transfers between devices with their start and end apart: 22, of which 7 were waited for; matrix products, arithmetic and copies ran while one was open for 43% of the time, Pallas kernels for 0%

profile of v10, /device:TPU:0, one launch (start us, length us, event | category | flops | bytes accessed | tf_op | source)
XLA Modules:
  0.0 120.0 jit_solution(18057864959184102018)
XLA Ops:
  0.0 3.4 %rev.11 = bf16[2,6,3,1024]{3,0,2,1:T(2,128)(2,1)S(1)} reverse(bf16[2,6,3,1024]{3,0,2,1:T(2,128)(2,1)} %bitcast.92), dimensions={3} | reverse | bytes 147456 | tf_op jit(solution)/shard_map/jit(_flip)/rev | solution.py:76
  3.4 1.1 collective-permute-start
  4.5 0.7 collective-permute-start.1
  5.1 0.2 collective-permute-start.2
  5.3 0.7 broadcast_add_fusion
  6.0 0.7 multiply_exponential_fusion
  6.7 0.7 broadcast_compare_fusion
  7.4 0.1 sub.72
  7.5 2.2 %collective-permute-done.1 = bf16[2,6,3,1024]{3,0,2,1:T(2,128)(2,1)S(1)} collective-permute-done((bf16[2,6,3,1024]{3,0,2,1:T(2,128)(2,1)S(1)}, bf16[2,6,3,1024]{3,0,2,1:T(2,128)(2,1)S(1)}, u32[]{:S(2)}, u32[]{:S(2)}) %collective-permute-start.1) | collective-permute-done | bytes 73760 | tf_op jit(solution)/shard_map/ppermute | solution.py:27
  9.7 0.2 broadcast_select_fusion.4
  10.0 3.1 %collective-permute-start.3 = (bf16[2,6,3,1024]{3,0,2,1:T(2,128)(2,1)S(1)}, bf16[2,6,3,1024]{3,0,2,1:T(2,128)(2,1)S(1)}, u32[]{:S(2)}, u32[]{:S(2)}) collective-permute-start(bf16[2,6,3,1024]{3,0,2,1:T(2,128)(2,1)S(1)} %broadcast_select_fusion.4), channel_id=1, source_target_pairs={{0,12},{1,13},{2,14},{3,15},{4,0},{5,1},{6,2},{7,3},{8,4},{9,5},{1... | collective-permute-start | bytes 221192 | tf_op jit(solution)/shard_map/ppermute | solution.py:27
  13.1 0.6 collective-permute-start.4
  13.7 1.0 collective-permute-start.5
  14.7 0.5 and_select_fusion.3.shift_ref
  15.2 0.1 copy.15
  15.3 0.6 reshape.53.weight_ref
  15.9 3.1 %collective-permute-done.4 = bf16[2,6,3,1024]{3,0,2,1:T(2,128)(2,1)S(1)} collective-permute-done((bf16[2,6,3,1024]{3,0,2,1:T(2,128)(2,1)S(1)}, bf16[2,6,3,1024]{3,0,2,1:T(2,128)(2,1)S(1)}, u32[]{:S(2)}, u32[]{:S(2)}) %collective-permute-start.4) | collective-permute-done | bytes 73760 | tf_op jit(solution)/shard_map/ppermute | solution.py:27
  19.0 0.7 collective-permute-done.5
  19.7 0.2 fusion.40
  20.0 0.9 reshape.74.rev_ref
  20.9 9.0 %shard_map.55 = (bf16[4608,256]{1,0:T(8,128)(2,1)}, bf16[4608,256]{1,0:T(8,128)(2,1)}, bf16[4608,256]{1,0:T(8,128)(2,1)}, bf16[4608,256]{1,0:T(8,128)(2,1)}) custom-call(s32[36]{0:T(128)} %and_select_fusion.3.shift_ref, f32[18]{0:T(128)} %reshape.53.weight_ref, f32[36,1,1024]{2,1,0:T(1,128)} %reshape.74.rev_ref), custom_call_target="tpu_custom_call" | custom-call | bytes 9437184 | tf_op jit(solution)/shard_map/pallas_call | solution.py:59
  29.9 4.0 %fusion.16 = f32[256,256]{1,0:T(8,128)} fusion(bf16[18,256,256]{2,1,0:T(8,128)(2,1)} %bitcast.86, bf16[18,1024,256]{2,1,0:T(8,128)(2,1)} %bitcast.72, s32[]{:T(128)S(6)} %select_n.193), kind=kOutput, calls=%fused_computation.18 | convolution fusion | flops 603979776 | bytes 4980740 | tf_op jit(solution)/shard_map/rpt,rtn->pn/dot_general | solution.py:93
  33.9 1.9 %collective-permute-start.6 = (f32[256,256]{1,0:T(8,128)}, f32[256,256]{1,0:T(8,128)}, u32[]{:S(2)}, u32[]{:S(2)}) collective-permute-start(f32[256,256]{1,0:T(8,128)} %fusion.16), channel_id=1, source_target_pairs={{0,32},{16,48},{32,64},{48,80},{64,96},{80,112},{96,0},{112,16},{1... | collective-permute-start | bytes 786440 | tf_op jit(solution)/shard_map/ppermute | solution.py:113
  35.8 3.9 %fusion.19 = f32[256,256]{1,0:T(8,128)} fusion(bf16[18,256,256]{2,1,0:T(8,128)(2,1)} %bitcast.87, bf16[18,1024,256]{2,1,0:T(8,128)(2,1)} %bitcast.73, s32[]{:T(128)S(6)} %select_n.214), kind=kOutput, calls=%fused_computation.19 | convolution fusion | flops 603979776 | bytes 4980740 | tf_op jit(solution)/shard_map/rpt,rtn->pn/dot_general | solution.py:93
  39.7 3.3 %fusion.22 = f32[256,256]{1,0:T(8,128)} fusion(bf16[18,256,256]{2,1,0:T(8,128)(2,1)} %bitcast.88, bf16[18,1024,256]{2,1,0:T(8,128)(2,1)S(1)} %bitcast.79, s32[]{:T(128)S(6)} %select_n.216), kind=kOutput, calls=%fused_computation.20 | convolution fusion | flops 603979776 | bytes 4980740 | tf_op jit(solution)/shard_map/rpt,rtn->pn/dot_general | solution.py:93
  43.0 1.5 %fusion.25 = f32[256,256]{1,0:T(8,128)} fusion(bf16[18,256,256]{2,1,0:T(8,128)(2,1)S(1)} %bitcast.89, bf16[18,1024,256]{2,1,0:T(8,128)(2,1)S(1)} %bitcast.80, s32[]{:T(128)S(6)} %select_n.218), kind=kOutput, calls=%fused_computation.21 | convolution fusion | flops 603979776 | bytes 4980740 | tf_op jit(solution)/shard_map/rpt,rtn->pn/dot_general | solution.py:93
  44.5 0.2 copy-done.11
  44.7 2.7 %convolution_bitcast_fusion.1 = f32[1024,256]{0,1:T(8,128)S(1)} fusion(bf16[18,256,256]{2,1,0:T(8,128)(2,1)S(1)} %bitcast.94, bf16[18,1024,256]{2,1,0:T(8,128)(2,1)S(1)} %bitcast.81), kind=kOutput, calls=%fused_computation.17 | convolution fusion | flops 2415919104 | bytes 12845056 | tf_op jit(solution)/shard_map/rpt,rtn->pn/dot_general | solution.py:93
  47.3 0.9 reshape.58
  48.2 6.0 %convolution_bitcast_fusion = f32[1024,256]{0,1:T(8,128)S(1)} fusion(bf16[18,256,256]{2,1,0:T(8,128)(2,1)} %bitcast.93, bf16[18,1024,256]{2,1,0:T(8,128)(2,1)} %bitcast.74), kind=kOutput, calls=%fused_computation.16 | convolution fusion | flops 2415919104 | bytes 12845056 | tf_op jit(solution)/shard_map/rpt,rtn->pn/dot_general | solution.py:93
  54.3 1.9 %reshape.61 = f32[4,2,128,256]{2,1,0,3:T(2,128)} reshape(f32[1024,256]{0,1:T(8,128)S(1)} %convolution_bitcast_fusion) | data formatting | bytes 2097152 | tf_op jit(solution)/shard_map/reshape | solution.py:104
  56.1 4.6 %constant_dynamic-slice_fusion.1 = (f32[4,1,128,256]{2,1,0,3:T(1,128)}, f32[4,1,128,256]{2,1,0,3:T(1,128)}, f32[4,1,128,256]{2,1,0,3:T(1,128)}, f32[4,1,128,256]{2,1,0,3:T(1,128)}) fusion(f32[4,2,128,256]{2,1,0,3:T(2,128)} %reshape.61, s32[]{:T(128)S(6)} %select_n.222, s32[]{:T(128)S(6)} %select_n.223, f32[4,2,128,256]{2,1,0,3:T(2,128)S(1)} %reshape.58), kind=kLoop, calls=%fused_computation.49 | loop fusion | bytes 4194312 | tf_op jit(solution)/shard_map/jit(dynamic_index_in_dim)/dynamic_slice | solution.py:106
  60.8 1.9 %copy.20 = f32[4,1,128,256]{3,2,0,1:T(8,128)} copy(f32[4,1,128,256]{2,1,0,3:T(1,128)} %get-tuple-element.27) | data formatting | bytes 1048576 | tf_op jit(solution)/shard_map/jit(dynamic_index_in_dim)/dynamic_slice | solution.py:105
  62.7 3.0 %collective-permute-start.10 = (f32[4,128,256]{2,1,0:T(8,128)}, f32[4,128,256]{2,1,0:T(8,128)}, u32[]{:S(2)}, u32[]{:S(2)}) collective-permute-start(f32[4,128,256]{2,1,0:T(8,128)} %bitcast.13), channel_id=1, source_target_pairs={{0,16},{16,0},{32,48},{48,32},{64,80},{80,64},{96,112},{112,96},{1... | collective-permute-start | bytes 1572872 | tf_op jit(solution)/shard_map/ppermute | solution.py:107
  65.7 3.1 %fusion.28 = f32[256,256]{1,0:T(8,128)} fusion(bf16[18,256,256]{2,1,0:T(8,128)(2,1)S(1)} %bitcast.82, bf16[18,1024,256]{2,1,0:T(8,128)(2,1)} %bitcast.75, s32[]{:T(128)S(6)} %select_n.229), kind=kOutput, calls=%fused_computation.22 | convolution fusion | flops 603979776 | bytes 4980740 | tf_op jit(solution)/shard_map/rpt,rtn->pn/dot_general | solution.py:93
  68.8 2.3 %collective-permute-start.14 = (f32[256,256]{1,0:T(8,128)}, f32[256,256]{1,0:T(8,128)}, u32[]{:S(2)}, u32[]{:S(2)}) collective-permute-start(f32[256,256]{1,0:T(8,128)} %fusion.28), channel_id=1, source_target_pairs={{0,96},{16,112},{32,0},{48,16},{64,32},{80,48},{96,64},{112,80},{1... | collective-permute-start | bytes 786440 | tf_op jit(solution)/shard_map/ppermute | solution.py:113
  71.2 3.2 %fusion.31 = f32[256,256]{1,0:T(8,128)} fusion(bf16[18,256,256]{2,1,0:T(8,128)(2,1)S(1)} %bitcast.83, bf16[18,1024,256]{2,1,0:T(8,128)(2,1)} %bitcast.76, s32[]{:T(128)S(6)} %select_n.231), kind=kOutput, calls=%fused_computation.23 | convolution fusion | flops 603979776 | bytes 4980740 | tf_op jit(solution)/shard_map/rpt,rtn->pn/dot_general | solution.py:93
  74.3 1.2 copy.23
  75.5 0.5 collective-permute-start.18
  76.0 3.1 %fusion.34 = f32[256,256]{1,0:T(8,128)} fusion(bf16[18,256,256]{2,1,0:T(8,128)(2,1)S(1)} %bitcast.84, bf16[18,1024,256]{2,1,0:T(8,128)(2,1)} %bitcast.77, s32[]{:T(128)S(6)} %select_n.233), kind=kOutput, calls=%fused_computation.24 | convolution fusion | flops 603979776 | bytes 4980740 | tf_op jit(solution)/shard_map/rpt,rtn->pn/dot_general | solution.py:93
  79.2 1.7 %add.268 = f32[256,256]{1,0:T(8,128)} add(f32[256,256]{1,0:T(8,128)} %collective-permute-done.6, f32[256,256]{1,0:T(8,128)S(1)} %copy-done.10) | non-fusion elementwise | flops 65536 | bytes 786432 | tf_op jit(solution)/shard_map/add | solution.py:115
  80.9 3.2 %fusion.37 = f32[256,256]{1,0:T(8,128)} fusion(bf16[18,256,256]{2,1,0:T(8,128)(2,1)S(1)} %bitcast.85, bf16[18,1024,256]{2,1,0:T(8,128)(2,1)} %bitcast.78, s32[]{:T(128)S(6)} %select_n.235), kind=kOutput, calls=%fused_computation.25 | convolution fusion | flops 603979776 | bytes 4980740 | tf_op jit(solution)/shard_map/rpt,rtn->pn/dot_general | solution.py:93
  84.1 0.5 copy.19
  84.6 0.5 copy.22
  85.1 1.1 add.293
  86.2 3.2 %collective-permute-start.15 = (f32[256,256]{1,0:T(8,128)S(1)}, f32[256,256]{1,0:T(8,128)S(1)}, u32[]{:S(2)}, u32[]{:S(2)}) collective-permute-start(f32[256,256]{1,0:T(8,128)S(1)} %add.293), channel_id=1, source_target_pairs={{0,96},{16,112},{32,0},{48,16},{64,32},{80,48},{96,64},{112,80},{1... | collective-permute-start | bytes 786440 | tf_op jit(solution)/shard_map/ppermute | solution.py:113
  89.4 1.0 add.271
  90.5 1.1 bitcast_add_fusion.1
  91.6 0.5 collective-permute-start.11
  92.1 1.7 %collective-permute-done.15 = f32[256,256]{1,0:T(8,128)S(1)} collective-permute-done((f32[256,256]{1,0:T(8,128)S(1)}, f32[256,256]{1,0:T(8,128)S(1)}, u32[]{:S(2)}, u32[]{:S(2)}) %collective-permute-start.15) | collective-permute-done | bytes 262176 | tf_op jit(solution)/shard_map/ppermute | solution.py:113
  93.9 3.8 %collective-permute-start.16 = (f32[256,256]{1,0:T(8,128)S(1)}, f32[256,256]{1,0:T(8,128)S(1)}, u32[]{:S(2)}, u32[]{:S(2)}) collective-permute-start(f32[256,256]{1,0:T(8,128)S(1)} %add.296), channel_id=1, source_target_pairs={{0,96},{16,112},{32,0},{48,16},{64,32},{80,48},{96,64},{112,80},{1... | collective-permute-start | bytes 786440 | tf_op jit(solution)/shard_map/ppermute | solution.py:113
  97.6 1.1 bitcast_add_fusion
  98.8 0.1 collective-permute-start.19
  98.9 1.4 %collective-permute-done.11 = f32[128,256]{1,0:T(8,128)S(1)} collective-permute-done((f32[128,256]{1,0:T(8,128)S(1)}, f32[128,256]{1,0:T(8,128)S(1)}, u32[]{:S(2)}, u32[]{:S(2)}) %collective-permute-start.11) | collective-permute-done | bytes 131104 | tf_op jit(solution)/shard_map/ppermute | solution.py:116
  100.3 0.6 collective-permute-start.12
  101.0 3.4 %collective-permute-done.19 = f32[128,256]{1,0:T(8,128)S(1)} collective-permute-done((f32[128,256]{1,0:T(8,128)S(1)}, f32[128,256]{1,0:T(8,128)S(1)}, u32[]{:S(2)}, u32[]{:S(2)}) %collective-permute-start.19) | collective-permute-done | bytes 131104 | tf_op jit(solution)/shard_map/ppermute | solution.py:116
  104.4 3.8 %collective-permute-start.20 = (f32[128,256]{1,0:T(8,128)S(1)}, f32[128,256]{1,0:T(8,128)S(1)}, u32[]{:S(2)}, u32[]{:S(2)}) collective-permute-start(f32[128,256]{1,0:T(8,128)S(1)} %bitcast_add_fusion.4), channel_id=1, source_target_pairs={{0,96},{16,112},{32,0},{48,16},{64,32},{80,48},{96,64},{112,80},{1... | collective-permute-start | bytes 393224 | tf_op jit(solution)/shard_map/ppermute | solution.py:116
  108.2 3.3 %collective-permute-start.9 = (f32[128,256]{1,0:T(8,128)S(1)}, f32[128,256]{1,0:T(8,128)S(1)}, u32[]{:S(2)}, u32[]{:S(2)}) collective-permute-start(f32[128,256]{1,0:T(8,128)S(1)} %constant_dynamic-slice_fusion.5), channel_id=1, source_target_pairs={{0,16},{16,0},{32,48},{48,32},{64,80},{80,64},{96,112},{112,96},{1... | collective-permute-start | bytes 393224 | tf_op jit(solution)/shard_map/ppermute | solution.py:120
  111.7 0.4 collective-permute-start.17
  112.1 3.3 %collective-permute-start.21 = (f32[128,256]{1,0:T(8,128)S(1)}, f32[128,256]{1,0:T(8,128)S(1)}, u32[]{:S(2)}, u32[]{:S(2)}) collective-permute-start(f32[128,256]{1,0:T(8,128)S(1)} %bitcast_add_fusion.3), channel_id=1, source_target_pairs={{0,96},{16,112},{32,0},{48,16},{64,32},{80,48},{96,64},{112,80},{1... | collective-permute-start | bytes 393224 | tf_op jit(solution)/shard_map/ppermute | solution.py:116
  115.4 2.4 %collective-permute-done.13 = f32[128,256]{1,0:T(8,128)S(1)} collective-permute-done((f32[128,256]{1,0:T(8,128)S(1)}, f32[128,256]{1,0:T(8,128)S(1)}, u32[]{:S(2)}, u32[]{:S(2)}) %collective-permute-start.13) | collective-permute-done | bytes 131104 | tf_op jit(solution)/shard_map/ppermute | solution.py:116
  117.8 0.4 rev.12
  118.3 0.4 rev.13
  118.8 1.2 copy.24
  (63 shorter events, 0.8 us)
Async XLA Ops:
  3.4 4.1 %collective-permute-start = (bf16[2,6,3,1024]{3,0,2,1:T(2,128)(2,1)S(1)}, bf16[2,6,3,1024]{3,0,2,1:T(2,128)(2,1)S(1)}, u32[]{:S(2)}, u32[]{:S(2)}) collective-permute-start(bf16[2,6,3,1024]{3,0,2,1:T(2,128)(2,1)S(1)} %rev.11), channel_id=1, source_target_pairs={{0,3},{1,0},{2,1},{3,2},{4,7},{5,4},{6,5},{7,6},{8,11},{9,8},{10,9... | collective-permute-start | bytes 221192 | tf_op jit(solution)/shard_map/ppermute | solution.py:27
  4.5 5.2 %collective-permute-start.1 = (bf16[2,6,3,1024]{3,0,2,1:T(2,128)(2,1)S(1)}, bf16[2,6,3,1024]{3,0,2,1:T(2,128)(2,1)S(1)}, u32[]{:S(2)}, u32[]{:S(2)}) collective-permute-start(bf16[2,6,3,1024]{3,0,2,1:T(2,128)(2,1)S(1)} %rev.11), channel_id=1, source_target_pairs={{0,2},{1,3},{2,0},{3,1},{4,6},{5,7},{6,4},{7,5},{8,10},{9,11},{10,... | collective-permute-start | bytes 221192 | tf_op jit(solution)/shard_map/ppermute | solution.py:27
  5.1 4.6 %collective-permute-start.2 = (bf16[2,6,3,1024]{3,0,2,1:T(2,128)(2,1)S(1)}, bf16[2,6,3,1024]{3,0,2,1:T(2,128)(2,1)S(1)}, u32[]{:S(2)}, u32[]{:S(2)}) collective-permute-start(bf16[2,6,3,1024]{3,0,2,1:T(2,128)(2,1)S(1)} %rev.11), channel_id=1, source_target_pairs={{0,1},{1,2},{2,3},{3,0},{4,5},{5,6},{6,7},{7,4},{8,9},{9,10},{10,1... | collective-permute-start | bytes 221192 | tf_op jit(solution)/shard_map/ppermute | solution.py:27
  10.0 5.9 %collective-permute-start.3 = (bf16[2,6,3,1024]{3,0,2,1:T(2,128)(2,1)S(1)}, bf16[2,6,3,1024]{3,0,2,1:T(2,128)(2,1)S(1)}, u32[]{:S(2)}, u32[]{:S(2)}) collective-permute-start(bf16[2,6,3,1024]{3,0,2,1:T(2,128)(2,1)S(1)} %broadcast_select_fusion.4), channel_id=1, source_target_pairs={{0,12},{1,13},{2,14},{3,15},{4,0},{5,1},{6,2},{7,3},{8,4},{9,5},{1... | collective-permute-start | bytes 221192 | tf_op jit(solution)/shard_map/ppermute | solution.py:27
  13.1 5.9 %collective-permute-start.4 = (bf16[2,6,3,1024]{3,0,2,1:T(2,128)(2,1)S(1)}, bf16[2,6,3,1024]{3,0,2,1:T(2,128)(2,1)S(1)}, u32[]{:S(2)}, u32[]{:S(2)}) collective-permute-start(bf16[2,6,3,1024]{3,0,2,1:T(2,128)(2,1)S(1)} %broadcast_select_fusion.4), channel_id=1, source_target_pairs={{0,8},{1,9},{2,10},{3,11},{4,12},{5,13},{6,14},{7,15},{8,0},{9,1},... | collective-permute-start | bytes 221192 | tf_op jit(solution)/shard_map/ppermute | solution.py:27
  13.7 6.0 %collective-permute-start.5 = (bf16[2,6,3,1024]{3,0,2,1:T(2,128)(2,1)S(1)}, bf16[2,6,3,1024]{3,0,2,1:T(2,128)(2,1)S(1)}, u32[]{:S(2)}, u32[]{:S(2)}) collective-permute-start(bf16[2,6,3,1024]{3,0,2,1:T(2,128)(2,1)S(1)} %broadcast_select_fusion.4), channel_id=1, source_target_pairs={{0,4},{1,5},{2,6},{3,7},{4,8},{5,9},{6,10},{7,11},{8,12},{9,13},{1... | collective-permute-start | bytes 221192 | tf_op jit(solution)/shard_map/ppermute | solution.py:27
  29.9 9.8 %copy-start = (bf16[1024,6,3,256]{3,0,2,1:T(8,128)(2,1)S(1)}, bf16[1024,6,3,256]{3,0,2,1:T(8,128)(2,1)}, u32[]{:S(2)}) copy-start(bf16[1024,6,3,256]{3,0,2,1:T(8,128)(2,1)} %param.5) | copy-start | bytes 28311556
  33.9 45.2 %collective-permute-start.6 = (f32[256,256]{1,0:T(8,128)}, f32[256,256]{1,0:T(8,128)}, u32[]{:S(2)}, u32[]{:S(2)}) collective-permute-start(f32[256,256]{1,0:T(8,128)} %fusion.16), channel_id=1, source_target_pairs={{0,32},{16,48},{32,64},{48,80},{64,96},{80,112},{96,0},{112,16},{1... | collective-permute-start | bytes 786440 | tf_op jit(solution)/shard_map/ppermute | solution.py:113
  39.7 3.3 %copy-start.2 = (bf16[4608,256]{1,0:T(8,128)(2,1)S(1)}, bf16[4608,256]{1,0:T(8,128)(2,1)}, u32[]{:S(2)}) copy-start(bf16[4608,256]{1,0:T(8,128)(2,1)} %get-tuple-element.9) | copy-start | bytes 7077892
  43.0 1.7 %copy-start.11 = (bf16[4608,256]{1,0:T(8,128)(2,1)S(1)}, bf16[4608,256]{1,0:T(8,128)(2,1)}, u32[]{:S(2)}) copy-start(bf16[4608,256]{1,0:T(8,128)(2,1)} %get-tuple-element.10) | copy-start | bytes 7077892
  56.1 9.6 %copy-start.1 = (bf16[4608,256]{1,0:T(8,128)(2,1)S(1)}, bf16[4608,256]{1,0:T(8,128)(2,1)}, u32[]{:S(2)}) copy-start(bf16[4608,256]{1,0:T(8,128)(2,1)} %get-tuple-element.11) | copy-start | bytes 7077892
  62.7 27.8 %collective-permute-start.10 = (f32[4,128,256]{2,1,0:T(8,128)}, f32[4,128,256]{2,1,0:T(8,128)}, u32[]{:S(2)}, u32[]{:S(2)}) collective-permute-start(f32[4,128,256]{2,1,0:T(8,128)} %bitcast.13), channel_id=1, source_target_pairs={{0,16},{16,0},{32,48},{48,32},{64,80},{80,64},{96,112},{112,96},{1... | collective-permute-start | bytes 1572872 | tf_op jit(solution)/shard_map/ppermute | solution.py:107
  68.8 5.5 %copy-start.5 = (f32[4,1,128,256]{2,1,0,3:T(1,128)S(1)}, f32[4,1,128,256]{2,1,0,3:T(1,128)}, u32[]{:S(2)}) copy-start(f32[4,1,128,256]{2,1,0,3:T(1,128)} %get-tuple-element.20) | copy-start | bytes 1572868
  68.8 16.3 %collective-permute-start.14 = (f32[256,256]{1,0:T(8,128)}, f32[256,256]{1,0:T(8,128)}, u32[]{:S(2)}, u32[]{:S(2)}) collective-permute-start(f32[256,256]{1,0:T(8,128)} %fusion.28), channel_id=1, source_target_pairs={{0,96},{16,112},{32,0},{48,16},{64,32},{80,48},{96,64},{112,80},{1... | collective-permute-start | bytes 786440 | tf_op jit(solution)/shard_map/ppermute | solution.py:113
  75.5 3.7 %copy-start.10 = (f32[256,256]{1,0:T(8,128)S(1)}, f32[256,256]{1,0:T(8,128)}, u32[]{:S(2)}) copy-start(f32[256,256]{1,0:T(8,128)} %fusion.19) | copy-start | bytes 786436
  75.5 22.2 %collective-permute-start.18 = (f32[4,128,256]{2,1,0:T(8,128)}, f32[4,128,256]{2,1,0:T(8,128)}, u32[]{:S(2)}, u32[]{:S(2)}) collective-permute-start(f32[4,128,256]{2,1,0:T(8,128)} %bitcast.28), channel_id=1, source_target_pairs={{0,16},{16,0},{32,48},{48,32},{64,80},{80,64},{96,112},{112,96},{1... | collective-permute-start | bytes 1572872 | tf_op jit(solution)/shard_map/ppermute | solution.py:107
  80.9 3.2 %copy-start.4 = (f32[4,1,128,256]{2,1,0,3:T(1,128)S(1)}, f32[4,1,128,256]{2,1,0,3:T(1,128)}, u32[]{:S(2)}) copy-start(f32[4,1,128,256]{2,1,0,3:T(1,128)} %get-tuple-element.28) | copy-start | bytes 1572868
  80.9 3.8 %copy-start.3 = (f32[4,1,128,256]{2,1,0,3:T(1,128)S(1)}, f32[4,1,128,256]{2,1,0,3:T(1,128)}, u32[]{:S(2)}) copy-start(f32[4,1,128,256]{2,1,0,3:T(1,128)} %get-tuple-element.19) | copy-start | bytes 1572868
  80.9 8.5 %collective-permute-start.7 = (f32[256,256]{1,0:T(8,128)}, f32[256,256]{1,0:T(8,128)}, u32[]{:S(2)}, u32[]{:S(2)}) collective-permute-start(f32[256,256]{1,0:T(8,128)} %add.268), channel_id=1, source_target_pairs={{0,32},{16,48},{32,64},{48,80},{64,96},{80,112},{96,0},{112,16},{1... | collective-permute-start | bytes 786440 | tf_op jit(solution)/shard_map/ppermute | solution.py:113
  84.1 5.3 %copy-start.8 = (f32[256,256]{1,0:T(8,128)S(1)}, f32[256,256]{1,0:T(8,128)}, u32[]{:S(2)}) copy-start(f32[256,256]{1,0:T(8,128)} %fusion.22) | copy-start | bytes 786436
  84.6 9.2 %copy-start.9 = (f32[256,256]{1,0:T(8,128)S(1)}, f32[256,256]{1,0:T(8,128)}, u32[]{:S(2)}) copy-start(f32[256,256]{1,0:T(8,128)} %fusion.34) | copy-start | bytes 786436
  86.2 7.6 %collective-permute-start.15 = (f32[256,256]{1,0:T(8,128)S(1)}, f32[256,256]{1,0:T(8,128)S(1)}, u32[]{:S(2)}, u32[]{:S(2)}) collective-permute-start(f32[256,256]{1,0:T(8,128)S(1)} %add.293), channel_id=1, source_target_pairs={{0,96},{16,112},{32,0},{48,16},{64,32},{80,48},{96,64},{112,80},{1... | collective-permute-start | bytes 786440 | tf_op jit(solution)/shard_map/ppermute | solution.py:113
  90.4 17.7 %copy-start.6 = (f32[256,256]{1,0:T(8,128)S(1)}, f32[256,256]{1,0:T(8,128)}, u32[]{:S(2)}) copy-start(f32[256,256]{1,0:T(8,128)} %fusion.25) | copy-start | bytes 786436
  90.4 17.7 %collective-permute-start.8 = (f32[256,256]{1,0:T(8,128)S(1)}, f32[256,256]{1,0:T(8,128)S(1)}, u32[]{:S(2)}, u32[]{:S(2)}) collective-permute-start(f32[256,256]{1,0:T(8,128)S(1)} %add.271), channel_id=1, source_target_pairs={{0,32},{16,48},{32,64},{48,80},{64,96},{80,112},{96,0},{112,16},{1... | collective-permute-start | bytes 786440 | tf_op jit(solution)/shard_map/ppermute | solution.py:113
  91.6 20.0 %copy-start.7 = (f32[256,256]{1,0:T(8,128)S(1)}, f32[256,256]{1,0:T(8,128)}, u32[]{:S(2)}) copy-start(f32[256,256]{1,0:T(8,128)} %fusion.37) | copy-start | bytes 786436
  91.6 8.7 %collective-permute-start.11 = (f32[128,256]{1,0:T(8,128)S(1)}, f32[128,256]{1,0:T(8,128)S(1)}, u32[]{:S(2)}, u32[]{:S(2)}) collective-permute-start(f32[128,256]{1,0:T(8,128)S(1)} %dynamic-slice_bitcast_fusion.1), channel_id=1, source_target_pairs={{0,32},{16,48},{32,64},{48,80},{64,96},{80,112},{96,0},{112,16},{1... | collective-permute-start | bytes 393224 | tf_op jit(solution)/shard_map/ppermute | solution.py:116
  93.9 17.7 %collective-permute-start.16 = (f32[256,256]{1,0:T(8,128)S(1)}, f32[256,256]{1,0:T(8,128)S(1)}, u32[]{:S(2)}, u32[]{:S(2)}) collective-permute-start(f32[256,256]{1,0:T(8,128)S(1)} %add.296), channel_id=1, source_target_pairs={{0,96},{16,112},{32,0},{48,16},{64,32},{80,48},{96,64},{112,80},{1... | collective-permute-start | bytes 786440 | tf_op jit(solution)/shard_map/ppermute | solution.py:113
  98.8 5.6 %collective-permute-start.19 = (f32[128,256]{1,0:T(8,128)S(1)}, f32[128,256]{1,0:T(8,128)S(1)}, u32[]{:S(2)}, u32[]{:S(2)}) collective-permute-start(f32[128,256]{1,0:T(8,128)S(1)} %dynamic-slice_bitcast_fusion), channel_id=1, source_target_pairs={{0,96},{16,112},{32,0},{48,16},{64,32},{80,48},{96,64},{112,80},{1... | collective-permute-start | bytes 393224 | tf_op jit(solution)/shard_map/ppermute | solution.py:116
  100.3 11.2 %collective-permute-start.12 = (f32[128,256]{1,0:T(8,128)S(1)}, f32[128,256]{1,0:T(8,128)S(1)}, u32[]{:S(2)}, u32[]{:S(2)}) collective-permute-start(f32[128,256]{1,0:T(8,128)S(1)} %bitcast_add_fusion.7), channel_id=1, source_target_pairs={{0,32},{16,48},{32,64},{48,80},{64,96},{80,112},{96,0},{112,16},{1... | collective-permute-start | bytes 393224 | tf_op jit(solution)/shard_map/ppermute | solution.py:116
  104.4 7.7 %collective-permute-start.20 = (f32[128,256]{1,0:T(8,128)S(1)}, f32[128,256]{1,0:T(8,128)S(1)}, u32[]{:S(2)}, u32[]{:S(2)}) collective-permute-start(f32[128,256]{1,0:T(8,128)S(1)} %bitcast_add_fusion.4), channel_id=1, source_target_pairs={{0,96},{16,112},{32,0},{48,16},{64,32},{80,48},{96,64},{112,80},{1... | collective-permute-start | bytes 393224 | tf_op jit(solution)/shard_map/ppermute | solution.py:116
  108.2 7.2 %collective-permute-start.9 = (f32[128,256]{1,0:T(8,128)S(1)}, f32[128,256]{1,0:T(8,128)S(1)}, u32[]{:S(2)}, u32[]{:S(2)}) collective-permute-start(f32[128,256]{1,0:T(8,128)S(1)} %constant_dynamic-slice_fusion.5), channel_id=1, source_target_pairs={{0,16},{16,0},{32,48},{48,32},{64,80},{80,64},{96,112},{112,96},{1... | collective-permute-start | bytes 393224 | tf_op jit(solution)/shard_map/ppermute | solution.py:120
  111.5 6.2 %collective-permute-start.13 = (f32[128,256]{1,0:T(8,128)S(1)}, f32[128,256]{1,0:T(8,128)S(1)}, u32[]{:S(2)}, u32[]{:S(2)}) collective-permute-start(f32[128,256]{1,0:T(8,128)S(1)} %bitcast_add_fusion.6), channel_id=1, source_target_pairs={{0,32},{16,48},{32,64},{48,80},{64,96},{80,112},{96,0},{112,16},{1... | collective-permute-start | bytes 393224 | tf_op jit(solution)/shard_map/ppermute | solution.py:116
  111.7 6.6 %collective-permute-start.17 = (f32[128,256]{1,0:T(8,128)S(1)}, f32[128,256]{1,0:T(8,128)S(1)}, u32[]{:S(2)}, u32[]{:S(2)}) collective-permute-start(f32[128,256]{1,0:T(8,128)S(1)} %constant_dynamic-slice_fusion.2), channel_id=1, source_target_pairs={{0,16},{16,0},{32,48},{48,32},{64,80},{80,64},{96,112},{112,96},{1... | collective-permute-start | bytes 393224 | tf_op jit(solution)/shard_map/ppermute | solution.py:120
  112.1 6.2 %collective-permute-start.21 = (f32[128,256]{1,0:T(8,128)S(1)}, f32[128,256]{1,0:T(8,128)S(1)}, u32[]{:S(2)}, u32[]{:S(2)}) collective-permute-start(f32[128,256]{1,0:T(8,128)S(1)} %bitcast_add_fusion.3), channel_id=1, source_target_pairs={{0,96},{16,112},{32,0},{48,16},{64,32},{80,48},{96,64},{112,80},{1... | collective-permute-start | bytes 393224 | tf_op jit(solution)/shard_map/ppermute | solution.py:116

commit v11 on v9

--- a/solution.py
+++ b/solution.py
@@ -69,9 +69,11 @@
     point_rows = green.shape[0]
     rows = green.shape[1] * green.shape[2]
     green_t = jnp.transpose(green, (1, 2, 0, 3)).reshape(rows, point_rows, NT)
-    flipped = jnp.flip(records_buffer[0], axis=-1)
-    traces = from_owners(flipped, "loc", owners)
-    rev = traces.astype(jnp.float32).reshape(EV * rows, 1, SAMPLES)
+    traces = from_owners(records_buffer[0], "loc", owners).reshape(EV * rows, SAMPLES)
+    i = lax.broadcasted_iota(jnp.int32, (SAMPLES, SAMPLES), 0)
+    j = lax.broadcasted_iota(jnp.int32, (SAMPLES, SAMPLES), 1)
+    anti = (i + j == SAMPLES - 1).astype(jnp.bfloat16)
+    rev = jnp.dot(traces, anti, preferred_element_type=jnp.float32).reshape(EV * rows, 1, SAMPLES)
     shifts = ((jnp.repeat(onsets.astype(jnp.int32), 3, axis=1) - LAGS) % SAMPLES).reshape(-1)
     weights = jnp.exp2(-codes.astype(jnp.float32)).reshape(-1)
     bands = toeplitz_reversed(rev, shifts, weights)
@@ -91,10 +93,12 @@
     def ring_perm(step):
         return [(i, ((i // xs + step) % zs) * xs + i % xs) for i in range(size)]
 
+    steps = (1, zs - 1)
+    firsts = lax.optimization_barrier(tuple(piece(bands[e], (z + zs - st) % zs) for e, st in enumerate(steps)))
     outs = []
-    for e, step in zip(range(EV), (1, zs - 1)):
+    for e, step in zip(range(EV), steps):
         band = bands[e]
-        acc = piece(band, (z + zs - step) % zs)
+        acc = firsts[e]
         for k in range(zs - 1):
             got = lax.ppermute(acc, "sens", ring_perm(step))
             part = lax.optimization_barrier(piece(band, (z + 4 * zs - step * (k + 2)) % zs))

time: 87.5 us -> 91.7 us (1.048)
  matrix products: 17.4 us -> 22.5 us
  local copies, waits for them, and re-layouts: 7.95 us -> 4.58 us
  waiting for transfers between devices: 25.5 us -> 26.9 us
    dot_general x8, matrix products: 17.4 us -> 22.2 us  [piece(): jnp.einsum('rpt,rtn->pn', g, band.reshape(rows, NT, LAGS), preferred_elem...]
    rev x1 -> x0, local copies, waits for them, and re-layouts: 3.39 us -> none  [local(): flipped = jnp.flip(records_buffer[0], axis=-1)]
    ppermute x6, waiting for transfers between devices: 15.2 us -> 16.4 us  [local(): got = lax.ppermute(acc, 'sens', ring_perm(step))]
    select_n x1 -> x2, other arithmetic: 0.23 us -> 1.34 us  [from_owners(): jnp.where((src == digit).reshape((-1,) + (1,) * (x.ndim - 1)), got, out)]
  transfers between devices with their start and end apart: 14 -> 14, of which waited for: 11 -> 9; matrix products, arithmetic and copies ran while one was open for 21% -> 22% of each run, Pallas kernels for 0% -> 0%
where the time goes in v11:
time: 91.7 us; the launch traced here: 91.4 us
  waiting for transfers between devices  26.9 us (29%)
  starting transfers between devices  23.5 us (26%)
  matrix products  22.5 us (25%)
  Pallas kernels  9.12 us (10%)
  local copies, waits for them, and re-layouts  4.58 us (5%)
  other arithmetic  4.53 us (5%)
    dot_general x8, matrix products, piece(): jnp.einsum('rpt,rtn->pn', g, band.reshape(rows, NT, LAGS), preferred_elem...  22.2 us
    ppermute x6, waiting for transfers between devices, local(): got = lax.ppermute(acc, 'sens', ring_perm(step))  16.4 us
    ppermute x6, starting transfers between devices, local(): got = lax.ppermute(acc, 'sens', ring_perm(step))  11.9 us
    pallas_call x1, Pallas kernels, toeplitz_reversed(): pl.pallas_call(_toeplitz_kernel, in_specs=[pl.BlockSpec(memory_space=pltp...  9.12 us
    ppermute x6, starting transfers between devices, from_owners(): got = lax.ppermute(x, axis, perm)  6.49 us
    ppermute x6, waiting for transfers between devices, from_owners(): got = lax.ppermute(x, axis, perm)  6.25 us
    ppermute x2, starting transfers between devices, local(): got = lax.ppermute(theirs, 'sens', [(i, i ^ 1) for i in range(size)])  5.09 us
    ppermute x2, waiting for transfers between devices, local(): got = lax.ppermute(theirs, 'sens', [(i, i ^ 1) for i in range(size)])  4.21 us
  transfers between devices with their start and end apart: 14, of which 9 were waited for; matrix products, arithmetic and copies ran while one was open for 22% of the time, Pallas kernels for 0%

profile of v11, /device:TPU:0, one launch (start us, length us, event | category | flops | bytes accessed | tf_op | source)
XLA Modules:
  0.0 91.4 jit_solution(470122219052405688)
XLA Ops:
  0.0 1.0 %collective-permute-start = (bf16[2,6,3,1024]{3,0,2,1:T(2,128)(2,1)}, bf16[2,6,3,1024]{3,0,2,1:T(2,128)(2,1)S(1)}, u32[]{:S(2)}, u32[]{:S(2)}) collective-permute-start(bf16[2,6,3,1024]{3,0,2,1:T(2,128)(2,1)} %bitcast.36), channel_id=1, source_target_pairs={{0,3},{1,0},{2,1},{3,2},{4,7},{5,4},{6,5},{7,6},{8,11},{9,8},{10,9... | collective-permute-start | bytes 221192 | tf_op jit(solution)/shard_map/ppermute | solution.py:26
  1.0 0.6 collective-permute-start.1
  1.6 0.2 collective-permute-start.2
  1.8 0.7 broadcast_add_fusion
  2.5 0.7 multiply_exponential_fusion
  3.2 0.7 broadcast_compare_fusion
  3.9 0.1 broadcast_in_dim.36
  4.0 0.1 sub.68
  4.0 0.0 collective-permute-done
  4.0 2.4 %collective-permute-done.1 = bf16[2,6,3,1024]{3,0,2,1:T(2,128)(2,1)S(1)} collective-permute-done((bf16[2,6,3,1024]{3,0,2,1:T(2,128)(2,1)}, bf16[2,6,3,1024]{3,0,2,1:T(2,128)(2,1)S(1)}, u32[]{:S(2)}, u32[]{:S(2)}) %collective-permute-start.1) | collective-permute-done | bytes 73760 | tf_op jit(solution)/shard_map/ppermute | solution.py:26
  6.5 0.0 collective-permute-done.2
  6.5 1.1 %broadcast_select_fusion.4 = bf16[2,6,3,1024]{3,0,2,1:T(2,128)(2,1)S(1)} fusion(bf16[2,6,3,1024]{3,0,2,1:T(2,128)(2,1)S(1)} %collective-permute-done, pred[2]{0:T(512)(128)(4,1)S(1)} %get-tuple-element.26, bf16[2,6,3,1024]{3,0,2,1:T(2,128)(2,1)S(1)} %collective-permute-done.1, pred[2]{0:T(512)(128)(4,1)S(1)} %get-tuple-element.25, ...), kind=kLoop, calls=%fused_computation.34 | loop fusion | flops 110592 | bytes 368646 | tf_op jit(solution)/shard_map/jit(_where)/select_n | solution.py:28
  7.6 3.1 %collective-permute-start.3 = (bf16[2,6,3,1024]{3,0,2,1:T(2,128)(2,1)S(1)}, bf16[2,6,3,1024]{3,0,2,1:T(2,128)(2,1)S(1)}, u32[]{:S(2)}, u32[]{:S(2)}) collective-permute-start(bf16[2,6,3,1024]{3,0,2,1:T(2,128)(2,1)S(1)} %broadcast_select_fusion.4), channel_id=1, source_target_pairs={{0,12},{1,13},{2,14},{3,15},{4,0},{5,1},{6,2},{7,3},{8,4},{9,5},{1... | collective-permute-start | bytes 221192 | tf_op jit(solution)/shard_map/ppermute | solution.py:26
  10.7 0.6 collective-permute-start.4
  11.3 1.0 %collective-permute-start.5 = (bf16[2,6,3,1024]{3,0,2,1:T(2,128)(2,1)S(1)}, bf16[2,6,3,1024]{3,0,2,1:T(2,128)(2,1)S(1)}, u32[]{:S(2)}, u32[]{:S(2)}) collective-permute-start(bf16[2,6,3,1024]{3,0,2,1:T(2,128)(2,1)S(1)} %broadcast_select_fusion.4), channel_id=1, source_target_pairs={{0,4},{1,5},{2,6},{3,7},{4,8},{5,9},{6,10},{7,11},{8,12},{9,13},{1... | collective-permute-start | bytes 221192 | tf_op jit(solution)/shard_map/ppermute | solution.py:26
  12.3 0.5 and_select_fusion.3.shift_ref
  12.8 0.1 copy.8
  12.9 0.6 reshape.42.weight_ref
  13.5 0.0 collective-permute-done.3
  13.5 3.1 %collective-permute-done.4 = bf16[2,6,3,1024]{3,0,2,1:T(2,128)(2,1)S(1)} collective-permute-done((bf16[2,6,3,1024]{3,0,2,1:T(2,128)(2,1)S(1)}, bf16[2,6,3,1024]{3,0,2,1:T(2,128)(2,1)S(1)}, u32[]{:S(2)}, u32[]{:S(2)}) %collective-permute-start.4) | collective-permute-done | bytes 73760 | tf_op jit(solution)/shard_map/ppermute | solution.py:26
  16.6 0.7 collective-permute-done.5
  17.3 0.2 broadcast_select_fusion.5
  17.6 0.1 reshape.43
  17.7 0.3 fusion
  18.0 0.8 reshape.44.rev_ref
  18.7 9.1 %shard_map.55 = (bf16[4608,512]{1,0:T(8,128)(2,1)}, bf16[4608,512]{1,0:T(8,128)(2,1)}) custom-call(s32[36]{0:T(128)} %and_select_fusion.3.shift_ref, f32[18]{0:T(128)} %reshape.42.weight_ref, f32[36,1,1024]{2,1,0:T(1,128)} %reshape.44.rev_ref), custom_call_target="tpu_custom_call" | custom-call | bytes 9437184 | tf_op jit(solution)/shard_map/pallas_call | solution.py:55
  27.9 4.6 %fusion.18 = f32[256,512]{1,0:T(8,128)S(1)} fusion(bf16[18,256,512]{2,1,0:T(8,128)(2,1)} %bitcast.49, bf16[18,1024,256]{2,1,0:T(8,128)(2,1)} %bitcast.39, s32[]{:T(128)S(6)} %select_n.155), kind=kOutput, calls=%fused_computation.19 | convolution fusion | flops 1207959552 | bytes 7602180 | tf_op jit(solution)/shard_map/rpt,rtn->pn/dot_general | solution.py:91
  32.5 3.0 %fusion.21 = f32[256,512]{1,0:T(8,128)S(1)} fusion(bf16[18,256,512]{2,1,0:T(8,128)(2,1)S(1)} %bitcast.59, bf16[18,1024,256]{2,1,0:T(8,128)(2,1)} %bitcast.40, s32[]{:T(128)S(6)} %select_n.176), kind=kOutput, calls=%fused_computation.20 | convolution fusion | flops 1207959552 | bytes 7602180 | tf_op jit(solution)/shard_map/rpt,rtn->pn/dot_general | solution.py:91
  35.5 4.1 %collective-permute-start.10 = (f32[256,512]{1,0:T(8,128)S(1)}, f32[256,512]{1,0:T(8,128)S(1)}, u32[]{:S(2)}, u32[]{:S(2)}) collective-permute-start(f32[256,512]{1,0:T(8,128)S(1)} %fusion.21), channel_id=1, source_target_pairs={{0,96},{16,112},{32,0},{48,16},{64,32},{80,48},{96,64},{112,80},{1... | collective-permute-start | bytes 1572872 | tf_op jit(solution)/shard_map/ppermute | solution.py:103
  39.6 4.6 %fusion.33 = f32[256,512]{1,0:T(8,128)S(1)} fusion(bf16[18,256,512]{2,1,0:T(8,128)(2,1)} %bitcast.55, bf16[18,1024,256]{2,1,0:T(8,128)(2,1)} %bitcast.41, s32[]{:T(128)S(6)} %select_n.187), kind=kOutput, calls=%fused_computation.24 | convolution fusion | flops 1207959552 | bytes 7602180 | tf_op jit(solution)/shard_map/rpt,rtn->pn/dot_general | solution.py:91
  44.2 0.1 collective-permute-start.6
  44.3 4.5 %collective-permute-done.10 = f32[256,512]{1,0:T(8,128)S(1)} collective-permute-done((f32[256,512]{1,0:T(8,128)S(1)}, f32[256,512]{1,0:T(8,128)S(1)}, u32[]{:S(2)}, u32[]{:S(2)}) %collective-permute-start.10) | collective-permute-done | bytes 524320 | tf_op jit(solution)/shard_map/ppermute | solution.py:103
  48.8 0.1 add.224
  48.8 0.0 slice-start.2
  48.9 0.0 slice-start.4
  48.9 3.8 %collective-permute-start.11 = (f32[256,512]{1,0:T(8,128)S(1)}, f32[256,512]{1,0:T(8,128)S(1)}, u32[]{:S(2)}, u32[]{:S(2)}) collective-permute-start(f32[256,512]{1,0:T(8,128)S(1)} %add.224), channel_id=1, source_target_pairs={{0,96},{16,112},{32,0},{48,16},{64,32},{80,48},{96,64},{112,80},{1... | collective-permute-start | bytes 1572872 | tf_op jit(solution)/shard_map/ppermute | solution.py:103
  52.6 4.6 %fusion.36 = f32[256,512]{1,0:T(8,128)S(1)} fusion(bf16[18,256,512]{2,1,0:T(8,128)(2,1)} %bitcast.56, bf16[18,1024,256]{2,1,0:T(8,128)(2,1)} %bitcast.42, s32[]{:T(128)S(6)} %select_n.189), kind=kOutput, calls=%fused_computation.25 | convolution fusion | flops 1207959552 | bytes 7602180 | tf_op jit(solution)/shard_map/rpt,rtn->pn/dot_general | solution.py:91
  57.3 0.0 slice-start.8
  57.3 1.4 %fusion.24 = f32[256,512]{1,0:T(8,128)S(1)} fusion(bf16[18,256,512]{2,1,0:T(8,128)(2,1)S(1)} %bitcast.52, bf16[18,1024,256]{2,1,0:T(8,128)(2,1)S(1)} %bitcast.45, s32[]{:T(128)S(6)} %select_n.178), kind=kOutput, calls=%fused_computation.21 | convolution fusion | flops 1207959552 | bytes 7602180 | tf_op jit(solution)/shard_map/rpt,rtn->pn/dot_general | solution.py:91
  58.7 0.0 collective-permute-done.6
  58.7 0.1 add.211
  58.8 0.1 collective-permute-start.7
  58.8 2.0 %collective-permute-done.11 = f32[256,512]{1,0:T(8,128)S(1)} collective-permute-done((f32[256,512]{1,0:T(8,128)S(1)}, f32[256,512]{1,0:T(8,128)S(1)}, u32[]{:S(2)}, u32[]{:S(2)}) %collective-permute-start.11) | collective-permute-done | bytes 524320 | tf_op jit(solution)/shard_map/ppermute | solution.py:103
  60.8 0.1 add.227
  60.9 3.8 %collective-permute-start.12 = (f32[256,512]{1,0:T(8,128)S(1)}, f32[256,512]{1,0:T(8,128)S(1)}, u32[]{:S(2)}, u32[]{:S(2)}) collective-permute-start(f32[256,512]{1,0:T(8,128)S(1)} %add.227), channel_id=1, source_target_pairs={{0,96},{16,112},{32,0},{48,16},{64,32},{80,48},{96,64},{112,80},{1... | collective-permute-start | bytes 1572872 | tf_op jit(solution)/shard_map/ppermute | solution.py:103
  64.7 1.4 %fusion.39 = f32[256,512]{1,0:T(8,128)S(1)} fusion(bf16[18,256,512]{2,1,0:T(8,128)(2,1)S(1)} %bitcast.62, bf16[18,1024,256]{2,1,0:T(8,128)(2,1)S(1)} %bitcast.46, s32[]{:T(128)S(6)} %select_n.191), kind=kOutput, calls=%fused_computation.26 | convolution fusion | flops 1207959552 | bytes 7602180 | tf_op jit(solution)/shard_map/rpt,rtn->pn/dot_general | solution.py:91
  66.1 1.4 %fusion.27 = f32[256,512]{1,0:T(8,128)S(1)} fusion(bf16[18,256,512]{2,1,0:T(8,128)(2,1)S(1)} %bitcast.53, bf16[18,1024,256]{2,1,0:T(8,128)(2,1)S(1)} %bitcast.47, s32[]{:T(128)S(6)} %select_n.180), kind=kOutput, calls=%fused_computation.22 | convolution fusion | flops 1207959552 | bytes 7602180 | tf_op jit(solution)/shard_map/rpt,rtn->pn/dot_general | solution.py:91
  67.5 3.3 %collective-permute-done.7 = f32[256,512]{1,0:T(8,128)S(1)} collective-permute-done((f32[256,512]{1,0:T(8,128)S(1)}, f32[256,512]{1,0:T(8,128)S(1)}, u32[]{:S(2)}, u32[]{:S(2)}) %collective-permute-start.7) | collective-permute-done | bytes 524320 | tf_op jit(solution)/shard_map/ppermute | solution.py:103
  70.8 0.1 add.214
  70.8 0.1 collective-permute-start.8
  70.9 1.1 %collective-permute-done.12 = f32[256,512]{1,0:T(8,128)S(1)} collective-permute-done((f32[256,512]{1,0:T(8,128)S(1)}, f32[256,512]{1,0:T(8,128)S(1)}, u32[]{:S(2)}, u32[]{:S(2)}) %collective-permute-start.12) | collective-permute-done | bytes 524320 | tf_op jit(solution)/shard_map/ppermute | solution.py:103
  72.1 0.1 add.230
  72.2 2.5 %collective-permute-start.13 = (f32[128,512]{1,0:T(8,128)S(1)}, f32[128,512]{1,0:T(8,128)S(1)}, u32[]{:S(2)}, u32[]{:S(2)}) collective-permute-start(f32[128,512]{1,0:T(8,128)S(1)} %get-tuple-element.19), channel_id=1, source_target_pairs={{0,16},{16,0},{32,48},{48,32},{64,80},{80,64},{96,112},{112,96},{1... | collective-permute-start | bytes 786440 | tf_op jit(solution)/shard_map/ppermute | solution.py:108
  74.7 1.4 %fusion.30 = f32[256,512]{1,0:T(8,128)S(1)} fusion(bf16[18,256,512]{2,1,0:T(8,128)(2,1)S(1)} %bitcast.54, bf16[18,1024,256]{2,1,0:T(8,128)(2,1)S(1)} %bitcast.48, s32[]{:T(128)S(6)} %select_n.182), kind=kOutput, calls=%fused_computation.23 | convolution fusion | flops 1207959552 | bytes 7602180 | tf_op jit(solution)/shard_map/rpt,rtn->pn/dot_general | solution.py:91
  76.1 5.6 %collective-permute-done.8 = f32[256,512]{1,0:T(8,128)S(1)} collective-permute-done((f32[256,512]{1,0:T(8,128)S(1)}, f32[256,512]{1,0:T(8,128)S(1)}, u32[]{:S(2)}, u32[]{:S(2)}) %collective-permute-start.8) | collective-permute-done | bytes 524320 | tf_op jit(solution)/shard_map/ppermute | solution.py:103
  81.7 0.1 add.217
  81.8 2.5 %collective-permute-start.9 = (f32[128,512]{1,0:T(8,128)S(1)}, f32[128,512]{1,0:T(8,128)S(1)}, u32[]{:S(2)}, u32[]{:S(2)}) collective-permute-start(f32[128,512]{1,0:T(8,128)S(1)} %get-tuple-element.17), channel_id=1, source_target_pairs={{0,16},{16,0},{32,48},{48,32},{64,80},{80,64},{96,112},{112,96},{1... | collective-permute-start | bytes 786440 | tf_op jit(solution)/shard_map/ppermute | solution.py:108
  84.4 0.4 rev.15
  84.7 0.4 rev.13
  85.1 0.0 collective-permute-done.13
  85.1 0.4 rev.16
  85.6 4.2 %collective-permute-done.9 = f32[128,512]{1,0:T(8,128)S(1)} collective-permute-done((f32[128,512]{1,0:T(8,128)S(1)}, f32[128,512]{1,0:T(8,128)S(1)}, u32[]{:S(2)}, u32[]{:S(2)}) %collective-permute-start.9) | collective-permute-done | bytes 262176 | tf_op jit(solution)/shard_map/ppermute | solution.py:108
  89.8 0.4 rev.14
  90.2 1.2 %copy.10 = f32[128,2,512]{2,1,0:T(2,128)} copy(f32[128,2,512]{2,0,1:T(8,128)S(1)} %pad_maximum_fusion) | data formatting | bytes 1048576 | tf_op jit(solution)/shard_map/stack | solution.py:110
  (27 shorter events, 0.3 us)
Async XLA Ops:
  0.0 4.0 %collective-permute-start = (bf16[2,6,3,1024]{3,0,2,1:T(2,128)(2,1)}, bf16[2,6,3,1024]{3,0,2,1:T(2,128)(2,1)S(1)}, u32[]{:S(2)}, u32[]{:S(2)}) collective-permute-start(bf16[2,6,3,1024]{3,0,2,1:T(2,128)(2,1)} %bitcast.36), channel_id=1, source_target_pairs={{0,3},{1,0},{2,1},{3,2},{4,7},{5,4},{6,5},{7,6},{8,11},{9,8},{10,9... | collective-permute-start | bytes 221192 | tf_op jit(solution)/shard_map/ppermute | solution.py:26
  1.0 5.5 %collective-permute-start.1 = (bf16[2,6,3,1024]{3,0,2,1:T(2,128)(2,1)}, bf16[2,6,3,1024]{3,0,2,1:T(2,128)(2,1)S(1)}, u32[]{:S(2)}, u32[]{:S(2)}) collective-permute-start(bf16[2,6,3,1024]{3,0,2,1:T(2,128)(2,1)} %bitcast.37), channel_id=1, source_target_pairs={{0,2},{1,3},{2,0},{3,1},{4,6},{5,7},{6,4},{7,5},{8,10},{9,11},{10,... | collective-permute-start | bytes 221192 | tf_op jit(solution)/shard_map/ppermute | solution.py:26
  1.6 4.9 %collective-permute-start.2 = (bf16[2,6,3,1024]{3,0,2,1:T(2,128)(2,1)}, bf16[2,6,3,1024]{3,0,2,1:T(2,128)(2,1)S(1)}, u32[]{:S(2)}, u32[]{:S(2)}) collective-permute-start(bf16[2,6,3,1024]{3,0,2,1:T(2,128)(2,1)} %bitcast.38), channel_id=1, source_target_pairs={{0,1},{1,2},{2,3},{3,0},{4,5},{5,6},{6,7},{7,4},{8,9},{9,10},{10,1... | collective-permute-start | bytes 221192 | tf_op jit(solution)/shard_map/ppermute | solution.py:26
  7.6 5.9 %collective-permute-start.3 = (bf16[2,6,3,1024]{3,0,2,1:T(2,128)(2,1)S(1)}, bf16[2,6,3,1024]{3,0,2,1:T(2,128)(2,1)S(1)}, u32[]{:S(2)}, u32[]{:S(2)}) collective-permute-start(bf16[2,6,3,1024]{3,0,2,1:T(2,128)(2,1)S(1)} %broadcast_select_fusion.4), channel_id=1, source_target_pairs={{0,12},{1,13},{2,14},{3,15},{4,0},{5,1},{6,2},{7,3},{8,4},{9,5},{1... | collective-permute-start | bytes 221192 | tf_op jit(solution)/shard_map/ppermute | solution.py:26
  10.7 5.9 %collective-permute-start.4 = (bf16[2,6,3,1024]{3,0,2,1:T(2,128)(2,1)S(1)}, bf16[2,6,3,1024]{3,0,2,1:T(2,128)(2,1)S(1)}, u32[]{:S(2)}, u32[]{:S(2)}) collective-permute-start(bf16[2,6,3,1024]{3,0,2,1:T(2,128)(2,1)S(1)} %broadcast_select_fusion.4), channel_id=1, source_target_pairs={{0,8},{1,9},{2,10},{3,11},{4,12},{5,13},{6,14},{7,15},{8,0},{9,1},... | collective-permute-start | bytes 221192 | tf_op jit(solution)/shard_map/ppermute | solution.py:26
  11.3 6.0 %collective-permute-start.5 = (bf16[2,6,3,1024]{3,0,2,1:T(2,128)(2,1)S(1)}, bf16[2,6,3,1024]{3,0,2,1:T(2,128)(2,1)S(1)}, u32[]{:S(2)}, u32[]{:S(2)}) collective-permute-start(bf16[2,6,3,1024]{3,0,2,1:T(2,128)(2,1)S(1)} %broadcast_select_fusion.4), channel_id=1, source_target_pairs={{0,4},{1,5},{2,6},{3,7},{4,8},{5,9},{6,10},{7,11},{8,12},{9,13},{1... | collective-permute-start | bytes 221192 | tf_op jit(solution)/shard_map/ppermute | solution.py:26
  27.9 4.6 %slice-start.5 = ((s8[4718592]{0:T(1024)(128)(4,1)}), s8[4194304]{0:T(1024)(128)(4,1)S(1)}, s32[]{:S(2)}) async-start(s8[4718592]{0:T(1024)(128)(4,1)} %bitcast.57), calls=%async_computation.5 | async-start | bytes 8388608
  27.9 4.6 %slice-start.6 = ((s8[4718592]{0:T(1024)(128)(4,1)}), s8[524288]{0:T(1024)(128)(4,1)S(1)}, s32[]{:S(2)}) async-start(s8[4718592]{0:T(1024)(128)(4,1)} %bitcast.57), calls=%async_computation.6 | async-start | bytes 1048576
  35.5 13.2 %collective-permute-start.10 = (f32[256,512]{1,0:T(8,128)S(1)}, f32[256,512]{1,0:T(8,128)S(1)}, u32[]{:S(2)}, u32[]{:S(2)}) collective-permute-start(f32[256,512]{1,0:T(8,128)S(1)} %fusion.21), channel_id=1, source_target_pairs={{0,96},{16,112},{32,0},{48,16},{64,32},{80,48},{96,64},{112,80},{1... | collective-permute-start | bytes 1572872 | tf_op jit(solution)/shard_map/ppermute | solution.py:103
  39.6 17.6 %slice-start = ((s8[9437184]{0:T(1024)(128)(4,1)}), s8[4194304]{0:T(1024)(128)(4,1)S(1)}, s32[]{:S(2)}) async-start(s8[9437184]{0:T(1024)(128)(4,1)} %bitcast.43), calls=%async_computation | async-start | bytes 8388608
  39.6 17.6 %slice-start.1 = ((s8[9437184]{0:T(1024)(128)(4,1)}), s8[4194304]{0:T(1024)(128)(4,1)S(1)}, s32[]{:S(2)}) async-start(s8[9437184]{0:T(1024)(128)(4,1)} %bitcast.43), calls=%async_computation.1 | async-start | bytes 8388608
  44.2 14.5 %collective-permute-start.6 = (f32[256,512]{1,0:T(8,128)S(1)}, f32[256,512]{1,0:T(8,128)S(1)}, u32[]{:S(2)}, u32[]{:S(2)}) collective-permute-start(f32[256,512]{1,0:T(8,128)S(1)} %fusion.18), channel_id=1, source_target_pairs={{0,32},{16,48},{32,64},{48,80},{64,96},{80,112},{96,0},{112,16},{1... | collective-permute-start | bytes 1572872 | tf_op jit(solution)/shard_map/ppermute | solution.py:103
  48.8 8.5 %slice-start.3 = ((s8[4718592]{0:T(1024)(128)(4,1)}), s8[4194304]{0:T(1024)(128)(4,1)S(1)}, s32[]{:S(2)}) async-start(s8[4718592]{0:T(1024)(128)(4,1)} %bitcast.50), calls=%async_computation.3 | async-start | bytes 8388608
  48.8 8.4 %slice-start.2 = ((s8[9437184]{0:T(1024)(128)(4,1)}), s8[1048576]{0:T(1024)(128)(4,1)S(1)}, s32[]{:S(2)}) async-start(s8[9437184]{0:T(1024)(128)(4,1)} %bitcast.43), calls=%async_computation.2 | async-start | bytes 2097152
  48.9 8.4 %slice-start.4 = ((s8[4718592]{0:T(1024)(128)(4,1)}), s8[524288]{0:T(1024)(128)(4,1)S(1)}, s32[]{:S(2)}) async-start(s8[4718592]{0:T(1024)(128)(4,1)} %bitcast.50), calls=%async_computation.4 | async-start | bytes 1048576
  48.9 12.0 %collective-permute-start.11 = (f32[256,512]{1,0:T(8,128)S(1)}, f32[256,512]{1,0:T(8,128)S(1)}, u32[]{:S(2)}, u32[]{:S(2)}) collective-permute-start(f32[256,512]{1,0:T(8,128)S(1)} %add.224), channel_id=1, source_target_pairs={{0,96},{16,112},{32,0},{48,16},{64,32},{80,48},{96,64},{112,80},{1... | collective-permute-start | bytes 1572872 | tf_op jit(solution)/shard_map/ppermute | solution.py:103
  52.6 12.1 %slice-start.7 = ((s8[4718592]{0:T(1024)(128)(4,1)}), s8[4194304]{0:T(1024)(128)(4,1)S(1)}, s32[]{:S(2)}) async-start(s8[4718592]{0:T(1024)(128)(4,1)} %bitcast.60), calls=%async_computation.7 | async-start | bytes 8388608
  57.3 7.4 %slice-start.8 = ((s8[4718592]{0:T(1024)(128)(4,1)}), s8[524288]{0:T(1024)(128)(4,1)S(1)}, s32[]{:S(2)}) async-start(s8[4718592]{0:T(1024)(128)(4,1)} %bitcast.60), calls=%async_computation.8 | async-start | bytes 1048576
  58.8 12.0 %collective-permute-start.7 = (f32[256,512]{1,0:T(8,128)S(1)}, f32[256,512]{1,0:T(8,128)S(1)}, u32[]{:S(2)}, u32[]{:S(2)}) collective-permute-start(f32[256,512]{1,0:T(8,128)S(1)} %add.211), channel_id=1, source_target_pairs={{0,32},{16,48},{32,64},{48,80},{64,96},{80,112},{96,0},{112,16},{1... | collective-permute-start | bytes 1572872 | tf_op jit(solution)/shard_map/ppermute | solution.py:103
  60.9 11.2 %collective-permute-start.12 = (f32[256,512]{1,0:T(8,128)S(1)}, f32[256,512]{1,0:T(8,128)S(1)}, u32[]{:S(2)}, u32[]{:S(2)}) collective-permute-start(f32[256,512]{1,0:T(8,128)S(1)} %add.227), channel_id=1, source_target_pairs={{0,96},{16,112},{32,0},{48,16},{64,32},{80,48},{96,64},{112,80},{1... | collective-permute-start | bytes 1572872 | tf_op jit(solution)/shard_map/ppermute | solution.py:103
  70.8 10.8 %collective-permute-start.8 = (f32[256,512]{1,0:T(8,128)S(1)}, f32[256,512]{1,0:T(8,128)S(1)}, u32[]{:S(2)}, u32[]{:S(2)}) collective-permute-start(f32[256,512]{1,0:T(8,128)S(1)} %add.214), channel_id=1, source_target_pairs={{0,32},{16,48},{32,64},{48,80},{64,96},{80,112},{96,0},{112,16},{1... | collective-permute-start | bytes 1572872 | tf_op jit(solution)/shard_map/ppermute | solution.py:103
  72.2 12.9 %collective-permute-start.13 = (f32[128,512]{1,0:T(8,128)S(1)}, f32[128,512]{1,0:T(8,128)S(1)}, u32[]{:S(2)}, u32[]{:S(2)}) collective-permute-start(f32[128,512]{1,0:T(8,128)S(1)} %get-tuple-element.19), channel_id=1, source_target_pairs={{0,16},{16,0},{32,48},{48,32},{64,80},{80,64},{96,112},{112,96},{1... | collective-permute-start | bytes 786440 | tf_op jit(solution)/shard_map/ppermute | solution.py:108
  81.8 8.0 %collective-permute-start.9 = (f32[128,512]{1,0:T(8,128)S(1)}, f32[128,512]{1,0:T(8,128)S(1)}, u32[]{:S(2)}, u32[]{:S(2)}) collective-permute-start(f32[128,512]{1,0:T(8,128)S(1)} %get-tuple-element.17), channel_id=1, source_target_pairs={{0,16},{16,0},{32,48},{48,32},{64,80},{80,64},{96,112},{112,96},{1... | collective-permute-start | bytes 786440 | tf_op jit(solution)/shard_map/ppermute | solution.py:108

commit v12 on v11

--- a/solution.py
+++ b/solution.py
@@ -86,25 +86,34 @@
     quarter = point_rows // zs
     block = quarter // xs
 
-    def piece(band, c):
-        g = lax.dynamic_slice_in_dim(green_t, c * quarter, quarter, 1)
+    def piece(band, c, src=None):
+        g = lax.dynamic_slice_in_dim(green_t if src is None else src, c * quarter, quarter, 1)
         return jnp.einsum("rpt,rtn->pn", g, band.reshape(rows, NT, LAGS), preferred_element_type=jnp.float32)
 
     def ring_perm(step):
         return [(i, ((i // xs + step) % zs) * xs + i % xs) for i in range(size)]
 
     steps = (1, zs - 1)
-    firsts = lax.optimization_barrier(tuple(piece(bands[e], (z + zs - st) % zs) for e, st in enumerate(steps)))
+    g = green_t
+
+    def ordered(e, c, g):
+        return lax.optimization_barrier((piece(bands[e], c, g), green_t))
+
+    accs, gots = [], []
+    for e, step in enumerate(steps):
+        acc, g = ordered(e, (z + zs - step) % zs, g)
+        accs.append(acc)
+        gots.append(lax.ppermute(acc, "sens", ring_perm(step)))
+    for k in range(zs - 1):
+        for e, step in enumerate(steps):
+            part, g = ordered(e, (z + 4 * zs - step * (k + 2)) % zs, g)
+            accs[e] = gots[e] + part
+            if k < zs - 2:
+                gots[e] = lax.ppermute(accs[e], "sens", ring_perm(step))
     outs = []
-    for e, step in zip(range(EV), steps):
-        band = bands[e]
-        acc = firsts[e]
-        for k in range(zs - 1):
-            got = lax.ppermute(acc, "sens", ring_perm(step))
-            part = lax.optimization_barrier(piece(band, (z + 4 * zs - step * (k + 2)) % zs))
-            acc = got + part
-        theirs = lax.dynamic_slice_in_dim(acc, (1 - xh) * block, block, 0)
-        kept = lax.dynamic_slice_in_dim(acc, xh * block, block, 0)
+    for e in range(EV):
+        theirs = lax.dynamic_slice_in_dim(accs[e], (1 - xh) * block, block, 0)
+        kept = lax.dynamic_slice_in_dim(accs[e], xh * block, block, 0)
         got = lax.ppermute(theirs, "sens", [(i, i ^ 1) for i in range(size)])
         outs.append(jnp.flip(kept, axis=-1) + jnp.flip(got, axis=-1))
     return jnp.stack(outs, axis=1)

time: 91.7 us -> 86.7 us (0.945)
  matrix products: 22.5 us -> 18.6 us
  waiting for transfers between devices: 26.9 us -> 24.7 us
    dot_general x8, matrix products: 22.2 us -> 18.3 us  [piece(): jnp.einsum('rpt,rtn->pn', g, band.reshape(rows, NT, LAGS), preferred_elem...]
    ppermute x6, waiting for transfers between devices: 16.4 us -> 14.2 us  [the longest x4 8.73 us: local(): gots[e] = lax.ppermute(accs[e], 'sens', ring_perm(step))]
  transfers between devices with their start and end apart: 14 -> 14, of which waited for: 9 -> 11; matrix products, arithmetic and copies ran while one was open for 22% -> 22% of each run, Pallas kernels for 0% -> 0%
where the time goes in v12:
time: 86.7 us; the launch traced here: 86.5 us
  waiting for transfers between devices  24.7 us (28%)
  starting transfers between devices  24.1 us (28%)
  matrix products  18.6 us (21%)
  Pallas kernels  9.12 us (11%)
  local copies, waits for them, and re-layouts  5.25 us (6%)
  other arithmetic  4.56 us (5%)
    dot_general x8, matrix products, piece(): jnp.einsum('rpt,rtn->pn', g, band.reshape(rows, NT, LAGS), preferred_elem...  18.3 us
    pallas_call x1, Pallas kernels, toeplitz_reversed(): pl.pallas_call(_toeplitz_kernel, in_specs=[pl.BlockSpec(memory_space=pltp...  9.12 us
    ppermute x4, waiting for transfers between devices, local(): gots[e] = lax.ppermute(accs[e], 'sens', ring_perm(step))  8.73 us
    ppermute x4, starting transfers between devices, local(): gots[e] = lax.ppermute(accs[e], 'sens', ring_perm(step))  7.72 us
    ppermute x6, starting transfers between devices, from_owners(): got = lax.ppermute(x, axis, perm)  6.49 us
    ppermute x6, waiting for transfers between devices, from_owners(): got = lax.ppermute(x, axis, perm)  6.27 us
    ppermute x2, waiting for transfers between devices, local(): gots.append(lax.ppermute(acc, 'sens', ring_perm(step)))  5.43 us
    ppermute x2, starting transfers between devices, local(): gots.append(lax.ppermute(acc, 'sens', ring_perm(step)))  4.93 us
  transfers between devices with their start and end apart: 14, of which 11 were waited for; matrix products, arithmetic and copies ran while one was open for 22% of the time, Pallas kernels for 0%

profile of v12, /device:TPU:0, one launch (start us, length us, event | category | flops | bytes accessed | tf_op | source)
XLA Modules:
  0.0 86.5 jit_solution(15681875047746414697)
XLA Ops:
  0.0 1.0 %collective-permute-start = (bf16[2,6,3,1024]{3,0,2,1:T(2,128)(2,1)}, bf16[2,6,3,1024]{3,0,2,1:T(2,128)(2,1)S(1)}, u32[]{:S(2)}, u32[]{:S(2)}) collective-permute-start(bf16[2,6,3,1024]{3,0,2,1:T(2,128)(2,1)} %bitcast.36), channel_id=1, source_target_pairs={{0,3},{1,0},{2,1},{3,2},{4,7},{5,4},{6,5},{7,6},{8,11},{9,8},{10,9... | collective-permute-start | bytes 221192 | tf_op jit(solution)/shard_map/ppermute | solution.py:26
  1.0 0.6 collective-permute-start.1
  1.6 0.2 collective-permute-start.2
  1.8 0.7 broadcast_add_fusion
  2.5 0.7 multiply_exponential_fusion
  3.2 0.7 broadcast_compare_fusion
  3.9 0.1 broadcast_in_dim.36
  4.0 0.1 sub.68
  4.0 0.0 collective-permute-done
  4.0 2.4 %collective-permute-done.1 = bf16[2,6,3,1024]{3,0,2,1:T(2,128)(2,1)S(1)} collective-permute-done((bf16[2,6,3,1024]{3,0,2,1:T(2,128)(2,1)}, bf16[2,6,3,1024]{3,0,2,1:T(2,128)(2,1)S(1)}, u32[]{:S(2)}, u32[]{:S(2)}) %collective-permute-start.1) | collective-permute-done | bytes 73760 | tf_op jit(solution)/shard_map/ppermute | solution.py:26
  6.5 0.0 collective-permute-done.2
  6.5 1.1 %broadcast_select_fusion.4 = bf16[2,6,3,1024]{3,0,2,1:T(2,128)(2,1)S(1)} fusion(bf16[2,6,3,1024]{3,0,2,1:T(2,128)(2,1)S(1)} %collective-permute-done, pred[2]{0:T(512)(128)(4,1)S(1)} %get-tuple-element.52, bf16[2,6,3,1024]{3,0,2,1:T(2,128)(2,1)S(1)} %collective-permute-done.1, pred[2]{0:T(512)(128)(4,1)S(1)} %get-tuple-element.51, ...), kind=kLoop, calls=%fused_computation.34 | loop fusion | flops 110592 | bytes 368646 | tf_op jit(solution)/shard_map/jit(_where)/select_n | solution.py:28
  7.6 3.1 %collective-permute-start.3 = (bf16[2,6,3,1024]{3,0,2,1:T(2,128)(2,1)S(1)}, bf16[2,6,3,1024]{3,0,2,1:T(2,128)(2,1)S(1)}, u32[]{:S(2)}, u32[]{:S(2)}) collective-permute-start(bf16[2,6,3,1024]{3,0,2,1:T(2,128)(2,1)S(1)} %broadcast_select_fusion.4), channel_id=1, source_target_pairs={{0,12},{1,13},{2,14},{3,15},{4,0},{5,1},{6,2},{7,3},{8,4},{9,5},{1... | collective-permute-start | bytes 221192 | tf_op jit(solution)/shard_map/ppermute | solution.py:26
  10.7 0.6 collective-permute-start.4
  11.3 1.0 %collective-permute-start.5 = (bf16[2,6,3,1024]{3,0,2,1:T(2,128)(2,1)S(1)}, bf16[2,6,3,1024]{3,0,2,1:T(2,128)(2,1)S(1)}, u32[]{:S(2)}, u32[]{:S(2)}) collective-permute-start(bf16[2,6,3,1024]{3,0,2,1:T(2,128)(2,1)S(1)} %broadcast_select_fusion.4), channel_id=1, source_target_pairs={{0,4},{1,5},{2,6},{3,7},{4,8},{5,9},{6,10},{7,11},{8,12},{9,13},{1... | collective-permute-start | bytes 221192 | tf_op jit(solution)/shard_map/ppermute | solution.py:26
  12.3 0.6 and_select_fusion.3.shift_ref
  12.8 0.1 copy.8
  12.9 0.6 reshape.42.weight_ref
  13.5 0.0 collective-permute-done.3
  13.5 3.1 %collective-permute-done.4 = bf16[2,6,3,1024]{3,0,2,1:T(2,128)(2,1)S(1)} collective-permute-done((bf16[2,6,3,1024]{3,0,2,1:T(2,128)(2,1)S(1)}, bf16[2,6,3,1024]{3,0,2,1:T(2,128)(2,1)S(1)}, u32[]{:S(2)}, u32[]{:S(2)}) %collective-permute-start.4) | collective-permute-done | bytes 73760 | tf_op jit(solution)/shard_map/ppermute | solution.py:26
  16.6 0.7 collective-permute-done.5
  17.3 0.2 broadcast_select_fusion.5
  17.6 0.1 reshape.43
  17.7 0.3 fusion
  18.0 0.8 reshape.44.rev_ref
  18.7 9.1 %shard_map.55 = (bf16[4608,512]{1,0:T(8,128)(2,1)}, bf16[4608,512]{1,0:T(8,128)(2,1)}) custom-call(s32[36]{0:T(128)} %and_select_fusion.3.shift_ref, f32[18]{0:T(128)} %reshape.42.weight_ref, f32[36,1,1024]{2,1,0:T(1,128)} %reshape.44.rev_ref), custom_call_target="tpu_custom_call" | custom-call | bytes 9437184 | tf_op jit(solution)/shard_map/pallas_call | solution.py:55
  27.9 4.6 %fusion.18 = f32[256,512]{1,0:T(8,128)S(1)} fusion(bf16[18,256,512]{2,1,0:T(8,128)(2,1)} %bitcast.53, bf16[18,1024,256]{2,1,0:T(8,128)(2,1)} %bitcast.39, s32[]{:T(128)S(6)} %select_n.155), kind=kOutput, calls=%fused_computation.19 | convolution fusion | flops 1207959552 | bytes 7602180 | tf_op jit(solution)/shard_map/rpt,rtn->pn/dot_general | solution.py:91
  32.5 2.0 %collective-permute-start.6 = (f32[256,512]{1,0:T(8,128)S(1)}, f32[256,512]{1,0:T(8,128)S(1)}, u32[]{:S(2)}, u32[]{:S(2)}) collective-permute-start(f32[256,512]{1,0:T(8,128)S(1)} %fusion.18), channel_id=1, source_target_pairs={{0,32},{16,48},{32,64},{48,80},{64,96},{80,112},{96,0},{112,16},{1... | collective-permute-start | bytes 1572872 | tf_op jit(solution)/shard_map/ppermute | solution.py:106
  34.5 3.1 %fusion.21 = f32[256,512]{1,0:T(8,128)S(1)} fusion(bf16[18,256,512]{2,1,0:T(8,128)(2,1)S(1)} %bitcast.49, bf16[18,1024,256]{2,1,0:T(8,128)(2,1)} %bitcast.40, s32[]{:T(128)S(6)} %select_n.176), kind=kOutput, calls=%fused_computation.20 | convolution fusion | flops 1207959552 | bytes 7602180 | tf_op jit(solution)/shard_map/rpt,rtn->pn/dot_general | solution.py:91
  37.6 3.7 %fusion.24 = f32[256,512]{1,0:T(8,128)S(1)} fusion(bf16[18,256,512]{2,1,0:T(8,128)(2,1)} %bitcast.54, bf16[18,1024,256]{2,1,0:T(8,128)(2,1)S(1)} %bitcast.43, s32[]{:T(128)S(6)} %select_n.178), kind=kOutput, calls=%fused_computation.21 | convolution fusion | flops 1207959552 | bytes 7602180 | tf_op jit(solution)/shard_map/rpt,rtn->pn/dot_general | solution.py:91
  41.3 2.9 %collective-permute-start.10 = (f32[256,512]{1,0:T(8,128)S(1)}, f32[256,512]{1,0:T(8,128)S(1)}, u32[]{:S(2)}, u32[]{:S(2)}) collective-permute-start(f32[256,512]{1,0:T(8,128)S(1)} %fusion.21), channel_id=1, source_target_pairs={{0,96},{16,112},{32,0},{48,16},{64,32},{80,48},{96,64},{112,80},{1... | collective-permute-start | bytes 1572872 | tf_op jit(solution)/shard_map/ppermute | solution.py:106
  44.3 2.1 %collective-permute-done.6 = f32[256,512]{1,0:T(8,128)S(1)} collective-permute-done((f32[256,512]{1,0:T(8,128)S(1)}, f32[256,512]{1,0:T(8,128)S(1)}, u32[]{:S(2)}, u32[]{:S(2)}) %collective-permute-start.6) | collective-permute-done | bytes 524320 | tf_op jit(solution)/shard_map/ppermute | solution.py:106
  46.4 0.1 add.211
  46.5 0.0 slice-start.4
  46.5 0.1 collective-permute-start.7
  46.6 1.4 %fusion.27 = f32[256,512]{1,0:T(8,128)S(1)} fusion(bf16[18,256,512]{2,1,0:T(8,128)(2,1)S(1)} %bitcast.50, bf16[18,1024,256]{2,1,0:T(8,128)(2,1)S(1)} %bitcast.44, s32[]{:T(128)S(6)} %select_n.180), kind=kOutput, calls=%fused_computation.22 | convolution fusion | flops 1207959552 | bytes 7602180 | tf_op jit(solution)/shard_map/rpt,rtn->pn/dot_general | solution.py:91
  48.0 0.6 slice-done.3
  48.6 0.1 slice-done.4
  48.7 1.4 %fusion.30 = f32[256,512]{1,0:T(8,128)S(1)} fusion(bf16[18,256,512]{2,1,0:T(8,128)(2,1)S(1)} %bitcast.57, bf16[18,1024,256]{2,1,0:T(8,128)(2,1)S(1)} %bitcast.45, s32[]{:T(128)S(6)} %select_n.182), kind=kOutput, calls=%fused_computation.23 | convolution fusion | flops 1207959552 | bytes 7602180 | tf_op jit(solution)/shard_map/rpt,rtn->pn/dot_general | solution.py:91
  50.1 3.3 %collective-permute-done.10 = f32[256,512]{1,0:T(8,128)S(1)} collective-permute-done((f32[256,512]{1,0:T(8,128)S(1)}, f32[256,512]{1,0:T(8,128)S(1)}, u32[]{:S(2)}, u32[]{:S(2)}) %collective-permute-start.10) | collective-permute-done | bytes 524320 | tf_op jit(solution)/shard_map/ppermute | solution.py:106
  53.4 0.1 add.226
  53.5 3.8 %collective-permute-start.11 = (f32[256,512]{1,0:T(8,128)S(1)}, f32[256,512]{1,0:T(8,128)S(1)}, u32[]{:S(2)}, u32[]{:S(2)}) collective-permute-start(f32[256,512]{1,0:T(8,128)S(1)} %add.226), channel_id=1, source_target_pairs={{0,96},{16,112},{32,0},{48,16},{64,32},{80,48},{96,64},{112,80},{1... | collective-permute-start | bytes 1572872 | tf_op jit(solution)/shard_map/ppermute | solution.py:112
  57.3 1.5 %collective-permute-done.7 = f32[256,512]{1,0:T(8,128)S(1)} collective-permute-done((f32[256,512]{1,0:T(8,128)S(1)}, f32[256,512]{1,0:T(8,128)S(1)}, u32[]{:S(2)}, u32[]{:S(2)}) %collective-permute-start.7) | collective-permute-done | bytes 524320 | tf_op jit(solution)/shard_map/ppermute | solution.py:112
  58.8 0.1 add.216
  58.8 0.1 collective-permute-start.8
  58.9 1.4 %fusion.33 = f32[256,512]{1,0:T(8,128)S(1)} fusion(bf16[18,256,512]{2,1,0:T(8,128)(2,1)S(1)} %bitcast.51, bf16[18,1024,256]{2,1,0:T(8,128)(2,1)S(1)} %bitcast.46, s32[]{:T(128)S(6)} %select_n.184), kind=kOutput, calls=%fused_computation.24 | convolution fusion | flops 1207959552 | bytes 7602180 | tf_op jit(solution)/shard_map/rpt,rtn->pn/dot_general | solution.py:91
  60.3 1.4 %fusion.36 = f32[256,512]{1,0:T(8,128)S(1)} fusion(bf16[18,256,512]{2,1,0:T(8,128)(2,1)S(1)} %bitcast.58, bf16[18,1024,256]{2,1,0:T(8,128)(2,1)S(1)} %bitcast.47, s32[]{:T(128)S(6)} %select_n.186), kind=kOutput, calls=%fused_computation.25 | convolution fusion | flops 1207959552 | bytes 7602180 | tf_op jit(solution)/shard_map/rpt,rtn->pn/dot_general | solution.py:91
  61.7 3.8 %collective-permute-done.11 = f32[256,512]{1,0:T(8,128)S(1)} collective-permute-done((f32[256,512]{1,0:T(8,128)S(1)}, f32[256,512]{1,0:T(8,128)S(1)}, u32[]{:S(2)}, u32[]{:S(2)}) %collective-permute-start.11) | collective-permute-done | bytes 524320 | tf_op jit(solution)/shard_map/ppermute | solution.py:112
  65.5 0.1 add.227
  65.5 3.8 %collective-permute-start.12 = (f32[256,512]{1,0:T(8,128)S(1)}, f32[256,512]{1,0:T(8,128)S(1)}, u32[]{:S(2)}, u32[]{:S(2)}) collective-permute-start(f32[256,512]{1,0:T(8,128)S(1)} %add.227), channel_id=1, source_target_pairs={{0,96},{16,112},{32,0},{48,16},{64,32},{80,48},{96,64},{112,80},{1... | collective-permute-start | bytes 1572872 | tf_op jit(solution)/shard_map/ppermute | solution.py:112
  69.3 0.8 collective-permute-done.8
  70.2 0.1 add.221
  70.3 2.4 %collective-permute-start.9 = (f32[128,512]{1,0:T(8,128)S(1)}, f32[128,512]{1,0:T(8,128)S(1)}, u32[]{:S(2)}, u32[]{:S(2)}) collective-permute-start(f32[128,512]{1,0:T(8,128)S(1)} %get-tuple-element.43), channel_id=1, source_target_pairs={{0,16},{16,0},{32,48},{48,32},{64,80},{80,64},{96,112},{112,96},{1... | collective-permute-start | bytes 786440 | tf_op jit(solution)/shard_map/ppermute | solution.py:117
  72.7 1.4 %fusion.39 = f32[256,512]{1,0:T(8,128)S(1)} fusion(bf16[18,256,512]{2,1,0:T(8,128)(2,1)S(1)} %bitcast.52, bf16[18,1024,256]{2,1,0:T(8,128)(2,1)S(1)} %bitcast.48, s32[]{:T(128)S(6)} %select_n.191), kind=kOutput, calls=%fused_computation.26 | convolution fusion | flops 1207959552 | bytes 7602180 | tf_op jit(solution)/shard_map/rpt,rtn->pn/dot_general | solution.py:91
  74.1 2.6 %collective-permute-done.12 = f32[256,512]{1,0:T(8,128)S(1)} collective-permute-done((f32[256,512]{1,0:T(8,128)S(1)}, f32[256,512]{1,0:T(8,128)S(1)}, u32[]{:S(2)}, u32[]{:S(2)}) %collective-permute-start.12) | collective-permute-done | bytes 524320 | tf_op jit(solution)/shard_map/ppermute | solution.py:112
  76.7 0.1 add.230
  76.8 2.5 %collective-permute-start.13 = (f32[128,512]{1,0:T(8,128)S(1)}, f32[128,512]{1,0:T(8,128)S(1)}, u32[]{:S(2)}, u32[]{:S(2)}) collective-permute-start(f32[128,512]{1,0:T(8,128)S(1)} %get-tuple-element.45), channel_id=1, source_target_pairs={{0,16},{16,0},{32,48},{48,32},{64,80},{80,64},{96,112},{112,96},{1... | collective-permute-start | bytes 786440 | tf_op jit(solution)/shard_map/ppermute | solution.py:117
  79.4 0.4 rev.13
  79.7 0.4 rev.15
  80.1 0.4 collective-permute-done.9
  80.5 0.4 rev.14
  80.9 3.9 %collective-permute-done.13 = f32[128,512]{1,0:T(8,128)S(1)} collective-permute-done((f32[128,512]{1,0:T(8,128)S(1)}, f32[128,512]{1,0:T(8,128)S(1)}, u32[]{:S(2)}, u32[]{:S(2)}) %collective-permute-start.13) | collective-permute-done | bytes 262176 | tf_op jit(solution)/shard_map/ppermute | solution.py:117
  84.8 0.4 rev.16
  85.3 1.2 %copy.10 = f32[128,2,512]{2,1,0:T(2,128)} copy(f32[128,2,512]{2,0,1:T(8,128)S(1)} %pad_maximum_fusion) | data formatting | bytes 1048576 | tf_op jit(solution)/shard_map/stack | solution.py:119
  (19 shorter events, 0.3 us)
Async XLA Ops:
  0.0 4.0 %collective-permute-start = (bf16[2,6,3,1024]{3,0,2,1:T(2,128)(2,1)}, bf16[2,6,3,1024]{3,0,2,1:T(2,128)(2,1)S(1)}, u32[]{:S(2)}, u32[]{:S(2)}) collective-permute-start(bf16[2,6,3,1024]{3,0,2,1:T(2,128)(2,1)} %bitcast.36), channel_id=1, source_target_pairs={{0,3},{1,0},{2,1},{3,2},{4,7},{5,4},{6,5},{7,6},{8,11},{9,8},{10,9... | collective-permute-start | bytes 221192 | tf_op jit(solution)/shard_map/ppermute | solution.py:26
  1.0 5.5 %collective-permute-start.1 = (bf16[2,6,3,1024]{3,0,2,1:T(2,128)(2,1)}, bf16[2,6,3,1024]{3,0,2,1:T(2,128)(2,1)S(1)}, u32[]{:S(2)}, u32[]{:S(2)}) collective-permute-start(bf16[2,6,3,1024]{3,0,2,1:T(2,128)(2,1)} %bitcast.37), channel_id=1, source_target_pairs={{0,2},{1,3},{2,0},{3,1},{4,6},{5,7},{6,4},{7,5},{8,10},{9,11},{10,... | collective-permute-start | bytes 221192 | tf_op jit(solution)/shard_map/ppermute | solution.py:26
  1.6 4.9 %collective-permute-start.2 = (bf16[2,6,3,1024]{3,0,2,1:T(2,128)(2,1)}, bf16[2,6,3,1024]{3,0,2,1:T(2,128)(2,1)S(1)}, u32[]{:S(2)}, u32[]{:S(2)}) collective-permute-start(bf16[2,6,3,1024]{3,0,2,1:T(2,128)(2,1)} %bitcast.38), channel_id=1, source_target_pairs={{0,1},{1,2},{2,3},{3,0},{4,5},{5,6},{6,7},{7,4},{8,9},{9,10},{10,1... | collective-permute-start | bytes 221192 | tf_op jit(solution)/shard_map/ppermute | solution.py:26
  7.6 5.9 %collective-permute-start.3 = (bf16[2,6,3,1024]{3,0,2,1:T(2,128)(2,1)S(1)}, bf16[2,6,3,1024]{3,0,2,1:T(2,128)(2,1)S(1)}, u32[]{:S(2)}, u32[]{:S(2)}) collective-permute-start(bf16[2,6,3,1024]{3,0,2,1:T(2,128)(2,1)S(1)} %broadcast_select_fusion.4), channel_id=1, source_target_pairs={{0,12},{1,13},{2,14},{3,15},{4,0},{5,1},{6,2},{7,3},{8,4},{9,5},{1... | collective-permute-start | bytes 221192 | tf_op jit(solution)/shard_map/ppermute | solution.py:26
  10.7 5.9 %collective-permute-start.4 = (bf16[2,6,3,1024]{3,0,2,1:T(2,128)(2,1)S(1)}, bf16[2,6,3,1024]{3,0,2,1:T(2,128)(2,1)S(1)}, u32[]{:S(2)}, u32[]{:S(2)}) collective-permute-start(bf16[2,6,3,1024]{3,0,2,1:T(2,128)(2,1)S(1)} %broadcast_select_fusion.4), channel_id=1, source_target_pairs={{0,8},{1,9},{2,10},{3,11},{4,12},{5,13},{6,14},{7,15},{8,0},{9,1},... | collective-permute-start | bytes 221192 | tf_op jit(solution)/shard_map/ppermute | solution.py:26
  11.3 6.0 %collective-permute-start.5 = (bf16[2,6,3,1024]{3,0,2,1:T(2,128)(2,1)S(1)}, bf16[2,6,3,1024]{3,0,2,1:T(2,128)(2,1)S(1)}, u32[]{:S(2)}, u32[]{:S(2)}) collective-permute-start(bf16[2,6,3,1024]{3,0,2,1:T(2,128)(2,1)S(1)} %broadcast_select_fusion.4), channel_id=1, source_target_pairs={{0,4},{1,5},{2,6},{3,7},{4,8},{5,9},{6,10},{7,11},{8,12},{9,13},{1... | collective-permute-start | bytes 221192 | tf_op jit(solution)/shard_map/ppermute | solution.py:26
  27.9 6.6 %copy-start = (bf16[4608,512]{1,0:T(8,128)(2,1)S(1)}, bf16[4608,512]{1,0:T(8,128)(2,1)}, u32[]{:S(2)}) copy-start(bf16[4608,512]{1,0:T(8,128)(2,1)} %get-tuple-element.25) | copy-start | bytes 14155780
  27.9 9.7 %slice-start = ((s8[9437184]{0:T(1024)(128)(4,1)}), s8[4194304]{0:T(1024)(128)(4,1)S(1)}, s32[]{:S(2)}) async-start(s8[9437184]{0:T(1024)(128)(4,1)} %bitcast.41), calls=%async_computation | async-start | bytes 8388608
  27.9 9.7 %slice-start.1 = ((s8[9437184]{0:T(1024)(128)(4,1)}), s8[4194304]{0:T(1024)(128)(4,1)S(1)}, s32[]{:S(2)}) async-start(s8[9437184]{0:T(1024)(128)(4,1)} %bitcast.41), calls=%async_computation.1 | async-start | bytes 8388608
  32.5 14.0 %collective-permute-start.6 = (f32[256,512]{1,0:T(8,128)S(1)}, f32[256,512]{1,0:T(8,128)S(1)}, u32[]{:S(2)}, u32[]{:S(2)}) collective-permute-start(f32[256,512]{1,0:T(8,128)S(1)} %fusion.18), channel_id=1, source_target_pairs={{0,32},{16,48},{32,64},{48,80},{64,96},{80,112},{96,0},{112,16},{1... | collective-permute-start | bytes 1572872 | tf_op jit(solution)/shard_map/ppermute | solution.py:106
  34.5 3.2 %slice-start.2 = ((s8[9437184]{0:T(1024)(128)(4,1)}), s8[1048576]{0:T(1024)(128)(4,1)S(1)}, s32[]{:S(2)}) async-start(s8[9437184]{0:T(1024)(128)(4,1)} %bitcast.41), calls=%async_computation.2 | async-start | bytes 2097152
  41.3 12.1 %collective-permute-start.10 = (f32[256,512]{1,0:T(8,128)S(1)}, f32[256,512]{1,0:T(8,128)S(1)}, u32[]{:S(2)}, u32[]{:S(2)}) collective-permute-start(f32[256,512]{1,0:T(8,128)S(1)} %fusion.21), channel_id=1, source_target_pairs={{0,96},{16,112},{32,0},{48,16},{64,32},{80,48},{96,64},{112,80},{1... | collective-permute-start | bytes 1572872 | tf_op jit(solution)/shard_map/ppermute | solution.py:106
  46.4 2.2 %slice-start.3 = ((s8[4718592]{0:T(1024)(128)(4,1)}), s8[4194304]{0:T(1024)(128)(4,1)S(1)}, s32[]{:S(2)}) async-start(s8[4718592]{0:T(1024)(128)(4,1)} %bitcast.55), calls=%async_computation.3 | async-start | bytes 8388608
  46.5 2.2 %slice-start.4 = ((s8[4718592]{0:T(1024)(128)(4,1)}), s8[524288]{0:T(1024)(128)(4,1)S(1)}, s32[]{:S(2)}) async-start(s8[4718592]{0:T(1024)(128)(4,1)} %bitcast.55), calls=%async_computation.4 | async-start | bytes 1048576
  46.5 12.2 %collective-permute-start.7 = (f32[256,512]{1,0:T(8,128)S(1)}, f32[256,512]{1,0:T(8,128)S(1)}, u32[]{:S(2)}, u32[]{:S(2)}) collective-permute-start(f32[256,512]{1,0:T(8,128)S(1)} %add.211), channel_id=1, source_target_pairs={{0,32},{16,48},{32,64},{48,80},{64,96},{80,112},{96,0},{112,16},{1... | collective-permute-start | bytes 1572872 | tf_op jit(solution)/shard_map/ppermute | solution.py:112
  53.5 12.0 %collective-permute-start.11 = (f32[256,512]{1,0:T(8,128)S(1)}, f32[256,512]{1,0:T(8,128)S(1)}, u32[]{:S(2)}, u32[]{:S(2)}) collective-permute-start(f32[256,512]{1,0:T(8,128)S(1)} %add.226), channel_id=1, source_target_pairs={{0,96},{16,112},{32,0},{48,16},{64,32},{80,48},{96,64},{112,80},{1... | collective-permute-start | bytes 1572872 | tf_op jit(solution)/shard_map/ppermute | solution.py:112
  58.8 11.3 %collective-permute-start.8 = (f32[256,512]{1,0:T(8,128)S(1)}, f32[256,512]{1,0:T(8,128)S(1)}, u32[]{:S(2)}, u32[]{:S(2)}) collective-permute-start(f32[256,512]{1,0:T(8,128)S(1)} %add.216), channel_id=1, source_target_pairs={{0,32},{16,48},{32,64},{48,80},{64,96},{80,112},{96,0},{112,16},{1... | collective-permute-start | bytes 1572872 | tf_op jit(solution)/shard_map/ppermute | solution.py:112
  65.5 11.2 %collective-permute-start.12 = (f32[256,512]{1,0:T(8,128)S(1)}, f32[256,512]{1,0:T(8,128)S(1)}, u32[]{:S(2)}, u32[]{:S(2)}) collective-permute-start(f32[256,512]{1,0:T(8,128)S(1)} %add.227), channel_id=1, source_target_pairs={{0,96},{16,112},{32,0},{48,16},{64,32},{80,48},{96,64},{112,80},{1... | collective-permute-start | bytes 1572872 | tf_op jit(solution)/shard_map/ppermute | solution.py:112
  70.3 10.2 %collective-permute-start.9 = (f32[128,512]{1,0:T(8,128)S(1)}, f32[128,512]{1,0:T(8,128)S(1)}, u32[]{:S(2)}, u32[]{:S(2)}) collective-permute-start(f32[128,512]{1,0:T(8,128)S(1)} %get-tuple-element.43), channel_id=1, source_target_pairs={{0,16},{16,0},{32,48},{48,32},{64,80},{80,64},{96,112},{112,96},{1... | collective-permute-start | bytes 786440 | tf_op jit(solution)/shard_map/ppermute | solution.py:117
  76.8 8.0 %collective-permute-start.13 = (f32[128,512]{1,0:T(8,128)S(1)}, f32[128,512]{1,0:T(8,128)S(1)}, u32[]{:S(2)}, u32[]{:S(2)}) collective-permute-start(f32[128,512]{1,0:T(8,128)S(1)} %get-tuple-element.45), channel_id=1, source_target_pairs={{0,16},{16,0},{32,48},{48,32},{64,80},{80,64},{96,112},{112,96},{1... | collective-permute-start | bytes 786440 | tf_op jit(solution)/shard_map/ppermute | solution.py:117

commit v13 on v12

--- a/solution.py
+++ b/solution.py
@@ -10,6 +10,7 @@
 SAMPLES = 1024
 EV = 2
 WIDE = LAGS + NT
+HALF = LAGS // 2
 
 
 def from_owners(x, axis, roots, radix=4):
@@ -35,14 +36,17 @@
     rows = weight_ref.shape[0]
 
     def body(r, carry):
-        for e, out_ref in enumerate(out_refs):
+        for e in range(len(out_refs) // 2):
+            out_ref = out_refs[2 * e : 2 * e + 2]
             row = rev_ref[e * rows + r]
             row = pltpu.roll(row, shift_ref[e * rows + r], 1)
             row = (row * weight_ref[r]).astype(jnp.bfloat16).astype(jnp.float32)
             row = jnp.concatenate([row[:, :LAGS], row[:, SAMPLES - NT :]], axis=1)
             wide = jnp.broadcast_to(row, (NT, WIDE))
             band = pltpu.roll(wide, 0, 1, stride=1, stride_axis=0)
-            out_ref[pl.ds(pl.multiple_of(r * NT, NT), NT), :] = band[:, :LAGS].astype(out_ref.dtype)
+            at = pl.ds(pl.multiple_of(r * NT, NT), NT)
+            for h, ref in enumerate(out_ref):
+                ref[at, :] = band[:, h * HALF : (h + 1) * HALF].astype(ref.dtype)
         return carry
 
     lax.fori_loop(0, rows, body, 0)
@@ -51,7 +55,7 @@
 def toeplitz_reversed(rev, shifts, weights):
     rows = weights.shape[0]
     ev = rev.shape[0] // rows
-    band = jax.ShapeDtypeStruct((rows * NT, LAGS), jnp.bfloat16)
+    band = jax.ShapeDtypeStruct((rows * NT, HALF), jnp.bfloat16)
     return pl.pallas_call(
         _toeplitz_kernel,
         in_specs=[
@@ -59,8 +63,8 @@
             pl.BlockSpec(memory_space=pltpu.SMEM),
             pl.BlockSpec(memory_space=pltpu.VMEM),
         ],
-        out_specs=[pl.BlockSpec(memory_space=pltpu.VMEM)] * ev,
-        out_shape=[band] * ev,
+        out_specs=[pl.BlockSpec(memory_space=pltpu.VMEM)] * (2 * ev),
+        out_shape=[band] * (2 * ev),
         cost_estimate=pl.CostEstimate(flops=0, transcendentals=0, bytes_accessed=ev * rows * NT * LAGS * 2),
     )(shifts, weights, rev)
 
@@ -86,36 +90,66 @@
     quarter = point_rows // zs
     block = quarter // xs
 
-    def piece(band, c, src=None):
-        g = lax.dynamic_slice_in_dim(green_t if src is None else src, c * quarter, quarter, 1)
-        return jnp.einsum("rpt,rtn->pn", g, band.reshape(rows, NT, LAGS), preferred_element_type=jnp.float32)
+    def piece(band, start, count, src):
+        g = lax.dynamic_slice_in_dim(src, start, count, 1)
+        return jnp.einsum("rpt,rtn->pn", g, band.reshape(rows, NT, -1), preferred_element_type=jnp.float32)
+
+    def ordered(band, start, count, g):
+        return lax.optimization_barrier((piece(band, start, count, g), green_t))
 
     def ring_perm(step):
         return [(i, ((i // xs + step) % zs) * xs + i % xs) for i in range(size)]
 
+    swap = [(i, i ^ 1) for i in range(size)]
     steps = (1, zs - 1)
+
     g = green_t
-
-    def ordered(e, c, g):
-        return lax.optimization_barrier((piece(bands[e], c, g), green_t))
-
-    accs, gots = [], []
+    acc_z, got_z = [], []
     for e, step in enumerate(steps):
-        acc, g = ordered(e, (z + zs - step) % zs, g)
-        accs.append(acc)
-        gots.append(lax.ppermute(acc, "sens", ring_perm(step)))
+        acc, g = ordered(bands[2 * e], ((z + zs - step) % zs) * quarter, quarter, g)
+        acc_z.append(acc)
+        got_z.append(lax.ppermute(acc, "sens", ring_perm(step)))
+    got_x = []
+    for e in range(EV):
+        theirs = []
+        for q in range(zs):
+            part, g = ordered(bands[2 * e + 1], (q * xs + 1 - xh) * block, block, g)
+            theirs.append(part)
+        got_x.append(lax.ppermute(jnp.stack(theirs), "sens", swap))
+    for e, step in enumerate(steps):
+        part, g = ordered(bands[2 * e], ((z + 4 * zs - 2 * step) % zs) * quarter, quarter, g)
+        acc_z[e] = got_z[e] + part
+        got_z[e] = lax.ppermute(acc_z[e], "sens", ring_perm(step))
+    paired = []
+    for e in range(EV):
+        mine = []
+        for q in range(zs):
+            part, g = ordered(bands[2 * e + 1], (q * xs + xh) * block, block, g)
+            mine.append(part)
+        paired.append(jnp.stack(mine) + got_x[e])
+    acc_x, gx = [], []
+    for e, step in enumerate(steps):
+        acc = lax.dynamic_index_in_dim(paired[e], (z + zs - step) % zs, 0, keepdims=False)
+        acc_x.append(acc)
+        gx.append(lax.ppermute(acc, "sens", ring_perm(step)))
+    for k in range(1, zs - 1):
+        for e, step in enumerate(steps):
+            part, g = ordered(bands[2 * e], ((z + 4 * zs - step * (k + 2)) % zs) * quarter, quarter, g)
+            acc_z[e] = got_z[e] + part
+            if k < zs - 2:
+                got_z[e] = lax.ppermute(acc_z[e], "sens", ring_perm(step))
     for k in range(zs - 1):
         for e, step in enumerate(steps):
-            part, g = ordered(e, (z + 4 * zs - step * (k + 2)) % zs, g)
-            accs[e] = gots[e] + part
+            c = (z + 4 * zs - step * (k + 2)) % zs
+            acc_x[e] = gx[e] + lax.dynamic_index_in_dim(paired[e], c, 0, keepdims=False)
             if k < zs - 2:
-                gots[e] = lax.ppermute(accs[e], "sens", ring_perm(step))
+                gx[e] = lax.ppermute(acc_x[e], "sens", ring_perm(step))
     outs = []
     for e in range(EV):
-        theirs = lax.dynamic_slice_in_dim(accs[e], (1 - xh) * block, block, 0)
-        kept = lax.dynamic_slice_in_dim(accs[e], xh * block, block, 0)
-        got = lax.ppermute(theirs, "sens", [(i, i ^ 1) for i in range(size)])
-        outs.append(jnp.flip(kept, axis=-1) + jnp.flip(got, axis=-1))
+        theirs = lax.dynamic_slice_in_dim(acc_z[e], (1 - xh) * block, block, 0)
+        kept = lax.dynamic_slice_in_dim(acc_z[e], xh * block, block, 0)
+        first = kept + lax.ppermute(theirs, "sens", swap)
+        outs.append(jnp.flip(jnp.concatenate([first, acc_x[e]], axis=1), axis=-1))
     return jnp.stack(outs, axis=1)
 
 

time: 86.7 us -> 97.8 us (1.13)
  starting transfers between devices: 24.1 us -> 38.1 us
  waiting for transfers between devices: 24.7 us -> 17.8 us
  matrix products: 18.6 us -> 21.4 us
    ppermute x8 -> x16, starting transfers between devices: 17.6 us -> 31.6 us  [the longest x4 7.15 us: local(): gx[e] = lax.ppermute(acc_x[e], 'sens', ring_perm(step))]
    ppermute x8 -> x16, waiting for transfers between devices: 18.4 us -> 11.5 us  [the longest x2 2.89 us: local(): got_x.append(lax.ppermute(jnp.stack(theirs), 'sens', swap))]
    dot_general x8 -> x24, matrix products: 18.3 us -> 21.1 us  [piece(): jnp.einsum('rpt,rtn->pn', g, band.reshape(rows, NT, -1), preferred_elemen...]
    unnamed x12 -> x10, local copies, waits for them, and re-layouts: 0.77 us -> 2.4 us
  transfers between devices with their start and end apart: 14 -> 22, of which waited for: 11 -> 10; matrix products, arithmetic and copies ran while one was open for 22% -> 12% of each run, Pallas kernels for 0% -> 0%
where the time goes in v13:
time: 97.8 us; the launch traced here: 97.5 us
  starting transfers between devices  38.1 us (39%)
  matrix products  21.4 us (22%)
  waiting for transfers between devices  17.8 us (18%)
  Pallas kernels  9.05 us (9%)
  local copies, waits for them, and re-layouts  6.12 us (6%)
  other arithmetic  4.58 us (5%)
    dot_general x24, matrix products, piece(): jnp.einsum('rpt,rtn->pn', g, band.reshape(rows, NT, -1), preferred_elemen...  21.1 us
    pallas_call x1, Pallas kernels, toeplitz_reversed(): pl.pallas_call(_toeplitz_kernel, in_specs=[pl.BlockSpec(memory_space=pltp...  9.05 us
    ppermute x4, starting transfers between devices, local(): gx[e] = lax.ppermute(acc_x[e], 'sens', ring_perm(step))  7.15 us
    ppermute x4, starting transfers between devices, local(): got_z[e] = lax.ppermute(acc_z[e], 'sens', ring_perm(step))  7.04 us
    ppermute x6, starting transfers between devices, from_owners(): got = lax.ppermute(x, axis, perm)  6.49 us
    ppermute x6, waiting for transfers between devices, from_owners(): got = lax.ppermute(x, axis, perm)  6.27 us
    ppermute x2, starting transfers between devices, local(): gx.append(lax.ppermute(acc, 'sens', ring_perm(step)))  5.08 us
    ppermute x2, starting transfers between devices, local(): got_z.append(lax.ppermute(acc, 'sens', ring_perm(step)))  4.99 us
  transfers between devices with their start and end apart: 22, of which 10 were waited for; matrix products, arithmetic and copies ran while one was open for 12% of the time, Pallas kernels for 0%

profile of v13, /device:TPU:0, one launch (start us, length us, event | category | flops | bytes accessed | tf_op | source)
XLA Modules:
  0.0 97.5 jit_solution(15739695732937743774)
XLA Ops:
  0.0 1.0 %collective-permute-start = (bf16[2,6,3,1024]{3,0,2,1:T(2,128)(2,1)}, bf16[2,6,3,1024]{3,0,2,1:T(2,128)(2,1)S(1)}, u32[]{:S(2)}, u32[]{:S(2)}) collective-permute-start(bf16[2,6,3,1024]{3,0,2,1:T(2,128)(2,1)} %bitcast.182), channel_id=1, source_target_pairs={{0,3},{1,0},{2,1},{3,2},{4,7},{5,4},{6,5},{7,6},{8,11},{9,8},{10,9... | collective-permute-start | bytes 221192 | tf_op jit(solution)/shard_map/ppermute | solution.py:27
  1.0 0.6 collective-permute-start.1
  1.8 0.7 broadcast_add_fusion
  2.5 0.7 multiply_exponential_fusion
  3.2 0.7 broadcast_compare_fusion
  4.0 2.4 %collective-permute-done.1 = bf16[2,6,3,1024]{3,0,2,1:T(2,128)(2,1)S(1)} collective-permute-done((bf16[2,6,3,1024]{3,0,2,1:T(2,128)(2,1)}, bf16[2,6,3,1024]{3,0,2,1:T(2,128)(2,1)S(1)}, u32[]{:S(2)}, u32[]{:S(2)}) %collective-permute-start.1) | collective-permute-done | bytes 73760 | tf_op jit(solution)/shard_map/ppermute | solution.py:27
  6.5 1.1 %broadcast_select_fusion.4 = bf16[2,6,3,1024]{3,0,2,1:T(2,128)(2,1)S(1)} fusion(bf16[2,6,3,1024]{3,0,2,1:T(2,128)(2,1)S(1)} %collective-permute-done, pred[2]{0:T(512)(128)(4,1)S(1)} %get-tuple-element.116, bf16[2,6,3,1024]{3,0,2,1:T(2,128)(2,1)S(1)} %collective-permute-done.1, pred[2]{0:T(512)(128)(4,1)S(1)} %get-tuple-element.115, ...), kind=kLoop, calls=%fused_computation.86 | loop fusion | flops 110592 | bytes 368646 | tf_op jit(solution)/shard_map/jit(_where)/select_n | solution.py:29
  7.6 3.1 %collective-permute-start.3 = (bf16[2,6,3,1024]{3,0,2,1:T(2,128)(2,1)S(1)}, bf16[2,6,3,1024]{3,0,2,1:T(2,128)(2,1)S(1)}, u32[]{:S(2)}, u32[]{:S(2)}) collective-permute-start(bf16[2,6,3,1024]{3,0,2,1:T(2,128)(2,1)S(1)} %broadcast_select_fusion.4), channel_id=1, source_target_pairs={{0,12},{1,13},{2,14},{3,15},{4,0},{5,1},{6,2},{7,3},{8,4},{9,5},{1... | collective-permute-start | bytes 221192 | tf_op jit(solution)/shard_map/ppermute | solution.py:27
  10.7 0.6 collective-permute-start.4
  11.3 1.0 collective-permute-start.5
  12.3 0.6 and_select_fusion.3.shift_ref
  12.9 0.6 reshape.26.weight_ref
  13.5 3.1 %collective-permute-done.4 = bf16[2,6,3,1024]{3,0,2,1:T(2,128)(2,1)S(1)} collective-permute-done((bf16[2,6,3,1024]{3,0,2,1:T(2,128)(2,1)S(1)}, bf16[2,6,3,1024]{3,0,2,1:T(2,128)(2,1)S(1)}, u32[]{:S(2)}, u32[]{:S(2)}) %collective-permute-start.4) | collective-permute-done | bytes 73760 | tf_op jit(solution)/shard_map/ppermute | solution.py:27
  16.6 0.7 collective-permute-done.5
  18.0 0.8 reshape.28.rev_ref
  18.7 9.1 %shard_map.55 = (bf16[4608,256]{1,0:T(8,128)(2,1)}, bf16[4608,256]{1,0:T(8,128)(2,1)}, bf16[4608,256]{1,0:T(8,128)(2,1)}, bf16[4608,256]{1,0:T(8,128)(2,1)}) custom-call(s32[36]{0:T(128)} %and_select_fusion.3.shift_ref, f32[18]{0:T(128)} %reshape.26.weight_ref, f32[36,1,1024]{2,1,0:T(1,128)} %reshape.28.rev_ref), custom_call_target="tpu_custom_call" | custom-call | bytes 9437184 | tf_op jit(solution)/shard_map/pallas_call | solution.py:59
  27.8 3.3 %fusion.50 = f32[256,256]{1,0:T(8,128)S(1)} fusion(bf16[18,256,256]{2,1,0:T(8,128)(2,1)} %bitcast.160, bf16[18,1024,256]{2,1,0:T(8,128)(2,1)} %bitcast.116, s32[]{:T(128)S(6)} %select_n.228), kind=kOutput, calls=%fused_computation.51 | convolution fusion | flops 603979776 | bytes 4980740 | tf_op jit(solution)/shard_map/rpt,rtn->pn/dot_general | solution.py:95
  31.1 3.7 %fusion.53 = f32[256,256]{1,0:T(8,128)S(1)} fusion(bf16[18,256,256]{2,1,0:T(8,128)(2,1)} %bitcast.156, bf16[18,1024,256]{2,1,0:T(8,128)(2,1)} %bitcast.117, s32[]{:T(128)S(6)} %select_n.249), kind=kOutput, calls=%fused_computation.52 | convolution fusion | flops 603979776 | bytes 4980740 | tf_op jit(solution)/shard_map/rpt,rtn->pn/dot_general | solution.py:95
  34.9 2.3 %fusion.74 = f32[128,256]{1,0:T(8,128)S(1)} fusion(bf16[18,256,256]{2,1,0:T(8,128)(2,1)} %bitcast.148, bf16[18,1024,256]{2,1,0:T(8,128)(2,1)S(1)} %bitcast.118, s32[]{:T(128)S(6)} %select_n.251), kind=kOutput, calls=%fused_computation.59 | convolution fusion | flops 301989888 | bytes 3670020 | tf_op jit(solution)/shard_map/rpt,rtn->pn/dot_general | solution.py:95
  37.2 0.5 fusion.77
  37.7 0.5 fusion.80
  38.2 0.5 fusion.83
  38.7 1.2 %copy-done.1 = bf16[4608,256]{1,0:T(8,128)(2,1)S(1)} copy-done((bf16[4608,256]{1,0:T(8,128)(2,1)S(1)}, bf16[4608,256]{1,0:T(8,128)(2,1)}, u32[]{:S(2)}) %copy-start.1) | copy-done | bytes 2359320
  39.8 0.5 fusion.86
  40.3 0.5 fusion.89
  40.8 0.5 fusion.92
  41.3 0.5 fusion.95
  41.8 1.2 %copy-done.4 = bf16[4608,256]{1,0:T(8,128)(2,1)S(1)} copy-done((bf16[4608,256]{1,0:T(8,128)(2,1)S(1)}, bf16[4608,256]{1,0:T(8,128)(2,1)}, u32[]{:S(2)}) %copy-start.4) | copy-done | bytes 2359320
  43.0 0.8 fusion.56
  43.7 2.2 %collective-permute-start.6 = (f32[256,256]{1,0:T(8,128)S(1)}, f32[256,256]{1,0:T(8,128)S(1)}, u32[]{:S(2)}, u32[]{:S(2)}) collective-permute-start(f32[256,256]{1,0:T(8,128)S(1)} %fusion.50), channel_id=1, source_target_pairs={{0,32},{16,48},{32,64},{48,80},{64,96},{80,112},{96,0},{112,16},{1... | collective-permute-start | bytes 786440 | tf_op jit(solution)/shard_map/ppermute | solution.py:111
  45.9 0.8 fusion.59
  46.7 0.5 fusion.98
  47.2 0.5 fusion.101
  47.7 0.5 fusion.104
  48.2 0.5 fusion.107
  48.6 0.5 fusion.110
  49.1 0.5 fusion.113
  49.6 0.5 fusion.116
  50.1 0.5 fusion.119
  50.6 0.8 fusion.62
  51.4 0.8 fusion.65
  52.2 3.1 %collective-permute-start.10 = (f32[4,128,256]{2,1,0:T(8,128)S(1)}, f32[4,128,256]{2,1,0:T(8,128)S(1)}, u32[]{:S(2)}, u32[]{:S(2)}) collective-permute-start(f32[4,128,256]{2,1,0:T(8,128)S(1)} %pad_maximum_fusion), channel_id=1, source_target_pairs={{0,16},{16,0},{32,48},{48,32},{64,80},{80,64},{96,112},{112,96},{1... | collective-permute-start | bytes 1572872 | tf_op jit(solution)/shard_map/ppermute | solution.py:118
  55.3 0.8 fusion.68
  56.0 2.8 %collective-permute-start.14 = (f32[256,256]{1,0:T(8,128)S(1)}, f32[256,256]{1,0:T(8,128)S(1)}, u32[]{:S(2)}, u32[]{:S(2)}) collective-permute-start(f32[256,256]{1,0:T(8,128)S(1)} %fusion.53), channel_id=1, source_target_pairs={{0,96},{16,112},{32,0},{48,16},{64,32},{80,48},{96,64},{112,80},{1... | collective-permute-start | bytes 786440 | tf_op jit(solution)/shard_map/ppermute | solution.py:111
  58.9 0.6 collective-permute-start.18
  59.6 0.8 fusion.71
  60.4 2.7 %collective-permute-done.14 = f32[256,256]{1,0:T(8,128)S(1)} collective-permute-done((f32[256,256]{1,0:T(8,128)S(1)}, f32[256,256]{1,0:T(8,128)S(1)}, u32[]{:S(2)}, u32[]{:S(2)}) %collective-permute-start.14) | collective-permute-done | bytes 262176 | tf_op jit(solution)/shard_map/ppermute | solution.py:111
  63.1 3.4 %collective-permute-start.15 = (f32[256,256]{1,0:T(8,128)S(1)}, f32[256,256]{1,0:T(8,128)S(1)}, u32[]{:S(2)}, u32[]{:S(2)}) collective-permute-start(f32[256,256]{1,0:T(8,128)S(1)} %add.354), channel_id=1, source_target_pairs={{0,96},{16,112},{32,0},{48,16},{64,32},{80,48},{96,64},{112,80},{1... | collective-permute-start | bytes 786440 | tf_op jit(solution)/shard_map/ppermute | solution.py:122
  66.5 0.7 collective-permute-done.7
  67.3 1.3 %collective-permute-done.10 = f32[4,128,256]{2,1,0:T(8,128)S(1)} collective-permute-done((f32[4,128,256]{2,1,0:T(8,128)S(1)}, f32[4,128,256]{2,1,0:T(8,128)S(1)}, u32[]{:S(2)}, u32[]{:S(2)}) %collective-permute-start.10) | collective-permute-done | bytes 524320 | tf_op jit(solution)/shard_map/ppermute | solution.py:118
  68.7 2.0 %collective-permute-start.11 = (f32[128,256]{1,0:T(8,128)S(1)}, f32[128,256]{1,0:T(8,128)S(1)}, u32[]{:S(2)}, u32[]{:S(2)}) collective-permute-start(f32[128,256]{1,0:T(8,128)S(1)} %dynamic-slice_bitcast_fusion.1), channel_id=1, source_target_pairs={{0,32},{16,48},{32,64},{48,80},{64,96},{80,112},{96,0},{112,16},{1... | collective-permute-start | bytes 393224 | tf_op jit(solution)/shard_map/ppermute | solution.py:134
  70.7 0.5 collective-permute-done.15
  71.3 3.4 %collective-permute-start.16 = (f32[256,256]{1,0:T(8,128)S(1)}, f32[256,256]{1,0:T(8,128)S(1)}, u32[]{:S(2)}, u32[]{:S(2)}) collective-permute-start(f32[256,256]{1,0:T(8,128)S(1)} %add.355), channel_id=1, source_target_pairs={{0,96},{16,112},{32,0},{48,16},{64,32},{80,48},{96,64},{112,80},{1... | collective-permute-start | bytes 786440 | tf_op jit(solution)/shard_map/ppermute | solution.py:140
  74.7 1.6 %collective-permute-done.18 = f32[4,128,256]{2,1,0:T(8,128)S(1)} collective-permute-done((f32[4,128,256]{2,1,0:T(8,128)S(1)}, f32[4,128,256]{2,1,0:T(8,128)S(1)}, u32[]{:S(2)}, u32[]{:S(2)}) %collective-permute-start.18) | collective-permute-done | bytes 524320 | tf_op jit(solution)/shard_map/ppermute | solution.py:118
  76.4 3.1 %collective-permute-start.19 = (f32[128,256]{1,0:T(8,128)S(1)}, f32[128,256]{1,0:T(8,128)S(1)}, u32[]{:S(2)}, u32[]{:S(2)}) collective-permute-start(f32[128,256]{1,0:T(8,128)S(1)} %dynamic-slice_bitcast_fusion), channel_id=1, source_target_pairs={{0,96},{16,112},{32,0},{48,16},{64,32},{80,48},{96,64},{112,80},{1... | collective-permute-start | bytes 393224 | tf_op jit(solution)/shard_map/ppermute | solution.py:134
  79.6 2.4 %collective-permute-done.19 = f32[128,256]{1,0:T(8,128)S(1)} collective-permute-done((f32[128,256]{1,0:T(8,128)S(1)}, f32[128,256]{1,0:T(8,128)S(1)}, u32[]{:S(2)}, u32[]{:S(2)}) %collective-permute-start.19) | collective-permute-done | bytes 131104 | tf_op jit(solution)/shard_map/ppermute | solution.py:134
  82.1 3.7 %collective-permute-start.20 = (f32[128,256]{1,0:T(8,128)S(1)}, f32[128,256]{1,0:T(8,128)S(1)}, u32[]{:S(2)}, u32[]{:S(2)}) collective-permute-start(f32[128,256]{1,0:T(8,128)S(1)} %bitcast_add_fusion.2), channel_id=1, source_target_pairs={{0,96},{16,112},{32,0},{48,16},{64,32},{80,48},{96,64},{112,80},{1... | collective-permute-start | bytes 393224 | tf_op jit(solution)/shard_map/ppermute | solution.py:146
  85.9 3.2 %collective-permute-start.9 = (f32[128,256]{1,0:T(8,128)S(1)}, f32[128,256]{1,0:T(8,128)S(1)}, u32[]{:S(2)}, u32[]{:S(2)}) collective-permute-start(f32[128,256]{1,0:T(8,128)S(1)} %constant_dynamic-slice_fusion.1), channel_id=1, source_target_pairs={{0,16},{16,0},{32,48},{48,32},{64,80},{80,64},{96,112},{112,96},{1... | collective-permute-start | bytes 393224 | tf_op jit(solution)/shard_map/ppermute | solution.py:151
  89.3 0.5 collective-permute-start.17
  89.8 3.3 %collective-permute-start.21 = (f32[128,256]{1,0:T(8,128)S(1)}, f32[128,256]{1,0:T(8,128)S(1)}, u32[]{:S(2)}, u32[]{:S(2)}) collective-permute-start(f32[128,256]{1,0:T(8,128)S(1)} %bitcast_add_fusion.1), channel_id=1, source_target_pairs={{0,96},{16,112},{32,0},{48,16},{64,32},{80,48},{96,64},{112,80},{1... | collective-permute-start | bytes 393224 | tf_op jit(solution)/shard_map/ppermute | solution.py:146
  93.1 2.3 %collective-permute-done.13 = f32[128,256]{1,0:T(8,128)S(1)} collective-permute-done((f32[128,256]{1,0:T(8,128)S(1)}, f32[128,256]{1,0:T(8,128)S(1)}, u32[]{:S(2)}, u32[]{:S(2)}) %collective-permute-start.13) | collective-permute-done | bytes 131104 | tf_op jit(solution)/shard_map/ppermute | solution.py:146
  95.4 0.4 rev.7
  95.9 0.4 rev.8
  96.3 1.2 %copy.10 = f32[128,2,512]{2,1,0:T(2,128)} copy(f32[128,2,512]{2,0,1:T(8,128)S(1)} %pad_maximum_fusion.2) | data formatting | bytes 1048576 | tf_op jit(solution)/shard_map/stack | solution.py:153
  (59 shorter events, 2.2 us)
Async XLA Ops:
  0.0 4.0 %collective-permute-start = (bf16[2,6,3,1024]{3,0,2,1:T(2,128)(2,1)}, bf16[2,6,3,1024]{3,0,2,1:T(2,128)(2,1)S(1)}, u32[]{:S(2)}, u32[]{:S(2)}) collective-permute-start(bf16[2,6,3,1024]{3,0,2,1:T(2,128)(2,1)} %bitcast.182), channel_id=1, source_target_pairs={{0,3},{1,0},{2,1},{3,2},{4,7},{5,4},{6,5},{7,6},{8,11},{9,8},{10,9... | collective-permute-start | bytes 221192 | tf_op jit(solution)/shard_map/ppermute | solution.py:27
  1.0 5.5 %collective-permute-start.1 = (bf16[2,6,3,1024]{3,0,2,1:T(2,128)(2,1)}, bf16[2,6,3,1024]{3,0,2,1:T(2,128)(2,1)S(1)}, u32[]{:S(2)}, u32[]{:S(2)}) collective-permute-start(bf16[2,6,3,1024]{3,0,2,1:T(2,128)(2,1)} %bitcast.183), channel_id=1, source_target_pairs={{0,2},{1,3},{2,0},{3,1},{4,6},{5,7},{6,4},{7,5},{8,10},{9,11},{10,... | collective-permute-start | bytes 221192 | tf_op jit(solution)/shard_map/ppermute | solution.py:27
  1.6 4.9 %collective-permute-start.2 = (bf16[2,6,3,1024]{3,0,2,1:T(2,128)(2,1)}, bf16[2,6,3,1024]{3,0,2,1:T(2,128)(2,1)S(1)}, u32[]{:S(2)}, u32[]{:S(2)}) collective-permute-start(bf16[2,6,3,1024]{3,0,2,1:T(2,128)(2,1)} %bitcast.184), channel_id=1, source_target_pairs={{0,1},{1,2},{2,3},{3,0},{4,5},{5,6},{6,7},{7,4},{8,9},{9,10},{10,1... | collective-permute-start | bytes 221192 | tf_op jit(solution)/shard_map/ppermute | solution.py:27
  7.6 5.9 %collective-permute-start.3 = (bf16[2,6,3,1024]{3,0,2,1:T(2,128)(2,1)S(1)}, bf16[2,6,3,1024]{3,0,2,1:T(2,128)(2,1)S(1)}, u32[]{:S(2)}, u32[]{:S(2)}) collective-permute-start(bf16[2,6,3,1024]{3,0,2,1:T(2,128)(2,1)S(1)} %broadcast_select_fusion.4), channel_id=1, source_target_pairs={{0,12},{1,13},{2,14},{3,15},{4,0},{5,1},{6,2},{7,3},{8,4},{9,5},{1... | collective-permute-start | bytes 221192 | tf_op jit(solution)/shard_map/ppermute | solution.py:27
  10.7 5.9 %collective-permute-start.4 = (bf16[2,6,3,1024]{3,0,2,1:T(2,128)(2,1)S(1)}, bf16[2,6,3,1024]{3,0,2,1:T(2,128)(2,1)S(1)}, u32[]{:S(2)}, u32[]{:S(2)}) collective-permute-start(bf16[2,6,3,1024]{3,0,2,1:T(2,128)(2,1)S(1)} %broadcast_select_fusion.4), channel_id=1, source_target_pairs={{0,8},{1,9},{2,10},{3,11},{4,12},{5,13},{6,14},{7,15},{8,0},{9,1},... | collective-permute-start | bytes 221192 | tf_op jit(solution)/shard_map/ppermute | solution.py:27
  11.3 6.0 %collective-permute-start.5 = (bf16[2,6,3,1024]{3,0,2,1:T(2,128)(2,1)S(1)}, bf16[2,6,3,1024]{3,0,2,1:T(2,128)(2,1)S(1)}, u32[]{:S(2)}, u32[]{:S(2)}) collective-permute-start(bf16[2,6,3,1024]{3,0,2,1:T(2,128)(2,1)S(1)} %broadcast_select_fusion.4), channel_id=1, source_target_pairs={{0,4},{1,5},{2,6},{3,7},{4,8},{5,9},{6,10},{7,11},{8,12},{9,13},{1... | collective-permute-start | bytes 221192 | tf_op jit(solution)/shard_map/ppermute | solution.py:27
  27.8 7.1 %copy-start = (bf16[1024,6,3,256]{3,0,2,1:T(8,128)(2,1)S(1)}, bf16[1024,6,3,256]{3,0,2,1:T(8,128)(2,1)}, u32[]{:S(2)}) copy-start(bf16[1024,6,3,256]{3,0,2,1:T(8,128)(2,1)} %param.5) | copy-start | bytes 28311556
  34.8 2.4 %copy-start.2 = (bf16[4608,256]{1,0:T(8,128)(2,1)S(1)}, bf16[4608,256]{1,0:T(8,128)(2,1)}, u32[]{:S(2)}) copy-start(bf16[4608,256]{1,0:T(8,128)(2,1)} %get-tuple-element.61) | copy-start | bytes 7077892
  38.2 1.7 %copy-start.1 = (bf16[4608,256]{1,0:T(8,128)(2,1)S(1)}, bf16[4608,256]{1,0:T(8,128)(2,1)}, u32[]{:S(2)}) copy-start(bf16[4608,256]{1,0:T(8,128)(2,1)} %get-tuple-element.66) | copy-start | bytes 7077892
  41.3 1.7 %copy-start.4 = (bf16[4608,256]{1,0:T(8,128)(2,1)S(1)}, bf16[4608,256]{1,0:T(8,128)(2,1)}, u32[]{:S(2)}) copy-start(bf16[4608,256]{1,0:T(8,128)(2,1)} %get-tuple-element.56) | copy-start | bytes 7077892
  43.0 3.0 %copy-start.3 = (bf16[4608,256]{1,0:T(8,128)(2,1)S(1)}, bf16[4608,256]{1,0:T(8,128)(2,1)}, u32[]{:S(2)}) copy-start(bf16[4608,256]{1,0:T(8,128)(2,1)} %get-tuple-element.59) | copy-start | bytes 7077892
  43.7 15.8 %collective-permute-start.6 = (f32[256,256]{1,0:T(8,128)S(1)}, f32[256,256]{1,0:T(8,128)S(1)}, u32[]{:S(2)}, u32[]{:S(2)}) collective-permute-start(f32[256,256]{1,0:T(8,128)S(1)} %fusion.50), channel_id=1, source_target_pairs={{0,32},{16,48},{32,64},{48,80},{64,96},{80,112},{96,0},{112,16},{1... | collective-permute-start | bytes 786440 | tf_op jit(solution)/shard_map/ppermute | solution.py:111
  52.2 16.4 %collective-permute-start.10 = (f32[4,128,256]{2,1,0:T(8,128)S(1)}, f32[4,128,256]{2,1,0:T(8,128)S(1)}, u32[]{:S(2)}, u32[]{:S(2)}) collective-permute-start(f32[4,128,256]{2,1,0:T(8,128)S(1)} %pad_maximum_fusion), channel_id=1, source_target_pairs={{0,16},{16,0},{32,48},{48,32},{64,80},{80,64},{96,112},{112,96},{1... | collective-permute-start | bytes 1572872 | tf_op jit(solution)/shard_map/ppermute | solution.py:118
  56.0 7.0 %collective-permute-start.14 = (f32[256,256]{1,0:T(8,128)S(1)}, f32[256,256]{1,0:T(8,128)S(1)}, u32[]{:S(2)}, u32[]{:S(2)}) collective-permute-start(f32[256,256]{1,0:T(8,128)S(1)} %fusion.53), channel_id=1, source_target_pairs={{0,96},{16,112},{32,0},{48,16},{64,32},{80,48},{96,64},{112,80},{1... | collective-permute-start | bytes 786440 | tf_op jit(solution)/shard_map/ppermute | solution.py:111
  58.9 17.4 %collective-permute-start.18 = (f32[4,128,256]{2,1,0:T(8,128)S(1)}, f32[4,128,256]{2,1,0:T(8,128)S(1)}, u32[]{:S(2)}, u32[]{:S(2)}) collective-permute-start(f32[4,128,256]{2,1,0:T(8,128)S(1)} %pad_maximum_fusion.1), channel_id=1, source_target_pairs={{0,16},{16,0},{32,48},{48,32},{64,80},{80,64},{96,112},{112,96},{1... | collective-permute-start | bytes 1572872 | tf_op jit(solution)/shard_map/ppermute | solution.py:118
  59.6 7.7 %collective-permute-start.7 = (f32[256,256]{1,0:T(8,128)S(1)}, f32[256,256]{1,0:T(8,128)S(1)}, u32[]{:S(2)}, u32[]{:S(2)}) collective-permute-start(f32[256,256]{1,0:T(8,128)S(1)} %add.325), channel_id=1, source_target_pairs={{0,32},{16,48},{32,64},{48,80},{64,96},{80,112},{96,0},{112,16},{1... | collective-permute-start | bytes 786440 | tf_op jit(solution)/shard_map/ppermute | solution.py:122
  63.1 8.1 %collective-permute-start.15 = (f32[256,256]{1,0:T(8,128)S(1)}, f32[256,256]{1,0:T(8,128)S(1)}, u32[]{:S(2)}, u32[]{:S(2)}) collective-permute-start(f32[256,256]{1,0:T(8,128)S(1)} %add.354), channel_id=1, source_target_pairs={{0,96},{16,112},{32,0},{48,16},{64,32},{80,48},{96,64},{112,80},{1... | collective-permute-start | bytes 786440 | tf_op jit(solution)/shard_map/ppermute | solution.py:122
  67.2 18.6 %collective-permute-start.8 = (f32[256,256]{1,0:T(8,128)S(1)}, f32[256,256]{1,0:T(8,128)S(1)}, u32[]{:S(2)}, u32[]{:S(2)}) collective-permute-start(f32[256,256]{1,0:T(8,128)S(1)} %add.337), channel_id=1, source_target_pairs={{0,32},{16,48},{32,64},{48,80},{64,96},{80,112},{96,0},{112,16},{1... | collective-permute-start | bytes 786440 | tf_op jit(solution)/shard_map/ppermute | solution.py:140
  68.7 10.8 %collective-permute-start.11 = (f32[128,256]{1,0:T(8,128)S(1)}, f32[128,256]{1,0:T(8,128)S(1)}, u32[]{:S(2)}, u32[]{:S(2)}) collective-permute-start(f32[128,256]{1,0:T(8,128)S(1)} %dynamic-slice_bitcast_fusion.1), channel_id=1, source_target_pairs={{0,32},{16,48},{32,64},{48,80},{64,96},{80,112},{96,0},{112,16},{1... | collective-permute-start | bytes 393224 | tf_op jit(solution)/shard_map/ppermute | solution.py:134
  71.3 17.9 %collective-permute-start.16 = (f32[256,256]{1,0:T(8,128)S(1)}, f32[256,256]{1,0:T(8,128)S(1)}, u32[]{:S(2)}, u32[]{:S(2)}) collective-permute-start(f32[256,256]{1,0:T(8,128)S(1)} %add.355), channel_id=1, source_target_pairs={{0,96},{16,112},{32,0},{48,16},{64,32},{80,48},{96,64},{112,80},{1... | collective-permute-start | bytes 786440 | tf_op jit(solution)/shard_map/ppermute | solution.py:140
  76.4 5.6 %collective-permute-start.19 = (f32[128,256]{1,0:T(8,128)S(1)}, f32[128,256]{1,0:T(8,128)S(1)}, u32[]{:S(2)}, u32[]{:S(2)}) collective-permute-start(f32[128,256]{1,0:T(8,128)S(1)} %dynamic-slice_bitcast_fusion), channel_id=1, source_target_pairs={{0,96},{16,112},{32,0},{48,16},{64,32},{80,48},{96,64},{112,80},{1... | collective-permute-start | bytes 393224 | tf_op jit(solution)/shard_map/ppermute | solution.py:134
  79.5 9.5 %collective-permute-start.12 = (f32[128,256]{1,0:T(8,128)S(1)}, f32[128,256]{1,0:T(8,128)S(1)}, u32[]{:S(2)}, u32[]{:S(2)}) collective-permute-start(f32[128,256]{1,0:T(8,128)S(1)} %bitcast_add_fusion.5), channel_id=1, source_target_pairs={{0,32},{16,48},{32,64},{48,80},{64,96},{80,112},{96,0},{112,16},{1... | collective-permute-start | bytes 393224 | tf_op jit(solution)/shard_map/ppermute | solution.py:146
  82.1 7.7 %collective-permute-start.20 = (f32[128,256]{1,0:T(8,128)S(1)}, f32[128,256]{1,0:T(8,128)S(1)}, u32[]{:S(2)}, u32[]{:S(2)}) collective-permute-start(f32[128,256]{1,0:T(8,128)S(1)} %bitcast_add_fusion.2), channel_id=1, source_target_pairs={{0,96},{16,112},{32,0},{48,16},{64,32},{80,48},{96,64},{112,80},{1... | collective-permute-start | bytes 393224 | tf_op jit(solution)/shard_map/ppermute | solution.py:146
  85.9 7.2 %collective-permute-start.9 = (f32[128,256]{1,0:T(8,128)S(1)}, f32[128,256]{1,0:T(8,128)S(1)}, u32[]{:S(2)}, u32[]{:S(2)}) collective-permute-start(f32[128,256]{1,0:T(8,128)S(1)} %constant_dynamic-slice_fusion.1), channel_id=1, source_target_pairs={{0,16},{16,0},{32,48},{48,32},{64,80},{80,64},{96,112},{112,96},{1... | collective-permute-start | bytes 393224 | tf_op jit(solution)/shard_map/ppermute | solution.py:151
  89.1 6.2 %collective-permute-start.13 = (f32[128,256]{1,0:T(8,128)S(1)}, f32[128,256]{1,0:T(8,128)S(1)}, u32[]{:S(2)}, u32[]{:S(2)}) collective-permute-start(f32[128,256]{1,0:T(8,128)S(1)} %bitcast_add_fusion.4), channel_id=1, source_target_pairs={{0,32},{16,48},{32,64},{48,80},{64,96},{80,112},{96,0},{112,16},{1... | collective-permute-start | bytes 393224 | tf_op jit(solution)/shard_map/ppermute | solution.py:146
  89.3 6.6 %collective-permute-start.17 = (f32[128,256]{1,0:T(8,128)S(1)}, f32[128,256]{1,0:T(8,128)S(1)}, u32[]{:S(2)}, u32[]{:S(2)}) collective-permute-start(f32[128,256]{1,0:T(8,128)S(1)} %constant_dynamic-slice_fusion), channel_id=1, source_target_pairs={{0,16},{16,0},{32,48},{48,32},{64,80},{80,64},{96,112},{112,96},{1... | collective-permute-start | bytes 393224 | tf_op jit(solution)/shard_map/ppermute | solution.py:151
  89.8 6.1 %collective-permute-start.21 = (f32[128,256]{1,0:T(8,128)S(1)}, f32[128,256]{1,0:T(8,128)S(1)}, u32[]{:S(2)}, u32[]{:S(2)}) collective-permute-start(f32[128,256]{1,0:T(8,128)S(1)} %bitcast_add_fusion.1), channel_id=1, source_target_pairs={{0,96},{16,112},{32,0},{48,16},{64,32},{80,48},{96,64},{112,80},{1... | collective-permute-start | bytes 393224 | tf_op jit(solution)/shard_map/ppermute | solution.py:146

commit v14 on v12

--- a/solution.py
+++ b/solution.py
@@ -31,11 +31,24 @@
     return x
 
 
-def _toeplitz_kernel(shift_ref, weight_ref, rev_ref, *out_refs):
+def _toeplitz_kernel(chunk_ref, shift_ref, weight_ref, rev_ref, green_hbm, *refs):
+    ev = chunk_ref.shape[0]
+    bands, firsts, gbuf, sem = refs[:ev], refs[ev : 2 * ev], refs[2 * ev], refs[2 * ev + 1]
     rows = weight_ref.shape[0]
+    count = gbuf.shape[2]
+    copies = [
+        pltpu.make_async_copy(
+            green_hbm.at[:, pl.ds(pl.multiple_of(chunk_ref[e] * count, count), count), :],
+            gbuf.at[e],
+            sem.at[e],
+        )
+        for e in range(ev)
+    ]
+    for c in copies:
+        c.start()
 
     def body(r, carry):
-        for e, out_ref in enumerate(out_refs):
+        for e, out_ref in enumerate(bands):
             row = rev_ref[e * rows + r]
             row = pltpu.roll(row, shift_ref[e * rows + r], 1)
             row = (row * weight_ref[r]).astype(jnp.bfloat16).astype(jnp.float32)
@@ -46,23 +59,42 @@
         return carry
 
     lax.fori_loop(0, rows, body, 0)
+    for e in range(ev):
+        copies[e].wait()
+        firsts[e][...] = jnp.zeros(firsts[e].shape, firsts[e].dtype)
+
+        def mm(r, carry, e=e):
+            g = gbuf[e, r]
+            b = bands[e][pl.ds(pl.multiple_of(r * NT, NT), NT), :]
+            firsts[e][...] += jnp.dot(g, b, preferred_element_type=jnp.float32)
+            return carry
+
+        lax.fori_loop(0, rows, mm, 0)
 
 
-def toeplitz_reversed(rev, shifts, weights):
+def toeplitz_reversed(rev, shifts, weights, green_t, chunks, count):
     rows = weights.shape[0]
     ev = rev.shape[0] // rows
     band = jax.ShapeDtypeStruct((rows * NT, LAGS), jnp.bfloat16)
-    return pl.pallas_call(
+    first = jax.ShapeDtypeStruct((count, LAGS), jnp.float32)
+    smem = pl.BlockSpec(memory_space=pltpu.SMEM)
+    vmem = pl.BlockSpec(memory_space=pltpu.VMEM)
+    outs = pl.pallas_call(
         _toeplitz_kernel,
-        in_specs=[
-            pl.BlockSpec(memory_space=pltpu.SMEM),
-            pl.BlockSpec(memory_space=pltpu.SMEM),
-            pl.BlockSpec(memory_space=pltpu.VMEM),
+        in_specs=[smem, smem, smem, vmem, pl.BlockSpec(memory_space=pl.ANY)],
+        out_specs=[vmem] * (2 * ev),
+        out_shape=[band] * ev + [first] * ev,
+        scratch_shapes=[
+            pltpu.VMEM((ev, rows, count, NT), jnp.bfloat16),
+            pltpu.SemaphoreType.DMA((ev,)),
         ],
-        out_specs=[pl.BlockSpec(memory_space=pltpu.VMEM)] * ev,
-        out_shape=[band] * ev,
-        cost_estimate=pl.CostEstimate(flops=0, transcendentals=0, bytes_accessed=ev * rows * NT * LAGS * 2),
-    )(shifts, weights, rev)
+        cost_estimate=pl.CostEstimate(
+            flops=2 * ev * count * rows * NT * LAGS,
+            transcendentals=0,
+            bytes_accessed=ev * rows * NT * (LAGS + count) * 2,
+        ),
+    )(chunks, shifts, weights, rev, green_t)
+    return outs[:ev], outs[ev:]
 
 
 def local(green, records_buffer, owners, onsets, codes):
@@ -76,7 +108,6 @@
     rev = jnp.dot(traces, anti, preferred_element_type=jnp.float32).reshape(EV * rows, 1, SAMPLES)
     shifts = ((jnp.repeat(onsets.astype(jnp.int32), 3, axis=1) - LAGS) % SAMPLES).reshape(-1)
     weights = jnp.exp2(-codes.astype(jnp.float32)).reshape(-1)
-    bands = toeplitz_reversed(rev, shifts, weights)
 
     size = lax.axis_size("sens")
     me = lax.axis_index("sens")
@@ -94,16 +125,15 @@
         return [(i, ((i // xs + step) % zs) * xs + i % xs) for i in range(size)]
 
     steps = (1, zs - 1)
+    chunks = jnp.stack([(z + zs - st) % zs for st in steps]).astype(jnp.int32)
+    bands, firsts = toeplitz_reversed(rev, shifts, weights, green_t, chunks, quarter)
     g = green_t
 
     def ordered(e, c, g):
         return lax.optimization_barrier((piece(bands[e], c, g), green_t))
 
-    accs, gots = [], []
-    for e, step in enumerate(steps):
-        acc, g = ordered(e, (z + zs - step) % zs, g)
-        accs.append(acc)
-        gots.append(lax.ppermute(acc, "sens", ring_perm(step)))
+    accs = list(firsts)
+    gots = [lax.ppermute(accs[e], "sens", ring_perm(step)) for e, step in enumerate(steps)]
     for k in range(zs - 1):
         for e, step in enumerate(steps):
             part, g = ordered(e, (z + 4 * zs - step * (k + 2)) % zs, g)

time: 86.7 us -> 95.8 us (1.10)
  waiting for transfers between devices: 24.7 us -> 34.7 us
  Pallas kernels: 9.12 us -> 17.7 us
  starting transfers between devices: 24.1 us -> 18.3 us
  matrix products: 18.6 us -> 14.9 us
    pallas_call x1, Pallas kernels: 9.12 us -> 17.7 us  [toeplitz_reversed(): pl.pallas_call(_toeplitz_kernel, in_specs=[smem, smem, smem, vmem, pl.Blo...]
    ppermute x4, waiting for transfers between devices: 8.73 us -> 14.5 us  [local(): gots[e] = lax.ppermute(accs[e], 'sens', ring_perm(step))]
    ppermute x2, starting transfers between devices: 4.91 us -> 0.26 us  [local(): got = lax.ppermute(theirs, 'sens', [(i, i ^ 1) for i in range(size)])]
    dot_general x8 -> x6, matrix products: 18.3 us -> 14.6 us  [piece(): jnp.einsum('rpt,rtn->pn', g, band.reshape(rows, NT, LAGS), preferred_elem...]
    ppermute x2, waiting for transfers between devices: 4.23 us -> 7.07 us  [local(): got = lax.ppermute(theirs, 'sens', [(i, i ^ 1) for i in range(size)])]
    ppermute x2, waiting for transfers between devices: 5.43 us -> 6.97 us  [local(): lax.ppermute(accs[e], 'sens', ring_perm(step))]
  transfers between devices with their start and end apart: 14 -> 14, of which waited for: 11 -> 11; matrix products, arithmetic and copies ran while one was open for 22% -> 21% of each run, Pallas kernels for 0% -> 0%
where the time goes in v14:
time: 95.8 us; the launch traced here: 95.6 us
  waiting for transfers between devices  34.7 us (36%)
  starting transfers between devices  18.3 us (19%)
  Pallas kernels  17.7 us (18%)
  matrix products  14.9 us (16%)
  other arithmetic  5.08 us (5%)
  local copies, waits for them, and re-layouts  4.58 us (5%)
    pallas_call x1, Pallas kernels, toeplitz_reversed(): pl.pallas_call(_toeplitz_kernel, in_specs=[smem, smem, smem, vmem, pl.Blo...  17.7 us
    dot_general x6, matrix products, piece(): jnp.einsum('rpt,rtn->pn', g, band.reshape(rows, NT, LAGS), preferred_elem...  14.6 us
    ppermute x4, waiting for transfers between devices, local(): gots[e] = lax.ppermute(accs[e], 'sens', ring_perm(step))  14.5 us
    ppermute x4, starting transfers between devices, local(): gots[e] = lax.ppermute(accs[e], 'sens', ring_perm(step))  7.17 us
    ppermute x2, waiting for transfers between devices, local(): got = lax.ppermute(theirs, 'sens', [(i, i ^ 1) for i in range(size)])  7.07 us
    ppermute x2, waiting for transfers between devices, local(): lax.ppermute(accs[e], 'sens', ring_perm(step))  6.97 us
    ppermute x6, starting transfers between devices, from_owners(): got = lax.ppermute(x, axis, perm)  6.49 us
    ppermute x6, waiting for transfers between devices, from_owners(): got = lax.ppermute(x, axis, perm)  6.15 us
  transfers between devices with their start and end apart: 14, of which 11 were waited for; matrix products, arithmetic and copies ran while one was open for 21% of the time, Pallas kernels for 0%

profile of v14, /device:TPU:0, one launch (start us, length us, event | category | flops | bytes accessed | tf_op | source)
XLA Modules:
  0.0 95.6 jit_solution(8930570907369020058)
XLA Ops:
  0.0 1.0 %collective-permute-start = (bf16[2,6,3,1024]{3,0,2,1:T(2,128)(2,1)}, bf16[2,6,3,1024]{3,0,2,1:T(2,128)(2,1)S(1)}, u32[]{:S(2)}, u32[]{:S(2)}) collective-permute-start(bf16[2,6,3,1024]{3,0,2,1:T(2,128)(2,1)} %bitcast.41), channel_id=1, source_target_pairs={{0,3},{1,0},{2,1},{3,2},{4,7},{5,4},{6,5},{7,6},{8,11},{9,8},{10,9... | collective-permute-start | bytes 221192 | tf_op jit(solution)/shard_map/ppermute | solution.py:26
  1.0 0.6 collective-permute-start.1
  1.6 0.2 collective-permute-start.2
  1.8 0.7 broadcast_add_fusion
  2.5 0.1 broadcast_in_dim.36
  2.6 0.1 sub.69
  2.6 0.7 multiply_exponential_fusion
  3.3 0.7 broadcast_compare_fusion
  4.0 0.5 and_select_fusion.3.shift_ref
  4.5 0.1 copy.8
  4.6 0.6 reshape.39.weight_ref
  5.2 0.0 collective-permute-done
  5.2 1.2 %collective-permute-done.1 = bf16[2,6,3,1024]{3,0,2,1:T(2,128)(2,1)S(1)} collective-permute-done((bf16[2,6,3,1024]{3,0,2,1:T(2,128)(2,1)}, bf16[2,6,3,1024]{3,0,2,1:T(2,128)(2,1)S(1)}, u32[]{:S(2)}, u32[]{:S(2)}) %collective-permute-start.1) | collective-permute-done | bytes 73760 | tf_op jit(solution)/shard_map/ppermute | solution.py:26
  6.5 0.0 collective-permute-done.2
  6.5 1.1 %broadcast_select_fusion.4 = bf16[2,6,3,1024]{3,0,2,1:T(2,128)(2,1)S(1)} fusion(bf16[2,6,3,1024]{3,0,2,1:T(2,128)(2,1)S(1)} %collective-permute-done, pred[2]{0:T(512)(128)(4,1)S(1)} %get-tuple-element.48, bf16[2,6,3,1024]{3,0,2,1:T(2,128)(2,1)S(1)} %collective-permute-done.1, pred[2]{0:T(512)(128)(4,1)S(1)} %get-tuple-element.47, ...), kind=kLoop, calls=%fused_computation.28 | loop fusion | flops 110592 | bytes 368646 | tf_op jit(solution)/shard_map/jit(_where)/select_n | solution.py:28
  7.6 3.1 %collective-permute-start.3 = (bf16[2,6,3,1024]{3,0,2,1:T(2,128)(2,1)S(1)}, bf16[2,6,3,1024]{3,0,2,1:T(2,128)(2,1)S(1)}, u32[]{:S(2)}, u32[]{:S(2)}) collective-permute-start(bf16[2,6,3,1024]{3,0,2,1:T(2,128)(2,1)S(1)} %broadcast_select_fusion.4), channel_id=1, source_target_pairs={{0,12},{1,13},{2,14},{3,15},{4,0},{5,1},{6,2},{7,3},{8,4},{9,5},{1... | collective-permute-start | bytes 221192 | tf_op jit(solution)/shard_map/ppermute | solution.py:26
  10.7 0.6 collective-permute-start.4
  11.3 1.0 %collective-permute-start.5 = (bf16[2,6,3,1024]{3,0,2,1:T(2,128)(2,1)S(1)}, bf16[2,6,3,1024]{3,0,2,1:T(2,128)(2,1)S(1)}, u32[]{:S(2)}, u32[]{:S(2)}) collective-permute-start(bf16[2,6,3,1024]{3,0,2,1:T(2,128)(2,1)S(1)} %broadcast_select_fusion.4), channel_id=1, source_target_pairs={{0,4},{1,5},{2,6},{3,7},{4,8},{5,9},{6,10},{7,11},{8,12},{9,13},{1... | collective-permute-start | bytes 221192 | tf_op jit(solution)/shard_map/ppermute | solution.py:26
  12.3 0.6 pad_add_fusion.chunk_ref
  12.9 1.2 %collective-permute-done.3 = bf16[2,6,3,1024]{3,0,2,1:T(2,128)(2,1)S(1)} collective-permute-done((bf16[2,6,3,1024]{3,0,2,1:T(2,128)(2,1)S(1)}, bf16[2,6,3,1024]{3,0,2,1:T(2,128)(2,1)S(1)}, u32[]{:S(2)}, u32[]{:S(2)}) %collective-permute-start.3) | collective-permute-done | bytes 73760 | tf_op jit(solution)/shard_map/ppermute | solution.py:26
  14.1 2.9 %collective-permute-done.4 = bf16[2,6,3,1024]{3,0,2,1:T(2,128)(2,1)S(1)} collective-permute-done((bf16[2,6,3,1024]{3,0,2,1:T(2,128)(2,1)S(1)}, bf16[2,6,3,1024]{3,0,2,1:T(2,128)(2,1)S(1)}, u32[]{:S(2)}, u32[]{:S(2)}) %collective-permute-start.4) | collective-permute-done | bytes 73760 | tf_op jit(solution)/shard_map/ppermute | solution.py:26
  17.0 0.8 collective-permute-done.5
  17.8 0.2 broadcast_select_fusion.5
  18.1 0.1 reshape.40
  18.1 0.3 fusion
  18.4 0.8 reshape.41.rev_ref
  19.2 17.7 %shard_map.55 = (bf16[4608,512]{1,0:T(8,128)(2,1)}, bf16[4608,512]{1,0:T(8,128)(2,1)}, f32[256,512]{1,0:T(8,128)}, f32[256,512]{1,0:T(8,128)}) custom-call(s32[2]{0:T(128)} %pad_add_fusion.chunk_ref, s32[36]{0:T(128)} %and_select_fusion.3.shift_ref, f32[18]{0:T(128)} %reshape.39.weight_ref, f32[36,1,1024]{2,1,0:T(1,128)} %reshape.41.rev_ref, ...), custom_call_target="tpu_custom_call" | custom-call | flops 2415919104 | bytes 14155776 | tf_op jit(solution)/shard_map/pallas_call | solution.py:82
  36.9 2.0 %collective-permute-start.6 = (f32[256,512]{1,0:T(8,128)}, f32[256,512]{1,0:T(8,128)S(1)}, u32[]{:S(2)}, u32[]{:S(2)}) collective-permute-start(f32[256,512]{1,0:T(8,128)} %get-tuple-element.20), channel_id=1, source_target_pairs={{0,32},{16,48},{32,64},{48,80},{64,96},{80,112},{96,0},{112,16},{1... | collective-permute-start | bytes 1572872 | tf_op jit(solution)/shard_map/ppermute | solution.py:136
  38.9 4.6 %fusion.14 = f32[256,512]{1,0:T(8,128)S(1)} fusion(bf16[18,256,512]{2,1,0:T(8,128)(2,1)} %bitcast.49, bf16[18,1024,256]{2,1,0:T(8,128)(2,1)} %bitcast.33, s32[]{:T(128)S(6)} %select_n.170), kind=kOutput, calls=%fused_computation.15 | convolution fusion | flops 1207959552 | bytes 7602180 | tf_op jit(solution)/shard_map/rpt,rtn->pn/dot_general | solution.py:122
  43.4 0.0 slice-start.6
  43.5 2.4 %collective-permute-start.10 = (f32[256,512]{1,0:T(8,128)S(1)}, f32[256,512]{1,0:T(8,128)S(1)}, u32[]{:S(2)}, u32[]{:S(2)}) collective-permute-start(f32[256,512]{1,0:T(8,128)S(1)} %copy-done), channel_id=1, source_target_pairs={{0,96},{16,112},{32,0},{48,16},{64,32},{80,48},{96,64},{112,80},{1... | collective-permute-start | bytes 1572872 | tf_op jit(solution)/shard_map/ppermute | solution.py:136
  45.8 7.0 %collective-permute-done.6 = f32[256,512]{1,0:T(8,128)S(1)} collective-permute-done((f32[256,512]{1,0:T(8,128)}, f32[256,512]{1,0:T(8,128)S(1)}, u32[]{:S(2)}, u32[]{:S(2)}) %collective-permute-start.6) | collective-permute-done | bytes 524320 | tf_op jit(solution)/shard_map/ppermute | solution.py:136
  52.8 0.1 add.203
  52.9 0.1 collective-permute-start.7
  53.0 0.0 slice-start.2
  53.0 0.0 slice-start.3
  53.0 4.6 %fusion.17 = f32[256,512]{1,0:T(8,128)S(1)} fusion(bf16[18,256,512]{2,1,0:T(8,128)(2,1)} %bitcast.44, bf16[18,1024,256]{2,1,0:T(8,128)(2,1)} %bitcast.34, s32[]{:T(128)S(6)} %select_n.172), kind=kOutput, calls=%fused_computation.16 | convolution fusion | flops 1207959552 | bytes 7602180 | tf_op jit(solution)/shard_map/rpt,rtn->pn/dot_general | solution.py:122
  57.7 0.0 slice-start.4
  57.7 1.4 %fusion.20 = f32[256,512]{1,0:T(8,128)S(1)} fusion(bf16[18,256,512]{2,1,0:T(8,128)(2,1)S(1)} %bitcast.52, bf16[18,1024,256]{2,1,0:T(8,128)(2,1)S(1)} %bitcast.37, s32[]{:T(128)S(6)} %select_n.174), kind=kOutput, calls=%fused_computation.17 | convolution fusion | flops 1207959552 | bytes 7602180 | tf_op jit(solution)/shard_map/rpt,rtn->pn/dot_general | solution.py:122
  59.1 0.0 collective-permute-done.10
  59.1 0.1 add.218
  59.2 3.3 %collective-permute-start.11 = (f32[256,512]{1,0:T(8,128)S(1)}, f32[256,512]{1,0:T(8,128)S(1)}, u32[]{:S(2)}, u32[]{:S(2)}) collective-permute-start(f32[256,512]{1,0:T(8,128)S(1)} %add.218), channel_id=1, source_target_pairs={{0,96},{16,112},{32,0},{48,16},{64,32},{80,48},{96,64},{112,80},{1... | collective-permute-start | bytes 1572872 | tf_op jit(solution)/shard_map/ppermute | solution.py:142
  62.4 4.5 %collective-permute-done.7 = f32[256,512]{1,0:T(8,128)S(1)} collective-permute-done((f32[256,512]{1,0:T(8,128)S(1)}, f32[256,512]{1,0:T(8,128)S(1)}, u32[]{:S(2)}, u32[]{:S(2)}) %collective-permute-start.7) | collective-permute-done | bytes 524320 | tf_op jit(solution)/shard_map/ppermute | solution.py:142
  67.0 0.1 add.208
  67.0 0.1 collective-permute-start.8
  67.2 1.4 %fusion.23 = f32[256,512]{1,0:T(8,128)S(1)} fusion(bf16[18,256,512]{2,1,0:T(8,128)(2,1)S(1)} %bitcast.47, bf16[18,1024,256]{2,1,0:T(8,128)(2,1)S(1)} %bitcast.38, s32[]{:T(128)S(6)} %select_n.176), kind=kOutput, calls=%fused_computation.18 | convolution fusion | flops 1207959552 | bytes 7602180 | tf_op jit(solution)/shard_map/rpt,rtn->pn/dot_general | solution.py:122
  68.5 1.4 %fusion.26 = f32[256,512]{1,0:T(8,128)S(1)} fusion(bf16[18,256,512]{2,1,0:T(8,128)(2,1)S(1)} %bitcast.53, bf16[18,1024,256]{2,1,0:T(8,128)(2,1)S(1)} %bitcast.39, s32[]{:T(128)S(6)} %select_n.178), kind=kOutput, calls=%fused_computation.19 | convolution fusion | flops 1207959552 | bytes 7602180 | tf_op jit(solution)/shard_map/rpt,rtn->pn/dot_general | solution.py:122
  69.9 2.5 %collective-permute-done.11 = f32[256,512]{1,0:T(8,128)S(1)} collective-permute-done((f32[256,512]{1,0:T(8,128)S(1)}, f32[256,512]{1,0:T(8,128)S(1)}, u32[]{:S(2)}, u32[]{:S(2)}) %collective-permute-start.11) | collective-permute-done | bytes 524320 | tf_op jit(solution)/shard_map/ppermute | solution.py:142
  72.4 0.1 add.219
  72.5 3.8 %collective-permute-start.12 = (f32[256,512]{1,0:T(8,128)S(1)}, f32[256,512]{1,0:T(8,128)S(1)}, u32[]{:S(2)}, u32[]{:S(2)}) collective-permute-start(f32[256,512]{1,0:T(8,128)S(1)} %add.219), channel_id=1, source_target_pairs={{0,96},{16,112},{32,0},{48,16},{64,32},{80,48},{96,64},{112,80},{1... | collective-permute-start | bytes 1572872 | tf_op jit(solution)/shard_map/ppermute | solution.py:142
  76.3 3.9 %collective-permute-done.8 = f32[256,512]{1,0:T(8,128)S(1)} collective-permute-done((f32[256,512]{1,0:T(8,128)S(1)}, f32[256,512]{1,0:T(8,128)S(1)}, u32[]{:S(2)}, u32[]{:S(2)}) %collective-permute-start.8) | collective-permute-done | bytes 524320 | tf_op jit(solution)/shard_map/ppermute | solution.py:142
  80.2 0.1 add.213
  80.3 0.1 collective-permute-start.9
  80.4 1.4 %fusion.29 = f32[256,512]{1,0:T(8,128)S(1)} fusion(bf16[18,256,512]{2,1,0:T(8,128)(2,1)S(1)} %bitcast.48, bf16[18,1024,256]{2,1,0:T(8,128)(2,1)S(1)} %bitcast.40, s32[]{:T(128)S(6)} %select_n.183), kind=kOutput, calls=%fused_computation.20 | convolution fusion | flops 1207959552 | bytes 7602180 | tf_op jit(solution)/shard_map/rpt,rtn->pn/dot_general | solution.py:122
  81.8 3.5 %collective-permute-done.12 = f32[256,512]{1,0:T(8,128)S(1)} collective-permute-done((f32[256,512]{1,0:T(8,128)S(1)}, f32[256,512]{1,0:T(8,128)S(1)}, u32[]{:S(2)}, u32[]{:S(2)}) %collective-permute-start.12) | collective-permute-done | bytes 524320 | tf_op jit(solution)/shard_map/ppermute | solution.py:142
  85.4 0.1 add.222
  85.5 0.1 collective-permute-start.13
  85.6 0.4 rev.13
  86.0 0.4 rev.15
  86.4 3.6 %collective-permute-done.9 = f32[128,512]{1,0:T(8,128)S(1)} collective-permute-done((f32[128,512]{1,0:T(8,128)S(1)}, f32[128,512]{1,0:T(8,128)S(1)}, u32[]{:S(2)}, u32[]{:S(2)}) %collective-permute-start.9) | collective-permute-done | bytes 262176 | tf_op jit(solution)/shard_map/ppermute | solution.py:147
  90.0 0.4 rev.14
  90.4 3.4 %collective-permute-done.13 = f32[128,512]{1,0:T(8,128)S(1)} collective-permute-done((f32[128,512]{1,0:T(8,128)S(1)}, f32[128,512]{1,0:T(8,128)S(1)}, u32[]{:S(2)}, u32[]{:S(2)}) %collective-permute-start.13) | collective-permute-done | bytes 262176 | tf_op jit(solution)/shard_map/ppermute | solution.py:147
  93.9 0.4 rev.16
  94.4 1.2 %copy.10 = f32[128,2,512]{2,1,0:T(2,128)} copy(f32[128,2,512]{2,0,1:T(8,128)S(1)} %pad_maximum_fusion) | data formatting | bytes 1048576 | tf_op jit(solution)/shard_map/stack | solution.py:149
  (23 shorter events, 0.3 us)
Async XLA Ops:
  0.0 5.2 %collective-permute-start = (bf16[2,6,3,1024]{3,0,2,1:T(2,128)(2,1)}, bf16[2,6,3,1024]{3,0,2,1:T(2,128)(2,1)S(1)}, u32[]{:S(2)}, u32[]{:S(2)}) collective-permute-start(bf16[2,6,3,1024]{3,0,2,1:T(2,128)(2,1)} %bitcast.41), channel_id=1, source_target_pairs={{0,3},{1,0},{2,1},{3,2},{4,7},{5,4},{6,5},{7,6},{8,11},{9,8},{10,9... | collective-permute-start | bytes 221192 | tf_op jit(solution)/shard_map/ppermute | solution.py:26
  1.0 5.5 %collective-permute-start.1 = (bf16[2,6,3,1024]{3,0,2,1:T(2,128)(2,1)}, bf16[2,6,3,1024]{3,0,2,1:T(2,128)(2,1)S(1)}, u32[]{:S(2)}, u32[]{:S(2)}) collective-permute-start(bf16[2,6,3,1024]{3,0,2,1:T(2,128)(2,1)} %bitcast.42), channel_id=1, source_target_pairs={{0,2},{1,3},{2,0},{3,1},{4,6},{5,7},{6,4},{7,5},{8,10},{9,11},{10,... | collective-permute-start | bytes 221192 | tf_op jit(solution)/shard_map/ppermute | solution.py:26
  1.6 4.9 %collective-permute-start.2 = (bf16[2,6,3,1024]{3,0,2,1:T(2,128)(2,1)}, bf16[2,6,3,1024]{3,0,2,1:T(2,128)(2,1)S(1)}, u32[]{:S(2)}, u32[]{:S(2)}) collective-permute-start(bf16[2,6,3,1024]{3,0,2,1:T(2,128)(2,1)} %bitcast.43), channel_id=1, source_target_pairs={{0,1},{1,2},{2,3},{3,0},{4,5},{5,6},{6,7},{7,4},{8,9},{9,10},{10,1... | collective-permute-start | bytes 221192 | tf_op jit(solution)/shard_map/ppermute | solution.py:26
  7.6 6.5 %collective-permute-start.3 = (bf16[2,6,3,1024]{3,0,2,1:T(2,128)(2,1)S(1)}, bf16[2,6,3,1024]{3,0,2,1:T(2,128)(2,1)S(1)}, u32[]{:S(2)}, u32[]{:S(2)}) collective-permute-start(bf16[2,6,3,1024]{3,0,2,1:T(2,128)(2,1)S(1)} %broadcast_select_fusion.4), channel_id=1, source_target_pairs={{0,12},{1,13},{2,14},{3,15},{4,0},{5,1},{6,2},{7,3},{8,4},{9,5},{1... | collective-permute-start | bytes 221192 | tf_op jit(solution)/shard_map/ppermute | solution.py:26
  10.7 6.3 %collective-permute-start.4 = (bf16[2,6,3,1024]{3,0,2,1:T(2,128)(2,1)S(1)}, bf16[2,6,3,1024]{3,0,2,1:T(2,128)(2,1)S(1)}, u32[]{:S(2)}, u32[]{:S(2)}) collective-permute-start(bf16[2,6,3,1024]{3,0,2,1:T(2,128)(2,1)S(1)} %broadcast_select_fusion.4), channel_id=1, source_target_pairs={{0,8},{1,9},{2,10},{3,11},{4,12},{5,13},{6,14},{7,15},{8,0},{9,1},... | collective-permute-start | bytes 221192 | tf_op jit(solution)/shard_map/ppermute | solution.py:26
  11.3 6.5 %collective-permute-start.5 = (bf16[2,6,3,1024]{3,0,2,1:T(2,128)(2,1)S(1)}, bf16[2,6,3,1024]{3,0,2,1:T(2,128)(2,1)S(1)}, u32[]{:S(2)}, u32[]{:S(2)}) collective-permute-start(bf16[2,6,3,1024]{3,0,2,1:T(2,128)(2,1)S(1)} %broadcast_select_fusion.4), channel_id=1, source_target_pairs={{0,4},{1,5},{2,6},{3,7},{4,8},{5,9},{6,10},{7,11},{8,12},{9,13},{1... | collective-permute-start | bytes 221192 | tf_op jit(solution)/shard_map/ppermute | solution.py:26
  36.9 6.6 %copy-start = (f32[256,512]{1,0:T(8,128)S(1)}, f32[256,512]{1,0:T(8,128)}, u32[]{:S(2)}) copy-start(f32[256,512]{1,0:T(8,128)} %get-tuple-element.30) | copy-start | bytes 1572868
  36.9 15.9 %collective-permute-start.6 = (f32[256,512]{1,0:T(8,128)}, f32[256,512]{1,0:T(8,128)S(1)}, u32[]{:S(2)}, u32[]{:S(2)}) collective-permute-start(f32[256,512]{1,0:T(8,128)} %get-tuple-element.20), channel_id=1, source_target_pairs={{0,32},{16,48},{32,64},{48,80},{64,96},{80,112},{96,0},{112,16},{1... | collective-permute-start | bytes 1572872 | tf_op jit(solution)/shard_map/ppermute | solution.py:136
  38.9 18.7 %slice-start = ((s8[9437184]{0:T(1024)(128)(4,1)}), s8[4194304]{0:T(1024)(128)(4,1)S(1)}, s32[]{:S(2)}) async-start(s8[9437184]{0:T(1024)(128)(4,1)} %bitcast.35), calls=%async_computation | async-start | bytes 8388608
  38.9 18.8 %slice-start.1 = ((s8[9437184]{0:T(1024)(128)(4,1)}), s8[4194304]{0:T(1024)(128)(4,1)S(1)}, s32[]{:S(2)}) async-start(s8[9437184]{0:T(1024)(128)(4,1)} %bitcast.35), calls=%async_computation.1 | async-start | bytes 8388608
  38.9 18.8 %slice-start.5 = ((s8[4718592]{0:T(1024)(128)(4,1)}), s8[4194304]{0:T(1024)(128)(4,1)S(1)}, s32[]{:S(2)}) async-start(s8[4718592]{0:T(1024)(128)(4,1)} %bitcast.50), calls=%async_computation.5 | async-start | bytes 8388608
  43.4 14.2 %slice-start.6 = ((s8[4718592]{0:T(1024)(128)(4,1)}), s8[524288]{0:T(1024)(128)(4,1)S(1)}, s32[]{:S(2)}) async-start(s8[4718592]{0:T(1024)(128)(4,1)} %bitcast.50), calls=%async_computation.6 | async-start | bytes 1048576
  43.5 15.6 %collective-permute-start.10 = (f32[256,512]{1,0:T(8,128)S(1)}, f32[256,512]{1,0:T(8,128)S(1)}, u32[]{:S(2)}, u32[]{:S(2)}) collective-permute-start(f32[256,512]{1,0:T(8,128)S(1)} %copy-done), channel_id=1, source_target_pairs={{0,96},{16,112},{32,0},{48,16},{64,32},{80,48},{96,64},{112,80},{1... | collective-permute-start | bytes 1572872 | tf_op jit(solution)/shard_map/ppermute | solution.py:136
  52.9 14.1 %collective-permute-start.7 = (f32[256,512]{1,0:T(8,128)S(1)}, f32[256,512]{1,0:T(8,128)S(1)}, u32[]{:S(2)}, u32[]{:S(2)}) collective-permute-start(f32[256,512]{1,0:T(8,128)S(1)} %add.203), channel_id=1, source_target_pairs={{0,32},{16,48},{32,64},{48,80},{64,96},{80,112},{96,0},{112,16},{1... | collective-permute-start | bytes 1572872 | tf_op jit(solution)/shard_map/ppermute | solution.py:142
  53.0 4.7 %slice-start.2 = ((s8[9437184]{0:T(1024)(128)(4,1)}), s8[1048576]{0:T(1024)(128)(4,1)S(1)}, s32[]{:S(2)}) async-start(s8[9437184]{0:T(1024)(128)(4,1)} %bitcast.35), calls=%async_computation.2 | async-start | bytes 2097152
  53.0 14.1 %slice-start.3 = ((s8[4718592]{0:T(1024)(128)(4,1)}), s8[4194304]{0:T(1024)(128)(4,1)S(1)}, s32[]{:S(2)}) async-start(s8[4718592]{0:T(1024)(128)(4,1)} %bitcast.45), calls=%async_computation.3 | async-start | bytes 8388608
  57.7 9.5 %slice-start.4 = ((s8[4718592]{0:T(1024)(128)(4,1)}), s8[524288]{0:T(1024)(128)(4,1)S(1)}, s32[]{:S(2)}) async-start(s8[4718592]{0:T(1024)(128)(4,1)} %bitcast.45), calls=%async_computation.4 | async-start | bytes 1048576
  59.2 13.3 %collective-permute-start.11 = (f32[256,512]{1,0:T(8,128)S(1)}, f32[256,512]{1,0:T(8,128)S(1)}, u32[]{:S(2)}, u32[]{:S(2)}) collective-permute-start(f32[256,512]{1,0:T(8,128)S(1)} %add.218), channel_id=1, source_target_pairs={{0,96},{16,112},{32,0},{48,16},{64,32},{80,48},{96,64},{112,80},{1... | collective-permute-start | bytes 1572872 | tf_op jit(solution)/shard_map/ppermute | solution.py:142
  67.0 13.1 %collective-permute-start.8 = (f32[256,512]{1,0:T(8,128)S(1)}, f32[256,512]{1,0:T(8,128)S(1)}, u32[]{:S(2)}, u32[]{:S(2)}) collective-permute-start(f32[256,512]{1,0:T(8,128)S(1)} %add.208), channel_id=1, source_target_pairs={{0,32},{16,48},{32,64},{48,80},{64,96},{80,112},{96,0},{112,16},{1... | collective-permute-start | bytes 1572872 | tf_op jit(solution)/shard_map/ppermute | solution.py:142
  72.5 12.9 %collective-permute-start.12 = (f32[256,512]{1,0:T(8,128)S(1)}, f32[256,512]{1,0:T(8,128)S(1)}, u32[]{:S(2)}, u32[]{:S(2)}) collective-permute-start(f32[256,512]{1,0:T(8,128)S(1)} %add.219), channel_id=1, source_target_pairs={{0,96},{16,112},{32,0},{48,16},{64,32},{80,48},{96,64},{112,80},{1... | collective-permute-start | bytes 1572872 | tf_op jit(solution)/shard_map/ppermute | solution.py:142
  80.3 9.7 %collective-permute-start.9 = (f32[128,512]{1,0:T(8,128)S(1)}, f32[128,512]{1,0:T(8,128)S(1)}, u32[]{:S(2)}, u32[]{:S(2)}) collective-permute-start(f32[128,512]{1,0:T(8,128)S(1)} %get-tuple-element.39), channel_id=1, source_target_pairs={{0,16},{16,0},{32,48},{48,32},{64,80},{80,64},{96,112},{112,96},{1... | collective-permute-start | bytes 786440 | tf_op jit(solution)/shard_map/ppermute | solution.py:147
  85.5 8.4 %collective-permute-start.13 = (f32[128,512]{1,0:T(8,128)S(1)}, f32[128,512]{1,0:T(8,128)S(1)}, u32[]{:S(2)}, u32[]{:S(2)}) collective-permute-start(f32[128,512]{1,0:T(8,128)S(1)} %get-tuple-element.41), channel_id=1, source_target_pairs={{0,16},{16,0},{32,48},{48,32},{64,80},{80,64},{96,112},{112,96},{1... | collective-permute-start | bytes 786440 | tf_op jit(solution)/shard_map/ppermute | solution.py:147

commit v15 on v12

--- a/solution.py
+++ b/solution.py
@@ -62,6 +62,7 @@
         out_specs=[pl.BlockSpec(memory_space=pltpu.VMEM)] * ev,
         out_shape=[band] * ev,
         cost_estimate=pl.CostEstimate(flops=0, transcendentals=0, bytes_accessed=ev * rows * NT * LAGS * 2),
+        compiler_params=pltpu.CompilerParams(vmem_limit_bytes=24 * 1024 * 1024),
     )(shifts, weights, rev)
 
 

time: 86.7 us -> 77.9 us (0.90)
  waiting for transfers between devices: 24.7 us -> 30.9 us
  matrix products: 18.6 us -> 12.9 us
  Pallas kernels: 9.12 us -> 5.14 us
  starting transfers between devices: 24.1 us -> 21.1 us
  local copies, waits for them, and re-layouts: 5.25 us -> 3.33 us
    dot_general x8, matrix products: 18.3 us -> 12.7 us  [piece(): jnp.einsum('rpt,rtn->pn', g, band.reshape(rows, NT, LAGS), preferred_elem...]
    pallas_call x1, Pallas kernels: 9.12 us -> 5.14 us  [toeplitz_reversed(): pl.pallas_call(_toeplitz_kernel, in_specs=[pl.BlockSpec(memory_space=pltp...]
    ppermute x4, waiting for transfers between devices: 8.73 us -> 11.1 us  [local(): gots[e] = lax.ppermute(accs[e], 'sens', ring_perm(step))]
    ppermute x2, waiting for transfers between devices: 5.43 us -> 7.01 us  [local(): gots.append(lax.ppermute(acc, 'sens', ring_perm(step)))]
    ppermute x2, waiting for transfers between devices: 4.23 us -> 5.46 us  [local(): got = lax.ppermute(theirs, 'sens', [(i, i ^ 1) for i in range(size)])]
    ppermute x2, starting transfers between devices: 4.91 us -> 3.69 us  [local(): got = lax.ppermute(theirs, 'sens', [(i, i ^ 1) for i in range(size)])]
    ppermute x6, waiting for transfers between devices: 6.27 us -> 7.29 us  [from_owners(): got = lax.ppermute(x, axis, perm)]
    ppermute x4, starting transfers between devices: 7.72 us -> 6.73 us  [local(): gots[e] = lax.ppermute(accs[e], 'sens', ring_perm(step))]
  transfers between devices with their start and end apart: 14 -> 14, of which waited for: 11 -> 9; matrix products, arithmetic and copies ran while one was open for 22% -> 18% of each run, Pallas kernels for 0% -> 0%
where the time goes in v15:
time: 77.9 us; the launch traced here: 77.7 us
  waiting for transfers between devices  30.9 us (40%)
  starting transfers between devices  21.1 us (27%)
  matrix products  12.9 us (17%)
  Pallas kernels  5.14 us (7%)
  other arithmetic  4.03 us (5%)
  local copies, waits for them, and re-layouts  3.33 us (4%)
    dot_general x8, matrix products, piece(): jnp.einsum('rpt,rtn->pn', g, band.reshape(rows, NT, LAGS), preferred_elem...  12.7 us
    ppermute x4, waiting for transfers between devices, local(): gots[e] = lax.ppermute(accs[e], 'sens', ring_perm(step))  11.1 us
    ppermute x6, waiting for transfers between devices, from_owners(): got = lax.ppermute(x, axis, perm)  7.29 us
    ppermute x2, waiting for transfers between devices, local(): gots.append(lax.ppermute(acc, 'sens', ring_perm(step)))  7.01 us
    ppermute x4, starting transfers between devices, local(): gots[e] = lax.ppermute(accs[e], 'sens', ring_perm(step))  6.73 us
    ppermute x6, starting transfers between devices, from_owners(): got = lax.ppermute(x, axis, perm)  6.49 us
    ppermute x2, waiting for transfers between devices, local(): got = lax.ppermute(theirs, 'sens', [(i, i ^ 1) for i in range(size)])  5.46 us
    pallas_call x1, Pallas kernels, toeplitz_reversed(): pl.pallas_call(_toeplitz_kernel, in_specs=[pl.BlockSpec(memory_space=pltp...  5.14 us
  transfers between devices with their start and end apart: 14, of which 9 were waited for; matrix products, arithmetic and copies ran while one was open for 18% of the time, Pallas kernels for 0%

profile of v15, /device:TPU:0, one launch (start us, length us, event | category | flops | bytes accessed | tf_op | source)
XLA Modules:
  0.0 77.7 jit_solution(996918766040637569)
XLA Ops:
  0.0 1.0 %collective-permute-start = (bf16[2,6,3,1024]{3,0,2,1:T(2,128)(2,1)}, bf16[2,6,3,1024]{3,0,2,1:T(2,128)(2,1)S(1)}, u32[]{:S(2)}, u32[]{:S(2)}) collective-permute-start(bf16[2,6,3,1024]{3,0,2,1:T(2,128)(2,1)} %bitcast.44), channel_id=1, source_target_pairs={{0,3},{1,0},{2,1},{3,2},{4,7},{5,4},{6,5},{7,6},{8,11},{9,8},{10,9... | collective-permute-start | bytes 221192 | tf_op jit(solution)/shard_map/ppermute | solution.py:26
  1.0 0.6 collective-permute-start.1
  1.6 0.2 collective-permute-start.2
  1.8 0.7 broadcast_add_fusion
  2.5 0.7 multiply_exponential_fusion
  3.2 0.7 broadcast_compare_fusion
  3.9 0.1 broadcast_in_dim.36
  4.0 0.1 sub.68
  4.0 0.0 collective-permute-done
  4.0 2.4 %collective-permute-done.1 = bf16[2,6,3,1024]{3,0,2,1:T(2,128)(2,1)S(1)} collective-permute-done((bf16[2,6,3,1024]{3,0,2,1:T(2,128)(2,1)}, bf16[2,6,3,1024]{3,0,2,1:T(2,128)(2,1)S(1)}, u32[]{:S(2)}, u32[]{:S(2)}) %collective-permute-start.1) | collective-permute-done | bytes 73760 | tf_op jit(solution)/shard_map/ppermute | solution.py:26
  6.5 0.0 collective-permute-done.2
  6.5 1.1 %broadcast_select_fusion.4 = bf16[2,6,3,1024]{3,0,2,1:T(2,128)(2,1)S(1)} fusion(bf16[2,6,3,1024]{3,0,2,1:T(2,128)(2,1)S(1)} %collective-permute-done, pred[2]{0:T(512)(128)(4,1)S(1)} %get-tuple-element.52, bf16[2,6,3,1024]{3,0,2,1:T(2,128)(2,1)S(1)} %collective-permute-done.1, pred[2]{0:T(512)(128)(4,1)S(1)} %get-tuple-element.51, ...), kind=kLoop, calls=%fused_computation.34 | loop fusion | flops 110592 | bytes 368646 | tf_op jit(solution)/shard_map/jit(_where)/select_n | solution.py:28
  7.6 3.1 %collective-permute-start.3 = (bf16[2,6,3,1024]{3,0,2,1:T(2,128)(2,1)S(1)}, bf16[2,6,3,1024]{3,0,2,1:T(2,128)(2,1)S(1)}, u32[]{:S(2)}, u32[]{:S(2)}) collective-permute-start(bf16[2,6,3,1024]{3,0,2,1:T(2,128)(2,1)S(1)} %broadcast_select_fusion.4), channel_id=1, source_target_pairs={{0,12},{1,13},{2,14},{3,15},{4,0},{5,1},{6,2},{7,3},{8,4},{9,5},{1... | collective-permute-start | bytes 221192 | tf_op jit(solution)/shard_map/ppermute | solution.py:26
  10.7 0.6 collective-permute-start.4
  11.3 1.0 %collective-permute-start.5 = (bf16[2,6,3,1024]{3,0,2,1:T(2,128)(2,1)S(1)}, bf16[2,6,3,1024]{3,0,2,1:T(2,128)(2,1)S(1)}, u32[]{:S(2)}, u32[]{:S(2)}) collective-permute-start(bf16[2,6,3,1024]{3,0,2,1:T(2,128)(2,1)S(1)} %broadcast_select_fusion.4), channel_id=1, source_target_pairs={{0,4},{1,5},{2,6},{3,7},{4,8},{5,9},{6,10},{7,11},{8,12},{9,13},{1... | collective-permute-start | bytes 221192 | tf_op jit(solution)/shard_map/ppermute | solution.py:26
  12.3 0.1 copy.8
  12.4 0.1 reshape.42.weight_ref
  12.5 0.2 collective-permute-done.3
  12.7 3.9 %collective-permute-done.4 = bf16[2,6,3,1024]{3,0,2,1:T(2,128)(2,1)S(1)} collective-permute-done((bf16[2,6,3,1024]{3,0,2,1:T(2,128)(2,1)S(1)}, bf16[2,6,3,1024]{3,0,2,1:T(2,128)(2,1)S(1)}, u32[]{:S(2)}, u32[]{:S(2)}) %collective-permute-start.4) | collective-permute-done | bytes 73760 | tf_op jit(solution)/shard_map/ppermute | solution.py:26
  16.6 0.7 collective-permute-done.5
  17.3 0.2 broadcast_select_fusion.5
  17.6 0.1 reshape.43
  17.7 0.0 copy-start
  17.7 0.3 fusion
  18.0 0.1 reshape.44.rev_ref
  18.1 5.1 %shard_map.55 = (bf16[4608,512]{1,0:T(8,128)(2,1)S(1)}, bf16[4608,512]{1,0:T(8,128)(2,1)S(1)}) custom-call(s32[36]{0:T(128)S(1)} %and_select_fusion.3.shift_ref, f32[18]{0:T(128)S(1)} %reshape.42.weight_ref, f32[36,1,1024]{2,1,0:T(1,128)S(1)} %reshape.44.rev_ref), custom_call_target="tpu_custom_call" | custom-call | bytes 9437184 | tf_op jit(solution)/shard_map/pallas_call | solution.py:55
  23.2 3.0 %fusion.18 = f32[256,512]{1,0:T(8,128)S(1)} fusion(bf16[18,256,512]{2,1,0:T(8,128)(2,1)S(1)} %bitcast.40, bf16[18,1024,256]{2,1,0:T(8,128)(2,1)} %bitcast.47, s32[]{:T(128)S(6)} %select_n.155), kind=kOutput, calls=%fused_computation.19 | convolution fusion | flops 1207959552 | bytes 7602180 | tf_op jit(solution)/shard_map/rpt,rtn->pn/dot_general | solution.py:92
  26.3 2.0 %collective-permute-start.6 = (f32[256,512]{1,0:T(8,128)S(1)}, f32[256,512]{1,0:T(8,128)S(1)}, u32[]{:S(2)}, u32[]{:S(2)}) collective-permute-start(f32[256,512]{1,0:T(8,128)S(1)} %fusion.18), channel_id=1, source_target_pairs={{0,32},{16,48},{32,64},{48,80},{64,96},{80,112},{96,0},{112,16},{1... | collective-permute-start | bytes 1572872 | tf_op jit(solution)/shard_map/ppermute | solution.py:107
  28.3 0.0 copy-done
  28.3 1.4 %fusion.21 = f32[256,512]{1,0:T(8,128)S(1)} fusion(bf16[18,256,512]{2,1,0:T(8,128)(2,1)S(1)} %bitcast.36, bf16[18,1024,256]{2,1,0:T(8,128)(2,1)S(1)} %bitcast.48, s32[]{:T(128)S(6)} %select_n.176), kind=kOutput, calls=%fused_computation.20 | convolution fusion | flops 1207959552 | bytes 7602180 | tf_op jit(solution)/shard_map/rpt,rtn->pn/dot_general | solution.py:92
  29.7 1.4 %fusion.24 = f32[256,512]{1,0:T(8,128)S(1)} fusion(bf16[18,256,512]{2,1,0:T(8,128)(2,1)S(1)} %bitcast.41, bf16[18,1024,256]{2,1,0:T(8,128)(2,1)S(1)} %bitcast.49, s32[]{:T(128)S(6)} %select_n.178), kind=kOutput, calls=%fused_computation.21 | convolution fusion | flops 1207959552 | bytes 7602180 | tf_op jit(solution)/shard_map/rpt,rtn->pn/dot_general | solution.py:92
  31.0 2.2 %collective-permute-start.10 = (f32[256,512]{1,0:T(8,128)S(1)}, f32[256,512]{1,0:T(8,128)S(1)}, u32[]{:S(2)}, u32[]{:S(2)}) collective-permute-start(f32[256,512]{1,0:T(8,128)S(1)} %fusion.21), channel_id=1, source_target_pairs={{0,96},{16,112},{32,0},{48,16},{64,32},{80,48},{96,64},{112,80},{1... | collective-permute-start | bytes 1572872 | tf_op jit(solution)/shard_map/ppermute | solution.py:107
  33.3 7.0 %collective-permute-done.6 = f32[256,512]{1,0:T(8,128)S(1)} collective-permute-done((f32[256,512]{1,0:T(8,128)S(1)}, f32[256,512]{1,0:T(8,128)S(1)}, u32[]{:S(2)}, u32[]{:S(2)}) %collective-permute-start.6) | collective-permute-done | bytes 524320 | tf_op jit(solution)/shard_map/ppermute | solution.py:107
  40.3 0.1 add.211
  40.4 0.1 collective-permute-start.7
  40.4 1.4 %fusion.27 = f32[256,512]{1,0:T(8,128)S(1)} fusion(bf16[18,256,512]{2,1,0:T(8,128)(2,1)S(1)} %bitcast.37, bf16[18,1024,256]{2,1,0:T(8,128)(2,1)S(1)} %bitcast.50, s32[]{:T(128)S(6)} %select_n.180), kind=kOutput, calls=%fused_computation.22 | convolution fusion | flops 1207959552 | bytes 7602180 | tf_op jit(solution)/shard_map/rpt,rtn->pn/dot_general | solution.py:92
  41.8 1.4 %fusion.30 = f32[256,512]{1,0:T(8,128)S(1)} fusion(bf16[18,256,512]{2,1,0:T(8,128)(2,1)S(1)} %bitcast.42, bf16[18,1024,256]{2,1,0:T(8,128)(2,1)S(1)} %bitcast.51, s32[]{:T(128)S(6)} %select_n.182), kind=kOutput, calls=%fused_computation.23 | convolution fusion | flops 1207959552 | bytes 7602180 | tf_op jit(solution)/shard_map/rpt,rtn->pn/dot_general | solution.py:92
  43.2 0.0 collective-permute-done.10
  43.2 0.1 add.226
  43.3 3.3 %collective-permute-start.11 = (f32[256,512]{1,0:T(8,128)S(1)}, f32[256,512]{1,0:T(8,128)S(1)}, u32[]{:S(2)}, u32[]{:S(2)}) collective-permute-start(f32[256,512]{1,0:T(8,128)S(1)} %add.226), channel_id=1, source_target_pairs={{0,96},{16,112},{32,0},{48,16},{64,32},{80,48},{96,64},{112,80},{1... | collective-permute-start | bytes 1572872 | tf_op jit(solution)/shard_map/ppermute | solution.py:113
  46.6 6.0 %collective-permute-done.7 = f32[256,512]{1,0:T(8,128)S(1)} collective-permute-done((f32[256,512]{1,0:T(8,128)S(1)}, f32[256,512]{1,0:T(8,128)S(1)}, u32[]{:S(2)}, u32[]{:S(2)}) %collective-permute-start.7) | collective-permute-done | bytes 524320 | tf_op jit(solution)/shard_map/ppermute | solution.py:113
  52.6 0.1 add.216
  52.7 0.1 collective-permute-start.8
  52.8 1.4 %fusion.33 = f32[256,512]{1,0:T(8,128)S(1)} fusion(bf16[18,256,512]{2,1,0:T(8,128)(2,1)S(1)} %bitcast.38, bf16[18,1024,256]{2,1,0:T(8,128)(2,1)S(1)} %bitcast.52, s32[]{:T(128)S(6)} %select_n.184), kind=kOutput, calls=%fused_computation.24 | convolution fusion | flops 1207959552 | bytes 7602180 | tf_op jit(solution)/shard_map/rpt,rtn->pn/dot_general | solution.py:92
  54.1 1.4 %fusion.36 = f32[256,512]{1,0:T(8,128)S(1)} fusion(bf16[18,256,512]{2,1,0:T(8,128)(2,1)S(1)} %bitcast.43, bf16[18,1024,256]{2,1,0:T(8,128)(2,1)S(1)} %bitcast.53, s32[]{:T(128)S(6)} %select_n.186), kind=kOutput, calls=%fused_computation.25 | convolution fusion | flops 1207959552 | bytes 7602180 | tf_op jit(solution)/shard_map/rpt,rtn->pn/dot_general | solution.py:92
  55.5 0.0 collective-permute-done.11
  55.5 0.1 add.227
  55.6 3.3 %collective-permute-start.12 = (f32[256,512]{1,0:T(8,128)S(1)}, f32[256,512]{1,0:T(8,128)S(1)}, u32[]{:S(2)}, u32[]{:S(2)}) collective-permute-start(f32[256,512]{1,0:T(8,128)S(1)} %add.227), channel_id=1, source_target_pairs={{0,96},{16,112},{32,0},{48,16},{64,32},{80,48},{96,64},{112,80},{1... | collective-permute-start | bytes 1572872 | tf_op jit(solution)/shard_map/ppermute | solution.py:113
  58.9 5.1 %collective-permute-done.8 = f32[256,512]{1,0:T(8,128)S(1)} collective-permute-done((f32[256,512]{1,0:T(8,128)S(1)}, f32[256,512]{1,0:T(8,128)S(1)}, u32[]{:S(2)}, u32[]{:S(2)}) %collective-permute-start.8) | collective-permute-done | bytes 524320 | tf_op jit(solution)/shard_map/ppermute | solution.py:113
  64.0 0.1 add.221
  64.1 2.4 %collective-permute-start.9 = (f32[128,512]{1,0:T(8,128)S(1)}, f32[128,512]{1,0:T(8,128)S(1)}, u32[]{:S(2)}, u32[]{:S(2)}) collective-permute-start(f32[128,512]{1,0:T(8,128)S(1)} %get-tuple-element.43), channel_id=1, source_target_pairs={{0,16},{16,0},{32,48},{48,32},{64,80},{80,64},{96,112},{112,96},{1... | collective-permute-start | bytes 786440 | tf_op jit(solution)/shard_map/ppermute | solution.py:118
  66.5 1.4 %fusion.39 = f32[256,512]{1,0:T(8,128)S(1)} fusion(bf16[18,256,512]{2,1,0:T(8,128)(2,1)S(1)} %bitcast.39, bf16[18,1024,256]{2,1,0:T(8,128)(2,1)S(1)} %bitcast.54, s32[]{:T(128)S(6)} %select_n.191), kind=kOutput, calls=%fused_computation.26 | convolution fusion | flops 1207959552 | bytes 7602180 | tf_op jit(solution)/shard_map/rpt,rtn->pn/dot_general | solution.py:92
  67.9 0.0 collective-permute-done.12
  67.9 0.1 add.230
  68.0 1.3 %collective-permute-start.13 = (f32[128,512]{1,0:T(8,128)S(1)}, f32[128,512]{1,0:T(8,128)S(1)}, u32[]{:S(2)}, u32[]{:S(2)}) collective-permute-start(f32[128,512]{1,0:T(8,128)S(1)} %get-tuple-element.45), channel_id=1, source_target_pairs={{0,16},{16,0},{32,48},{48,32},{64,80},{80,64},{96,112},{112,96},{1... | collective-permute-start | bytes 786440 | tf_op jit(solution)/shard_map/ppermute | solution.py:118
  69.4 0.4 rev.13
  69.7 0.4 rev.15
  70.1 2.5 %collective-permute-done.9 = f32[128,512]{1,0:T(8,128)S(1)} collective-permute-done((f32[128,512]{1,0:T(8,128)S(1)}, f32[128,512]{1,0:T(8,128)S(1)}, u32[]{:S(2)}, u32[]{:S(2)}) %collective-permute-start.9) | collective-permute-done | bytes 262176 | tf_op jit(solution)/shard_map/ppermute | solution.py:118
  72.6 0.4 rev.14
  73.1 2.9 %collective-permute-done.13 = f32[128,512]{1,0:T(8,128)S(1)} collective-permute-done((f32[128,512]{1,0:T(8,128)S(1)}, f32[128,512]{1,0:T(8,128)S(1)}, u32[]{:S(2)}, u32[]{:S(2)}) %collective-permute-start.13) | collective-permute-done | bytes 262176 | tf_op jit(solution)/shard_map/ppermute | solution.py:118
  76.0 0.4 rev.16
  76.5 1.2 %copy.10 = f32[128,2,512]{2,1,0:T(2,128)} copy(f32[128,2,512]{2,0,1:T(8,128)S(1)} %pad_maximum_fusion) | data formatting | bytes 1048576 | tf_op jit(solution)/shard_map/stack | solution.py:120
  (9 shorter events, 0.3 us)
Async XLA Ops:
  0.0 4.0 %collective-permute-start = (bf16[2,6,3,1024]{3,0,2,1:T(2,128)(2,1)}, bf16[2,6,3,1024]{3,0,2,1:T(2,128)(2,1)S(1)}, u32[]{:S(2)}, u32[]{:S(2)}) collective-permute-start(bf16[2,6,3,1024]{3,0,2,1:T(2,128)(2,1)} %bitcast.44), channel_id=1, source_target_pairs={{0,3},{1,0},{2,1},{3,2},{4,7},{5,4},{6,5},{7,6},{8,11},{9,8},{10,9... | collective-permute-start | bytes 221192 | tf_op jit(solution)/shard_map/ppermute | solution.py:26
  1.0 5.5 %collective-permute-start.1 = (bf16[2,6,3,1024]{3,0,2,1:T(2,128)(2,1)}, bf16[2,6,3,1024]{3,0,2,1:T(2,128)(2,1)S(1)}, u32[]{:S(2)}, u32[]{:S(2)}) collective-permute-start(bf16[2,6,3,1024]{3,0,2,1:T(2,128)(2,1)} %bitcast.45), channel_id=1, source_target_pairs={{0,2},{1,3},{2,0},{3,1},{4,6},{5,7},{6,4},{7,5},{8,10},{9,11},{10,... | collective-permute-start | bytes 221192 | tf_op jit(solution)/shard_map/ppermute | solution.py:26
  1.6 4.9 %collective-permute-start.2 = (bf16[2,6,3,1024]{3,0,2,1:T(2,128)(2,1)}, bf16[2,6,3,1024]{3,0,2,1:T(2,128)(2,1)S(1)}, u32[]{:S(2)}, u32[]{:S(2)}) collective-permute-start(bf16[2,6,3,1024]{3,0,2,1:T(2,128)(2,1)} %bitcast.46), channel_id=1, source_target_pairs={{0,1},{1,2},{2,3},{3,0},{4,5},{5,6},{6,7},{7,4},{8,9},{9,10},{10,1... | collective-permute-start | bytes 221192 | tf_op jit(solution)/shard_map/ppermute | solution.py:26
  7.6 5.1 %collective-permute-start.3 = (bf16[2,6,3,1024]{3,0,2,1:T(2,128)(2,1)S(1)}, bf16[2,6,3,1024]{3,0,2,1:T(2,128)(2,1)S(1)}, u32[]{:S(2)}, u32[]{:S(2)}) collective-permute-start(bf16[2,6,3,1024]{3,0,2,1:T(2,128)(2,1)S(1)} %broadcast_select_fusion.4), channel_id=1, source_target_pairs={{0,12},{1,13},{2,14},{3,15},{4,0},{5,1},{6,2},{7,3},{8,4},{9,5},{1... | collective-permute-start | bytes 221192 | tf_op jit(solution)/shard_map/ppermute | solution.py:26
  10.7 5.9 %collective-permute-start.4 = (bf16[2,6,3,1024]{3,0,2,1:T(2,128)(2,1)S(1)}, bf16[2,6,3,1024]{3,0,2,1:T(2,128)(2,1)S(1)}, u32[]{:S(2)}, u32[]{:S(2)}) collective-permute-start(bf16[2,6,3,1024]{3,0,2,1:T(2,128)(2,1)S(1)} %broadcast_select_fusion.4), channel_id=1, source_target_pairs={{0,8},{1,9},{2,10},{3,11},{4,12},{5,13},{6,14},{7,15},{8,0},{9,1},... | collective-permute-start | bytes 221192 | tf_op jit(solution)/shard_map/ppermute | solution.py:26
  11.3 6.0 %collective-permute-start.5 = (bf16[2,6,3,1024]{3,0,2,1:T(2,128)(2,1)S(1)}, bf16[2,6,3,1024]{3,0,2,1:T(2,128)(2,1)S(1)}, u32[]{:S(2)}, u32[]{:S(2)}) collective-permute-start(bf16[2,6,3,1024]{3,0,2,1:T(2,128)(2,1)S(1)} %broadcast_select_fusion.4), channel_id=1, source_target_pairs={{0,4},{1,5},{2,6},{3,7},{4,8},{5,9},{6,10},{7,11},{8,12},{9,13},{1... | collective-permute-start | bytes 221192 | tf_op jit(solution)/shard_map/ppermute | solution.py:26
  17.7 10.6 %copy-start = (bf16[1024,6,3,256]{3,0,2,1:T(8,128)(2,1)S(1)}, bf16[1024,6,3,256]{3,0,2,1:T(8,128)(2,1)}, u32[]{:S(2)}) copy-start(bf16[1024,6,3,256]{3,0,2,1:T(8,128)(2,1)} %param.5) | copy-start | bytes 28311556
  26.3 14.0 %collective-permute-start.6 = (f32[256,512]{1,0:T(8,128)S(1)}, f32[256,512]{1,0:T(8,128)S(1)}, u32[]{:S(2)}, u32[]{:S(2)}) collective-permute-start(f32[256,512]{1,0:T(8,128)S(1)} %fusion.18), channel_id=1, source_target_pairs={{0,32},{16,48},{32,64},{48,80},{64,96},{80,112},{96,0},{112,16},{1... | collective-permute-start | bytes 1572872 | tf_op jit(solution)/shard_map/ppermute | solution.py:107
  31.0 12.1 %collective-permute-start.10 = (f32[256,512]{1,0:T(8,128)S(1)}, f32[256,512]{1,0:T(8,128)S(1)}, u32[]{:S(2)}, u32[]{:S(2)}) collective-permute-start(f32[256,512]{1,0:T(8,128)S(1)} %fusion.21), channel_id=1, source_target_pairs={{0,96},{16,112},{32,0},{48,16},{64,32},{80,48},{96,64},{112,80},{1... | collective-permute-start | bytes 1572872 | tf_op jit(solution)/shard_map/ppermute | solution.py:107
  40.4 12.2 %collective-permute-start.7 = (f32[256,512]{1,0:T(8,128)S(1)}, f32[256,512]{1,0:T(8,128)S(1)}, u32[]{:S(2)}, u32[]{:S(2)}) collective-permute-start(f32[256,512]{1,0:T(8,128)S(1)} %add.211), channel_id=1, source_target_pairs={{0,32},{16,48},{32,64},{48,80},{64,96},{80,112},{96,0},{112,16},{1... | collective-permute-start | bytes 1572872 | tf_op jit(solution)/shard_map/ppermute | solution.py:113
  43.3 12.2 %collective-permute-start.11 = (f32[256,512]{1,0:T(8,128)S(1)}, f32[256,512]{1,0:T(8,128)S(1)}, u32[]{:S(2)}, u32[]{:S(2)}) collective-permute-start(f32[256,512]{1,0:T(8,128)S(1)} %add.226), channel_id=1, source_target_pairs={{0,96},{16,112},{32,0},{48,16},{64,32},{80,48},{96,64},{112,80},{1... | collective-permute-start | bytes 1572872 | tf_op jit(solution)/shard_map/ppermute | solution.py:113
  52.7 11.3 %collective-permute-start.8 = (f32[256,512]{1,0:T(8,128)S(1)}, f32[256,512]{1,0:T(8,128)S(1)}, u32[]{:S(2)}, u32[]{:S(2)}) collective-permute-start(f32[256,512]{1,0:T(8,128)S(1)} %add.216), channel_id=1, source_target_pairs={{0,32},{16,48},{32,64},{48,80},{64,96},{80,112},{96,0},{112,16},{1... | collective-permute-start | bytes 1572872 | tf_op jit(solution)/shard_map/ppermute | solution.py:113
  55.6 12.3 %collective-permute-start.12 = (f32[256,512]{1,0:T(8,128)S(1)}, f32[256,512]{1,0:T(8,128)S(1)}, u32[]{:S(2)}, u32[]{:S(2)}) collective-permute-start(f32[256,512]{1,0:T(8,128)S(1)} %add.227), channel_id=1, source_target_pairs={{0,96},{16,112},{32,0},{48,16},{64,32},{80,48},{96,64},{112,80},{1... | collective-permute-start | bytes 1572872 | tf_op jit(solution)/shard_map/ppermute | solution.py:113
  64.1 8.5 %collective-permute-start.9 = (f32[128,512]{1,0:T(8,128)S(1)}, f32[128,512]{1,0:T(8,128)S(1)}, u32[]{:S(2)}, u32[]{:S(2)}) collective-permute-start(f32[128,512]{1,0:T(8,128)S(1)} %get-tuple-element.43), channel_id=1, source_target_pairs={{0,16},{16,0},{32,48},{48,32},{64,80},{80,64},{96,112},{112,96},{1... | collective-permute-start | bytes 786440 | tf_op jit(solution)/shard_map/ppermute | solution.py:118
  68.0 8.0 %collective-permute-start.13 = (f32[128,512]{1,0:T(8,128)S(1)}, f32[128,512]{1,0:T(8,128)S(1)}, u32[]{:S(2)}, u32[]{:S(2)}) collective-permute-start(f32[128,512]{1,0:T(8,128)S(1)} %get-tuple-element.45), channel_id=1, source_target_pairs={{0,16},{16,0},{32,48},{48,32},{64,80},{80,64},{96,112},{112,96},{1... | collective-permute-start | bytes 786440 | tf_op jit(solution)/shard_map/ppermute | solution.py:118

commit v16 on v15

--- a/solution.py
+++ b/solution.py
@@ -77,7 +77,10 @@
     rev = jnp.dot(traces, anti, preferred_element_type=jnp.float32).reshape(EV * rows, 1, SAMPLES)
     shifts = ((jnp.repeat(onsets.astype(jnp.int32), 3, axis=1) - LAGS) % SAMPLES).reshape(-1)
     weights = jnp.exp2(-codes.astype(jnp.float32)).reshape(-1)
-    bands = toeplitz_reversed(rev, shifts, weights)
+    bands = [
+        toeplitz_reversed(rev[e * rows : (e + 1) * rows], shifts[e * rows : (e + 1) * rows], weights)[0]
+        for e in range(EV)
+    ]
 
     size = lax.axis_size("sens")
     me = lax.axis_index("sens")

time: 77.9 us -> 79.1 us (1.015)
  waiting for transfers between devices: 30.9 us -> 27.2 us
  Pallas kernels: 5.14 us -> 8.41 us
  starting transfers between devices: 21.1 us -> 22.5 us
    pallas_call x1 -> x2, Pallas kernels: 5.14 us -> 8.41 us  [toeplitz_reversed(): pl.pallas_call(_toeplitz_kernel, in_specs=[pl.BlockSpec(memory_space=pltp...]
    ppermute x4, waiting for transfers between devices: 11.1 us -> 8.86 us  [local(): gots[e] = lax.ppermute(accs[e], 'sens', ring_perm(step))]
    ppermute x2, waiting for transfers between devices: 5.46 us -> 4.23 us  [local(): got = lax.ppermute(theirs, 'sens', [(i, i ^ 1) for i in range(size)])]
    ppermute x2, starting transfers between devices: 3.69 us -> 4.91 us  [local(): got = lax.ppermute(theirs, 'sens', [(i, i ^ 1) for i in range(size)])]
  transfers between devices with their start and end apart: 14 -> 14, of which waited for: 9 -> 12; matrix products, arithmetic and copies ran while one was open for 18% -> 17% of each run, Pallas kernels for 0% -> 5%
where the time goes in v16:
time: 79.1 us; the launch traced here: 78.9 us
  waiting for transfers between devices  27.2 us (34%)
  starting transfers between devices  22.5 us (28%)
  matrix products  13 us (16%)
  Pallas kernels  8.41 us (11%)
  other arithmetic  4.04 us (5%)
  local copies, waits for them, and re-layouts  3.38 us (4%)
    dot_general x8, matrix products, piece(): jnp.einsum('rpt,rtn->pn', g, band.reshape(rows, NT, LAGS), preferred_elem...  12.7 us
    ppermute x4, waiting for transfers between devices, local(): gots[e] = lax.ppermute(accs[e], 'sens', ring_perm(step))  8.86 us
    pallas_call x2, Pallas kernels, toeplitz_reversed(): pl.pallas_call(_toeplitz_kernel, in_specs=[pl.BlockSpec(memory_space=pltp...  8.41 us
    ppermute x6, waiting for transfers between devices, from_owners(): got = lax.ppermute(x, axis, perm)  7.26 us
    ppermute x4, starting transfers between devices, local(): gots[e] = lax.ppermute(accs[e], 'sens', ring_perm(step))  6.89 us
    ppermute x2, waiting for transfers between devices, local(): gots.append(lax.ppermute(acc, 'sens', ring_perm(step)))  6.88 us
    ppermute x6, starting transfers between devices, from_owners(): got = lax.ppermute(x, axis, perm)  6.49 us
    ppermute x2, starting transfers between devices, local(): got = lax.ppermute(theirs, 'sens', [(i, i ^ 1) for i in range(size)])  4.91 us
  transfers between devices with their start and end apart: 14, of which 12 were waited for; matrix products, arithmetic and copies ran while one was open for 17% of the time, Pallas kernels for 5%

profile of v16, /device:TPU:0, one launch (start us, length us, event | category | flops | bytes accessed | tf_op | source)
XLA Modules:
  0.0 78.9 jit_solution(3048552363695941504)
XLA Ops:
  0.0 1.0 %collective-permute-start = (bf16[2,6,3,1024]{3,0,2,1:T(2,128)(2,1)}, bf16[2,6,3,1024]{3,0,2,1:T(2,128)(2,1)S(1)}, u32[]{:S(2)}, u32[]{:S(2)}) collective-permute-start(bf16[2,6,3,1024]{3,0,2,1:T(2,128)(2,1)} %bitcast.48), channel_id=1, source_target_pairs={{0,3},{1,0},{2,1},{3,2},{4,7},{5,4},{6,5},{7,6},{8,11},{9,8},{10,9... | collective-permute-start | bytes 221192 | tf_op jit(solution)/shard_map/ppermute | solution.py:26
  1.0 0.6 collective-permute-start.1
  1.6 0.2 collective-permute-start.2
  1.8 0.7 broadcast_add_fusion
  2.5 0.1 broadcast_in_dim.36
  2.6 0.1 sub.68
  2.7 0.7 multiply_exponential_fusion
  3.4 0.7 broadcast_compare_fusion
  4.1 0.0 collective-permute-done
  4.1 2.4 %collective-permute-done.1 = bf16[2,6,3,1024]{3,0,2,1:T(2,128)(2,1)S(1)} collective-permute-done((bf16[2,6,3,1024]{3,0,2,1:T(2,128)(2,1)}, bf16[2,6,3,1024]{3,0,2,1:T(2,128)(2,1)S(1)}, u32[]{:S(2)}, u32[]{:S(2)}) %collective-permute-start.1) | collective-permute-done | bytes 73760 | tf_op jit(solution)/shard_map/ppermute | solution.py:26
  6.5 1.1 %broadcast_select_fusion.4 = bf16[2,6,3,1024]{3,0,2,1:T(2,128)(2,1)S(1)} fusion(bf16[2,6,3,1024]{3,0,2,1:T(2,128)(2,1)S(1)} %collective-permute-done, pred[2]{0:T(512)(128)(4,1)S(1)} %get-tuple-element.52, bf16[2,6,3,1024]{3,0,2,1:T(2,128)(2,1)S(1)} %collective-permute-done.1, pred[2]{0:T(512)(128)(4,1)S(1)} %get-tuple-element.51, ...), kind=kLoop, calls=%fused_computation.34 | loop fusion | flops 110592 | bytes 368646 | tf_op jit(solution)/shard_map/jit(_where)/select_n | solution.py:28
  7.6 3.1 %collective-permute-start.3 = (bf16[2,6,3,1024]{3,0,2,1:T(2,128)(2,1)S(1)}, bf16[2,6,3,1024]{3,0,2,1:T(2,128)(2,1)S(1)}, u32[]{:S(2)}, u32[]{:S(2)}) collective-permute-start(bf16[2,6,3,1024]{3,0,2,1:T(2,128)(2,1)S(1)} %broadcast_select_fusion.4), channel_id=1, source_target_pairs={{0,12},{1,13},{2,14},{3,15},{4,0},{5,1},{6,2},{7,3},{8,4},{9,5},{1... | collective-permute-start | bytes 221192 | tf_op jit(solution)/shard_map/ppermute | solution.py:26
  10.7 0.6 collective-permute-start.4
  11.3 1.0 %collective-permute-start.5 = (bf16[2,6,3,1024]{3,0,2,1:T(2,128)(2,1)S(1)}, bf16[2,6,3,1024]{3,0,2,1:T(2,128)(2,1)S(1)}, u32[]{:S(2)}, u32[]{:S(2)}) collective-permute-start(bf16[2,6,3,1024]{3,0,2,1:T(2,128)(2,1)S(1)} %broadcast_select_fusion.4), channel_id=1, source_target_pairs={{0,4},{1,5},{2,6},{3,7},{4,8},{5,9},{6,10},{7,11},{8,12},{9,13},{1... | collective-permute-start | bytes 221192 | tf_op jit(solution)/shard_map/ppermute | solution.py:26
  12.3 0.1 copy.8
  12.4 0.1 reshape.43.weight_ref
  12.5 0.2 collective-permute-done.3
  12.7 3.9 %collective-permute-done.4 = bf16[2,6,3,1024]{3,0,2,1:T(2,128)(2,1)S(1)} collective-permute-done((bf16[2,6,3,1024]{3,0,2,1:T(2,128)(2,1)S(1)}, bf16[2,6,3,1024]{3,0,2,1:T(2,128)(2,1)S(1)}, u32[]{:S(2)}, u32[]{:S(2)}) %collective-permute-start.4) | collective-permute-done | bytes 73760 | tf_op jit(solution)/shard_map/ppermute | solution.py:26
  16.6 0.7 collective-permute-done.5
  17.3 0.2 broadcast_select_fusion.5
  17.6 0.1 reshape.44
  17.7 0.0 slice-start
  17.7 0.3 fusion
  18.0 0.1 slice.27.rev_ref
  18.1 0.0 slice-start.1
  18.1 4.2 %shard_map.55 = bf16[4608,512]{1,0:T(8,128)(2,1)S(1)} custom-call(s32[18]{0:T(128)S(1)} %get-tuple-element.45.shift_ref, f32[18]{0:T(128)S(1)} %reshape.43.weight_ref, f32[18,1,1024]{2,1,0:T(1,128)S(1)} %slice.27.rev_ref), custom_call_target="tpu_custom_call" | custom-call | bytes 4718592 | tf_op jit(solution)/shard_map/pallas_call | solution.py:55
  22.3 0.0 slice-start.2
  22.3 3.1 %fusion.18 = f32[256,512]{1,0:T(8,128)S(1)} fusion(bf16[18,256,512]{2,1,0:T(8,128)(2,1)S(1)} %bitcast.44, bf16[18,1024,256]{2,1,0:T(8,128)(2,1)} %bitcast.51, s32[]{:T(128)S(6)} %select_n.154), kind=kOutput, calls=%fused_computation.19 | convolution fusion | flops 1207959552 | bytes 7602180 | tf_op jit(solution)/shard_map/rpt,rtn->pn/dot_general | solution.py:95
  25.5 0.1 slice.31.rev_ref
  25.5 2.0 %collective-permute-start.6 = (f32[256,512]{1,0:T(8,128)S(1)}, f32[256,512]{1,0:T(8,128)S(1)}, u32[]{:S(2)}, u32[]{:S(2)}) collective-permute-start(f32[256,512]{1,0:T(8,128)S(1)} %fusion.18), channel_id=1, source_target_pairs={{0,32},{16,48},{32,64},{48,80},{64,96},{80,112},{96,0},{112,16},{1... | collective-permute-start | bytes 1572872 | tf_op jit(solution)/shard_map/ppermute | solution.py:110
  27.5 4.2 %shard_map.56 = bf16[4608,512]{1,0:T(8,128)(2,1)S(1)} custom-call(s32[18]{0:T(128)S(1)} %get-tuple-element.46.shift_ref, f32[18]{0:T(128)S(1)} %reshape.43.weight_ref, f32[18,1,1024]{2,1,0:T(1,128)S(1)} %slice.31.rev_ref), custom_call_target="tpu_custom_call" | custom-call | bytes 4718592 | tf_op jit(solution)/shard_map/pallas_call | solution.py:55
  31.8 1.4 %fusion.21 = f32[256,512]{1,0:T(8,128)S(1)} fusion(bf16[18,256,512]{2,1,0:T(8,128)(2,1)S(1)} %bitcast.40, bf16[18,1024,256]{2,1,0:T(8,128)(2,1)S(1)} %bitcast.54, s32[]{:T(128)S(6)} %select_n.175), kind=kOutput, calls=%fused_computation.20 | convolution fusion | flops 1207959552 | bytes 7602180 | tf_op jit(solution)/shard_map/rpt,rtn->pn/dot_general | solution.py:95
  33.1 1.4 %fusion.24 = f32[256,512]{1,0:T(8,128)S(1)} fusion(bf16[18,256,512]{2,1,0:T(8,128)(2,1)S(1)} %bitcast.45, bf16[18,1024,256]{2,1,0:T(8,128)(2,1)S(1)} %bitcast.55, s32[]{:T(128)S(6)} %select_n.177), kind=kOutput, calls=%fused_computation.21 | convolution fusion | flops 1207959552 | bytes 7602180 | tf_op jit(solution)/shard_map/rpt,rtn->pn/dot_general | solution.py:95
  34.5 2.2 %collective-permute-start.10 = (f32[256,512]{1,0:T(8,128)S(1)}, f32[256,512]{1,0:T(8,128)S(1)}, u32[]{:S(2)}, u32[]{:S(2)}) collective-permute-start(f32[256,512]{1,0:T(8,128)S(1)} %fusion.21), channel_id=1, source_target_pairs={{0,96},{16,112},{32,0},{48,16},{64,32},{80,48},{96,64},{112,80},{1... | collective-permute-start | bytes 1572872 | tf_op jit(solution)/shard_map/ppermute | solution.py:110
  36.7 2.8 %collective-permute-done.6 = f32[256,512]{1,0:T(8,128)S(1)} collective-permute-done((f32[256,512]{1,0:T(8,128)S(1)}, f32[256,512]{1,0:T(8,128)S(1)}, u32[]{:S(2)}, u32[]{:S(2)}) %collective-permute-start.6) | collective-permute-done | bytes 524320 | tf_op jit(solution)/shard_map/ppermute | solution.py:110
  39.5 0.1 add.209
  39.6 0.1 collective-permute-start.7
  39.7 1.4 %fusion.27 = f32[256,512]{1,0:T(8,128)S(1)} fusion(bf16[18,256,512]{2,1,0:T(8,128)(2,1)S(1)} %bitcast.41, bf16[18,1024,256]{2,1,0:T(8,128)(2,1)S(1)} %bitcast.56, s32[]{:T(128)S(6)} %select_n.179), kind=kOutput, calls=%fused_computation.22 | convolution fusion | flops 1207959552 | bytes 7602180 | tf_op jit(solution)/shard_map/rpt,rtn->pn/dot_general | solution.py:95
  41.0 1.4 %fusion.30 = f32[256,512]{1,0:T(8,128)S(1)} fusion(bf16[18,256,512]{2,1,0:T(8,128)(2,1)S(1)} %bitcast.46, bf16[18,1024,256]{2,1,0:T(8,128)(2,1)S(1)} %bitcast.57, s32[]{:T(128)S(6)} %select_n.181), kind=kOutput, calls=%fused_computation.23 | convolution fusion | flops 1207959552 | bytes 7602180 | tf_op jit(solution)/shard_map/rpt,rtn->pn/dot_general | solution.py:95
  42.4 4.1 %collective-permute-done.10 = f32[256,512]{1,0:T(8,128)S(1)} collective-permute-done((f32[256,512]{1,0:T(8,128)S(1)}, f32[256,512]{1,0:T(8,128)S(1)}, u32[]{:S(2)}, u32[]{:S(2)}) %collective-permute-start.10) | collective-permute-done | bytes 524320 | tf_op jit(solution)/shard_map/ppermute | solution.py:110
  46.5 0.1 add.224
  46.6 3.1 %collective-permute-start.11 = (f32[256,512]{1,0:T(8,128)S(1)}, f32[256,512]{1,0:T(8,128)S(1)}, u32[]{:S(2)}, u32[]{:S(2)}) collective-permute-start(f32[256,512]{1,0:T(8,128)S(1)} %add.224), channel_id=1, source_target_pairs={{0,96},{16,112},{32,0},{48,16},{64,32},{80,48},{96,64},{112,80},{1... | collective-permute-start | bytes 1572872 | tf_op jit(solution)/shard_map/ppermute | solution.py:116
  49.7 2.1 %collective-permute-done.7 = f32[256,512]{1,0:T(8,128)S(1)} collective-permute-done((f32[256,512]{1,0:T(8,128)S(1)}, f32[256,512]{1,0:T(8,128)S(1)}, u32[]{:S(2)}, u32[]{:S(2)}) %collective-permute-start.7) | collective-permute-done | bytes 524320 | tf_op jit(solution)/shard_map/ppermute | solution.py:116
  51.8 0.1 add.214
  51.9 0.1 collective-permute-start.8
  52.0 1.4 %fusion.33 = f32[256,512]{1,0:T(8,128)S(1)} fusion(bf16[18,256,512]{2,1,0:T(8,128)(2,1)S(1)} %bitcast.42, bf16[18,1024,256]{2,1,0:T(8,128)(2,1)S(1)} %bitcast.58, s32[]{:T(128)S(6)} %select_n.183), kind=kOutput, calls=%fused_computation.24 | convolution fusion | flops 1207959552 | bytes 7602180 | tf_op jit(solution)/shard_map/rpt,rtn->pn/dot_general | solution.py:95
  53.4 1.4 %fusion.36 = f32[256,512]{1,0:T(8,128)S(1)} fusion(bf16[18,256,512]{2,1,0:T(8,128)(2,1)S(1)} %bitcast.47, bf16[18,1024,256]{2,1,0:T(8,128)(2,1)S(1)} %bitcast.59, s32[]{:T(128)S(6)} %select_n.185), kind=kOutput, calls=%fused_computation.25 | convolution fusion | flops 1207959552 | bytes 7602180 | tf_op jit(solution)/shard_map/rpt,rtn->pn/dot_general | solution.py:95
  54.7 3.3 %collective-permute-done.11 = f32[256,512]{1,0:T(8,128)S(1)} collective-permute-done((f32[256,512]{1,0:T(8,128)S(1)}, f32[256,512]{1,0:T(8,128)S(1)}, u32[]{:S(2)}, u32[]{:S(2)}) %collective-permute-start.11) | collective-permute-done | bytes 524320 | tf_op jit(solution)/shard_map/ppermute | solution.py:116
  58.0 0.1 add.225
  58.1 3.7 %collective-permute-start.12 = (f32[256,512]{1,0:T(8,128)S(1)}, f32[256,512]{1,0:T(8,128)S(1)}, u32[]{:S(2)}, u32[]{:S(2)}) collective-permute-start(f32[256,512]{1,0:T(8,128)S(1)} %add.225), channel_id=1, source_target_pairs={{0,96},{16,112},{32,0},{48,16},{64,32},{80,48},{96,64},{112,80},{1... | collective-permute-start | bytes 1572872 | tf_op jit(solution)/shard_map/ppermute | solution.py:116
  61.8 1.4 %collective-permute-done.8 = f32[256,512]{1,0:T(8,128)S(1)} collective-permute-done((f32[256,512]{1,0:T(8,128)S(1)}, f32[256,512]{1,0:T(8,128)S(1)}, u32[]{:S(2)}, u32[]{:S(2)}) %collective-permute-start.8) | collective-permute-done | bytes 524320 | tf_op jit(solution)/shard_map/ppermute | solution.py:116
  63.2 0.1 add.219
  63.4 2.4 %collective-permute-start.9 = (f32[128,512]{1,0:T(8,128)S(1)}, f32[128,512]{1,0:T(8,128)S(1)}, u32[]{:S(2)}, u32[]{:S(2)}) collective-permute-start(f32[128,512]{1,0:T(8,128)S(1)} %get-tuple-element.39), channel_id=1, source_target_pairs={{0,16},{16,0},{32,48},{48,32},{64,80},{80,64},{96,112},{112,96},{1... | collective-permute-start | bytes 786440 | tf_op jit(solution)/shard_map/ppermute | solution.py:121
  65.7 1.4 %fusion.39 = f32[256,512]{1,0:T(8,128)S(1)} fusion(bf16[18,256,512]{2,1,0:T(8,128)(2,1)S(1)} %bitcast.43, bf16[18,1024,256]{2,1,0:T(8,128)(2,1)S(1)} %bitcast.60, s32[]{:T(128)S(6)} %select_n.190), kind=kOutput, calls=%fused_computation.26 | convolution fusion | flops 1207959552 | bytes 7602180 | tf_op jit(solution)/shard_map/rpt,rtn->pn/dot_general | solution.py:95
  67.1 2.0 %collective-permute-done.12 = f32[256,512]{1,0:T(8,128)S(1)} collective-permute-done((f32[256,512]{1,0:T(8,128)S(1)}, f32[256,512]{1,0:T(8,128)S(1)}, u32[]{:S(2)}, u32[]{:S(2)}) %collective-permute-start.12) | collective-permute-done | bytes 524320 | tf_op jit(solution)/shard_map/ppermute | solution.py:116
  69.1 0.1 add.228
  69.3 2.5 %collective-permute-start.13 = (f32[128,512]{1,0:T(8,128)S(1)}, f32[128,512]{1,0:T(8,128)S(1)}, u32[]{:S(2)}, u32[]{:S(2)}) collective-permute-start(f32[128,512]{1,0:T(8,128)S(1)} %get-tuple-element.41), channel_id=1, source_target_pairs={{0,16},{16,0},{32,48},{48,32},{64,80},{80,64},{96,112},{112,96},{1... | collective-permute-start | bytes 786440 | tf_op jit(solution)/shard_map/ppermute | solution.py:121
  71.8 0.4 rev.13
  72.2 0.4 rev.15
  72.6 1.6 %collective-permute-done.9 = f32[128,512]{1,0:T(8,128)S(1)} collective-permute-done((f32[128,512]{1,0:T(8,128)S(1)}, f32[128,512]{1,0:T(8,128)S(1)}, u32[]{:S(2)}, u32[]{:S(2)}) %collective-permute-start.9) | collective-permute-done | bytes 262176 | tf_op jit(solution)/shard_map/ppermute | solution.py:121
  74.1 0.4 rev.14
  74.5 2.7 %collective-permute-done.13 = f32[128,512]{1,0:T(8,128)S(1)} collective-permute-done((f32[128,512]{1,0:T(8,128)S(1)}, f32[128,512]{1,0:T(8,128)S(1)}, u32[]{:S(2)}, u32[]{:S(2)}) %collective-permute-start.13) | collective-permute-done | bytes 262176 | tf_op jit(solution)/shard_map/ppermute | solution.py:121
  77.2 0.4 rev.16
  77.7 1.2 %copy.10 = f32[128,2,512]{2,1,0:T(2,128)} copy(f32[128,2,512]{2,0,1:T(8,128)S(1)} %pad_maximum_fusion) | data formatting | bytes 1048576 | tf_op jit(solution)/shard_map/stack | solution.py:123
  (16 shorter events, 0.3 us)
Async XLA Ops:
  0.0 4.1 %collective-permute-start = (bf16[2,6,3,1024]{3,0,2,1:T(2,128)(2,1)}, bf16[2,6,3,1024]{3,0,2,1:T(2,128)(2,1)S(1)}, u32[]{:S(2)}, u32[]{:S(2)}) collective-permute-start(bf16[2,6,3,1024]{3,0,2,1:T(2,128)(2,1)} %bitcast.48), channel_id=1, source_target_pairs={{0,3},{1,0},{2,1},{3,2},{4,7},{5,4},{6,5},{7,6},{8,11},{9,8},{10,9... | collective-permute-start | bytes 221192 | tf_op jit(solution)/shard_map/ppermute | solution.py:26
  1.0 5.5 %collective-permute-start.1 = (bf16[2,6,3,1024]{3,0,2,1:T(2,128)(2,1)}, bf16[2,6,3,1024]{3,0,2,1:T(2,128)(2,1)S(1)}, u32[]{:S(2)}, u32[]{:S(2)}) collective-permute-start(bf16[2,6,3,1024]{3,0,2,1:T(2,128)(2,1)} %bitcast.49), channel_id=1, source_target_pairs={{0,2},{1,3},{2,0},{3,1},{4,6},{5,7},{6,4},{7,5},{8,10},{9,11},{10,... | collective-permute-start | bytes 221192 | tf_op jit(solution)/shard_map/ppermute | solution.py:26
  1.6 4.9 %collective-permute-start.2 = (bf16[2,6,3,1024]{3,0,2,1:T(2,128)(2,1)}, bf16[2,6,3,1024]{3,0,2,1:T(2,128)(2,1)S(1)}, u32[]{:S(2)}, u32[]{:S(2)}) collective-permute-start(bf16[2,6,3,1024]{3,0,2,1:T(2,128)(2,1)} %bitcast.50), channel_id=1, source_target_pairs={{0,1},{1,2},{2,3},{3,0},{4,5},{5,6},{6,7},{7,4},{8,9},{9,10},{10,1... | collective-permute-start | bytes 221192 | tf_op jit(solution)/shard_map/ppermute | solution.py:26
  7.6 5.1 %collective-permute-start.3 = (bf16[2,6,3,1024]{3,0,2,1:T(2,128)(2,1)S(1)}, bf16[2,6,3,1024]{3,0,2,1:T(2,128)(2,1)S(1)}, u32[]{:S(2)}, u32[]{:S(2)}) collective-permute-start(bf16[2,6,3,1024]{3,0,2,1:T(2,128)(2,1)S(1)} %broadcast_select_fusion.4), channel_id=1, source_target_pairs={{0,12},{1,13},{2,14},{3,15},{4,0},{5,1},{6,2},{7,3},{8,4},{9,5},{1... | collective-permute-start | bytes 221192 | tf_op jit(solution)/shard_map/ppermute | solution.py:26
  10.7 5.9 %collective-permute-start.4 = (bf16[2,6,3,1024]{3,0,2,1:T(2,128)(2,1)S(1)}, bf16[2,6,3,1024]{3,0,2,1:T(2,128)(2,1)S(1)}, u32[]{:S(2)}, u32[]{:S(2)}) collective-permute-start(bf16[2,6,3,1024]{3,0,2,1:T(2,128)(2,1)S(1)} %broadcast_select_fusion.4), channel_id=1, source_target_pairs={{0,8},{1,9},{2,10},{3,11},{4,12},{5,13},{6,14},{7,15},{8,0},{9,1},... | collective-permute-start | bytes 221192 | tf_op jit(solution)/shard_map/ppermute | solution.py:26
  11.3 6.0 %collective-permute-start.5 = (bf16[2,6,3,1024]{3,0,2,1:T(2,128)(2,1)S(1)}, bf16[2,6,3,1024]{3,0,2,1:T(2,128)(2,1)S(1)}, u32[]{:S(2)}, u32[]{:S(2)}) collective-permute-start(bf16[2,6,3,1024]{3,0,2,1:T(2,128)(2,1)S(1)} %broadcast_select_fusion.4), channel_id=1, source_target_pairs={{0,4},{1,5},{2,6},{3,7},{4,8},{5,9},{6,10},{7,11},{8,12},{9,13},{1... | collective-permute-start | bytes 221192 | tf_op jit(solution)/shard_map/ppermute | solution.py:26
  17.7 14.0 %slice-start = ((s8[9437184]{0:T(1024)(128)(4,1)}), s8[4194304]{0:T(1024)(128)(4,1)S(1)}, s32[]{:S(2)}) async-start(s8[9437184]{0:T(1024)(128)(4,1)} %bitcast.52), calls=%async_computation | async-start | bytes 8388608
  18.1 13.7 %slice-start.1 = ((s8[9437184]{0:T(1024)(128)(4,1)}), s8[4194304]{0:T(1024)(128)(4,1)S(1)}, s32[]{:S(2)}) async-start(s8[9437184]{0:T(1024)(128)(4,1)} %bitcast.52), calls=%async_computation.1 | async-start | bytes 8388608
  22.3 9.4 %slice-start.2 = ((s8[9437184]{0:T(1024)(128)(4,1)}), s8[1048576]{0:T(1024)(128)(4,1)S(1)}, s32[]{:S(2)}) async-start(s8[9437184]{0:T(1024)(128)(4,1)} %bitcast.52), calls=%async_computation.2 | async-start | bytes 2097152
  25.5 14.0 %collective-permute-start.6 = (f32[256,512]{1,0:T(8,128)S(1)}, f32[256,512]{1,0:T(8,128)S(1)}, u32[]{:S(2)}, u32[]{:S(2)}) collective-permute-start(f32[256,512]{1,0:T(8,128)S(1)} %fusion.18), channel_id=1, source_target_pairs={{0,32},{16,48},{32,64},{48,80},{64,96},{80,112},{96,0},{112,16},{1... | collective-permute-start | bytes 1572872 | tf_op jit(solution)/shard_map/ppermute | solution.py:110
  34.5 12.0 %collective-permute-start.10 = (f32[256,512]{1,0:T(8,128)S(1)}, f32[256,512]{1,0:T(8,128)S(1)}, u32[]{:S(2)}, u32[]{:S(2)}) collective-permute-start(f32[256,512]{1,0:T(8,128)S(1)} %fusion.21), channel_id=1, source_target_pairs={{0,96},{16,112},{32,0},{48,16},{64,32},{80,48},{96,64},{112,80},{1... | collective-permute-start | bytes 1572872 | tf_op jit(solution)/shard_map/ppermute | solution.py:110
  39.6 12.2 %collective-permute-start.7 = (f32[256,512]{1,0:T(8,128)S(1)}, f32[256,512]{1,0:T(8,128)S(1)}, u32[]{:S(2)}, u32[]{:S(2)}) collective-permute-start(f32[256,512]{1,0:T(8,128)S(1)} %add.209), channel_id=1, source_target_pairs={{0,32},{16,48},{32,64},{48,80},{64,96},{80,112},{96,0},{112,16},{1... | collective-permute-start | bytes 1572872 | tf_op jit(solution)/shard_map/ppermute | solution.py:116
  46.6 11.4 %collective-permute-start.11 = (f32[256,512]{1,0:T(8,128)S(1)}, f32[256,512]{1,0:T(8,128)S(1)}, u32[]{:S(2)}, u32[]{:S(2)}) collective-permute-start(f32[256,512]{1,0:T(8,128)S(1)} %add.224), channel_id=1, source_target_pairs={{0,96},{16,112},{32,0},{48,16},{64,32},{80,48},{96,64},{112,80},{1... | collective-permute-start | bytes 1572872 | tf_op jit(solution)/shard_map/ppermute | solution.py:116
  51.9 11.3 %collective-permute-start.8 = (f32[256,512]{1,0:T(8,128)S(1)}, f32[256,512]{1,0:T(8,128)S(1)}, u32[]{:S(2)}, u32[]{:S(2)}) collective-permute-start(f32[256,512]{1,0:T(8,128)S(1)} %add.214), channel_id=1, source_target_pairs={{0,32},{16,48},{32,64},{48,80},{64,96},{80,112},{96,0},{112,16},{1... | collective-permute-start | bytes 1572872 | tf_op jit(solution)/shard_map/ppermute | solution.py:116
  58.1 11.0 %collective-permute-start.12 = (f32[256,512]{1,0:T(8,128)S(1)}, f32[256,512]{1,0:T(8,128)S(1)}, u32[]{:S(2)}, u32[]{:S(2)}) collective-permute-start(f32[256,512]{1,0:T(8,128)S(1)} %add.225), channel_id=1, source_target_pairs={{0,96},{16,112},{32,0},{48,16},{64,32},{80,48},{96,64},{112,80},{1... | collective-permute-start | bytes 1572872 | tf_op jit(solution)/shard_map/ppermute | solution.py:116
  63.4 10.8 %collective-permute-start.9 = (f32[128,512]{1,0:T(8,128)S(1)}, f32[128,512]{1,0:T(8,128)S(1)}, u32[]{:S(2)}, u32[]{:S(2)}) collective-permute-start(f32[128,512]{1,0:T(8,128)S(1)} %get-tuple-element.39), channel_id=1, source_target_pairs={{0,16},{16,0},{32,48},{48,32},{64,80},{80,64},{96,112},{112,96},{1... | collective-permute-start | bytes 786440 | tf_op jit(solution)/shard_map/ppermute | solution.py:121
  69.3 8.0 %collective-permute-start.13 = (f32[128,512]{1,0:T(8,128)S(1)}, f32[128,512]{1,0:T(8,128)S(1)}, u32[]{:S(2)}, u32[]{:S(2)}) collective-permute-start(f32[128,512]{1,0:T(8,128)S(1)} %get-tuple-element.41), channel_id=1, source_target_pairs={{0,16},{16,0},{32,48},{48,32},{64,80},{80,64},{96,112},{112,96},{1... | collective-permute-start | bytes 786440 | tf_op jit(solution)/shard_map/ppermute | solution.py:121

commit v17 on v15

--- a/solution.py
+++ b/solution.py
@@ -15,19 +15,20 @@
 def from_owners(x, axis, roots, radix=4):
     size = lax.axis_size(axis)
     me = lax.axis_index(axis)
-    span = 1
+    spans, span = [], 1
     while span < size:
-        radix = min(radix, size // span)
-        digit = (roots // span) % radix
-        mine = (me // span) % radix
+        spans.append((span, min(radix, size // span)))
+        span *= radix
+    for span, r in reversed(spans):
+        digit = (roots // span) % r
+        mine = (me // span) % r
         out = x
-        for d in range(1, radix):
-            perm = [(i, i - ((i // span) % radix) * span + (((i // span) % radix + d) % radix) * span) for i in range(size)]
+        for d in range(1, r):
+            perm = [(i, i - ((i // span) % r) * span + (((i // span) % r + d) % r) * span) for i in range(size)]
             got = lax.ppermute(x, axis, perm)
-            src = (mine + radix - d) % radix
+            src = (mine + r - d) % r
             out = jnp.where((src == digit).reshape((-1,) + (1,) * (x.ndim - 1)), got, out)
         x = out
-        span *= radix
     return x
 
 

time: 77.9 us -> 82.3 us (1.056)
  waiting for transfers between devices: 30.9 us -> 34.9 us
    ppermute x4, waiting for transfers between devices: 11.1 us -> 12.8 us  [local(): gots[e] = lax.ppermute(accs[e], 'sens', ring_perm(step))]
    ppermute x2, waiting for transfers between devices: 5.46 us -> 6.78 us  [local(): got = lax.ppermute(theirs, 'sens', [(i, i ^ 1) for i in range(size)])]
    ppermute x2, waiting for transfers between devices: 7.01 us -> 7.86 us  [local(): gots.append(lax.ppermute(acc, 'sens', ring_perm(step)))]
  transfers between devices with their start and end apart: 14 -> 14, of which waited for: 9 -> 9; matrix products, arithmetic and copies ran while one was open for 18% -> 17% of each run, Pallas kernels for 0% -> 0%
where the time goes in v17:
time: 82.3 us; the launch traced here: 82.1 us
  waiting for transfers between devices  34.9 us (42%)
  starting transfers between devices  21.5 us (26%)
  matrix products  12.9 us (16%)
  Pallas kernels  5.14 us (6%)
  other arithmetic  4.03 us (5%)
  local copies, waits for them, and re-layouts  3.34 us (4%)
    ppermute x4, waiting for transfers between devices, local(): gots[e] = lax.ppermute(accs[e], 'sens', ring_perm(step))  12.8 us
    dot_general x8, matrix products, piece(): jnp.einsum('rpt,rtn->pn', g, band.reshape(rows, NT, LAGS), preferred_elem...  12.7 us
    ppermute x2, waiting for transfers between devices, local(): gots.append(lax.ppermute(acc, 'sens', ring_perm(step)))  7.86 us
    ppermute x6, waiting for transfers between devices, from_owners(): got = lax.ppermute(x, axis, perm)  7.42 us
    ppermute x2, waiting for transfers between devices, local(): got = lax.ppermute(theirs, 'sens', [(i, i ^ 1) for i in range(size)])  6.78 us
    ppermute x4, starting transfers between devices, local(): gots[e] = lax.ppermute(accs[e], 'sens', ring_perm(step))  6.73 us
    ppermute x6, starting transfers between devices, from_owners(): got = lax.ppermute(x, axis, perm)  6.49 us
    pallas_call x1, Pallas kernels, toeplitz_reversed(): pl.pallas_call(_toeplitz_kernel, in_specs=[pl.BlockSpec(memory_space=pltp...  5.14 us
  transfers between devices with their start and end apart: 14, of which 9 were waited for; matrix products, arithmetic and copies ran while one was open for 17% of the time, Pallas kernels for 0%

profile of v17, /device:TPU:0, one launch (start us, length us, event | category | flops | bytes accessed | tf_op | source)
XLA Modules:
  0.0 82.1 jit_solution(10570393678785461978)
XLA Ops:
  0.0 3.1 %collective-permute-start = (bf16[2,6,3,1024]{3,0,2,1:T(2,128)(2,1)}, bf16[2,6,3,1024]{3,0,2,1:T(2,128)(2,1)S(1)}, u32[]{:S(2)}, u32[]{:S(2)}) collective-permute-start(bf16[2,6,3,1024]{3,0,2,1:T(2,128)(2,1)} %bitcast.44), channel_id=1, source_target_pairs={{0,12},{1,13},{2,14},{3,15},{4,0},{5,1},{6,2},{7,3},{8,4},{9,5},{1... | collective-permute-start | bytes 221192 | tf_op jit(solution)/shard_map/ppermute | solution.py:28
  3.1 0.6 collective-permute-start.1
  3.7 1.0 %collective-permute-start.2 = (bf16[2,6,3,1024]{3,0,2,1:T(2,128)(2,1)}, bf16[2,6,3,1024]{3,0,2,1:T(2,128)(2,1)S(1)}, u32[]{:S(2)}, u32[]{:S(2)}) collective-permute-start(bf16[2,6,3,1024]{3,0,2,1:T(2,128)(2,1)} %bitcast.46), channel_id=1, source_target_pairs={{0,4},{1,5},{2,6},{3,7},{4,8},{5,9},{6,10},{7,11},{8,12},{9,13},{1... | collective-permute-start | bytes 221192 | tf_op jit(solution)/shard_map/ppermute | solution.py:28
  4.7 0.7 broadcast_add_fusion
  5.4 0.7 multiply_exponential_fusion
  6.1 0.7 broadcast_compare_fusion
  6.8 0.1 broadcast_in_dim.36
  6.8 0.1 sub.68
  6.9 0.0 collective-permute-done
  6.9 2.4 %collective-permute-done.1 = bf16[2,6,3,1024]{3,0,2,1:T(2,128)(2,1)S(1)} collective-permute-done((bf16[2,6,3,1024]{3,0,2,1:T(2,128)(2,1)}, bf16[2,6,3,1024]{3,0,2,1:T(2,128)(2,1)S(1)}, u32[]{:S(2)}, u32[]{:S(2)}) %collective-permute-start.1) | collective-permute-done | bytes 73760 | tf_op jit(solution)/shard_map/ppermute | solution.py:28
  9.4 0.7 collective-permute-done.2
  10.1 1.1 %broadcast_select_fusion.4 = bf16[2,6,3,1024]{3,0,2,1:T(2,128)(2,1)S(1)} fusion(bf16[2,6,3,1024]{3,0,2,1:T(2,128)(2,1)S(1)} %collective-permute-done, pred[2]{0:T(512)(128)(4,1)S(1)} %get-tuple-element.52, bf16[2,6,3,1024]{3,0,2,1:T(2,128)(2,1)S(1)} %collective-permute-done.1, pred[2]{0:T(512)(128)(4,1)S(1)} %get-tuple-element.51, ...), kind=kLoop, calls=%fused_computation.34 | loop fusion | flops 110592 | bytes 368646 | tf_op jit(solution)/shard_map/jit(_where)/select_n | solution.py:30
  11.2 0.1 collective-permute-start.3
  11.3 1.6 %collective-permute-start.4 = (bf16[2,6,3,1024]{3,0,2,1:T(2,128)(2,1)S(1)}, bf16[2,6,3,1024]{3,0,2,1:T(2,128)(2,1)S(1)}, u32[]{:S(2)}, u32[]{:S(2)}) collective-permute-start(bf16[2,6,3,1024]{3,0,2,1:T(2,128)(2,1)S(1)} %broadcast_select_fusion.4), channel_id=1, source_target_pairs={{0,2},{1,3},{2,0},{3,1},{4,6},{5,7},{6,4},{7,5},{8,10},{9,11},{10,... | collective-permute-start | bytes 221192 | tf_op jit(solution)/shard_map/ppermute | solution.py:28
  12.9 0.2 collective-permute-start.5
  13.1 0.1 copy.8
  13.2 0.1 reshape.42.weight_ref
  13.3 0.0 collective-permute-done.3
  13.3 4.1 %collective-permute-done.4 = bf16[2,6,3,1024]{3,0,2,1:T(2,128)(2,1)S(1)} collective-permute-done((bf16[2,6,3,1024]{3,0,2,1:T(2,128)(2,1)S(1)}, bf16[2,6,3,1024]{3,0,2,1:T(2,128)(2,1)S(1)}, u32[]{:S(2)}, u32[]{:S(2)}) %collective-permute-start.4) | collective-permute-done | bytes 73760 | tf_op jit(solution)/shard_map/ppermute | solution.py:28
  17.4 0.1 collective-permute-done.5
  17.5 0.2 broadcast_select_fusion.5
  17.8 0.1 reshape.43
  17.8 0.0 copy-start
  17.9 0.3 fusion
  18.1 0.1 reshape.44.rev_ref
  18.3 5.1 %shard_map.55 = (bf16[4608,512]{1,0:T(8,128)(2,1)S(1)}, bf16[4608,512]{1,0:T(8,128)(2,1)S(1)}) custom-call(s32[36]{0:T(128)S(1)} %and_select_fusion.3.shift_ref, f32[18]{0:T(128)S(1)} %reshape.42.weight_ref, f32[36,1,1024]{2,1,0:T(1,128)S(1)} %reshape.44.rev_ref), custom_call_target="tpu_custom_call" | custom-call | bytes 9437184 | tf_op jit(solution)/shard_map/pallas_call | solution.py:56
  23.4 3.0 %fusion.18 = f32[256,512]{1,0:T(8,128)S(1)} fusion(bf16[18,256,512]{2,1,0:T(8,128)(2,1)S(1)} %bitcast.40, bf16[18,1024,256]{2,1,0:T(8,128)(2,1)} %bitcast.47, s32[]{:T(128)S(6)} %select_n.155), kind=kOutput, calls=%fused_computation.19 | convolution fusion | flops 1207959552 | bytes 7602180 | tf_op jit(solution)/shard_map/rpt,rtn->pn/dot_general | solution.py:93
  26.5 2.0 %collective-permute-start.6 = (f32[256,512]{1,0:T(8,128)S(1)}, f32[256,512]{1,0:T(8,128)S(1)}, u32[]{:S(2)}, u32[]{:S(2)}) collective-permute-start(f32[256,512]{1,0:T(8,128)S(1)} %fusion.18), channel_id=1, source_target_pairs={{0,32},{16,48},{32,64},{48,80},{64,96},{80,112},{96,0},{112,16},{1... | collective-permute-start | bytes 1572872 | tf_op jit(solution)/shard_map/ppermute | solution.py:108
  28.5 0.0 copy-done
  28.5 1.4 %fusion.21 = f32[256,512]{1,0:T(8,128)S(1)} fusion(bf16[18,256,512]{2,1,0:T(8,128)(2,1)S(1)} %bitcast.36, bf16[18,1024,256]{2,1,0:T(8,128)(2,1)S(1)} %bitcast.48, s32[]{:T(128)S(6)} %select_n.176), kind=kOutput, calls=%fused_computation.20 | convolution fusion | flops 1207959552 | bytes 7602180 | tf_op jit(solution)/shard_map/rpt,rtn->pn/dot_general | solution.py:93
  29.8 1.4 %fusion.24 = f32[256,512]{1,0:T(8,128)S(1)} fusion(bf16[18,256,512]{2,1,0:T(8,128)(2,1)S(1)} %bitcast.41, bf16[18,1024,256]{2,1,0:T(8,128)(2,1)S(1)} %bitcast.49, s32[]{:T(128)S(6)} %select_n.178), kind=kOutput, calls=%fused_computation.21 | convolution fusion | flops 1207959552 | bytes 7602180 | tf_op jit(solution)/shard_map/rpt,rtn->pn/dot_general | solution.py:93
  31.2 2.2 %collective-permute-start.10 = (f32[256,512]{1,0:T(8,128)S(1)}, f32[256,512]{1,0:T(8,128)S(1)}, u32[]{:S(2)}, u32[]{:S(2)}) collective-permute-start(f32[256,512]{1,0:T(8,128)S(1)} %fusion.21), channel_id=1, source_target_pairs={{0,96},{16,112},{32,0},{48,16},{64,32},{80,48},{96,64},{112,80},{1... | collective-permute-start | bytes 1572872 | tf_op jit(solution)/shard_map/ppermute | solution.py:108
  33.4 7.9 %collective-permute-done.6 = f32[256,512]{1,0:T(8,128)S(1)} collective-permute-done((f32[256,512]{1,0:T(8,128)S(1)}, f32[256,512]{1,0:T(8,128)S(1)}, u32[]{:S(2)}, u32[]{:S(2)}) %collective-permute-start.6) | collective-permute-done | bytes 524320 | tf_op jit(solution)/shard_map/ppermute | solution.py:108
  41.3 0.1 add.211
  41.4 0.1 collective-permute-start.7
  41.5 1.4 %fusion.27 = f32[256,512]{1,0:T(8,128)S(1)} fusion(bf16[18,256,512]{2,1,0:T(8,128)(2,1)S(1)} %bitcast.37, bf16[18,1024,256]{2,1,0:T(8,128)(2,1)S(1)} %bitcast.50, s32[]{:T(128)S(6)} %select_n.180), kind=kOutput, calls=%fused_computation.22 | convolution fusion | flops 1207959552 | bytes 7602180 | tf_op jit(solution)/shard_map/rpt,rtn->pn/dot_general | solution.py:93
  42.8 1.4 %fusion.30 = f32[256,512]{1,0:T(8,128)S(1)} fusion(bf16[18,256,512]{2,1,0:T(8,128)(2,1)S(1)} %bitcast.42, bf16[18,1024,256]{2,1,0:T(8,128)(2,1)S(1)} %bitcast.51, s32[]{:T(128)S(6)} %select_n.182), kind=kOutput, calls=%fused_computation.23 | convolution fusion | flops 1207959552 | bytes 7602180 | tf_op jit(solution)/shard_map/rpt,rtn->pn/dot_general | solution.py:93
  44.2 0.0 collective-permute-done.10
  44.2 0.1 add.226
  44.3 3.3 %collective-permute-start.11 = (f32[256,512]{1,0:T(8,128)S(1)}, f32[256,512]{1,0:T(8,128)S(1)}, u32[]{:S(2)}, u32[]{:S(2)}) collective-permute-start(f32[256,512]{1,0:T(8,128)S(1)} %add.226), channel_id=1, source_target_pairs={{0,96},{16,112},{32,0},{48,16},{64,32},{80,48},{96,64},{112,80},{1... | collective-permute-start | bytes 1572872 | tf_op jit(solution)/shard_map/ppermute | solution.py:114
  47.6 6.9 %collective-permute-done.7 = f32[256,512]{1,0:T(8,128)S(1)} collective-permute-done((f32[256,512]{1,0:T(8,128)S(1)}, f32[256,512]{1,0:T(8,128)S(1)}, u32[]{:S(2)}, u32[]{:S(2)}) %collective-permute-start.7) | collective-permute-done | bytes 524320 | tf_op jit(solution)/shard_map/ppermute | solution.py:114
  54.5 0.1 add.216
  54.5 0.1 collective-permute-start.8
  54.6 1.4 %fusion.33 = f32[256,512]{1,0:T(8,128)S(1)} fusion(bf16[18,256,512]{2,1,0:T(8,128)(2,1)S(1)} %bitcast.38, bf16[18,1024,256]{2,1,0:T(8,128)(2,1)S(1)} %bitcast.52, s32[]{:T(128)S(6)} %select_n.184), kind=kOutput, calls=%fused_computation.24 | convolution fusion | flops 1207959552 | bytes 7602180 | tf_op jit(solution)/shard_map/rpt,rtn->pn/dot_general | solution.py:93
  56.0 1.4 %fusion.36 = f32[256,512]{1,0:T(8,128)S(1)} fusion(bf16[18,256,512]{2,1,0:T(8,128)(2,1)S(1)} %bitcast.43, bf16[18,1024,256]{2,1,0:T(8,128)(2,1)S(1)} %bitcast.53, s32[]{:T(128)S(6)} %select_n.186), kind=kOutput, calls=%fused_computation.25 | convolution fusion | flops 1207959552 | bytes 7602180 | tf_op jit(solution)/shard_map/rpt,rtn->pn/dot_general | solution.py:93
  57.4 0.0 collective-permute-done.11
  57.4 0.1 add.227
  57.5 3.3 %collective-permute-start.12 = (f32[256,512]{1,0:T(8,128)S(1)}, f32[256,512]{1,0:T(8,128)S(1)}, u32[]{:S(2)}, u32[]{:S(2)}) collective-permute-start(f32[256,512]{1,0:T(8,128)S(1)} %add.227), channel_id=1, source_target_pairs={{0,96},{16,112},{32,0},{48,16},{64,32},{80,48},{96,64},{112,80},{1... | collective-permute-start | bytes 1572872 | tf_op jit(solution)/shard_map/ppermute | solution.py:114
  60.8 5.9 %collective-permute-done.8 = f32[256,512]{1,0:T(8,128)S(1)} collective-permute-done((f32[256,512]{1,0:T(8,128)S(1)}, f32[256,512]{1,0:T(8,128)S(1)}, u32[]{:S(2)}, u32[]{:S(2)}) %collective-permute-start.8) | collective-permute-done | bytes 524320 | tf_op jit(solution)/shard_map/ppermute | solution.py:114
  66.7 0.1 add.221
  66.8 3.4 %collective-permute-start.9 = (f32[128,512]{1,0:T(8,128)S(1)}, f32[128,512]{1,0:T(8,128)S(1)}, u32[]{:S(2)}, u32[]{:S(2)}) collective-permute-start(f32[128,512]{1,0:T(8,128)S(1)} %get-tuple-element.43), channel_id=1, source_target_pairs={{0,16},{16,0},{32,48},{48,32},{64,80},{80,64},{96,112},{112,96},{1... | collective-permute-start | bytes 786440 | tf_op jit(solution)/shard_map/ppermute | solution.py:119
  70.3 1.4 %fusion.39 = f32[256,512]{1,0:T(8,128)S(1)} fusion(bf16[18,256,512]{2,1,0:T(8,128)(2,1)S(1)} %bitcast.39, bf16[18,1024,256]{2,1,0:T(8,128)(2,1)S(1)} %bitcast.54, s32[]{:T(128)S(6)} %select_n.191), kind=kOutput, calls=%fused_computation.26 | convolution fusion | flops 1207959552 | bytes 7602180 | tf_op jit(solution)/shard_map/rpt,rtn->pn/dot_general | solution.py:93
  71.6 0.0 collective-permute-done.12
  71.6 0.1 add.230
  71.8 0.7 collective-permute-start.13
  72.4 0.4 rev.13
  72.8 0.4 rev.15
  73.2 4.4 %collective-permute-done.9 = f32[128,512]{1,0:T(8,128)S(1)} collective-permute-done((f32[128,512]{1,0:T(8,128)S(1)}, f32[128,512]{1,0:T(8,128)S(1)}, u32[]{:S(2)}, u32[]{:S(2)}) %collective-permute-start.9) | collective-permute-done | bytes 262176 | tf_op jit(solution)/shard_map/ppermute | solution.py:119
  77.6 0.4 rev.14
  78.0 2.4 %collective-permute-done.13 = f32[128,512]{1,0:T(8,128)S(1)} collective-permute-done((f32[128,512]{1,0:T(8,128)S(1)}, f32[128,512]{1,0:T(8,128)S(1)}, u32[]{:S(2)}, u32[]{:S(2)}) %collective-permute-start.13) | collective-permute-done | bytes 262176 | tf_op jit(solution)/shard_map/ppermute | solution.py:119
  80.4 0.4 rev.16
  80.9 1.2 %copy.10 = f32[128,2,512]{2,1,0:T(2,128)} copy(f32[128,2,512]{2,0,1:T(8,128)S(1)} %pad_maximum_fusion) | data formatting | bytes 1048576 | tf_op jit(solution)/shard_map/stack | solution.py:121
  (9 shorter events, 0.3 us)
Async XLA Ops:
  0.0 6.9 %collective-permute-start = (bf16[2,6,3,1024]{3,0,2,1:T(2,128)(2,1)}, bf16[2,6,3,1024]{3,0,2,1:T(2,128)(2,1)S(1)}, u32[]{:S(2)}, u32[]{:S(2)}) collective-permute-start(bf16[2,6,3,1024]{3,0,2,1:T(2,128)(2,1)} %bitcast.44), channel_id=1, source_target_pairs={{0,12},{1,13},{2,14},{3,15},{4,0},{5,1},{6,2},{7,3},{8,4},{9,5},{1... | collective-permute-start | bytes 221192 | tf_op jit(solution)/shard_map/ppermute | solution.py:28
  3.1 6.3 %collective-permute-start.1 = (bf16[2,6,3,1024]{3,0,2,1:T(2,128)(2,1)}, bf16[2,6,3,1024]{3,0,2,1:T(2,128)(2,1)S(1)}, u32[]{:S(2)}, u32[]{:S(2)}) collective-permute-start(bf16[2,6,3,1024]{3,0,2,1:T(2,128)(2,1)} %bitcast.45), channel_id=1, source_target_pairs={{0,8},{1,9},{2,10},{3,11},{4,12},{5,13},{6,14},{7,15},{8,0},{9,1},... | collective-permute-start | bytes 221192 | tf_op jit(solution)/shard_map/ppermute | solution.py:28
  3.7 6.4 %collective-permute-start.2 = (bf16[2,6,3,1024]{3,0,2,1:T(2,128)(2,1)}, bf16[2,6,3,1024]{3,0,2,1:T(2,128)(2,1)S(1)}, u32[]{:S(2)}, u32[]{:S(2)}) collective-permute-start(bf16[2,6,3,1024]{3,0,2,1:T(2,128)(2,1)} %bitcast.46), channel_id=1, source_target_pairs={{0,4},{1,5},{2,6},{3,7},{4,8},{5,9},{6,10},{7,11},{8,12},{9,13},{1... | collective-permute-start | bytes 221192 | tf_op jit(solution)/shard_map/ppermute | solution.py:28
  11.2 2.1 %collective-permute-start.3 = (bf16[2,6,3,1024]{3,0,2,1:T(2,128)(2,1)S(1)}, bf16[2,6,3,1024]{3,0,2,1:T(2,128)(2,1)S(1)}, u32[]{:S(2)}, u32[]{:S(2)}) collective-permute-start(bf16[2,6,3,1024]{3,0,2,1:T(2,128)(2,1)S(1)} %broadcast_select_fusion.4), channel_id=1, source_target_pairs={{0,3},{1,0},{2,1},{3,2},{4,7},{5,4},{6,5},{7,6},{8,11},{9,8},{10,9... | collective-permute-start | bytes 221192 | tf_op jit(solution)/shard_map/ppermute | solution.py:28
  11.3 6.1 %collective-permute-start.4 = (bf16[2,6,3,1024]{3,0,2,1:T(2,128)(2,1)S(1)}, bf16[2,6,3,1024]{3,0,2,1:T(2,128)(2,1)S(1)}, u32[]{:S(2)}, u32[]{:S(2)}) collective-permute-start(bf16[2,6,3,1024]{3,0,2,1:T(2,128)(2,1)S(1)} %broadcast_select_fusion.4), channel_id=1, source_target_pairs={{0,2},{1,3},{2,0},{3,1},{4,6},{5,7},{6,4},{7,5},{8,10},{9,11},{10,... | collective-permute-start | bytes 221192 | tf_op jit(solution)/shard_map/ppermute | solution.py:28
  12.9 4.6 %collective-permute-start.5 = (bf16[2,6,3,1024]{3,0,2,1:T(2,128)(2,1)S(1)}, bf16[2,6,3,1024]{3,0,2,1:T(2,128)(2,1)S(1)}, u32[]{:S(2)}, u32[]{:S(2)}) collective-permute-start(bf16[2,6,3,1024]{3,0,2,1:T(2,128)(2,1)S(1)} %broadcast_select_fusion.4), channel_id=1, source_target_pairs={{0,1},{1,2},{2,3},{3,0},{4,5},{5,6},{6,7},{7,4},{8,9},{9,10},{10,1... | collective-permute-start | bytes 221192 | tf_op jit(solution)/shard_map/ppermute | solution.py:28
  17.8 10.6 %copy-start = (bf16[1024,6,3,256]{3,0,2,1:T(8,128)(2,1)S(1)}, bf16[1024,6,3,256]{3,0,2,1:T(8,128)(2,1)}, u32[]{:S(2)}) copy-start(bf16[1024,6,3,256]{3,0,2,1:T(8,128)(2,1)} %param.5) | copy-start | bytes 28311556
  26.5 14.8 %collective-permute-start.6 = (f32[256,512]{1,0:T(8,128)S(1)}, f32[256,512]{1,0:T(8,128)S(1)}, u32[]{:S(2)}, u32[]{:S(2)}) collective-permute-start(f32[256,512]{1,0:T(8,128)S(1)} %fusion.18), channel_id=1, source_target_pairs={{0,32},{16,48},{32,64},{48,80},{64,96},{80,112},{96,0},{112,16},{1... | collective-permute-start | bytes 1572872 | tf_op jit(solution)/shard_map/ppermute | solution.py:108
  31.2 13.0 %collective-permute-start.10 = (f32[256,512]{1,0:T(8,128)S(1)}, f32[256,512]{1,0:T(8,128)S(1)}, u32[]{:S(2)}, u32[]{:S(2)}) collective-permute-start(f32[256,512]{1,0:T(8,128)S(1)} %fusion.21), channel_id=1, source_target_pairs={{0,96},{16,112},{32,0},{48,16},{64,32},{80,48},{96,64},{112,80},{1... | collective-permute-start | bytes 1572872 | tf_op jit(solution)/shard_map/ppermute | solution.py:108
  41.4 13.1 %collective-permute-start.7 = (f32[256,512]{1,0:T(8,128)S(1)}, f32[256,512]{1,0:T(8,128)S(1)}, u32[]{:S(2)}, u32[]{:S(2)}) collective-permute-start(f32[256,512]{1,0:T(8,128)S(1)} %add.211), channel_id=1, source_target_pairs={{0,32},{16,48},{32,64},{48,80},{64,96},{80,112},{96,0},{112,16},{1... | collective-permute-start | bytes 1572872 | tf_op jit(solution)/shard_map/ppermute | solution.py:114
  44.3 13.1 %collective-permute-start.11 = (f32[256,512]{1,0:T(8,128)S(1)}, f32[256,512]{1,0:T(8,128)S(1)}, u32[]{:S(2)}, u32[]{:S(2)}) collective-permute-start(f32[256,512]{1,0:T(8,128)S(1)} %add.226), channel_id=1, source_target_pairs={{0,96},{16,112},{32,0},{48,16},{64,32},{80,48},{96,64},{112,80},{1... | collective-permute-start | bytes 1572872 | tf_op jit(solution)/shard_map/ppermute | solution.py:114
  54.5 12.2 %collective-permute-start.8 = (f32[256,512]{1,0:T(8,128)S(1)}, f32[256,512]{1,0:T(8,128)S(1)}, u32[]{:S(2)}, u32[]{:S(2)}) collective-permute-start(f32[256,512]{1,0:T(8,128)S(1)} %add.216), channel_id=1, source_target_pairs={{0,32},{16,48},{32,64},{48,80},{64,96},{80,112},{96,0},{112,16},{1... | collective-permute-start | bytes 1572872 | tf_op jit(solution)/shard_map/ppermute | solution.py:114
  57.5 14.2 %collective-permute-start.12 = (f32[256,512]{1,0:T(8,128)S(1)}, f32[256,512]{1,0:T(8,128)S(1)}, u32[]{:S(2)}, u32[]{:S(2)}) collective-permute-start(f32[256,512]{1,0:T(8,128)S(1)} %add.227), channel_id=1, source_target_pairs={{0,96},{16,112},{32,0},{48,16},{64,32},{80,48},{96,64},{112,80},{1... | collective-permute-start | bytes 1572872 | tf_op jit(solution)/shard_map/ppermute | solution.py:114
  66.8 10.7 %collective-permute-start.9 = (f32[128,512]{1,0:T(8,128)S(1)}, f32[128,512]{1,0:T(8,128)S(1)}, u32[]{:S(2)}, u32[]{:S(2)}) collective-permute-start(f32[128,512]{1,0:T(8,128)S(1)} %get-tuple-element.43), channel_id=1, source_target_pairs={{0,16},{16,0},{32,48},{48,32},{64,80},{80,64},{96,112},{112,96},{1... | collective-permute-start | bytes 786440 | tf_op jit(solution)/shard_map/ppermute | solution.py:119
  71.8 8.6 %collective-permute-start.13 = (f32[128,512]{1,0:T(8,128)S(1)}, f32[128,512]{1,0:T(8,128)S(1)}, u32[]{:S(2)}, u32[]{:S(2)}) collective-permute-start(f32[128,512]{1,0:T(8,128)S(1)} %get-tuple-element.45), channel_id=1, source_target_pairs={{0,16},{16,0},{32,48},{48,32},{64,80},{80,64},{96,112},{112,96},{1... | collective-permute-start | bytes 786440 | tf_op jit(solution)/shard_map/ppermute | solution.py:119

commit v18 on v15

--- a/solution.py
+++ b/solution.py
@@ -36,7 +36,7 @@
 
     def body(r, carry):
         for e, out_ref in enumerate(out_refs):
-            row = rev_ref[e * rows + r]
+            row = rev_ref[r * len(out_refs) + e]
             row = pltpu.roll(row, shift_ref[e * rows + r], 1)
             row = (row * weight_ref[r]).astype(jnp.bfloat16).astype(jnp.float32)
             row = jnp.concatenate([row[:, :LAGS], row[:, SAMPLES - NT :]], axis=1)
@@ -70,7 +70,8 @@
     point_rows = green.shape[0]
     rows = green.shape[1] * green.shape[2]
     green_t = jnp.transpose(green, (1, 2, 0, 3)).reshape(rows, point_rows, NT)
-    traces = from_owners(records_buffer[0], "loc", owners).reshape(EV * rows, SAMPLES)
+    records = jnp.transpose(records_buffer[0], (1, 2, 0, 3)).reshape(rows * EV, SAMPLES)
+    traces = from_owners(records, "loc", jnp.tile(owners, rows))
     i = lax.broadcasted_iota(jnp.int32, (SAMPLES, SAMPLES), 0)
     j = lax.broadcasted_iota(jnp.int32, (SAMPLES, SAMPLES), 1)
     anti = (i + j == SAMPLES - 1).astype(jnp.bfloat16)

time: 77.9 us -> 77.9 us (level)
  other arithmetic: 4.03 us -> 2.12 us
  local copies, waits for them, and re-layouts: 3.33 us -> 4.91 us
    select_n x2 -> x1, other arithmetic: 1.34 us -> 0.09 us  [from_owners(): jnp.where((src == digit).reshape((-1,) + (1,) * (x.ndim - 1)), got, out)]
    reshape x1, local copies, waits for them, and re-layouts: 0.06 us -> 0.92 us  [local(): jnp.transpose(records_buffer[0], (1, 2, 0, 3)).reshape(rows * EV, SAMPLES)]
where the time goes in v18:
time: 77.9 us; the launch traced here: 77.6 us
  waiting for transfers between devices  31 us (40%)
  starting transfers between devices  21.2 us (27%)
  matrix products  13 us (17%)
  Pallas kernels  5.14 us (7%)
  local copies, waits for them, and re-layouts  4.91 us (6%)
  other arithmetic  2.12 us (3%)
    dot_general x8, matrix products, piece(): jnp.einsum('rpt,rtn->pn', g, band.reshape(rows, NT, LAGS), preferred_elem...  12.7 us
    ppermute x4, waiting for transfers between devices, local(): gots[e] = lax.ppermute(accs[e], 'sens', ring_perm(step))  11 us
    ppermute x6, waiting for transfers between devices, from_owners(): got = lax.ppermute(x, axis, perm)  7.5 us
    ppermute x2, waiting for transfers between devices, local(): gots.append(lax.ppermute(acc, 'sens', ring_perm(step)))  6.99 us
    ppermute x4, starting transfers between devices, local(): gots[e] = lax.ppermute(accs[e], 'sens', ring_perm(step))  6.73 us
    ppermute x6, starting transfers between devices, from_owners(): got = lax.ppermute(x, axis, perm)  6.58 us
    ppermute x2, waiting for transfers between devices, local(): got = lax.ppermute(theirs, 'sens', [(i, i ^ 1) for i in range(size)])  5.52 us
    pallas_call x1, Pallas kernels, toeplitz_reversed(): pl.pallas_call(_toeplitz_kernel, in_specs=[pl.BlockSpec(memory_space=pltp...  5.14 us
  transfers between devices with their start and end apart: 14, of which 9 were waited for; matrix products, arithmetic and copies ran while one was open for 18% of the time, Pallas kernels for 0%

profile of v18, /device:TPU:0, one launch (start us, length us, event | category | flops | bytes accessed | tf_op | source)
XLA Modules:
  0.0 77.6 jit_solution(10547802627574811849)
XLA Ops:
  0.0 0.9 %reshape.136 = bf16[36,1024]{1,0:T(8,128)(2,1)S(1)} reshape(bf16[6,3,2,1024]{3,2,1,0:T(2,128)(2,1)} %bitcast.44) | data formatting | bytes 147456 | tf_op jit(solution)/shard_map/reshape | solution.py:73
  0.9 1.1 %collective-permute-start = (bf16[36,1024]{1,0:T(8,128)(2,1)S(1)}, bf16[36,1024]{1,0:T(8,128)(2,1)S(1)}, u32[]{:S(2)}, u32[]{:S(2)}) collective-permute-start(bf16[36,1024]{1,0:T(8,128)(2,1)S(1)} %reshape.136), channel_id=1, source_target_pairs={{0,3},{1,0},{2,1},{3,2},{4,7},{5,4},{6,5},{7,6},{8,11},{9,8},{10,9... | collective-permute-start | bytes 221192 | tf_op jit(solution)/shard_map/ppermute | solution.py:26
  2.0 0.7 collective-permute-start.1
  2.7 0.2 collective-permute-start.2
  2.8 0.7 tile.4
  3.5 0.1 tile.10
  3.6 0.7 broadcast_add_fusion
  4.2 0.7 multiply_exponential_fusion
  5.0 0.1 broadcast_in_dim.36
  5.0 0.1 sub.71
  5.1 0.0 collective-permute-done
  5.1 2.5 %collective-permute-done.1 = bf16[36,1024]{1,0:T(8,128)(2,1)S(1)} collective-permute-done((bf16[36,1024]{1,0:T(8,128)(2,1)S(1)}, bf16[36,1024]{1,0:T(8,128)(2,1)S(1)}, u32[]{:S(2)}, u32[]{:S(2)}) %collective-permute-start.1) | collective-permute-done | bytes 73760 | tf_op jit(solution)/shard_map/ppermute | solution.py:26
  7.6 0.0 collective-permute-done.2
  7.6 0.1 select_select_fusion
  7.7 3.1 %collective-permute-start.3 = (bf16[36,1024]{1,0:T(8,128)(2,1)S(1)}, bf16[36,1024]{1,0:T(8,128)(2,1)S(1)}, u32[]{:S(2)}, u32[]{:S(2)}) collective-permute-start(bf16[36,1024]{1,0:T(8,128)(2,1)S(1)} %select_select_fusion), channel_id=1, source_target_pairs={{0,12},{1,13},{2,14},{3,15},{4,0},{5,1},{6,2},{7,3},{8,4},{9,5},{1... | collective-permute-start | bytes 221192 | tf_op jit(solution)/shard_map/ppermute | solution.py:26
  10.8 0.6 collective-permute-start.4
  11.4 1.0 %collective-permute-start.5 = (bf16[36,1024]{1,0:T(8,128)(2,1)S(1)}, bf16[36,1024]{1,0:T(8,128)(2,1)S(1)}, u32[]{:S(2)}, u32[]{:S(2)}) collective-permute-start(bf16[36,1024]{1,0:T(8,128)(2,1)S(1)} %select_select_fusion), channel_id=1, source_target_pairs={{0,4},{1,5},{2,6},{3,7},{4,8},{5,9},{6,10},{7,11},{8,12},{9,13},{1... | collective-permute-start | bytes 221192 | tf_op jit(solution)/shard_map/ppermute | solution.py:26
  12.4 0.1 copy.8
  12.5 0.1 reshape.135.weight_ref
  12.6 0.4 collective-permute-done.3
  13.0 3.8 %collective-permute-done.4 = bf16[36,1024]{1,0:T(8,128)(2,1)S(1)} collective-permute-done((bf16[36,1024]{1,0:T(8,128)(2,1)S(1)}, bf16[36,1024]{1,0:T(8,128)(2,1)S(1)}, u32[]{:S(2)}, u32[]{:S(2)}) %collective-permute-start.4) | collective-permute-done | bytes 73760 | tf_op jit(solution)/shard_map/ppermute | solution.py:26
  16.8 0.8 %collective-permute-done.5 = bf16[36,1024]{1,0:T(8,128)(2,1)S(1)} collective-permute-done((bf16[36,1024]{1,0:T(8,128)(2,1)S(1)}, bf16[36,1024]{1,0:T(8,128)(2,1)S(1)}, u32[]{:S(2)}, u32[]{:S(2)}) %collective-permute-start.5) | collective-permute-done | bytes 73760 | tf_op jit(solution)/shard_map/ppermute | solution.py:26
  17.6 0.0 copy-start
  17.6 0.3 fusion
  18.0 0.1 reshape.137.rev_ref
  18.1 5.1 %shard_map.55 = (bf16[4608,512]{1,0:T(8,128)(2,1)S(1)}, bf16[4608,512]{1,0:T(8,128)(2,1)S(1)}) custom-call(s32[36]{0:T(128)S(1)} %and_select_fusion.3.shift_ref, f32[18]{0:T(128)S(1)} %reshape.135.weight_ref, f32[36,1,1024]{2,1,0:T(1,128)S(1)} %reshape.137.rev_ref), custom_call_target="tpu_custom_call" | custom-call | bytes 9437184 | tf_op jit(solution)/shard_map/pallas_call | solution.py:55
  23.2 3.0 %fusion.18 = f32[256,512]{1,0:T(8,128)S(1)} fusion(bf16[18,256,512]{2,1,0:T(8,128)(2,1)S(1)} %bitcast.40, bf16[18,1024,256]{2,1,0:T(8,128)(2,1)} %bitcast.45, s32[]{:T(128)S(6)} %select_n.188), kind=kOutput, calls=%fused_computation.19 | convolution fusion | flops 1207959552 | bytes 7602180 | tf_op jit(solution)/shard_map/rpt,rtn->pn/dot_general | solution.py:93
  26.3 2.0 %collective-permute-start.6 = (f32[256,512]{1,0:T(8,128)S(1)}, f32[256,512]{1,0:T(8,128)S(1)}, u32[]{:S(2)}, u32[]{:S(2)}) collective-permute-start(f32[256,512]{1,0:T(8,128)S(1)} %fusion.18), channel_id=1, source_target_pairs={{0,32},{16,48},{32,64},{48,80},{64,96},{80,112},{96,0},{112,16},{1... | collective-permute-start | bytes 1572872 | tf_op jit(solution)/shard_map/ppermute | solution.py:108
  28.3 0.0 copy-done
  28.3 1.4 %fusion.21 = f32[256,512]{1,0:T(8,128)S(1)} fusion(bf16[18,256,512]{2,1,0:T(8,128)(2,1)S(1)} %bitcast.36, bf16[18,1024,256]{2,1,0:T(8,128)(2,1)S(1)} %bitcast.46, s32[]{:T(128)S(6)} %select_n.209), kind=kOutput, calls=%fused_computation.20 | convolution fusion | flops 1207959552 | bytes 7602180 | tf_op jit(solution)/shard_map/rpt,rtn->pn/dot_general | solution.py:93
  29.7 1.4 %fusion.24 = f32[256,512]{1,0:T(8,128)S(1)} fusion(bf16[18,256,512]{2,1,0:T(8,128)(2,1)S(1)} %bitcast.41, bf16[18,1024,256]{2,1,0:T(8,128)(2,1)S(1)} %bitcast.47, s32[]{:T(128)S(6)} %select_n.211), kind=kOutput, calls=%fused_computation.21 | convolution fusion | flops 1207959552 | bytes 7602180 | tf_op jit(solution)/shard_map/rpt,rtn->pn/dot_general | solution.py:93
  31.0 2.2 %collective-permute-start.10 = (f32[256,512]{1,0:T(8,128)S(1)}, f32[256,512]{1,0:T(8,128)S(1)}, u32[]{:S(2)}, u32[]{:S(2)}) collective-permute-start(f32[256,512]{1,0:T(8,128)S(1)} %fusion.21), channel_id=1, source_target_pairs={{0,96},{16,112},{32,0},{48,16},{64,32},{80,48},{96,64},{112,80},{1... | collective-permute-start | bytes 1572872 | tf_op jit(solution)/shard_map/ppermute | solution.py:108
  33.3 7.0 %collective-permute-done.6 = f32[256,512]{1,0:T(8,128)S(1)} collective-permute-done((f32[256,512]{1,0:T(8,128)S(1)}, f32[256,512]{1,0:T(8,128)S(1)}, u32[]{:S(2)}, u32[]{:S(2)}) %collective-permute-start.6) | collective-permute-done | bytes 524320 | tf_op jit(solution)/shard_map/ppermute | solution.py:108
  40.2 0.1 add.244
  40.3 0.1 collective-permute-start.7
  40.4 1.4 %fusion.27 = f32[256,512]{1,0:T(8,128)S(1)} fusion(bf16[18,256,512]{2,1,0:T(8,128)(2,1)S(1)} %bitcast.37, bf16[18,1024,256]{2,1,0:T(8,128)(2,1)S(1)} %bitcast.48, s32[]{:T(128)S(6)} %select_n.213), kind=kOutput, calls=%fused_computation.22 | convolution fusion | flops 1207959552 | bytes 7602180 | tf_op jit(solution)/shard_map/rpt,rtn->pn/dot_general | solution.py:93
  41.8 1.4 %fusion.30 = f32[256,512]{1,0:T(8,128)S(1)} fusion(bf16[18,256,512]{2,1,0:T(8,128)(2,1)S(1)} %bitcast.42, bf16[18,1024,256]{2,1,0:T(8,128)(2,1)S(1)} %bitcast.49, s32[]{:T(128)S(6)} %select_n.215), kind=kOutput, calls=%fused_computation.23 | convolution fusion | flops 1207959552 | bytes 7602180 | tf_op jit(solution)/shard_map/rpt,rtn->pn/dot_general | solution.py:93
  43.2 0.0 collective-permute-done.10
  43.2 0.1 add.259
  43.3 3.3 %collective-permute-start.11 = (f32[256,512]{1,0:T(8,128)S(1)}, f32[256,512]{1,0:T(8,128)S(1)}, u32[]{:S(2)}, u32[]{:S(2)}) collective-permute-start(f32[256,512]{1,0:T(8,128)S(1)} %add.259), channel_id=1, source_target_pairs={{0,96},{16,112},{32,0},{48,16},{64,32},{80,48},{96,64},{112,80},{1... | collective-permute-start | bytes 1572872 | tf_op jit(solution)/shard_map/ppermute | solution.py:114
  46.6 6.0 %collective-permute-done.7 = f32[256,512]{1,0:T(8,128)S(1)} collective-permute-done((f32[256,512]{1,0:T(8,128)S(1)}, f32[256,512]{1,0:T(8,128)S(1)}, u32[]{:S(2)}, u32[]{:S(2)}) %collective-permute-start.7) | collective-permute-done | bytes 524320 | tf_op jit(solution)/shard_map/ppermute | solution.py:114
  52.5 0.1 add.249
  52.6 0.1 collective-permute-start.8
  52.7 1.4 %fusion.33 = f32[256,512]{1,0:T(8,128)S(1)} fusion(bf16[18,256,512]{2,1,0:T(8,128)(2,1)S(1)} %bitcast.38, bf16[18,1024,256]{2,1,0:T(8,128)(2,1)S(1)} %bitcast.50, s32[]{:T(128)S(6)} %select_n.217), kind=kOutput, calls=%fused_computation.24 | convolution fusion | flops 1207959552 | bytes 7602180 | tf_op jit(solution)/shard_map/rpt,rtn->pn/dot_general | solution.py:93
  54.1 1.4 %fusion.36 = f32[256,512]{1,0:T(8,128)S(1)} fusion(bf16[18,256,512]{2,1,0:T(8,128)(2,1)S(1)} %bitcast.43, bf16[18,1024,256]{2,1,0:T(8,128)(2,1)S(1)} %bitcast.51, s32[]{:T(128)S(6)} %select_n.219), kind=kOutput, calls=%fused_computation.25 | convolution fusion | flops 1207959552 | bytes 7602180 | tf_op jit(solution)/shard_map/rpt,rtn->pn/dot_general | solution.py:93
  55.5 0.0 collective-permute-done.11
  55.5 0.1 add.260
  55.6 3.3 %collective-permute-start.12 = (f32[256,512]{1,0:T(8,128)S(1)}, f32[256,512]{1,0:T(8,128)S(1)}, u32[]{:S(2)}, u32[]{:S(2)}) collective-permute-start(f32[256,512]{1,0:T(8,128)S(1)} %add.260), channel_id=1, source_target_pairs={{0,96},{16,112},{32,0},{48,16},{64,32},{80,48},{96,64},{112,80},{1... | collective-permute-start | bytes 1572872 | tf_op jit(solution)/shard_map/ppermute | solution.py:114
  58.9 5.1 %collective-permute-done.8 = f32[256,512]{1,0:T(8,128)S(1)} collective-permute-done((f32[256,512]{1,0:T(8,128)S(1)}, f32[256,512]{1,0:T(8,128)S(1)}, u32[]{:S(2)}, u32[]{:S(2)}) %collective-permute-start.8) | collective-permute-done | bytes 524320 | tf_op jit(solution)/shard_map/ppermute | solution.py:114
  63.9 0.1 add.254
  64.1 2.4 %collective-permute-start.9 = (f32[128,512]{1,0:T(8,128)S(1)}, f32[128,512]{1,0:T(8,128)S(1)}, u32[]{:S(2)}, u32[]{:S(2)}) collective-permute-start(f32[128,512]{1,0:T(8,128)S(1)} %get-tuple-element.43), channel_id=1, source_target_pairs={{0,16},{16,0},{32,48},{48,32},{64,80},{80,64},{96,112},{112,96},{1... | collective-permute-start | bytes 786440 | tf_op jit(solution)/shard_map/ppermute | solution.py:119
  66.5 1.4 %fusion.39 = f32[256,512]{1,0:T(8,128)S(1)} fusion(bf16[18,256,512]{2,1,0:T(8,128)(2,1)S(1)} %bitcast.39, bf16[18,1024,256]{2,1,0:T(8,128)(2,1)S(1)} %bitcast.52, s32[]{:T(128)S(6)} %select_n.224), kind=kOutput, calls=%fused_computation.26 | convolution fusion | flops 1207959552 | bytes 7602180 | tf_op jit(solution)/shard_map/rpt,rtn->pn/dot_general | solution.py:93
  67.9 0.0 collective-permute-done.12
  67.9 0.1 add.263
  68.0 1.3 %collective-permute-start.13 = (f32[128,512]{1,0:T(8,128)S(1)}, f32[128,512]{1,0:T(8,128)S(1)}, u32[]{:S(2)}, u32[]{:S(2)}) collective-permute-start(f32[128,512]{1,0:T(8,128)S(1)} %get-tuple-element.45), channel_id=1, source_target_pairs={{0,16},{16,0},{32,48},{48,32},{64,80},{80,64},{96,112},{112,96},{1... | collective-permute-start | bytes 786440 | tf_op jit(solution)/shard_map/ppermute | solution.py:119
  69.3 0.4 rev.13
  69.6 0.4 rev.15
  70.0 2.6 %collective-permute-done.9 = f32[128,512]{1,0:T(8,128)S(1)} collective-permute-done((f32[128,512]{1,0:T(8,128)S(1)}, f32[128,512]{1,0:T(8,128)S(1)}, u32[]{:S(2)}, u32[]{:S(2)}) %collective-permute-start.9) | collective-permute-done | bytes 262176 | tf_op jit(solution)/shard_map/ppermute | solution.py:119
  72.6 0.4 rev.14
  73.0 2.9 %collective-permute-done.13 = f32[128,512]{1,0:T(8,128)S(1)} collective-permute-done((f32[128,512]{1,0:T(8,128)S(1)}, f32[128,512]{1,0:T(8,128)S(1)}, u32[]{:S(2)}, u32[]{:S(2)}) %collective-permute-start.13) | collective-permute-done | bytes 262176 | tf_op jit(solution)/shard_map/ppermute | solution.py:119
  76.0 0.4 rev.16
  76.4 1.2 %copy.9 = f32[128,2,512]{2,1,0:T(2,128)} copy(f32[128,2,512]{2,0,1:T(8,128)S(1)} %pad_maximum_fusion) | data formatting | bytes 1048576 | tf_op jit(solution)/shard_map/stack | solution.py:121
  (9 shorter events, 0.3 us)
Async XLA Ops:
  0.9 4.2 %collective-permute-start = (bf16[36,1024]{1,0:T(8,128)(2,1)S(1)}, bf16[36,1024]{1,0:T(8,128)(2,1)S(1)}, u32[]{:S(2)}, u32[]{:S(2)}) collective-permute-start(bf16[36,1024]{1,0:T(8,128)(2,1)S(1)} %reshape.136), channel_id=1, source_target_pairs={{0,3},{1,0},{2,1},{3,2},{4,7},{5,4},{6,5},{7,6},{8,11},{9,8},{10,9... | collective-permute-start | bytes 221192 | tf_op jit(solution)/shard_map/ppermute | solution.py:26
  2.0 5.6 %collective-permute-start.1 = (bf16[36,1024]{1,0:T(8,128)(2,1)S(1)}, bf16[36,1024]{1,0:T(8,128)(2,1)S(1)}, u32[]{:S(2)}, u32[]{:S(2)}) collective-permute-start(bf16[36,1024]{1,0:T(8,128)(2,1)S(1)} %reshape.136), channel_id=1, source_target_pairs={{0,2},{1,3},{2,0},{3,1},{4,6},{5,7},{6,4},{7,5},{8,10},{9,11},{10,... | collective-permute-start | bytes 221192 | tf_op jit(solution)/shard_map/ppermute | solution.py:26
  2.7 5.0 %collective-permute-start.2 = (bf16[36,1024]{1,0:T(8,128)(2,1)S(1)}, bf16[36,1024]{1,0:T(8,128)(2,1)S(1)}, u32[]{:S(2)}, u32[]{:S(2)}) collective-permute-start(bf16[36,1024]{1,0:T(8,128)(2,1)S(1)} %reshape.136), channel_id=1, source_target_pairs={{0,1},{1,2},{2,3},{3,0},{4,5},{5,6},{6,7},{7,4},{8,9},{9,10},{10,1... | collective-permute-start | bytes 221192 | tf_op jit(solution)/shard_map/ppermute | solution.py:26
  7.7 5.3 %collective-permute-start.3 = (bf16[36,1024]{1,0:T(8,128)(2,1)S(1)}, bf16[36,1024]{1,0:T(8,128)(2,1)S(1)}, u32[]{:S(2)}, u32[]{:S(2)}) collective-permute-start(bf16[36,1024]{1,0:T(8,128)(2,1)S(1)} %select_select_fusion), channel_id=1, source_target_pairs={{0,12},{1,13},{2,14},{3,15},{4,0},{5,1},{6,2},{7,3},{8,4},{9,5},{1... | collective-permute-start | bytes 221192 | tf_op jit(solution)/shard_map/ppermute | solution.py:26
  10.8 6.0 %collective-permute-start.4 = (bf16[36,1024]{1,0:T(8,128)(2,1)S(1)}, bf16[36,1024]{1,0:T(8,128)(2,1)S(1)}, u32[]{:S(2)}, u32[]{:S(2)}) collective-permute-start(bf16[36,1024]{1,0:T(8,128)(2,1)S(1)} %select_select_fusion), channel_id=1, source_target_pairs={{0,8},{1,9},{2,10},{3,11},{4,12},{5,13},{6,14},{7,15},{8,0},{9,1},... | collective-permute-start | bytes 221192 | tf_op jit(solution)/shard_map/ppermute | solution.py:26
  11.4 6.2 %collective-permute-start.5 = (bf16[36,1024]{1,0:T(8,128)(2,1)S(1)}, bf16[36,1024]{1,0:T(8,128)(2,1)S(1)}, u32[]{:S(2)}, u32[]{:S(2)}) collective-permute-start(bf16[36,1024]{1,0:T(8,128)(2,1)S(1)} %select_select_fusion), channel_id=1, source_target_pairs={{0,4},{1,5},{2,6},{3,7},{4,8},{5,9},{6,10},{7,11},{8,12},{9,13},{1... | collective-permute-start | bytes 221192 | tf_op jit(solution)/shard_map/ppermute | solution.py:26
  17.6 10.7 %copy-start = (bf16[1024,6,3,256]{3,0,2,1:T(8,128)(2,1)S(1)}, bf16[1024,6,3,256]{3,0,2,1:T(8,128)(2,1)}, u32[]{:S(2)}) copy-start(bf16[1024,6,3,256]{3,0,2,1:T(8,128)(2,1)} %param.5) | copy-start | bytes 28311556
  26.3 13.9 %collective-permute-start.6 = (f32[256,512]{1,0:T(8,128)S(1)}, f32[256,512]{1,0:T(8,128)S(1)}, u32[]{:S(2)}, u32[]{:S(2)}) collective-permute-start(f32[256,512]{1,0:T(8,128)S(1)} %fusion.18), channel_id=1, source_target_pairs={{0,32},{16,48},{32,64},{48,80},{64,96},{80,112},{96,0},{112,16},{1... | collective-permute-start | bytes 1572872 | tf_op jit(solution)/shard_map/ppermute | solution.py:108
  31.0 12.1 %collective-permute-start.10 = (f32[256,512]{1,0:T(8,128)S(1)}, f32[256,512]{1,0:T(8,128)S(1)}, u32[]{:S(2)}, u32[]{:S(2)}) collective-permute-start(f32[256,512]{1,0:T(8,128)S(1)} %fusion.21), channel_id=1, source_target_pairs={{0,96},{16,112},{32,0},{48,16},{64,32},{80,48},{96,64},{112,80},{1... | collective-permute-start | bytes 1572872 | tf_op jit(solution)/shard_map/ppermute | solution.py:108
  40.3 12.2 %collective-permute-start.7 = (f32[256,512]{1,0:T(8,128)S(1)}, f32[256,512]{1,0:T(8,128)S(1)}, u32[]{:S(2)}, u32[]{:S(2)}) collective-permute-start(f32[256,512]{1,0:T(8,128)S(1)} %add.244), channel_id=1, source_target_pairs={{0,32},{16,48},{32,64},{48,80},{64,96},{80,112},{96,0},{112,16},{1... | collective-permute-start | bytes 1572872 | tf_op jit(solution)/shard_map/ppermute | solution.py:114
  43.3 12.2 %collective-permute-start.11 = (f32[256,512]{1,0:T(8,128)S(1)}, f32[256,512]{1,0:T(8,128)S(1)}, u32[]{:S(2)}, u32[]{:S(2)}) collective-permute-start(f32[256,512]{1,0:T(8,128)S(1)} %add.259), channel_id=1, source_target_pairs={{0,96},{16,112},{32,0},{48,16},{64,32},{80,48},{96,64},{112,80},{1... | collective-permute-start | bytes 1572872 | tf_op jit(solution)/shard_map/ppermute | solution.py:114
  52.6 11.3 %collective-permute-start.8 = (f32[256,512]{1,0:T(8,128)S(1)}, f32[256,512]{1,0:T(8,128)S(1)}, u32[]{:S(2)}, u32[]{:S(2)}) collective-permute-start(f32[256,512]{1,0:T(8,128)S(1)} %add.249), channel_id=1, source_target_pairs={{0,32},{16,48},{32,64},{48,80},{64,96},{80,112},{96,0},{112,16},{1... | collective-permute-start | bytes 1572872 | tf_op jit(solution)/shard_map/ppermute | solution.py:114
  55.6 12.3 %collective-permute-start.12 = (f32[256,512]{1,0:T(8,128)S(1)}, f32[256,512]{1,0:T(8,128)S(1)}, u32[]{:S(2)}, u32[]{:S(2)}) collective-permute-start(f32[256,512]{1,0:T(8,128)S(1)} %add.260), channel_id=1, source_target_pairs={{0,96},{16,112},{32,0},{48,16},{64,32},{80,48},{96,64},{112,80},{1... | collective-permute-start | bytes 1572872 | tf_op jit(solution)/shard_map/ppermute | solution.py:114
  64.1 8.6 %collective-permute-start.9 = (f32[128,512]{1,0:T(8,128)S(1)}, f32[128,512]{1,0:T(8,128)S(1)}, u32[]{:S(2)}, u32[]{:S(2)}) collective-permute-start(f32[128,512]{1,0:T(8,128)S(1)} %get-tuple-element.43), channel_id=1, source_target_pairs={{0,16},{16,0},{32,48},{48,32},{64,80},{80,64},{96,112},{112,96},{1... | collective-permute-start | bytes 786440 | tf_op jit(solution)/shard_map/ppermute | solution.py:119
  68.0 8.0 %collective-permute-start.13 = (f32[128,512]{1,0:T(8,128)S(1)}, f32[128,512]{1,0:T(8,128)S(1)}, u32[]{:S(2)}, u32[]{:S(2)}) collective-permute-start(f32[128,512]{1,0:T(8,128)S(1)} %get-tuple-element.45), channel_id=1, source_target_pairs={{0,16},{16,0},{32,48},{48,32},{64,80},{80,64},{96,112},{112,96},{1... | collective-permute-start | bytes 786440 | tf_op jit(solution)/shard_map/ppermute | solution.py:119

commit v19 on v15

--- a/solution.py
+++ b/solution.py
@@ -38,7 +38,7 @@
         for e, out_ref in enumerate(out_refs):
             row = rev_ref[e * rows + r]
             row = pltpu.roll(row, shift_ref[e * rows + r], 1)
-            row = (row * weight_ref[r]).astype(jnp.bfloat16).astype(jnp.float32)
+            row = (row * weight_ref[r]).astype(jnp.bfloat16)
             row = jnp.concatenate([row[:, :LAGS], row[:, SAMPLES - NT :]], axis=1)
             wide = jnp.broadcast_to(row, (NT, WIDE))
             band = pltpu.roll(wide, 0, 1, stride=1, stride_axis=0)

time: 77.9 us -> 77.9 us (level)
  no operation moved by 1% of the time
where the time goes in v19:
time: 77.9 us; the launch traced here: 77.6 us
  waiting for transfers between devices  30.9 us (40%)
  starting transfers between devices  21.1 us (27%)
  matrix products  12.9 us (17%)
  Pallas kernels  5.1 us (7%)
  other arithmetic  4.03 us (5%)
  local copies, waits for them, and re-layouts  3.33 us (4%)
    dot_general x8, matrix products, piece(): jnp.einsum('rpt,rtn->pn', g, band.reshape(rows, NT, LAGS), preferred_elem...  12.7 us
    ppermute x4, waiting for transfers between devices, local(): gots[e] = lax.ppermute(accs[e], 'sens', ring_perm(step))  11.1 us
    ppermute x6, waiting for transfers between devices, from_owners(): got = lax.ppermute(x, axis, perm)  7.29 us
    ppermute x2, waiting for transfers between devices, local(): gots.append(lax.ppermute(acc, 'sens', ring_perm(step)))  7.01 us
    ppermute x4, starting transfers between devices, local(): gots[e] = lax.ppermute(accs[e], 'sens', ring_perm(step))  6.73 us
    ppermute x6, starting transfers between devices, from_owners(): got = lax.ppermute(x, axis, perm)  6.49 us
    ppermute x2, waiting for transfers between devices, local(): got = lax.ppermute(theirs, 'sens', [(i, i ^ 1) for i in range(size)])  5.46 us
    pallas_call x1, Pallas kernels, toeplitz_reversed(): pl.pallas_call(_toeplitz_kernel, in_specs=[pl.BlockSpec(memory_space=pltp...  5.1 us
  transfers between devices with their start and end apart: 14, of which 9 were waited for; matrix products, arithmetic and copies ran while one was open for 18% of the time, Pallas kernels for 0%

profile of v19, /device:TPU:0, one launch (start us, length us, event | category | flops | bytes accessed | tf_op | source)
XLA Modules:
  0.0 77.6 jit_solution(4408963209044587700)
XLA Ops:
  0.0 1.0 %collective-permute-start = (bf16[2,6,3,1024]{3,0,2,1:T(2,128)(2,1)}, bf16[2,6,3,1024]{3,0,2,1:T(2,128)(2,1)S(1)}, u32[]{:S(2)}, u32[]{:S(2)}) collective-permute-start(bf16[2,6,3,1024]{3,0,2,1:T(2,128)(2,1)} %bitcast.44), channel_id=1, source_target_pairs={{0,3},{1,0},{2,1},{3,2},{4,7},{5,4},{6,5},{7,6},{8,11},{9,8},{10,9... | collective-permute-start | bytes 221192 | tf_op jit(solution)/shard_map/ppermute | solution.py:26
  1.0 0.6 collective-permute-start.1
  1.6 0.2 collective-permute-start.2
  1.8 0.7 broadcast_add_fusion
  2.5 0.7 multiply_exponential_fusion
  3.2 0.7 broadcast_compare_fusion
  3.9 0.1 broadcast_in_dim.36
  4.0 0.1 sub.68
  4.0 0.0 collective-permute-done
  4.0 2.4 %collective-permute-done.1 = bf16[2,6,3,1024]{3,0,2,1:T(2,128)(2,1)S(1)} collective-permute-done((bf16[2,6,3,1024]{3,0,2,1:T(2,128)(2,1)}, bf16[2,6,3,1024]{3,0,2,1:T(2,128)(2,1)S(1)}, u32[]{:S(2)}, u32[]{:S(2)}) %collective-permute-start.1) | collective-permute-done | bytes 73760 | tf_op jit(solution)/shard_map/ppermute | solution.py:26
  6.5 0.0 collective-permute-done.2
  6.5 1.1 %broadcast_select_fusion.4 = bf16[2,6,3,1024]{3,0,2,1:T(2,128)(2,1)S(1)} fusion(bf16[2,6,3,1024]{3,0,2,1:T(2,128)(2,1)S(1)} %collective-permute-done, pred[2]{0:T(512)(128)(4,1)S(1)} %get-tuple-element.52, bf16[2,6,3,1024]{3,0,2,1:T(2,128)(2,1)S(1)} %collective-permute-done.1, pred[2]{0:T(512)(128)(4,1)S(1)} %get-tuple-element.51, ...), kind=kLoop, calls=%fused_computation.34 | loop fusion | flops 110592 | bytes 368646 | tf_op jit(solution)/shard_map/jit(_where)/select_n | solution.py:28
  7.6 3.1 %collective-permute-start.3 = (bf16[2,6,3,1024]{3,0,2,1:T(2,128)(2,1)S(1)}, bf16[2,6,3,1024]{3,0,2,1:T(2,128)(2,1)S(1)}, u32[]{:S(2)}, u32[]{:S(2)}) collective-permute-start(bf16[2,6,3,1024]{3,0,2,1:T(2,128)(2,1)S(1)} %broadcast_select_fusion.4), channel_id=1, source_target_pairs={{0,12},{1,13},{2,14},{3,15},{4,0},{5,1},{6,2},{7,3},{8,4},{9,5},{1... | collective-permute-start | bytes 221192 | tf_op jit(solution)/shard_map/ppermute | solution.py:26
  10.7 0.6 collective-permute-start.4
  11.3 1.0 %collective-permute-start.5 = (bf16[2,6,3,1024]{3,0,2,1:T(2,128)(2,1)S(1)}, bf16[2,6,3,1024]{3,0,2,1:T(2,128)(2,1)S(1)}, u32[]{:S(2)}, u32[]{:S(2)}) collective-permute-start(bf16[2,6,3,1024]{3,0,2,1:T(2,128)(2,1)S(1)} %broadcast_select_fusion.4), channel_id=1, source_target_pairs={{0,4},{1,5},{2,6},{3,7},{4,8},{5,9},{6,10},{7,11},{8,12},{9,13},{1... | collective-permute-start | bytes 221192 | tf_op jit(solution)/shard_map/ppermute | solution.py:26
  12.3 0.1 copy.8
  12.4 0.1 reshape.42.weight_ref
  12.5 0.2 collective-permute-done.3
  12.7 3.9 %collective-permute-done.4 = bf16[2,6,3,1024]{3,0,2,1:T(2,128)(2,1)S(1)} collective-permute-done((bf16[2,6,3,1024]{3,0,2,1:T(2,128)(2,1)S(1)}, bf16[2,6,3,1024]{3,0,2,1:T(2,128)(2,1)S(1)}, u32[]{:S(2)}, u32[]{:S(2)}) %collective-permute-start.4) | collective-permute-done | bytes 73760 | tf_op jit(solution)/shard_map/ppermute | solution.py:26
  16.6 0.7 collective-permute-done.5
  17.3 0.2 broadcast_select_fusion.5
  17.6 0.1 reshape.43
  17.7 0.0 copy-start
  17.7 0.3 fusion
  18.0 0.1 reshape.44.rev_ref
  18.1 5.1 %shard_map.55 = (bf16[4608,512]{1,0:T(8,128)(2,1)S(1)}, bf16[4608,512]{1,0:T(8,128)(2,1)S(1)}) custom-call(s32[36]{0:T(128)S(1)} %and_select_fusion.3.shift_ref, f32[18]{0:T(128)S(1)} %reshape.42.weight_ref, f32[36,1,1024]{2,1,0:T(1,128)S(1)} %reshape.44.rev_ref), custom_call_target="tpu_custom_call" | custom-call | bytes 9437184 | tf_op jit(solution)/shard_map/pallas_call | solution.py:55
  23.2 3.0 %fusion.18 = f32[256,512]{1,0:T(8,128)S(1)} fusion(bf16[18,256,512]{2,1,0:T(8,128)(2,1)S(1)} %bitcast.40, bf16[18,1024,256]{2,1,0:T(8,128)(2,1)} %bitcast.47, s32[]{:T(128)S(6)} %select_n.155), kind=kOutput, calls=%fused_computation.19 | convolution fusion | flops 1207959552 | bytes 7602180 | tf_op jit(solution)/shard_map/rpt,rtn->pn/dot_general | solution.py:92
  26.3 2.0 %collective-permute-start.6 = (f32[256,512]{1,0:T(8,128)S(1)}, f32[256,512]{1,0:T(8,128)S(1)}, u32[]{:S(2)}, u32[]{:S(2)}) collective-permute-start(f32[256,512]{1,0:T(8,128)S(1)} %fusion.18), channel_id=1, source_target_pairs={{0,32},{16,48},{32,64},{48,80},{64,96},{80,112},{96,0},{112,16},{1... | collective-permute-start | bytes 1572872 | tf_op jit(solution)/shard_map/ppermute | solution.py:107
  28.2 0.0 copy-done
  28.2 1.4 %fusion.21 = f32[256,512]{1,0:T(8,128)S(1)} fusion(bf16[18,256,512]{2,1,0:T(8,128)(2,1)S(1)} %bitcast.36, bf16[18,1024,256]{2,1,0:T(8,128)(2,1)S(1)} %bitcast.48, s32[]{:T(128)S(6)} %select_n.176), kind=kOutput, calls=%fused_computation.20 | convolution fusion | flops 1207959552 | bytes 7602180 | tf_op jit(solution)/shard_map/rpt,rtn->pn/dot_general | solution.py:92
  29.6 1.4 %fusion.24 = f32[256,512]{1,0:T(8,128)S(1)} fusion(bf16[18,256,512]{2,1,0:T(8,128)(2,1)S(1)} %bitcast.41, bf16[18,1024,256]{2,1,0:T(8,128)(2,1)S(1)} %bitcast.49, s32[]{:T(128)S(6)} %select_n.178), kind=kOutput, calls=%fused_computation.21 | convolution fusion | flops 1207959552 | bytes 7602180 | tf_op jit(solution)/shard_map/rpt,rtn->pn/dot_general | solution.py:92
  31.0 2.2 %collective-permute-start.10 = (f32[256,512]{1,0:T(8,128)S(1)}, f32[256,512]{1,0:T(8,128)S(1)}, u32[]{:S(2)}, u32[]{:S(2)}) collective-permute-start(f32[256,512]{1,0:T(8,128)S(1)} %fusion.21), channel_id=1, source_target_pairs={{0,96},{16,112},{32,0},{48,16},{64,32},{80,48},{96,64},{112,80},{1... | collective-permute-start | bytes 1572872 | tf_op jit(solution)/shard_map/ppermute | solution.py:107
  33.2 7.0 %collective-permute-done.6 = f32[256,512]{1,0:T(8,128)S(1)} collective-permute-done((f32[256,512]{1,0:T(8,128)S(1)}, f32[256,512]{1,0:T(8,128)S(1)}, u32[]{:S(2)}, u32[]{:S(2)}) %collective-permute-start.6) | collective-permute-done | bytes 524320 | tf_op jit(solution)/shard_map/ppermute | solution.py:107
  40.2 0.1 add.211
  40.3 0.1 collective-permute-start.7
  40.4 1.4 %fusion.27 = f32[256,512]{1,0:T(8,128)S(1)} fusion(bf16[18,256,512]{2,1,0:T(8,128)(2,1)S(1)} %bitcast.37, bf16[18,1024,256]{2,1,0:T(8,128)(2,1)S(1)} %bitcast.50, s32[]{:T(128)S(6)} %select_n.180), kind=kOutput, calls=%fused_computation.22 | convolution fusion | flops 1207959552 | bytes 7602180 | tf_op jit(solution)/shard_map/rpt,rtn->pn/dot_general | solution.py:92
  41.8 1.4 %fusion.30 = f32[256,512]{1,0:T(8,128)S(1)} fusion(bf16[18,256,512]{2,1,0:T(8,128)(2,1)S(1)} %bitcast.42, bf16[18,1024,256]{2,1,0:T(8,128)(2,1)S(1)} %bitcast.51, s32[]{:T(128)S(6)} %select_n.182), kind=kOutput, calls=%fused_computation.23 | convolution fusion | flops 1207959552 | bytes 7602180 | tf_op jit(solution)/shard_map/rpt,rtn->pn/dot_general | solution.py:92
  43.2 0.0 collective-permute-done.10
  43.2 0.1 add.226
  43.2 3.3 %collective-permute-start.11 = (f32[256,512]{1,0:T(8,128)S(1)}, f32[256,512]{1,0:T(8,128)S(1)}, u32[]{:S(2)}, u32[]{:S(2)}) collective-permute-start(f32[256,512]{1,0:T(8,128)S(1)} %add.226), channel_id=1, source_target_pairs={{0,96},{16,112},{32,0},{48,16},{64,32},{80,48},{96,64},{112,80},{1... | collective-permute-start | bytes 1572872 | tf_op jit(solution)/shard_map/ppermute | solution.py:113
  46.5 6.0 %collective-permute-done.7 = f32[256,512]{1,0:T(8,128)S(1)} collective-permute-done((f32[256,512]{1,0:T(8,128)S(1)}, f32[256,512]{1,0:T(8,128)S(1)}, u32[]{:S(2)}, u32[]{:S(2)}) %collective-permute-start.7) | collective-permute-done | bytes 524320 | tf_op jit(solution)/shard_map/ppermute | solution.py:113
  52.5 0.1 add.216
  52.6 0.1 collective-permute-start.8
  52.7 1.4 %fusion.33 = f32[256,512]{1,0:T(8,128)S(1)} fusion(bf16[18,256,512]{2,1,0:T(8,128)(2,1)S(1)} %bitcast.38, bf16[18,1024,256]{2,1,0:T(8,128)(2,1)S(1)} %bitcast.52, s32[]{:T(128)S(6)} %select_n.184), kind=kOutput, calls=%fused_computation.24 | convolution fusion | flops 1207959552 | bytes 7602180 | tf_op jit(solution)/shard_map/rpt,rtn->pn/dot_general | solution.py:92
  54.1 1.4 %fusion.36 = f32[256,512]{1,0:T(8,128)S(1)} fusion(bf16[18,256,512]{2,1,0:T(8,128)(2,1)S(1)} %bitcast.43, bf16[18,1024,256]{2,1,0:T(8,128)(2,1)S(1)} %bitcast.53, s32[]{:T(128)S(6)} %select_n.186), kind=kOutput, calls=%fused_computation.25 | convolution fusion | flops 1207959552 | bytes 7602180 | tf_op jit(solution)/shard_map/rpt,rtn->pn/dot_general | solution.py:92
  55.5 0.0 collective-permute-done.11
  55.5 0.1 add.227
  55.6 3.3 %collective-permute-start.12 = (f32[256,512]{1,0:T(8,128)S(1)}, f32[256,512]{1,0:T(8,128)S(1)}, u32[]{:S(2)}, u32[]{:S(2)}) collective-permute-start(f32[256,512]{1,0:T(8,128)S(1)} %add.227), channel_id=1, source_target_pairs={{0,96},{16,112},{32,0},{48,16},{64,32},{80,48},{96,64},{112,80},{1... | collective-permute-start | bytes 1572872 | tf_op jit(solution)/shard_map/ppermute | solution.py:113
  58.9 5.1 %collective-permute-done.8 = f32[256,512]{1,0:T(8,128)S(1)} collective-permute-done((f32[256,512]{1,0:T(8,128)S(1)}, f32[256,512]{1,0:T(8,128)S(1)}, u32[]{:S(2)}, u32[]{:S(2)}) %collective-permute-start.8) | collective-permute-done | bytes 524320 | tf_op jit(solution)/shard_map/ppermute | solution.py:113
  64.0 0.1 add.221
  64.1 2.4 %collective-permute-start.9 = (f32[128,512]{1,0:T(8,128)S(1)}, f32[128,512]{1,0:T(8,128)S(1)}, u32[]{:S(2)}, u32[]{:S(2)}) collective-permute-start(f32[128,512]{1,0:T(8,128)S(1)} %get-tuple-element.43), channel_id=1, source_target_pairs={{0,16},{16,0},{32,48},{48,32},{64,80},{80,64},{96,112},{112,96},{1... | collective-permute-start | bytes 786440 | tf_op jit(solution)/shard_map/ppermute | solution.py:118
  66.5 1.4 %fusion.39 = f32[256,512]{1,0:T(8,128)S(1)} fusion(bf16[18,256,512]{2,1,0:T(8,128)(2,1)S(1)} %bitcast.39, bf16[18,1024,256]{2,1,0:T(8,128)(2,1)S(1)} %bitcast.54, s32[]{:T(128)S(6)} %select_n.191), kind=kOutput, calls=%fused_computation.26 | convolution fusion | flops 1207959552 | bytes 7602180 | tf_op jit(solution)/shard_map/rpt,rtn->pn/dot_general | solution.py:92
  67.8 0.0 collective-permute-done.12
  67.9 0.1 add.230
  68.0 1.3 %collective-permute-start.13 = (f32[128,512]{1,0:T(8,128)S(1)}, f32[128,512]{1,0:T(8,128)S(1)}, u32[]{:S(2)}, u32[]{:S(2)}) collective-permute-start(f32[128,512]{1,0:T(8,128)S(1)} %get-tuple-element.45), channel_id=1, source_target_pairs={{0,16},{16,0},{32,48},{48,32},{64,80},{80,64},{96,112},{112,96},{1... | collective-permute-start | bytes 786440 | tf_op jit(solution)/shard_map/ppermute | solution.py:118
  69.3 0.4 rev.13
  69.7 0.4 rev.15
  70.1 2.5 %collective-permute-done.9 = f32[128,512]{1,0:T(8,128)S(1)} collective-permute-done((f32[128,512]{1,0:T(8,128)S(1)}, f32[128,512]{1,0:T(8,128)S(1)}, u32[]{:S(2)}, u32[]{:S(2)}) %collective-permute-start.9) | collective-permute-done | bytes 262176 | tf_op jit(solution)/shard_map/ppermute | solution.py:118
  72.6 0.4 rev.14
  73.0 2.9 %collective-permute-done.13 = f32[128,512]{1,0:T(8,128)S(1)} collective-permute-done((f32[128,512]{1,0:T(8,128)S(1)}, f32[128,512]{1,0:T(8,128)S(1)}, u32[]{:S(2)}, u32[]{:S(2)}) %collective-permute-start.13) | collective-permute-done | bytes 262176 | tf_op jit(solution)/shard_map/ppermute | solution.py:118
  76.0 0.4 rev.16
  76.4 1.2 %copy.10 = f32[128,2,512]{2,1,0:T(2,128)} copy(f32[128,2,512]{2,0,1:T(8,128)S(1)} %pad_maximum_fusion) | data formatting | bytes 1048576 | tf_op jit(solution)/shard_map/stack | solution.py:120
  (9 shorter events, 0.3 us)
Async XLA Ops:
  0.0 4.0 %collective-permute-start = (bf16[2,6,3,1024]{3,0,2,1:T(2,128)(2,1)}, bf16[2,6,3,1024]{3,0,2,1:T(2,128)(2,1)S(1)}, u32[]{:S(2)}, u32[]{:S(2)}) collective-permute-start(bf16[2,6,3,1024]{3,0,2,1:T(2,128)(2,1)} %bitcast.44), channel_id=1, source_target_pairs={{0,3},{1,0},{2,1},{3,2},{4,7},{5,4},{6,5},{7,6},{8,11},{9,8},{10,9... | collective-permute-start | bytes 221192 | tf_op jit(solution)/shard_map/ppermute | solution.py:26
  1.0 5.5 %collective-permute-start.1 = (bf16[2,6,3,1024]{3,0,2,1:T(2,128)(2,1)}, bf16[2,6,3,1024]{3,0,2,1:T(2,128)(2,1)S(1)}, u32[]{:S(2)}, u32[]{:S(2)}) collective-permute-start(bf16[2,6,3,1024]{3,0,2,1:T(2,128)(2,1)} %bitcast.45), channel_id=1, source_target_pairs={{0,2},{1,3},{2,0},{3,1},{4,6},{5,7},{6,4},{7,5},{8,10},{9,11},{10,... | collective-permute-start | bytes 221192 | tf_op jit(solution)/shard_map/ppermute | solution.py:26
  1.6 4.9 %collective-permute-start.2 = (bf16[2,6,3,1024]{3,0,2,1:T(2,128)(2,1)}, bf16[2,6,3,1024]{3,0,2,1:T(2,128)(2,1)S(1)}, u32[]{:S(2)}, u32[]{:S(2)}) collective-permute-start(bf16[2,6,3,1024]{3,0,2,1:T(2,128)(2,1)} %bitcast.46), channel_id=1, source_target_pairs={{0,1},{1,2},{2,3},{3,0},{4,5},{5,6},{6,7},{7,4},{8,9},{9,10},{10,1... | collective-permute-start | bytes 221192 | tf_op jit(solution)/shard_map/ppermute | solution.py:26
  7.6 5.1 %collective-permute-start.3 = (bf16[2,6,3,1024]{3,0,2,1:T(2,128)(2,1)S(1)}, bf16[2,6,3,1024]{3,0,2,1:T(2,128)(2,1)S(1)}, u32[]{:S(2)}, u32[]{:S(2)}) collective-permute-start(bf16[2,6,3,1024]{3,0,2,1:T(2,128)(2,1)S(1)} %broadcast_select_fusion.4), channel_id=1, source_target_pairs={{0,12},{1,13},{2,14},{3,15},{4,0},{5,1},{6,2},{7,3},{8,4},{9,5},{1... | collective-permute-start | bytes 221192 | tf_op jit(solution)/shard_map/ppermute | solution.py:26
  10.7 5.9 %collective-permute-start.4 = (bf16[2,6,3,1024]{3,0,2,1:T(2,128)(2,1)S(1)}, bf16[2,6,3,1024]{3,0,2,1:T(2,128)(2,1)S(1)}, u32[]{:S(2)}, u32[]{:S(2)}) collective-permute-start(bf16[2,6,3,1024]{3,0,2,1:T(2,128)(2,1)S(1)} %broadcast_select_fusion.4), channel_id=1, source_target_pairs={{0,8},{1,9},{2,10},{3,11},{4,12},{5,13},{6,14},{7,15},{8,0},{9,1},... | collective-permute-start | bytes 221192 | tf_op jit(solution)/shard_map/ppermute | solution.py:26
  11.3 6.0 %collective-permute-start.5 = (bf16[2,6,3,1024]{3,0,2,1:T(2,128)(2,1)S(1)}, bf16[2,6,3,1024]{3,0,2,1:T(2,128)(2,1)S(1)}, u32[]{:S(2)}, u32[]{:S(2)}) collective-permute-start(bf16[2,6,3,1024]{3,0,2,1:T(2,128)(2,1)S(1)} %broadcast_select_fusion.4), channel_id=1, source_target_pairs={{0,4},{1,5},{2,6},{3,7},{4,8},{5,9},{6,10},{7,11},{8,12},{9,13},{1... | collective-permute-start | bytes 221192 | tf_op jit(solution)/shard_map/ppermute | solution.py:26
  17.7 10.6 %copy-start = (bf16[1024,6,3,256]{3,0,2,1:T(8,128)(2,1)S(1)}, bf16[1024,6,3,256]{3,0,2,1:T(8,128)(2,1)}, u32[]{:S(2)}) copy-start(bf16[1024,6,3,256]{3,0,2,1:T(8,128)(2,1)} %param.5) | copy-start | bytes 28311556
  26.3 14.0 %collective-permute-start.6 = (f32[256,512]{1,0:T(8,128)S(1)}, f32[256,512]{1,0:T(8,128)S(1)}, u32[]{:S(2)}, u32[]{:S(2)}) collective-permute-start(f32[256,512]{1,0:T(8,128)S(1)} %fusion.18), channel_id=1, source_target_pairs={{0,32},{16,48},{32,64},{48,80},{64,96},{80,112},{96,0},{112,16},{1... | collective-permute-start | bytes 1572872 | tf_op jit(solution)/shard_map/ppermute | solution.py:107
  31.0 12.1 %collective-permute-start.10 = (f32[256,512]{1,0:T(8,128)S(1)}, f32[256,512]{1,0:T(8,128)S(1)}, u32[]{:S(2)}, u32[]{:S(2)}) collective-permute-start(f32[256,512]{1,0:T(8,128)S(1)} %fusion.21), channel_id=1, source_target_pairs={{0,96},{16,112},{32,0},{48,16},{64,32},{80,48},{96,64},{112,80},{1... | collective-permute-start | bytes 1572872 | tf_op jit(solution)/shard_map/ppermute | solution.py:107
  40.3 12.2 %collective-permute-start.7 = (f32[256,512]{1,0:T(8,128)S(1)}, f32[256,512]{1,0:T(8,128)S(1)}, u32[]{:S(2)}, u32[]{:S(2)}) collective-permute-start(f32[256,512]{1,0:T(8,128)S(1)} %add.211), channel_id=1, source_target_pairs={{0,32},{16,48},{32,64},{48,80},{64,96},{80,112},{96,0},{112,16},{1... | collective-permute-start | bytes 1572872 | tf_op jit(solution)/shard_map/ppermute | solution.py:113
  43.2 12.2 %collective-permute-start.11 = (f32[256,512]{1,0:T(8,128)S(1)}, f32[256,512]{1,0:T(8,128)S(1)}, u32[]{:S(2)}, u32[]{:S(2)}) collective-permute-start(f32[256,512]{1,0:T(8,128)S(1)} %add.226), channel_id=1, source_target_pairs={{0,96},{16,112},{32,0},{48,16},{64,32},{80,48},{96,64},{112,80},{1... | collective-permute-start | bytes 1572872 | tf_op jit(solution)/shard_map/ppermute | solution.py:113
  52.6 11.3 %collective-permute-start.8 = (f32[256,512]{1,0:T(8,128)S(1)}, f32[256,512]{1,0:T(8,128)S(1)}, u32[]{:S(2)}, u32[]{:S(2)}) collective-permute-start(f32[256,512]{1,0:T(8,128)S(1)} %add.216), channel_id=1, source_target_pairs={{0,32},{16,48},{32,64},{48,80},{64,96},{80,112},{96,0},{112,16},{1... | collective-permute-start | bytes 1572872 | tf_op jit(solution)/shard_map/ppermute | solution.py:113
  55.6 12.3 %collective-permute-start.12 = (f32[256,512]{1,0:T(8,128)S(1)}, f32[256,512]{1,0:T(8,128)S(1)}, u32[]{:S(2)}, u32[]{:S(2)}) collective-permute-start(f32[256,512]{1,0:T(8,128)S(1)} %add.227), channel_id=1, source_target_pairs={{0,96},{16,112},{32,0},{48,16},{64,32},{80,48},{96,64},{112,80},{1... | collective-permute-start | bytes 1572872 | tf_op jit(solution)/shard_map/ppermute | solution.py:113
  64.1 8.5 %collective-permute-start.9 = (f32[128,512]{1,0:T(8,128)S(1)}, f32[128,512]{1,0:T(8,128)S(1)}, u32[]{:S(2)}, u32[]{:S(2)}) collective-permute-start(f32[128,512]{1,0:T(8,128)S(1)} %get-tuple-element.43), channel_id=1, source_target_pairs={{0,16},{16,0},{32,48},{48,32},{64,80},{80,64},{96,112},{112,96},{1... | collective-permute-start | bytes 786440 | tf_op jit(solution)/shard_map/ppermute | solution.py:118
  68.0 8.0 %collective-permute-start.13 = (f32[128,512]{1,0:T(8,128)S(1)}, f32[128,512]{1,0:T(8,128)S(1)}, u32[]{:S(2)}, u32[]{:S(2)}) collective-permute-start(f32[128,512]{1,0:T(8,128)S(1)} %get-tuple-element.45), channel_id=1, source_target_pairs={{0,16},{16,0},{32,48},{48,32},{64,80},{80,64},{96,112},{112,96},{1... | collective-permute-start | bytes 786440 | tf_op jit(solution)/shard_map/ppermute | solution.py:118

commit v20 on v15

--- a/solution.py
+++ b/solution.py
@@ -45,7 +45,7 @@
             out_ref[pl.ds(pl.multiple_of(r * NT, NT), NT), :] = band[:, :LAGS].astype(out_ref.dtype)
         return carry
 
-    lax.fori_loop(0, rows, body, 0)
+    lax.fori_loop(0, rows, body, 0, unroll=3)
 
 
 def toeplitz_reversed(rev, shifts, weights):

time: 77.9 us -> 78 us (level)
  no operation moved by 1% of the time
where the time goes in v20:
time: 78 us; the launch traced here: 77.8 us
  waiting for transfers between devices  30.9 us (40%)
  starting transfers between devices  21.1 us (27%)
  matrix products  12.9 us (17%)
  Pallas kernels  5.25 us (7%)
  other arithmetic  4.03 us (5%)
  local copies, waits for them, and re-layouts  3.33 us (4%)
    dot_general x8, matrix products, piece(): jnp.einsum('rpt,rtn->pn', g, band.reshape(rows, NT, LAGS), preferred_elem...  12.7 us
    ppermute x4, waiting for transfers between devices, local(): gots[e] = lax.ppermute(accs[e], 'sens', ring_perm(step))  11.1 us
    ppermute x6, waiting for transfers between devices, from_owners(): got = lax.ppermute(x, axis, perm)  7.29 us
    ppermute x2, waiting for transfers between devices, local(): gots.append(lax.ppermute(acc, 'sens', ring_perm(step)))  7.01 us
    ppermute x4, starting transfers between devices, local(): gots[e] = lax.ppermute(accs[e], 'sens', ring_perm(step))  6.73 us
    ppermute x6, starting transfers between devices, from_owners(): got = lax.ppermute(x, axis, perm)  6.49 us
    ppermute x2, waiting for transfers between devices, local(): got = lax.ppermute(theirs, 'sens', [(i, i ^ 1) for i in range(size)])  5.45 us
    pallas_call x1, Pallas kernels, toeplitz_reversed(): pl.pallas_call(_toeplitz_kernel, in_specs=[pl.BlockSpec(memory_space=pltp...  5.25 us
  transfers between devices with their start and end apart: 14, of which 9 were waited for; matrix products, arithmetic and copies ran while one was open for 18% of the time, Pallas kernels for 0%

profile of v20, /device:TPU:0, one launch (start us, length us, event | category | flops | bytes accessed | tf_op | source)
XLA Modules:
  0.0 77.8 jit_solution(6317714245619163053)
XLA Ops:
  0.0 1.0 %collective-permute-start = (bf16[2,6,3,1024]{3,0,2,1:T(2,128)(2,1)}, bf16[2,6,3,1024]{3,0,2,1:T(2,128)(2,1)S(1)}, u32[]{:S(2)}, u32[]{:S(2)}) collective-permute-start(bf16[2,6,3,1024]{3,0,2,1:T(2,128)(2,1)} %bitcast.44), channel_id=1, source_target_pairs={{0,3},{1,0},{2,1},{3,2},{4,7},{5,4},{6,5},{7,6},{8,11},{9,8},{10,9... | collective-permute-start | bytes 221192 | tf_op jit(solution)/shard_map/ppermute | solution.py:26
  1.0 0.6 collective-permute-start.1
  1.6 0.2 collective-permute-start.2
  1.8 0.7 broadcast_add_fusion
  2.5 0.7 multiply_exponential_fusion
  3.2 0.7 broadcast_compare_fusion
  3.9 0.1 broadcast_in_dim.36
  4.0 0.1 sub.68
  4.0 0.0 collective-permute-done
  4.0 2.4 %collective-permute-done.1 = bf16[2,6,3,1024]{3,0,2,1:T(2,128)(2,1)S(1)} collective-permute-done((bf16[2,6,3,1024]{3,0,2,1:T(2,128)(2,1)}, bf16[2,6,3,1024]{3,0,2,1:T(2,128)(2,1)S(1)}, u32[]{:S(2)}, u32[]{:S(2)}) %collective-permute-start.1) | collective-permute-done | bytes 73760 | tf_op jit(solution)/shard_map/ppermute | solution.py:26
  6.5 0.0 collective-permute-done.2
  6.5 1.1 %broadcast_select_fusion.4 = bf16[2,6,3,1024]{3,0,2,1:T(2,128)(2,1)S(1)} fusion(bf16[2,6,3,1024]{3,0,2,1:T(2,128)(2,1)S(1)} %collective-permute-done, pred[2]{0:T(512)(128)(4,1)S(1)} %get-tuple-element.52, bf16[2,6,3,1024]{3,0,2,1:T(2,128)(2,1)S(1)} %collective-permute-done.1, pred[2]{0:T(512)(128)(4,1)S(1)} %get-tuple-element.51, ...), kind=kLoop, calls=%fused_computation.34 | loop fusion | flops 110592 | bytes 368646 | tf_op jit(solution)/shard_map/jit(_where)/select_n | solution.py:28
  7.6 3.1 %collective-permute-start.3 = (bf16[2,6,3,1024]{3,0,2,1:T(2,128)(2,1)S(1)}, bf16[2,6,3,1024]{3,0,2,1:T(2,128)(2,1)S(1)}, u32[]{:S(2)}, u32[]{:S(2)}) collective-permute-start(bf16[2,6,3,1024]{3,0,2,1:T(2,128)(2,1)S(1)} %broadcast_select_fusion.4), channel_id=1, source_target_pairs={{0,12},{1,13},{2,14},{3,15},{4,0},{5,1},{6,2},{7,3},{8,4},{9,5},{1... | collective-permute-start | bytes 221192 | tf_op jit(solution)/shard_map/ppermute | solution.py:26
  10.7 0.6 collective-permute-start.4
  11.3 1.0 %collective-permute-start.5 = (bf16[2,6,3,1024]{3,0,2,1:T(2,128)(2,1)S(1)}, bf16[2,6,3,1024]{3,0,2,1:T(2,128)(2,1)S(1)}, u32[]{:S(2)}, u32[]{:S(2)}) collective-permute-start(bf16[2,6,3,1024]{3,0,2,1:T(2,128)(2,1)S(1)} %broadcast_select_fusion.4), channel_id=1, source_target_pairs={{0,4},{1,5},{2,6},{3,7},{4,8},{5,9},{6,10},{7,11},{8,12},{9,13},{1... | collective-permute-start | bytes 221192 | tf_op jit(solution)/shard_map/ppermute | solution.py:26
  12.3 0.1 copy.8
  12.4 0.1 reshape.42.weight_ref
  12.5 0.2 collective-permute-done.3
  12.7 3.9 %collective-permute-done.4 = bf16[2,6,3,1024]{3,0,2,1:T(2,128)(2,1)S(1)} collective-permute-done((bf16[2,6,3,1024]{3,0,2,1:T(2,128)(2,1)S(1)}, bf16[2,6,3,1024]{3,0,2,1:T(2,128)(2,1)S(1)}, u32[]{:S(2)}, u32[]{:S(2)}) %collective-permute-start.4) | collective-permute-done | bytes 73760 | tf_op jit(solution)/shard_map/ppermute | solution.py:26
  16.6 0.7 collective-permute-done.5
  17.3 0.2 broadcast_select_fusion.5
  17.6 0.1 reshape.43
  17.7 0.0 copy-start
  17.7 0.3 fusion
  18.0 0.1 reshape.44.rev_ref
  18.1 5.2 %shard_map.55 = (bf16[4608,512]{1,0:T(8,128)(2,1)S(1)}, bf16[4608,512]{1,0:T(8,128)(2,1)S(1)}) custom-call(s32[36]{0:T(128)S(1)} %and_select_fusion.3.shift_ref, f32[18]{0:T(128)S(1)} %reshape.42.weight_ref, f32[36,1,1024]{2,1,0:T(1,128)S(1)} %reshape.44.rev_ref), custom_call_target="tpu_custom_call" | custom-call | bytes 9437184 | tf_op jit(solution)/shard_map/pallas_call | solution.py:55
  23.4 3.0 %fusion.18 = f32[256,512]{1,0:T(8,128)S(1)} fusion(bf16[18,256,512]{2,1,0:T(8,128)(2,1)S(1)} %bitcast.40, bf16[18,1024,256]{2,1,0:T(8,128)(2,1)} %bitcast.47, s32[]{:T(128)S(6)} %select_n.155), kind=kOutput, calls=%fused_computation.19 | convolution fusion | flops 1207959552 | bytes 7602180 | tf_op jit(solution)/shard_map/rpt,rtn->pn/dot_general | solution.py:92
  26.4 2.0 %collective-permute-start.6 = (f32[256,512]{1,0:T(8,128)S(1)}, f32[256,512]{1,0:T(8,128)S(1)}, u32[]{:S(2)}, u32[]{:S(2)}) collective-permute-start(f32[256,512]{1,0:T(8,128)S(1)} %fusion.18), channel_id=1, source_target_pairs={{0,32},{16,48},{32,64},{48,80},{64,96},{80,112},{96,0},{112,16},{1... | collective-permute-start | bytes 1572872 | tf_op jit(solution)/shard_map/ppermute | solution.py:107
  28.4 0.0 copy-done
  28.4 1.4 %fusion.21 = f32[256,512]{1,0:T(8,128)S(1)} fusion(bf16[18,256,512]{2,1,0:T(8,128)(2,1)S(1)} %bitcast.36, bf16[18,1024,256]{2,1,0:T(8,128)(2,1)S(1)} %bitcast.48, s32[]{:T(128)S(6)} %select_n.176), kind=kOutput, calls=%fused_computation.20 | convolution fusion | flops 1207959552 | bytes 7602180 | tf_op jit(solution)/shard_map/rpt,rtn->pn/dot_general | solution.py:92
  29.8 1.4 %fusion.24 = f32[256,512]{1,0:T(8,128)S(1)} fusion(bf16[18,256,512]{2,1,0:T(8,128)(2,1)S(1)} %bitcast.41, bf16[18,1024,256]{2,1,0:T(8,128)(2,1)S(1)} %bitcast.49, s32[]{:T(128)S(6)} %select_n.178), kind=kOutput, calls=%fused_computation.21 | convolution fusion | flops 1207959552 | bytes 7602180 | tf_op jit(solution)/shard_map/rpt,rtn->pn/dot_general | solution.py:92
  31.2 2.2 %collective-permute-start.10 = (f32[256,512]{1,0:T(8,128)S(1)}, f32[256,512]{1,0:T(8,128)S(1)}, u32[]{:S(2)}, u32[]{:S(2)}) collective-permute-start(f32[256,512]{1,0:T(8,128)S(1)} %fusion.21), channel_id=1, source_target_pairs={{0,96},{16,112},{32,0},{48,16},{64,32},{80,48},{96,64},{112,80},{1... | collective-permute-start | bytes 1572872 | tf_op jit(solution)/shard_map/ppermute | solution.py:107
  33.4 7.0 %collective-permute-done.6 = f32[256,512]{1,0:T(8,128)S(1)} collective-permute-done((f32[256,512]{1,0:T(8,128)S(1)}, f32[256,512]{1,0:T(8,128)S(1)}, u32[]{:S(2)}, u32[]{:S(2)}) %collective-permute-start.6) | collective-permute-done | bytes 524320 | tf_op jit(solution)/shard_map/ppermute | solution.py:107
  40.4 0.1 add.211
  40.5 0.1 collective-permute-start.7
  40.5 1.4 %fusion.27 = f32[256,512]{1,0:T(8,128)S(1)} fusion(bf16[18,256,512]{2,1,0:T(8,128)(2,1)S(1)} %bitcast.37, bf16[18,1024,256]{2,1,0:T(8,128)(2,1)S(1)} %bitcast.50, s32[]{:T(128)S(6)} %select_n.180), kind=kOutput, calls=%fused_computation.22 | convolution fusion | flops 1207959552 | bytes 7602180 | tf_op jit(solution)/shard_map/rpt,rtn->pn/dot_general | solution.py:92
  41.9 1.4 %fusion.30 = f32[256,512]{1,0:T(8,128)S(1)} fusion(bf16[18,256,512]{2,1,0:T(8,128)(2,1)S(1)} %bitcast.42, bf16[18,1024,256]{2,1,0:T(8,128)(2,1)S(1)} %bitcast.51, s32[]{:T(128)S(6)} %select_n.182), kind=kOutput, calls=%fused_computation.23 | convolution fusion | flops 1207959552 | bytes 7602180 | tf_op jit(solution)/shard_map/rpt,rtn->pn/dot_general | solution.py:92
  43.3 0.0 collective-permute-done.10
  43.3 0.1 add.226
  43.4 3.3 %collective-permute-start.11 = (f32[256,512]{1,0:T(8,128)S(1)}, f32[256,512]{1,0:T(8,128)S(1)}, u32[]{:S(2)}, u32[]{:S(2)}) collective-permute-start(f32[256,512]{1,0:T(8,128)S(1)} %add.226), channel_id=1, source_target_pairs={{0,96},{16,112},{32,0},{48,16},{64,32},{80,48},{96,64},{112,80},{1... | collective-permute-start | bytes 1572872 | tf_op jit(solution)/shard_map/ppermute | solution.py:113
  46.7 6.0 %collective-permute-done.7 = f32[256,512]{1,0:T(8,128)S(1)} collective-permute-done((f32[256,512]{1,0:T(8,128)S(1)}, f32[256,512]{1,0:T(8,128)S(1)}, u32[]{:S(2)}, u32[]{:S(2)}) %collective-permute-start.7) | collective-permute-done | bytes 524320 | tf_op jit(solution)/shard_map/ppermute | solution.py:113
  52.7 0.1 add.216
  52.8 0.1 collective-permute-start.8
  52.9 1.4 %fusion.33 = f32[256,512]{1,0:T(8,128)S(1)} fusion(bf16[18,256,512]{2,1,0:T(8,128)(2,1)S(1)} %bitcast.38, bf16[18,1024,256]{2,1,0:T(8,128)(2,1)S(1)} %bitcast.52, s32[]{:T(128)S(6)} %select_n.184), kind=kOutput, calls=%fused_computation.24 | convolution fusion | flops 1207959552 | bytes 7602180 | tf_op jit(solution)/shard_map/rpt,rtn->pn/dot_general | solution.py:92
  54.3 1.4 %fusion.36 = f32[256,512]{1,0:T(8,128)S(1)} fusion(bf16[18,256,512]{2,1,0:T(8,128)(2,1)S(1)} %bitcast.43, bf16[18,1024,256]{2,1,0:T(8,128)(2,1)S(1)} %bitcast.53, s32[]{:T(128)S(6)} %select_n.186), kind=kOutput, calls=%fused_computation.25 | convolution fusion | flops 1207959552 | bytes 7602180 | tf_op jit(solution)/shard_map/rpt,rtn->pn/dot_general | solution.py:92
  55.6 0.0 collective-permute-done.11
  55.6 0.1 add.227
  55.7 3.3 %collective-permute-start.12 = (f32[256,512]{1,0:T(8,128)S(1)}, f32[256,512]{1,0:T(8,128)S(1)}, u32[]{:S(2)}, u32[]{:S(2)}) collective-permute-start(f32[256,512]{1,0:T(8,128)S(1)} %add.227), channel_id=1, source_target_pairs={{0,96},{16,112},{32,0},{48,16},{64,32},{80,48},{96,64},{112,80},{1... | collective-permute-start | bytes 1572872 | tf_op jit(solution)/shard_map/ppermute | solution.py:113
  59.0 5.1 %collective-permute-done.8 = f32[256,512]{1,0:T(8,128)S(1)} collective-permute-done((f32[256,512]{1,0:T(8,128)S(1)}, f32[256,512]{1,0:T(8,128)S(1)}, u32[]{:S(2)}, u32[]{:S(2)}) %collective-permute-start.8) | collective-permute-done | bytes 524320 | tf_op jit(solution)/shard_map/ppermute | solution.py:113
  64.1 0.1 add.221
  64.2 2.4 %collective-permute-start.9 = (f32[128,512]{1,0:T(8,128)S(1)}, f32[128,512]{1,0:T(8,128)S(1)}, u32[]{:S(2)}, u32[]{:S(2)}) collective-permute-start(f32[128,512]{1,0:T(8,128)S(1)} %get-tuple-element.43), channel_id=1, source_target_pairs={{0,16},{16,0},{32,48},{48,32},{64,80},{80,64},{96,112},{112,96},{1... | collective-permute-start | bytes 786440 | tf_op jit(solution)/shard_map/ppermute | solution.py:118
  66.6 1.4 %fusion.39 = f32[256,512]{1,0:T(8,128)S(1)} fusion(bf16[18,256,512]{2,1,0:T(8,128)(2,1)S(1)} %bitcast.39, bf16[18,1024,256]{2,1,0:T(8,128)(2,1)S(1)} %bitcast.54, s32[]{:T(128)S(6)} %select_n.191), kind=kOutput, calls=%fused_computation.26 | convolution fusion | flops 1207959552 | bytes 7602180 | tf_op jit(solution)/shard_map/rpt,rtn->pn/dot_general | solution.py:92
  68.0 0.0 collective-permute-done.12
  68.0 0.1 add.230
  68.1 1.3 %collective-permute-start.13 = (f32[128,512]{1,0:T(8,128)S(1)}, f32[128,512]{1,0:T(8,128)S(1)}, u32[]{:S(2)}, u32[]{:S(2)}) collective-permute-start(f32[128,512]{1,0:T(8,128)S(1)} %get-tuple-element.45), channel_id=1, source_target_pairs={{0,16},{16,0},{32,48},{48,32},{64,80},{80,64},{96,112},{112,96},{1... | collective-permute-start | bytes 786440 | tf_op jit(solution)/shard_map/ppermute | solution.py:118
  69.5 0.4 rev.13
  69.8 0.4 rev.15
  70.2 2.5 %collective-permute-done.9 = f32[128,512]{1,0:T(8,128)S(1)} collective-permute-done((f32[128,512]{1,0:T(8,128)S(1)}, f32[128,512]{1,0:T(8,128)S(1)}, u32[]{:S(2)}, u32[]{:S(2)}) %collective-permute-start.9) | collective-permute-done | bytes 262176 | tf_op jit(solution)/shard_map/ppermute | solution.py:118
  72.7 0.4 rev.14
  73.2 2.9 %collective-permute-done.13 = f32[128,512]{1,0:T(8,128)S(1)} collective-permute-done((f32[128,512]{1,0:T(8,128)S(1)}, f32[128,512]{1,0:T(8,128)S(1)}, u32[]{:S(2)}, u32[]{:S(2)}) %collective-permute-start.13) | collective-permute-done | bytes 262176 | tf_op jit(solution)/shard_map/ppermute | solution.py:118
  76.1 0.4 rev.16
  76.6 1.2 %copy.10 = f32[128,2,512]{2,1,0:T(2,128)} copy(f32[128,2,512]{2,0,1:T(8,128)S(1)} %pad_maximum_fusion) | data formatting | bytes 1048576 | tf_op jit(solution)/shard_map/stack | solution.py:120
  (9 shorter events, 0.3 us)
Async XLA Ops:
  0.0 4.0 %collective-permute-start = (bf16[2,6,3,1024]{3,0,2,1:T(2,128)(2,1)}, bf16[2,6,3,1024]{3,0,2,1:T(2,128)(2,1)S(1)}, u32[]{:S(2)}, u32[]{:S(2)}) collective-permute-start(bf16[2,6,3,1024]{3,0,2,1:T(2,128)(2,1)} %bitcast.44), channel_id=1, source_target_pairs={{0,3},{1,0},{2,1},{3,2},{4,7},{5,4},{6,5},{7,6},{8,11},{9,8},{10,9... | collective-permute-start | bytes 221192 | tf_op jit(solution)/shard_map/ppermute | solution.py:26
  1.0 5.5 %collective-permute-start.1 = (bf16[2,6,3,1024]{3,0,2,1:T(2,128)(2,1)}, bf16[2,6,3,1024]{3,0,2,1:T(2,128)(2,1)S(1)}, u32[]{:S(2)}, u32[]{:S(2)}) collective-permute-start(bf16[2,6,3,1024]{3,0,2,1:T(2,128)(2,1)} %bitcast.45), channel_id=1, source_target_pairs={{0,2},{1,3},{2,0},{3,1},{4,6},{5,7},{6,4},{7,5},{8,10},{9,11},{10,... | collective-permute-start | bytes 221192 | tf_op jit(solution)/shard_map/ppermute | solution.py:26
  1.6 4.9 %collective-permute-start.2 = (bf16[2,6,3,1024]{3,0,2,1:T(2,128)(2,1)}, bf16[2,6,3,1024]{3,0,2,1:T(2,128)(2,1)S(1)}, u32[]{:S(2)}, u32[]{:S(2)}) collective-permute-start(bf16[2,6,3,1024]{3,0,2,1:T(2,128)(2,1)} %bitcast.46), channel_id=1, source_target_pairs={{0,1},{1,2},{2,3},{3,0},{4,5},{5,6},{6,7},{7,4},{8,9},{9,10},{10,1... | collective-permute-start | bytes 221192 | tf_op jit(solution)/shard_map/ppermute | solution.py:26
  7.6 5.1 %collective-permute-start.3 = (bf16[2,6,3,1024]{3,0,2,1:T(2,128)(2,1)S(1)}, bf16[2,6,3,1024]{3,0,2,1:T(2,128)(2,1)S(1)}, u32[]{:S(2)}, u32[]{:S(2)}) collective-permute-start(bf16[2,6,3,1024]{3,0,2,1:T(2,128)(2,1)S(1)} %broadcast_select_fusion.4), channel_id=1, source_target_pairs={{0,12},{1,13},{2,14},{3,15},{4,0},{5,1},{6,2},{7,3},{8,4},{9,5},{1... | collective-permute-start | bytes 221192 | tf_op jit(solution)/shard_map/ppermute | solution.py:26
  10.7 5.9 %collective-permute-start.4 = (bf16[2,6,3,1024]{3,0,2,1:T(2,128)(2,1)S(1)}, bf16[2,6,3,1024]{3,0,2,1:T(2,128)(2,1)S(1)}, u32[]{:S(2)}, u32[]{:S(2)}) collective-permute-start(bf16[2,6,3,1024]{3,0,2,1:T(2,128)(2,1)S(1)} %broadcast_select_fusion.4), channel_id=1, source_target_pairs={{0,8},{1,9},{2,10},{3,11},{4,12},{5,13},{6,14},{7,15},{8,0},{9,1},... | collective-permute-start | bytes 221192 | tf_op jit(solution)/shard_map/ppermute | solution.py:26
  11.3 6.0 %collective-permute-start.5 = (bf16[2,6,3,1024]{3,0,2,1:T(2,128)(2,1)S(1)}, bf16[2,6,3,1024]{3,0,2,1:T(2,128)(2,1)S(1)}, u32[]{:S(2)}, u32[]{:S(2)}) collective-permute-start(bf16[2,6,3,1024]{3,0,2,1:T(2,128)(2,1)S(1)} %broadcast_select_fusion.4), channel_id=1, source_target_pairs={{0,4},{1,5},{2,6},{3,7},{4,8},{5,9},{6,10},{7,11},{8,12},{9,13},{1... | collective-permute-start | bytes 221192 | tf_op jit(solution)/shard_map/ppermute | solution.py:26
  17.7 10.7 %copy-start = (bf16[1024,6,3,256]{3,0,2,1:T(8,128)(2,1)S(1)}, bf16[1024,6,3,256]{3,0,2,1:T(8,128)(2,1)}, u32[]{:S(2)}) copy-start(bf16[1024,6,3,256]{3,0,2,1:T(8,128)(2,1)} %param.5) | copy-start | bytes 28311556
  26.4 14.0 %collective-permute-start.6 = (f32[256,512]{1,0:T(8,128)S(1)}, f32[256,512]{1,0:T(8,128)S(1)}, u32[]{:S(2)}, u32[]{:S(2)}) collective-permute-start(f32[256,512]{1,0:T(8,128)S(1)} %fusion.18), channel_id=1, source_target_pairs={{0,32},{16,48},{32,64},{48,80},{64,96},{80,112},{96,0},{112,16},{1... | collective-permute-start | bytes 1572872 | tf_op jit(solution)/shard_map/ppermute | solution.py:107
  31.2 12.1 %collective-permute-start.10 = (f32[256,512]{1,0:T(8,128)S(1)}, f32[256,512]{1,0:T(8,128)S(1)}, u32[]{:S(2)}, u32[]{:S(2)}) collective-permute-start(f32[256,512]{1,0:T(8,128)S(1)} %fusion.21), channel_id=1, source_target_pairs={{0,96},{16,112},{32,0},{48,16},{64,32},{80,48},{96,64},{112,80},{1... | collective-permute-start | bytes 1572872 | tf_op jit(solution)/shard_map/ppermute | solution.py:107
  40.5 12.2 %collective-permute-start.7 = (f32[256,512]{1,0:T(8,128)S(1)}, f32[256,512]{1,0:T(8,128)S(1)}, u32[]{:S(2)}, u32[]{:S(2)}) collective-permute-start(f32[256,512]{1,0:T(8,128)S(1)} %add.211), channel_id=1, source_target_pairs={{0,32},{16,48},{32,64},{48,80},{64,96},{80,112},{96,0},{112,16},{1... | collective-permute-start | bytes 1572872 | tf_op jit(solution)/shard_map/ppermute | solution.py:113
  43.4 12.2 %collective-permute-start.11 = (f32[256,512]{1,0:T(8,128)S(1)}, f32[256,512]{1,0:T(8,128)S(1)}, u32[]{:S(2)}, u32[]{:S(2)}) collective-permute-start(f32[256,512]{1,0:T(8,128)S(1)} %add.226), channel_id=1, source_target_pairs={{0,96},{16,112},{32,0},{48,16},{64,32},{80,48},{96,64},{112,80},{1... | collective-permute-start | bytes 1572872 | tf_op jit(solution)/shard_map/ppermute | solution.py:113
  52.8 11.3 %collective-permute-start.8 = (f32[256,512]{1,0:T(8,128)S(1)}, f32[256,512]{1,0:T(8,128)S(1)}, u32[]{:S(2)}, u32[]{:S(2)}) collective-permute-start(f32[256,512]{1,0:T(8,128)S(1)} %add.216), channel_id=1, source_target_pairs={{0,32},{16,48},{32,64},{48,80},{64,96},{80,112},{96,0},{112,16},{1... | collective-permute-start | bytes 1572872 | tf_op jit(solution)/shard_map/ppermute | solution.py:113
  55.7 12.3 %collective-permute-start.12 = (f32[256,512]{1,0:T(8,128)S(1)}, f32[256,512]{1,0:T(8,128)S(1)}, u32[]{:S(2)}, u32[]{:S(2)}) collective-permute-start(f32[256,512]{1,0:T(8,128)S(1)} %add.227), channel_id=1, source_target_pairs={{0,96},{16,112},{32,0},{48,16},{64,32},{80,48},{96,64},{112,80},{1... | collective-permute-start | bytes 1572872 | tf_op jit(solution)/shard_map/ppermute | solution.py:113
  64.2 8.5 %collective-permute-start.9 = (f32[128,512]{1,0:T(8,128)S(1)}, f32[128,512]{1,0:T(8,128)S(1)}, u32[]{:S(2)}, u32[]{:S(2)}) collective-permute-start(f32[128,512]{1,0:T(8,128)S(1)} %get-tuple-element.43), channel_id=1, source_target_pairs={{0,16},{16,0},{32,48},{48,32},{64,80},{80,64},{96,112},{112,96},{1... | collective-permute-start | bytes 786440 | tf_op jit(solution)/shard_map/ppermute | solution.py:118
  68.1 8.0 %collective-permute-start.13 = (f32[128,512]{1,0:T(8,128)S(1)}, f32[128,512]{1,0:T(8,128)S(1)}, u32[]{:S(2)}, u32[]{:S(2)}) collective-permute-start(f32[128,512]{1,0:T(8,128)S(1)} %get-tuple-element.45), channel_id=1, source_target_pairs={{0,16},{16,0},{32,48},{48,32},{64,80},{80,64},{96,112},{112,96},{1... | collective-permute-start | bytes 786440 | tf_op jit(solution)/shard_map/ppermute | solution.py:118
